TPU v7x, 128 devices: a whole 4x4x4 slice. The times are simulated.
128 devices in a mesh: lat: 4 (over z), lon: 32 (over x, y, core).
Axes of the slice: x: 4, y: 4, z: 4, core: 2. Of those that a mesh axis runs over, the one named last changes fastest.
Arguments:
- column_state: float32 [4, 32, 128, 4096], P(None, None, 'lat', 'lon'), may hold values from -6 to 6
- wind_speed: float32 [2, 32, 128, 4096], P(None, None, 'lat', 'lon'), may hold values from -0.4 to 0.4
- diffusivity: float32 [32, 128, 4096], P(None, 'lat', 'lon'), may hold values from 0.02 to 0.2
- batch_index: int32 [4, 131072, 1], P('lat', 'lon'), may hold values from 0 to 31; in each aligned block of 4096 rows (0 to 4095, 4096 to 8191, ..., all dimensions but the last counted through in order) at most 256 rows name the same one
- input_weight: bfloat16 [32, 512, 128], P('lon'), may hold values from -0.5 to 0.5
- middle_weight: bfloat16 [32, 3, 512, 512], P('lon'), may hold values from -0.25 to 0.25
- output_weight: bfloat16 [32, 128, 512], P('lon'), may hold values from -0.25 to 0.25
Outputs:
- new_state: float32 [4, 32, 128, 4096], P(None, None, 'lat', 'lon')
Inputs may be any that keep to these rules, and one draw needn't show every extreme that they name: `batch_index`: within the columns of one device no batch is named more than 256 times; some device names some batch exactly 256 times.
All inputs are finite; a program needn't handle non-finite values.
Results may differ from a plain program's by a relative error of at most 0.0012.
Values may be sent and summed in bfloat16 or wider, within the bound.
No kernel may reach another device: no remote copies, remote signals or barrier semaphores. Data moves between devices by JAX's collectives and lax.ppermute only.
A program may use at most 128 MiB of HBM per device.

v0:
```python
import jax
import jax.numpy as jnp
from jax import lax
from jax.sharding import PartitionSpec as P


def padded(block, sides, width, periodic):
    for axis, dim in sides:
        count = lax.axis_size(axis)
        forward = [(i, i + 1) for i in range(count - 1)]
        if periodic:
            forward.append((count - 1, 0))
        backward = [(target, source) for source, target in forward]
        low = lax.ppermute(
            lax.slice_in_dim(block, block.shape[dim] - width, None, axis=dim), axis, forward
        )
        high = lax.ppermute(lax.slice_in_dim(block, 0, width, axis=dim), axis, backward)
        block = jnp.concatenate([low, block, high], axis=dim)
    return block


def advect(extended, east_wind, north_wind, spread):
    middle = extended[:, :, 1:-1, 1:-1]
    north_cell = extended[:, :, 2:, 1:-1]
    south_cell = extended[:, :, :-2, 1:-1]
    east_cell = extended[:, :, 1:-1, 2:]
    west_cell = extended[:, :, 1:-1, :-2]
    return (
        middle
        - 0.5 * east_wind * (east_cell - west_cell)
        - 0.5 * north_wind * (north_cell - south_cell)
        + spread * (east_cell + west_cell + north_cell + south_cell - 4.0 * middle)
    )


def local(
    column_state, wind_speed, diffusivity, batch_index, input_weight, middle_weight, output_weight
):
    num_vars, levels, lat_cells, lon_cells = column_state.shape
    current = column_state
    for sweep_index in range(2):
        widened = padded(current, (("lat", 2),), 1, False)
        widened = padded(widened, (("lon", 3),), 1, True)
        current = advect(widened, wind_speed[0], wind_speed[1], diffusivity)
    features = num_vars * levels
    column_count = lat_cells * lon_cells
    columns = current.reshape(features, column_count).astype(jnp.bfloat16)
    experts = lax.axis_size("lon")
    capacity = 2 * column_count // experts
    targets_all = batch_index.reshape(column_count)
    onehot = (targets_all[:, None] == jnp.arange(experts, dtype=jnp.int32)[None, :]).astype(
        jnp.int32
    )
    position = jnp.sum((jnp.cumsum(onehot, axis=0) - onehot) * onehot, axis=1)
    targets = targets_all * capacity + position
    packed = jnp.zeros((features, experts * capacity), jnp.bfloat16).at[:, targets].set(columns)
    packed = packed.reshape(features, experts, capacity)
    received = lax.all_to_all(packed, "lon", split_axis=1, concat_axis=1, tiled=True)
    layout = received.shape
    flattened = received.reshape(layout[0], layout[1] * layout[2])
    hidden = jax.nn.silu(
        jnp.dot(input_weight[0], flattened, preferred_element_type=jnp.float32)
    ).astype(jnp.bfloat16)
    for layer_index in range(middle_weight.shape[1]):
        hidden = jax.nn.silu(
            jnp.dot(middle_weight[0, layer_index], hidden, preferred_element_type=jnp.float32)
        ).astype(jnp.bfloat16)
    result = jnp.dot(output_weight[0], hidden, preferred_element_type=jnp.float32).astype(
        jnp.bfloat16
    )
    answered = result.reshape(layout)
    returned = lax.all_to_all(answered, "lon", split_axis=1, concat_axis=1, tiled=True)
    tendency = returned.reshape(features, -1)[:, targets]
    return current + tendency.astype(jnp.float32).reshape(current.shape)


def solution(mesh):
    in_specs = (
        P(None, None, "lat", "lon"),
        P(None, None, "lat", "lon"),
        P(None, "lat", "lon"),
        P("lat", "lon", None),
        P("lon", None, None),
        P("lon", None, None, None),
        P("lon", None, None),
    )
    out_specs = P(None, None, "lat", "lon")
    return jax.shard_map(local, mesh=mesh, in_specs=in_specs, out_specs=out_specs, check_vma=False)
```

profile of v0, /device:TPU:1, one launch (start us, length us, event | category | flops | bytes accessed | tf_op | source)
XLA Modules:
  0.0 236.3 jit_solution(3957530726129885997)
XLA Ops:
  2.0 4.4 %collective-permute-start = (f32[4,32,1,128]{3,2,1,0:T(1,128)}, f32[4,32,1,128]{3,2,1,0:T(1,128)S(1)}, u32[]{:S(2)}, u32[]{:S(2)}) collective-permute-start(f32[4,32,1,128]{3,2,1,0:T(1,128)} %get-tuple-element.13), channel_id=1, source_target_pairs={{0,32},{32,64},{64,96},{1,33},{33,65},{65,97},{2,34},{34,66},{66,9... | collective-permute-start | bytes 196616 | tf_op jit(solution)/shard_map/ppermute | solution.py:14
  11.5 16.3 %reduce-window.6 = s32[32,32,128]{2,1,0:T(8,128)S(1)} reduce-window(s32[32,32,128]{2,1,0:T(8,128)} %fusion.43, s32[]{:T(128)} %constant.20.clone.1), window={size=1x1x128 pad=0_0x0_0x127_0}, to_apply=%region_0.0 | reduce-window | flops 16646144 | bytes 1048580 | tf_op jit(solution)/shard_map/reduce-window
  29.2 2.4 fusion.53
  31.5 2.7 %copy.14 = f32[4,32,34,1]{2,1,3,0:T(8,128)S(1)} copy(f32[4,32,34,1]{3,2,1,0:T(8,128)} %get-tuple-element.9) | data formatting | bytes 34816 | tf_op jit(solution)/shard_map/slice | solution.py:15
  41.4 2.5 %copy.15 = f32[4,32,34,1]{3,2,1,0:T(8,128)} copy(f32[4,32,34,1]{2,1,3,0:T(8,128)S(1)} %collective-permute-done.3) | data formatting | bytes 34816 | tf_op jit(solution)/shard_map/ppermute | solution.py:14
  43.9 2.5 %copy.13 = f32[4,32,34,1]{3,2,1,0:T(8,128)} copy(f32[4,32,34,1]{2,1,3,0:T(8,128)S(1)} %collective-permute-done.2) | data formatting | bytes 34816 | tf_op jit(solution)/shard_map/ppermute | solution.py:17
  46.5 7.8 %multiply_add_fusion.1 = f32[4,32,32,128]{3,2,1,0:T(8,128)S(1)} fusion(f32[4,32,32,128]{3,2,1,0:T(8,128)} %param.7, f32[4,32,1,128]{3,2,1,0:T(1,128)S(1)} %collective-permute-done.1, f32[4,32,1,128]{3,2,1,0:T(1,128)S(1)} %collective-permute-done, f32[4,32,34,1]{3,2,1,0:T(8,128)} %copy.13, f32[4,32,34,1]{3,2,1,0:T(8,128)} %copy.15, f32[32,32,128]{2,1,0:T(8,128)} %param.9, ...), kind=kLoop, calls=%fused_computation.52 | loop fusion | flops 11010048 | bytes 5933056 | tf_op jit(solution)/shard_map/add | solution.py:29
  55.7 4.8 %collective-permute-start.4 = (f32[4,32,1,128]{3,2,1,0:T(1,128)S(1)}, f32[4,32,1,128]{3,2,1,0:T(1,128)S(1)}, u32[]{:S(2)}, u32[]{:S(2)}) collective-permute-start(f32[4,32,1,128]{3,2,1,0:T(1,128)S(1)} %get-tuple-element.12), channel_id=1, source_target_pairs={{0,32},{32,64},{64,96},{1,33},{33,65},{65,97},{2,34},{34,66},{66,9... | collective-permute-start | bytes 196616 | tf_op jit(solution)/shard_map/ppermute | solution.py:14
  62.2 3.1 %fusion.52 = (f32[4,32,34,1]{3,2,1,0:T(8,128)}, f32[4,32,34,1]{3,2,1,0:T(8,128)}) fusion(f32[4,32,34,128]{3,2,1,0:T(8,128)S(1)} %pad_maximum_fusion.1), kind=kLoop, calls=%fused_computation.83 | loop fusion | bytes 69632 | tf_op jit(solution)/shard_map/slice | solution.py:17
  65.3 3.4 %copy.16 = f32[4,32,34,1]{2,1,3,0:T(8,128)} copy(f32[4,32,34,1]{3,2,1,0:T(8,128)} %get-tuple-element.7) | data formatting | bytes 34816 | tf_op jit(solution)/shard_map/slice | solution.py:17
  68.7 2.7 %copy.18 = f32[4,32,34,1]{2,1,3,0:T(8,128)S(1)} copy(f32[4,32,34,1]{3,2,1,0:T(8,128)} %get-tuple-element.8) | data formatting | bytes 34816 | tf_op jit(solution)/shard_map/slice | solution.py:15
  72.2 6.6 %collective-permute-start.6 = (f32[4,32,34,1]{2,1,3,0:T(8,128)}, f32[4,32,34,1]{2,1,3,0:T(8,128)}, u32[]{:S(2)}, u32[]{:S(2)}) collective-permute-start(f32[4,32,34,1]{2,1,3,0:T(8,128)} %copy.16), channel_id=1, source_target_pairs={{1,0},{2,1},{3,2},{4,3},{5,4},{6,5},{7,6},{8,7},{9,8},{10,9},{11,1... | collective-permute-start | bytes 52232 | tf_op jit(solution)/shard_map/ppermute | solution.py:17
  80.1 3.4 %copy.17 = f32[4,32,34,1]{3,2,1,0:T(8,128)} copy(f32[4,32,34,1]{2,1,3,0:T(8,128)} %collective-permute-done.6) | data formatting | bytes 34816 | tf_op jit(solution)/shard_map/ppermute | solution.py:17
  83.4 3.4 %copy.19 = f32[4,32,34,1]{3,2,1,0:T(8,128)} copy(f32[4,32,34,1]{2,1,3,0:T(8,128)} %collective-permute-done.7) | data formatting | bytes 34816 | tf_op jit(solution)/shard_map/ppermute | solution.py:14
  86.8 6.0 %fusion.51 = (bf16[4,32,32,128]{3,2,1,0:T(8,128)(2,1)S(1)}, f32[4,32,32,128]{3,2,1,0:T(8,128)}) fusion(f32[4,32,32,128]{3,2,1,0:T(8,128)S(1)} %multiply_add_fusion.1, f32[32,32,128]{2,1,0:T(8,128)} %param.9, f32[4,32,1,128]{3,2,1,0:T(1,128)S(1)} %collective-permute-done.4, f32[4,32,1,128]{3,2,1,0:T(1,128)S(1)} %collective-permute-done.5, ...), kind=kLoop, calls=%fused_computation.82 | loop fusion | flops 11534336 | bytes 6981632 | tf_op jit(solution)/shard_map/convert_element_type | solution.py:47
  93.9 11.5 %scatter_custom_fusion = bf16[128,8192]{0,1:T(8,128)(2,1)S(1)} fusion(s32[4096]{0:T(1024)S(1)} %bitcast.143, bf16[128,4096]{0,1:T(8,128)(2,1)S(1)} %copy.20, bf16[]{:T(256)} %constant.18.clone.1), kind=kCustom, calls=%fused_computation.54 | custom fusion | bytes 3145730 | tf_op jit(solution)/shard_map/scatter | solution.py:56
  105.4 40.4 %all_to_all.10 = bf16[128,32,256]{0,2,1:T(8,128)(2,1)} all-to-all(bf16[128,32,256]{0,2,1:T(8,128)(2,1)S(1)} %bitcast.132), channel_id=1, replica_groups=mesh['lat'=4,'lon'=32] {'lon'}, dimensions={1} | all-to-all | bytes 4194304 | tf_op jit(solution)/shard_map/all_to_all | solution.py:58
  145.8 13.5 %fusion.20 = f32[8192,512]{1,0:T(8,128)} fusion(bf16[128,8192]{0,1:T(8,128)(2,1)} %bitcast.137, bf16[1,3,512,512]{3,2,1,0:T(8,128)(2,1)} %param.12, bf16[1,512,128]{2,1,0:T(8,128)(2,1)S(1)} %copy-done), kind=kOutput, calls=%fused_computation.29 | convolution fusion | flops 5389680640 | bytes 19529728 | tf_op jit(solution)/shard_map/dot_general | solution.py:66
  159.3 11.6 %fusion.18 = f32[8192,512]{1,0:T(8,128)} fusion(f32[8192,512]{1,0:T(8,128)} %fusion.20, bf16[1,3,512,512]{3,2,1,0:T(8,128)(2,1)S(1)} %copy-done.8), kind=kOutput, calls=%fused_computation.28 | convolution fusion | flops 4315938816 | bytes 34078720 | tf_op jit(solution)/shard_map/dot_general | solution.py:66
  170.9 15.0 %convolution_convert_fusion = bf16[8192,128]{1,0:T(8,128)(2,1)} fusion(f32[8192,512]{1,0:T(8,128)} %fusion.18, bf16[1,3,512,512]{3,2,1,0:T(8,128)(2,1)S(1)} %copy-done.8, bf16[1,128,512]{2,1,0:T(8,128)(2,1)S(1)} %copy-done.9), kind=kOutput, calls=%fused_computation.26 | convolution fusion | flops 5411700736 | bytes 19529728 | tf_op jit(solution)/shard_map/dot_general | solution.py:68
  185.9 4.0 %all-to-all-start.1 = ((bf16[128,32,256]{0,2,1:T(8,128)(2,1)}), bf16[128,32,256]{0,2,1:T(8,128)(2,1)S(1)}, u32[]{:S(2)}, u32[]{:S(2)}) async-start(bf16[128,32,256]{0,2,1:T(8,128)(2,1)} %bitcast.136), calls=%async_computation.1 | async-start | bytes 4194304 | tf_op jit(solution)/shard_map/all_to_all | solution.py:72
  189.9 28.3 %all-to-all-done.1 = bf16[128,32,256]{0,2,1:T(8,128)(2,1)S(1)} async-done(((bf16[128,32,256]{0,2,1:T(8,128)(2,1)}), bf16[128,32,256]{0,2,1:T(8,128)(2,1)S(1)}, u32[]{:S(2)}, u32[]{:S(2)}) %all-to-all-start.1) | async-done | bytes 2097184 | tf_op jit(solution)/shard_map/all_to_all | solution.py:72
  218.2 12.1 %gather_fusion = bf16[4096,128]{1,0:T(8,128)(2,1)S(1)} fusion(bf16[128,8192]{0,1:T(8,128)(2,1)S(1)} %bitcast.130, s32[4096]{0:T(1024)S(1)} %broadcast_clamp_fusion), kind=kCustom, calls=%fused_computation | custom fusion | bytes 2113536 | tf_op jit(solution)/shard_map/gather | solution.py:73
  232.3 2.1 copy.24
  (51 shorter events, 25.8 us)
Async XLA Ops:
  0.0 145.8 %copy-start = (bf16[1,512,128]{2,1,0:T(8,128)(2,1)S(1)}, bf16[1,512,128]{2,1,0:T(8,128)(2,1)}, u32[]{:S(2)}) copy-start(bf16[1,512,128]{2,1,0:T(8,128)(2,1)} %param.11) | copy-start | bytes 393220
  2.0 26.8 %collective-permute-start = (f32[4,32,1,128]{3,2,1,0:T(1,128)}, f32[4,32,1,128]{3,2,1,0:T(1,128)S(1)}, u32[]{:S(2)}, u32[]{:S(2)}) collective-permute-start(f32[4,32,1,128]{3,2,1,0:T(1,128)} %get-tuple-element.13), channel_id=1, source_target_pairs={{0,32},{32,64},{64,96},{1,33},{33,65},{65,97},{2,34},{34,66},{66,9... | collective-permute-start | bytes 196616 | tf_op jit(solution)/shard_map/ppermute | solution.py:14
  6.3 22.4 %collective-permute-start.1 = (f32[4,32,1,128]{3,2,1,0:T(1,128)S(1)}, f32[4,32,1,128]{3,2,1,0:T(1,128)S(1)}, u32[]{:S(2)}, u32[]{:S(2)}) collective-permute-start(f32[4,32,1,128]{3,2,1,0:T(1,128)S(1)} %get-tuple-element.14), channel_id=1, source_target_pairs={{32,0},{64,32},{96,64},{33,1},{65,33},{97,65},{34,2},{66,34},{98,6... | collective-permute-start | bytes 196616 | tf_op jit(solution)/shard_map/ppermute | solution.py:17
  7.6 21.1 %copy-start.2 = (f32[4,32,32,128]{3,2,1,0:T(8,128)S(1)}, f32[4,32,32,128]{3,2,1,0:T(8,128)}, u32[]{:S(2)}) copy-start(f32[4,32,32,128]{3,2,1,0:T(8,128)} %param.7) | copy-start | bytes 6291460
  27.8 1.0 copy-start.5
  35.3 8.7 %collective-permute-start.2 = (f32[4,32,34,1]{2,1,3,0:T(8,128)S(1)}, f32[4,32,34,1]{2,1,3,0:T(8,128)S(1)}, u32[]{:S(2)}, u32[]{:S(2)}) collective-permute-start(f32[4,32,34,1]{2,1,3,0:T(8,128)S(1)} %copy.12), channel_id=1, source_target_pairs={{1,0},{2,1},{3,2},{4,3},{5,4},{6,5},{7,6},{8,7},{9,8},{10,9},{11,1... | collective-permute-start | bytes 52232 | tf_op jit(solution)/shard_map/ppermute | solution.py:17
  36.3 5.1 %collective-permute-start.3 = (f32[4,32,34,1]{2,1,3,0:T(8,128)S(1)}, f32[4,32,34,1]{2,1,3,0:T(8,128)S(1)}, u32[]{:S(2)}, u32[]{:S(2)}) collective-permute-start(f32[4,32,34,1]{2,1,3,0:T(8,128)S(1)} %copy.14), channel_id=1, source_target_pairs={{0,1},{1,2},{2,3},{3,4},{4,5},{5,6},{6,7},{7,8},{8,9},{9,10},{10,1... | collective-permute-start | bytes 52232 | tf_op jit(solution)/shard_map/ppermute | solution.py:14
  39.6 6.8 %copy-start.4 = (f32[32,32,128]{2,1,0:T(8,128)S(1)}, f32[32,32,128]{2,1,0:T(8,128)}, u32[]{:S(2)}) copy-start(f32[32,32,128]{2,1,0:T(8,128)} %get-tuple-element.16) | copy-start | bytes 1572868
  46.5 14.0 %copy-start.6 = (s32[32,32,128]{2,1,0:T(8,128)S(1)}, s32[32,32,128]{2,1,0:T(8,128)}, u32[]{:S(2)}) copy-start(s32[32,32,128]{2,1,0:T(8,128)} %broadcast_add_fusion) | copy-start | bytes 1572868
  46.5 14.0 %copy-start.7 = (s32[1,4096,1]{1,2,0:T(1,128)S(1)}, s32[1,4096,1]{1,2,0:T(1,128)}, u32[]{:S(2)}) copy-start(s32[1,4096,1]{1,2,0:T(1,128)} %param.10) | copy-start | bytes 49156
  54.4 6.5 %collective-permute-start.5 = (f32[4,32,1,128]{3,2,1,0:T(1,128)S(1)}, f32[4,32,1,128]{3,2,1,0:T(1,128)S(1)}, u32[]{:S(2)}, u32[]{:S(2)}) collective-permute-start(f32[4,32,1,128]{3,2,1,0:T(1,128)S(1)} %get-tuple-element.11), channel_id=1, source_target_pairs={{32,0},{64,32},{96,64},{33,1},{65,33},{97,65},{34,2},{66,34},{98,6... | collective-permute-start | bytes 196616 | tf_op jit(solution)/shard_map/ppermute | solution.py:17
  55.7 6.1 %collective-permute-start.4 = (f32[4,32,1,128]{3,2,1,0:T(1,128)S(1)}, f32[4,32,1,128]{3,2,1,0:T(1,128)S(1)}, u32[]{:S(2)}, u32[]{:S(2)}) collective-permute-start(f32[4,32,1,128]{3,2,1,0:T(1,128)S(1)} %get-tuple-element.12), channel_id=1, source_target_pairs={{0,32},{32,64},{64,96},{1,33},{33,65},{65,97},{2,34},{34,66},{66,9... | collective-permute-start | bytes 196616 | tf_op jit(solution)/shard_map/ppermute | solution.py:14
  71.4 12.0 %collective-permute-start.7 = (f32[4,32,34,1]{2,1,3,0:T(8,128)S(1)}, f32[4,32,34,1]{2,1,3,0:T(8,128)}, u32[]{:S(2)}, u32[]{:S(2)}) collective-permute-start(f32[4,32,34,1]{2,1,3,0:T(8,128)S(1)} %copy.18), channel_id=1, source_target_pairs={{0,1},{1,2},{2,3},{3,4},{4,5},{5,6},{6,7},{7,8},{8,9},{9,10},{10,1... | collective-permute-start | bytes 52232 | tf_op jit(solution)/shard_map/ppermute | solution.py:14
  72.2 7.8 %collective-permute-start.6 = (f32[4,32,34,1]{2,1,3,0:T(8,128)}, f32[4,32,34,1]{2,1,3,0:T(8,128)}, u32[]{:S(2)}, u32[]{:S(2)}) collective-permute-start(f32[4,32,34,1]{2,1,3,0:T(8,128)} %copy.16), channel_id=1, source_target_pairs={{1,0},{2,1},{3,2},{4,3},{5,4},{6,5},{7,6},{8,7},{9,8},{10,9},{11,1... | collective-permute-start | bytes 52232 | tf_op jit(solution)/shard_map/ppermute | solution.py:17
  145.8 13.5 %copy-start.8 = (bf16[1,3,512,512]{3,2,1,0:T(8,128)(2,1)S(1)}, bf16[1,3,512,512]{3,2,1,0:T(8,128)(2,1)}, u32[]{:S(2)}) copy-start(bf16[1,3,512,512]{3,2,1,0:T(8,128)(2,1)} %param.12) | copy-start | bytes 4718596
  159.3 11.6 %copy-start.9 = (bf16[1,128,512]{2,1,0:T(8,128)(2,1)S(1)}, bf16[1,128,512]{2,1,0:T(8,128)(2,1)}, u32[]{:S(2)}) copy-start(bf16[1,128,512]{2,1,0:T(8,128)(2,1)} %param.13) | copy-start | bytes 393220
  185.9 32.3 %all-to-all-start.1 = ((bf16[128,32,256]{0,2,1:T(8,128)(2,1)}), bf16[128,32,256]{0,2,1:T(8,128)(2,1)S(1)}, u32[]{:S(2)}, u32[]{:S(2)}) async-start(bf16[128,32,256]{0,2,1:T(8,128)(2,1)} %bitcast.136), calls=%async_computation.1 | async-start | bytes 4194304 | tf_op jit(solution)/shard_map/all_to_all | solution.py:72
  232.3 2.2 copy-start.3
  234.4 1.9 copy-start.1
where the time goes:
time: 238 us; the launch traced here: 236 us
  local copies, waits for them, and re-layouts  58.7 us (25%)
  blocking collectives  40.4 us (17%)
  matrix products  40.1 us (17%)
  other arithmetic  39.3 us (17%)
  waiting for transfers between devices  32.2 us (14%)
  starting transfers between devices  25.4 us (11%)
    all_to_all x1, blocking collectives, local(): lax.all_to_all(packed, 'lon', split_axis=1, concat_axis=1, tiled=True)  40.4 us
    all_to_all x1, waiting for transfers between devices, local(): lax.all_to_all(answered, 'lon', split_axis=1, concat_axis=1, tiled=True)  28.3 us
    dot_general x2, matrix products, local(): jnp.dot(middle_weight[0, layer_index], hidden, preferred_element_type=jnp...  25.1 us
    another operation x3, other arithmetic  18.6 us
    dot_general x1, matrix products, local(): jnp.dot(output_weight[0], hidden, preferred_element_type=jnp.float32)  15 us
    gather x1, local copies, waits for them, and re-layouts, local(): tendency = returned.reshape(features, -1)[:, targets]  12.1 us
    scatter x1, local copies, waits for them, and re-layouts, local(): jnp.zeros((features, experts * capacity), jnp.bfloat16).at[:, targets]  11.5 us
    ppermute x4, starting transfers between devices, padded(): lax.ppermute(lax.slice_in_dim(block, block.shape[dim] - width, None, axis...  11.3 us
  transfers between devices with their start and end apart: 9, of which 4 were waited for; matrix products, arithmetic and copies ran while one was open for 12% of the time, Pallas kernels for 0%

commit v1 on v0

--- a/solution.py
+++ b/solution.py
@@ -4,19 +4,32 @@
 from jax.sharding import PartitionSpec as P
 
 
-def padded(block, sides, width, periodic):
-    for axis, dim in sides:
-        count = lax.axis_size(axis)
-        forward = [(i, i + 1) for i in range(count - 1)]
-        if periodic:
-            forward.append((count - 1, 0))
-        backward = [(target, source) for source, target in forward]
-        low = lax.ppermute(
-            lax.slice_in_dim(block, block.shape[dim] - width, None, axis=dim), axis, forward
-        )
-        high = lax.ppermute(lax.slice_in_dim(block, 0, width, axis=dim), axis, backward)
-        block = jnp.concatenate([low, block, high], axis=dim)
-    return block
+def shifted(axis, pieces, periodic):
+    count = lax.axis_size(axis)
+    forward = [(i, i + 1) for i in range(count - 1)]
+    if periodic:
+        forward.append((count - 1, 0))
+    backward = [(target, source) for source, target in forward]
+    low_parts, high_parts = pieces
+    low = lax.ppermute(low_parts, axis, forward)
+    high = lax.ppermute(high_parts, axis, backward)
+    return low, high
+
+
+def pack(arrays):
+    flat = jnp.concatenate([a.reshape(-1) for a in arrays])
+    return flat
+
+
+def unpack(flat, shapes):
+    out, start = [], 0
+    for shape in shapes:
+        size = 1
+        for s in shape:
+            size *= s
+        out.append(flat[start:start + size].reshape(shape))
+        start += size
+    return out
 
 
 def advect(extended, east_wind, north_wind, spread):
@@ -33,25 +46,66 @@
     )
 
 
+def widen(q, fields):
+    v, l, rows, cols = q.shape
+    top = [q[:, :, rows - 2:, :]] + [f[:, rows - 1:, :] for f in fields]
+    bottom = [q[:, :, :2, :]] + [f[:, :1, :] for f in fields]
+    lat_shapes = [a.shape for a in top]
+    low, high = shifted("lat", (pack(top), pack(bottom)), False)
+    low, high = unpack(low, lat_shapes), unpack(high, lat_shapes)
+    q = jnp.concatenate([low[0], q, high[0]], axis=2)
+    fields = [jnp.concatenate([lo, f, hi], axis=1) for lo, f, hi in zip(low[1:], fields, high[1:])]
+    east = [jnp.swapaxes(q[..., cols - 2:], -1, -2)] + [jnp.swapaxes(f[..., cols - 1:], -1, -2) for f in fields]
+    west = [jnp.swapaxes(q[..., :2], -1, -2)] + [jnp.swapaxes(f[..., :1], -1, -2) for f in fields]
+    lon_shapes = [a.shape for a in east]
+    low, high = shifted("lon", (pack(east), pack(west)), True)
+    low, high = unpack(low, lon_shapes), unpack(high, lon_shapes)
+    q = jnp.concatenate([jnp.swapaxes(low[0], -1, -2), q, jnp.swapaxes(high[0], -1, -2)], axis=3)
+    fields = [
+        jnp.concatenate([jnp.swapaxes(lo, -1, -2), f, jnp.swapaxes(hi, -1, -2)], axis=2)
+        for lo, f, hi in zip(low[1:], fields, high[1:])
+    ]
+    return q, fields
+
+
+def positions(targets_all, experts):
+    count = targets_all.shape[0]
+    block = 128
+    onehot = (targets_all[:, None] == jnp.arange(experts, dtype=jnp.int32)[None, :]).astype(
+        jnp.bfloat16
+    )
+    blocks = onehot.reshape(count // block, block, experts)
+    rows = jnp.arange(block, dtype=jnp.int32)
+    before = (rows[:, None] > rows[None, :]).astype(jnp.bfloat16)
+    within = jnp.einsum("ij,bje->bie", before, blocks, preferred_element_type=jnp.float32)
+    totals = jnp.sum(blocks.astype(jnp.float32), axis=1)
+    offsets = jnp.cumsum(totals, axis=0) - totals
+    ranks = within + offsets[:, None, :]
+    position = jnp.sum(ranks * blocks.astype(jnp.float32), axis=2)
+    return position.reshape(count).astype(jnp.int32)
+
+
 def local(
     column_state, wind_speed, diffusivity, batch_index, input_weight, middle_weight, output_weight
 ):
     num_vars, levels, lat_cells, lon_cells = column_state.shape
-    current = column_state
-    for sweep_index in range(2):
-        widened = padded(current, (("lat", 2),), 1, False)
-        widened = padded(widened, (("lon", 3),), 1, True)
-        current = advect(widened, wind_speed[0], wind_speed[1], diffusivity)
+    q, (east_wind, north_wind, spread) = widen(
+        column_state, [wind_speed[0], wind_speed[1], diffusivity]
+    )
+    first = advect(q, east_wind, north_wind, spread)
+    lat_index = lax.axis_index("lat")
+    lat_count = lax.axis_size("lat")
+    row = jnp.arange(lat_cells + 2)[None, None, :, None]
+    outside = ((row == 0) & (lat_index == 0)) | ((row == lat_cells + 1) & (lat_index == lat_count - 1))
+    first = jnp.where(outside, 0.0, first)
+    current = advect(first, east_wind[:, 1:-1, 1:-1], north_wind[:, 1:-1, 1:-1], spread[:, 1:-1, 1:-1])
     features = num_vars * levels
     column_count = lat_cells * lon_cells
     columns = current.reshape(features, column_count).astype(jnp.bfloat16)
     experts = lax.axis_size("lon")
     capacity = 2 * column_count // experts
     targets_all = batch_index.reshape(column_count)
-    onehot = (targets_all[:, None] == jnp.arange(experts, dtype=jnp.int32)[None, :]).astype(
-        jnp.int32
-    )
-    position = jnp.sum((jnp.cumsum(onehot, axis=0) - onehot) * onehot, axis=1)
+    position = positions(targets_all, experts)
     targets = targets_all * capacity + position
     packed = jnp.zeros((features, experts * capacity), jnp.bfloat16).at[:, targets].set(columns)
     packed = packed.reshape(features, experts, capacity)

time: 238 us -> 222 us (0.933)
  starting transfers between devices: 25.4 us -> 13 us
  local copies, waits for them, and re-layouts: 58.7 us -> 67 us
  other arithmetic: 39.3 us -> 32.5 us
  blocking collectives: 40.4 us -> 36.7 us
    another operation x3 -> x1, other arithmetic: 18.6 us -> 0.05 us  [positions(): offsets = jnp.cumsum(totals, axis=0) - totals]
    transpose x0 -> x5, local copies, waits for them, and re-layouts: none -> 12.7 us  [the longest x2 5.73 us: widen(): jnp.swapaxes(q[..., cols - 2:], -1, -2)]
    ppermute x8 -> x4, starting transfers between devices: 21.5 us -> 9.06 us  [the longest x2 7.75 us: shifted(): low = lax.ppermute(low_parts, axis, forward)]
    ppermute x4 -> x0, local copies, waits for them, and re-layouts: 11.8 us -> none  [the longest x2 5.91 us: padded(): lax.ppermute(lax.slice_in_dim(block, block.shape[dim] - width, None, axis...]
    slice x9 -> x15, local copies, waits for them, and re-layouts: 18.1 us -> 7.76 us  [the longest x8 3.54 us: unpack(): out.append(flat[start:start + size].reshape(shape))]
    concatenate x2 -> x8, other arithmetic: 0.78 us -> 10.5 us  [the longest x1 5.25 us: widen(): jnp.concatenate([jnp.swapaxes(low[0], -1, -2), q, jnp.swapaxes(high[0], -...]
    select_n x0 -> x1, other arithmetic: none -> 8.9 us  [local(): first = jnp.where(outside, 0.0, first)]
    add x1 -> x0, other arithmetic: 7.8 us -> none  [advect(): middle - 0.5 * east_wind * (east_cell - west_cell)]
  transfers between devices with their start and end apart: 9 -> 5, of which waited for: 4 -> 4; matrix products, arithmetic and copies ran while one was open for 12% -> 3% of each run, Pallas kernels for 0% -> 0%
where the time goes in v1:
time: 222 us
  local copies, waits for them, and re-layouts  67 us (30%)
  matrix products  40.4 us (18%)
  blocking collectives  36.7 us (17%)
  other arithmetic  32.5 us (15%)
  waiting for transfers between devices  31.6 us (14%)
  starting transfers between devices  13 us (6%)
    all_to_all x1, blocking collectives, local(): lax.all_to_all(packed, 'lon', split_axis=1, concat_axis=1, tiled=True)  36.7 us
    all_to_all x1, waiting for transfers between devices, local(): lax.all_to_all(answered, 'lon', split_axis=1, concat_axis=1, tiled=True)  28.3 us
    dot_general x2, matrix products, local(): jnp.dot(middle_weight[0, layer_index], hidden, preferred_element_type=jnp...  25.1 us
    dot_general x1, matrix products, local(): jnp.dot(output_weight[0], hidden, preferred_element_type=jnp.float32)  15 us
    gather x1, local copies, waits for them, and re-layouts, local(): tendency = returned.reshape(features, -1)[:, targets]  12.1 us
    scatter x1, local copies, waits for them, and re-layouts, local(): jnp.zeros((features, experts * capacity), jnp.bfloat16).at[:, targets]  11.5 us
    select_n x1, other arithmetic, local(): first = jnp.where(outside, 0.0, first)  8.9 us
    ppermute x2, starting transfers between devices, shifted(): low = lax.ppermute(low_parts, axis, forward)  7.75 us
  transfers between devices with their start and end apart: 5, of which 4 were waited for; matrix products, arithmetic and copies ran while one was open for 3% of the time, Pallas kernels for 0%

profile of v1, /device:TPU:1, one launch (start us, length us, event | category | flops | bytes accessed | tf_op | source)
XLA Modules:
  0.0 221.6 jit_solution(11655371338631515701)
XLA Ops:
  2.4 2.5 %multiply_bitcast_fusion.1 = (f32[32,32,128]{2,1,0:T(8,128)}, f32[32,32,128]{2,1,0:T(8,128)}, f32[32,32,128]{2,1,0:T(8,128)S(1)}, f32[32,32,128]{2,1,0:T(8,128)S(1)}) fusion(f32[2,32,32,128]{3,2,1,0:T(8,128)} %param.8), kind=kLoop, calls=%fused_computation.75 | loop fusion | flops 262144 | bytes 3145728 | tf_op jit(solution)/shard_map/mul | solution.py:43
  6.2 5.0 %collective-permute-start = (f32[45056]{0:T(1024)S(1)}, f32[45056]{0:T(1024)S(1)}, u32[]{:S(2)}, u32[]{:S(2)}) collective-permute-start(f32[45056]{0:T(1024)S(1)} %pad_maximum_fusion.12), channel_id=1, source_target_pairs={{0,32},{32,64},{64,96},{1,33},{33,65},{65,97},{2,34},{34,66},{66,9... | collective-permute-start | bytes 540680 | tf_op jit(solution)/shard_map/ppermute | solution.py:14
  24.2 2.3 %slice_bitcast_fusion.1 = (f32[4,32,2,36]{2,3,1,0:T(8,128)}, f32[4,32,2,36]{2,3,1,0:T(8,128)S(1)}) fusion(f32[4,32,36,128]{3,2,1,0:T(8,128)S(1)} %pad_maximum_fusion.7), kind=kLoop, calls=%fused_computation.40 | loop fusion | bytes 147456 | tf_op jit(solution)/shard_map/transpose | solution.py:58
  26.6 3.4 %copy.10 = f32[4,32,2,36]{3,2,1,0:T(2,128)} copy(f32[4,32,2,36]{2,3,1,0:T(8,128)} %get-tuple-element.13) | data formatting | bytes 73728 | tf_op jit(solution)/shard_map/transpose | solution.py:58
  29.9 1.7 reshape.253
  33.1 2.7 %collective-permute-start.2 = (f32[12480]{0:T(1024)}, f32[12480]{0:T(1024)}, u32[]{:S(2)}, u32[]{:S(2)}) collective-permute-start(f32[12480]{0:T(1024)} %concatenate.64), channel_id=1, source_target_pairs={{0,1},{1,2},{2,3},{3,4},{4,5},{5,6},{6,7},{7,8},{8,9},{9,10},{10,1... | collective-permute-start | bytes 149768 | tf_op jit(solution)/shard_map/ppermute | solution.py:14
  51.4 1.9 copy.13
  53.4 3.4 %copy.12 = f32[4,32,36,2]{3,2,1,0:T(8,128)} copy(f32[4,32,36,2]{2,3,1,0:T(2,128)} %bitcast.162) | data formatting | bytes 73728 | tf_op jit(solution)/shard_map/transpose | solution.py:63
  56.8 3.4 %pad_maximum_fusion.8 = f32[32,34,130]{2,1,0:T(8,128)} fusion(f32[32,34,1]{2,1,0:T(8,128)} %transpose_reshape.13, f32[32,1,128]{2,1,0:T(1,128)} %bitcast.173, f32[32,32,128]{2,1,0:T(8,128)} %param.9, f32[32,1,128]{2,1,0:T(1,128)} %bitcast.175, f32[32,34,1]{2,1,0:T(8,128)} %transpose_reshape.12), kind=kLoop, calls=%fused_computation.47 | loop fusion | flops 565760 | bytes 1131520 | tf_op jit(solution)/shard_map/concatenate | solution.py:65
  60.2 5.2 %pad_maximum_fusion.6 = f32[4,32,36,132]{3,2,1,0:T(8,128)S(1)} fusion(f32[4,32,36,2]{3,2,1,0:T(8,128)S(1)} %copy.13, f32[4,32,2,128]{3,2,1,0:T(2,128)S(1)} %bitcast.153, f32[4,32,32,128]{3,2,1,0:T(8,128)} %param.7, f32[4,32,2,128]{3,2,1,0:T(2,128)S(1)} %bitcast.156, f32[4,32,36,2]{3,2,1,0:T(8,128)S(1)} %copy-done.2), kind=kLoop, calls=%fused_computation.36 | loop fusion | flops 2433024 | bytes 4866048 | tf_op jit(solution)/shard_map/concatenate | solution.py:63
  65.6 2.9 %maximum_multiply_fusion = (f32[32,34,130]{2,1,0:T(8,128)}, f32[32,34,130]{2,1,0:T(8,128)}) fusion(f32[32,34,1]{2,1,0:T(8,128)S(1)} %copy-done.9, f32[32,1,128]{2,1,0:T(1,128)S(1)} %bitcast.167, f32[32,32,128]{2,1,0:T(8,128)S(1)} %copy-done.7, f32[32,1,128]{2,1,0:T(1,128)S(1)} %bitcast.171, f32[32,34,1]{2,1,0:T(8,128)S(1)} %copy-done.10, ...), kind=kLoop, calls=%fused_computation.45 | loop fusion | flops 1414400 | bytes 2263040 | tf_op jit(solution)/shard_map/mul | solution.py:43
  68.5 8.9 %add_select_fusion = f32[4,32,34,130]{3,2,1,0:T(8,128)S(1)} fusion(f32[4,32,36,132]{3,2,1,0:T(8,128)S(1)} %pad_maximum_fusion.6, f32[4,32,36,2]{3,2,1,0:T(8,128)S(1)} %copy.13, f32[4,32,2,128]{3,2,1,0:T(2,128)S(1)} %bitcast.154, f32[4,32,32,128]{3,2,1,0:T(8,128)S(1)} %copy-done.4, f32[4,32,2,128]{3,2,1,0:T(2,128)S(1)} %bitcast.157, ...), kind=kLoop, calls=%fused_computation.37 | loop fusion | flops 11315200 | bytes 13182498 | tf_op jit(solution)/shard_map/jit(_where)/select_n | solution.py:100
  77.5 4.3 %fusion.54 = (bf16[4,32,32,128]{3,2,1,0:T(8,128)(2,1)S(1)}, f32[4,32,32,128]{3,2,1,0:T(8,128)}) fusion(f32[32,32,128]{2,1,0:T(8,128)S(1)} %copy-done.8, f32[4,32,34,130]{3,2,1,0:T(8,128)S(1)} %add_select_fusion, f32[32,32,128]{2,1,0:T(8,128)} %get-tuple-element.18, f32[32,32,128]{2,1,0:T(8,128)S(1)} %copy-done.13), kind=kLoop, calls=%fused_computation.92 | loop fusion | flops 7340032 | bytes 15204352 | tf_op jit(solution)/shard_map/convert_element_type | solution.py:104
  82.9 11.5 %scatter_custom_fusion = bf16[128,8192]{0,1:T(8,128)(2,1)S(1)} fusion(s32[4096]{0:T(1024)S(1)} %bitcast.178, bf16[128,4096]{0,1:T(8,128)(2,1)S(1)} %copy.22, bf16[]{:T(256)} %constant.11.clone.1), kind=kCustom, calls=%fused_computation.53 | custom fusion | bytes 3145730 | tf_op jit(solution)/shard_map/scatter | solution.py:110
  94.4 36.7 %all_to_all.10 = bf16[128,32,256]{0,2,1:T(8,128)(2,1)} all-to-all(bf16[128,32,256]{0,2,1:T(8,128)(2,1)S(1)} %bitcast.148), channel_id=1, replica_groups=mesh['lat'=4,'lon'=32] {'lon'}, dimensions={1} | all-to-all | bytes 4194304 | tf_op jit(solution)/shard_map/all_to_all | solution.py:112
  131.1 13.5 %fusion.20 = f32[8192,512]{1,0:T(8,128)} fusion(bf16[128,8192]{0,1:T(8,128)(2,1)} %bitcast.159, bf16[1,3,512,512]{3,2,1,0:T(8,128)(2,1)} %param.12, bf16[1,512,128]{2,1,0:T(8,128)(2,1)S(1)} %copy-done), kind=kOutput, calls=%fused_computation.29 | convolution fusion | flops 5389680640 | bytes 19529728 | tf_op jit(solution)/shard_map/dot_general | solution.py:120
  144.6 11.6 %fusion.18 = f32[8192,512]{1,0:T(8,128)} fusion(f32[8192,512]{1,0:T(8,128)} %fusion.20, bf16[1,3,512,512]{3,2,1,0:T(8,128)(2,1)S(1)} %copy-done.27), kind=kOutput, calls=%fused_computation.28 | convolution fusion | flops 4315938816 | bytes 34078720 | tf_op jit(solution)/shard_map/dot_general | solution.py:120
  156.2 15.0 %convolution_convert_fusion = bf16[8192,128]{1,0:T(8,128)(2,1)} fusion(f32[8192,512]{1,0:T(8,128)} %fusion.18, bf16[1,3,512,512]{3,2,1,0:T(8,128)(2,1)S(1)} %copy-done.27, bf16[1,128,512]{2,1,0:T(8,128)(2,1)S(1)} %copy-done.28), kind=kOutput, calls=%fused_computation.26 | convolution fusion | flops 5411700736 | bytes 19529728 | tf_op jit(solution)/shard_map/dot_general | solution.py:122
  171.2 3.9 %all-to-all-start.1 = ((bf16[128,32,256]{0,2,1:T(8,128)(2,1)}), bf16[128,32,256]{0,2,1:T(8,128)(2,1)S(1)}, u32[]{:S(2)}, u32[]{:S(2)}) async-start(bf16[128,32,256]{0,2,1:T(8,128)(2,1)} %bitcast.158), calls=%async_computation.1 | async-start | bytes 4194304 | tf_op jit(solution)/shard_map/all_to_all | solution.py:126
  175.2 28.3 %all-to-all-done.1 = bf16[128,32,256]{0,2,1:T(8,128)(2,1)S(1)} async-done(((bf16[128,32,256]{0,2,1:T(8,128)(2,1)}), bf16[128,32,256]{0,2,1:T(8,128)(2,1)S(1)}, u32[]{:S(2)}, u32[]{:S(2)}) %all-to-all-start.1) | async-done | bytes 2097184 | tf_op jit(solution)/shard_map/all_to_all | solution.py:126
  203.5 12.1 %gather_fusion = bf16[4096,128]{1,0:T(8,128)(2,1)S(1)} fusion(bf16[128,8192]{0,1:T(8,128)(2,1)S(1)} %bitcast.146, s32[4096]{0:T(1024)S(1)} %broadcast_clamp_fusion), kind=kCustom, calls=%fused_computation | custom fusion | bytes 2113536 | tf_op jit(solution)/shard_map/gather | solution.py:127
  215.7 1.8 copy.23
  217.6 2.1 copy.25
  219.8 1.8 bitcast_add_fusion
  (114 shorter events, 35.0 us)
Async XLA Ops:
  0.0 131.1 %copy-start = (bf16[1,512,128]{2,1,0:T(8,128)(2,1)S(1)}, bf16[1,512,128]{2,1,0:T(8,128)(2,1)}, u32[]{:S(2)}) copy-start(bf16[1,512,128]{2,1,0:T(8,128)(2,1)} %param.11) | copy-start | bytes 393220
  0.0 11.2 %copy-start.24 = (s32[1,4096,1]{1,2,0:T(1,128)S(1)}, s32[1,4096,1]{1,2,0:T(1,128)}, u32[]{:S(2)}) copy-start(s32[1,4096,1]{1,2,0:T(1,128)} %param.10) | copy-start | bytes 49156
  4.8 15.0 %copy-start.6 = (f32[32,32,128]{2,1,0:T(8,128)}, f32[32,32,128]{2,1,0:T(8,128)S(1)}, u32[]{:S(2)}) copy-start(f32[32,32,128]{2,1,0:T(8,128)S(1)} %get-tuple-element.20) | copy-start | bytes 1572868
  4.9 8.6 %collective-permute-start.1 = (f32[45056]{0:T(1024)S(1)}, f32[45056]{0:T(1024)S(1)}, u32[]{:S(2)}, u32[]{:S(2)}) collective-permute-start(f32[45056]{0:T(1024)S(1)} %pad_maximum_fusion.13), channel_id=1, source_target_pairs={{32,0},{64,32},{96,64},{33,1},{65,33},{97,65},{34,2},{66,34},{98,6... | collective-permute-start | bytes 540680 | tf_op jit(solution)/shard_map/ppermute | solution.py:15
  6.2 8.2 %collective-permute-start = (f32[45056]{0:T(1024)S(1)}, f32[45056]{0:T(1024)S(1)}, u32[]{:S(2)}, u32[]{:S(2)}) collective-permute-start(f32[45056]{0:T(1024)S(1)} %pad_maximum_fusion.12), channel_id=1, source_target_pairs={{0,32},{32,64},{64,96},{1,33},{33,65},{65,97},{2,34},{34,66},{66,9... | collective-permute-start | bytes 540680 | tf_op jit(solution)/shard_map/ppermute | solution.py:14
  13.5 6.3 %copy-start.16 = (f32[4096]{0:T(1024)}, f32[4096]{0:T(1024)S(1)}, u32[]{:S(2)}) copy-start(f32[4096]{0:T(1024)S(1)} %get-tuple-element.32) | copy-start | bytes 49156
  14.4 5.5 %copy-start.18 = (f32[4096]{0:T(1024)}, f32[4096]{0:T(1024)S(1)}, u32[]{:S(2)}) copy-start(f32[4096]{0:T(1024)S(1)} %get-tuple-element.28) | copy-start | bytes 49156
  14.4 5.5 %copy-start.20 = (f32[4096]{0:T(1024)}, f32[4096]{0:T(1024)S(1)}, u32[]{:S(2)}) copy-start(f32[4096]{0:T(1024)S(1)} %get-tuple-element.29) | copy-start | bytes 49156
  14.4 5.5 %copy-start.23 = (f32[4096]{0:T(1024)}, f32[4096]{0:T(1024)S(1)}, u32[]{:S(2)}) copy-start(f32[4096]{0:T(1024)S(1)} %get-tuple-element.27) | copy-start | bytes 49156
  16.6 7.3 %copy-start.3 = (f32[4,32,32,128]{3,2,1,0:T(8,128)S(1)}, f32[4,32,32,128]{3,2,1,0:T(8,128)}, u32[]{:S(2)}) copy-start(f32[4,32,32,128]{3,2,1,0:T(8,128)} %param.7) | copy-start | bytes 6291460
  33.1 6.9 %collective-permute-start.2 = (f32[12480]{0:T(1024)}, f32[12480]{0:T(1024)}, u32[]{:S(2)}, u32[]{:S(2)}) collective-permute-start(f32[12480]{0:T(1024)} %concatenate.64), channel_id=1, source_target_pairs={{0,1},{1,2},{2,3},{3,4},{4,5},{5,6},{6,7},{7,8},{8,9},{9,10},{10,1... | collective-permute-start | bytes 149768 | tf_op jit(solution)/shard_map/ppermute | solution.py:14
  39.4 3.6 %collective-permute-start.3 = (f32[12480]{0:T(1024)S(1)}, f32[12480]{0:T(1024)S(1)}, u32[]{:S(2)}, u32[]{:S(2)}) collective-permute-start(f32[12480]{0:T(1024)S(1)} %concatenate.65), channel_id=1, source_target_pairs={{1,0},{2,1},{3,2},{4,3},{5,4},{6,5},{7,6},{8,7},{9,8},{10,9},{11,1... | collective-permute-start | bytes 149768 | tf_op jit(solution)/shard_map/ppermute | solution.py:15
  60.2 5.3 %copy-start.9 = (f32[32,34,1]{2,1,0:T(8,128)S(1)}, f32[32,34,1]{2,1,0:T(8,128)}, u32[]{:S(2)}) copy-start(f32[32,34,1]{2,1,0:T(8,128)} %concatenate.77) | copy-start | bytes 13060
  60.2 5.3 %copy-start.10 = (f32[32,34,1]{2,1,0:T(8,128)S(1)}, f32[32,34,1]{2,1,0:T(8,128)}, u32[]{:S(2)}) copy-start(f32[32,34,1]{2,1,0:T(8,128)} %concatenate.76) | copy-start | bytes 13060
  60.2 5.3 %copy-start.11 = (f32[32,34,1]{2,1,0:T(8,128)S(1)}, f32[32,34,1]{2,1,0:T(8,128)}, u32[]{:S(2)}) copy-start(f32[32,34,1]{2,1,0:T(8,128)} %concatenate.79) | copy-start | bytes 13060
  60.2 5.3 %copy-start.12 = (f32[32,34,1]{2,1,0:T(8,128)S(1)}, f32[32,34,1]{2,1,0:T(8,128)}, u32[]{:S(2)}) copy-start(f32[32,34,1]{2,1,0:T(8,128)} %concatenate.78) | copy-start | bytes 13060
  60.2 5.3 %copy-start.17 = (f32[4096]{0:T(1024)S(1)}, f32[4096]{0:T(1024)}, u32[]{:S(2)}) copy-start(f32[4096]{0:T(1024)} %copy-done.16) | copy-start | bytes 49156
  60.2 5.3 %copy-start.19 = (f32[4096]{0:T(1024)S(1)}, f32[4096]{0:T(1024)}, u32[]{:S(2)}) copy-start(f32[4096]{0:T(1024)} %copy-done.18) | copy-start | bytes 49156
  60.2 5.3 %copy-start.21 = (f32[4096]{0:T(1024)S(1)}, f32[4096]{0:T(1024)}, u32[]{:S(2)}) copy-start(f32[4096]{0:T(1024)} %copy-done.20) | copy-start | bytes 49156
  68.5 8.9 %copy-start.8 = (f32[32,32,128]{2,1,0:T(8,128)S(1)}, f32[32,32,128]{2,1,0:T(8,128)}, u32[]{:S(2)}) copy-start(f32[32,32,128]{2,1,0:T(8,128)} %param.9) | copy-start | bytes 1572868
  68.5 8.9 %copy-start.13 = (f32[32,32,128]{2,1,0:T(8,128)S(1)}, f32[32,32,128]{2,1,0:T(8,128)}, u32[]{:S(2)}) copy-start(f32[32,32,128]{2,1,0:T(8,128)} %get-tuple-element.17) | copy-start | bytes 1572868
  131.1 13.5 %copy-start.27 = (bf16[1,3,512,512]{3,2,1,0:T(8,128)(2,1)S(1)}, bf16[1,3,512,512]{3,2,1,0:T(8,128)(2,1)}, u32[]{:S(2)}) copy-start(bf16[1,3,512,512]{3,2,1,0:T(8,128)(2,1)} %param.12) | copy-start | bytes 4718596
  144.6 11.6 %copy-start.28 = (bf16[1,128,512]{2,1,0:T(8,128)(2,1)S(1)}, bf16[1,128,512]{2,1,0:T(8,128)(2,1)}, u32[]{:S(2)}) copy-start(bf16[1,128,512]{2,1,0:T(8,128)(2,1)} %param.13) | copy-start | bytes 393220
  171.2 32.3 %all-to-all-start.1 = ((bf16[128,32,256]{0,2,1:T(8,128)(2,1)}), bf16[128,32,256]{0,2,1:T(8,128)(2,1)S(1)}, u32[]{:S(2)}, u32[]{:S(2)}) async-start(bf16[128,32,256]{0,2,1:T(8,128)(2,1)} %bitcast.158), calls=%async_computation.1 | async-start | bytes 4194304 | tf_op jit(solution)/shard_map/all_to_all | solution.py:126
  (10 other events, 29.9 us)

commit v2 on v0

v2 whole, which is shorter than its diff:
```python
import jax
import jax.numpy as jnp
from jax import lax
from jax.experimental import pallas as pl
from jax.experimental.pallas import tpu as pltpu
from jax.sharding import PartitionSpec as P


def neighbours(axis, periodic):
    count = lax.axis_size(axis)
    forward = [(i, i + 1) for i in range(count - 1)]
    if periodic:
        forward.append((count - 1, 0))
    backward = [(target, source) for source, target in forward]
    return forward, backward


FB = 32

def sweep_kernel(q_ref, hn_ref, hs_ref, he_ref, hw_ref, u_ref, v_ref, k_ref, o_ref):
    rows, cols = q_ref.shape[1], q_ref.shape[2]
    row = lax.broadcasted_iota(jnp.int32, (rows, cols), 0)
    lane = lax.broadcasted_iota(jnp.int32, (rows, cols), 1)
    he = he_ref[0]
    hw = hw_ref[0]
    for f in range(FB):
        q = q_ref[f]
        north = jnp.where(row == rows - 1, jnp.broadcast_to(hn_ref[f], (rows, cols)), pltpu.roll(q, rows - 1, 0))
        south = jnp.where(row == 0, jnp.broadcast_to(hs_ref[f], (rows, cols)), pltpu.roll(q, 1, 0))
        east = jnp.where(lane == cols - 1, jnp.broadcast_to(he[:, f:f + 1], (rows, cols)), pltpu.roll(q, cols - 1, 1))
        west = jnp.where(lane == 0, jnp.broadcast_to(hw[:, f:f + 1], (rows, cols)), pltpu.roll(q, 1, 1))
        u = u_ref[f]
        v = v_ref[f]
        k = k_ref[f]
        o_ref[f] = (q - 0.5 * u * (east - west) - 0.5 * v * (north - south)
                    + k * (east + west + north + south - 4.0 * q))


def sweep(q, hn, hs, he, hw, u, v, k):
    feats, rows, cols = q.shape
    levels = u.shape[0]
    nb = feats // FB
    per = levels // FB
    big = pl.BlockSpec((FB, rows, cols), lambda i: (i, 0, 0))
    field = pl.BlockSpec((FB, rows, cols), lambda i: (i % per, 0, 0))
    edge_row = pl.BlockSpec((FB, 1, cols), lambda i: (i, 0, 0))
    edge_col = pl.BlockSpec((1, rows, FB), lambda i: (i, 0, 0))
    return pl.pallas_call(
        sweep_kernel,
        grid=(nb,),
        in_specs=[big, edge_row, edge_row, edge_col, edge_col, field, field, field],
        out_specs=big,
        out_shape=jax.ShapeDtypeStruct(q.shape, q.dtype),
        cost_estimate=pl.CostEstimate(flops=20 * q.size, bytes_accessed=8 * q.size + 12 * u.size, transcendentals=0),
    )(q, hn, hs, he, hw, u, v, k)


def columns_of(edge):
    feats, rows = edge.shape
    return jnp.swapaxes(edge.reshape(feats // FB, FB, rows), 1, 2)


def step(x, u, v, k):
    feats, rows, cols = x.shape
    lat_forward, lat_backward = neighbours("lat", False)
    lon_forward, lon_backward = neighbours("lon", True)
    hn = lax.ppermute(x[:, :1, :], "lat", lat_backward)
    hs = lax.ppermute(x[:, rows - 1:, :], "lat", lat_forward)
    he = lax.ppermute(columns_of(x[:, :, 0]), "lon", lon_backward)
    hw = lax.ppermute(columns_of(x[:, :, cols - 1]), "lon", lon_forward)
    return sweep(x, hn, hs, he, hw, u, v, k)


def positions(targets_all, experts):
    count = targets_all.shape[0]
    block = 128
    onehot = (targets_all[:, None] == jnp.arange(experts, dtype=jnp.int32)[None, :]).astype(
        jnp.bfloat16
    )
    blocks = onehot.reshape(count // block, block, experts)
    rows = jnp.arange(block, dtype=jnp.int32)
    before = (rows[:, None] > rows[None, :]).astype(jnp.bfloat16)
    within = jnp.einsum("ij,bje->bie", before, blocks, preferred_element_type=jnp.float32)
    totals = jnp.sum(blocks.astype(jnp.float32), axis=1)
    offsets = jnp.cumsum(totals, axis=0) - totals
    ranks = within + offsets[:, None, :]
    position = jnp.sum(ranks * blocks.astype(jnp.float32), axis=2)
    return position.reshape(count).astype(jnp.int32)


def local(
    column_state, wind_speed, diffusivity, batch_index, input_weight, middle_weight, output_weight
):
    num_vars, levels, lat_cells, lon_cells = column_state.shape
    features = num_vars * levels
    current = column_state.reshape(features, lat_cells, lon_cells)
    for sweep_index in range(2):
        current = step(current, wind_speed[0], wind_speed[1], diffusivity)
    column_count = lat_cells * lon_cells
    columns = current.reshape(features, column_count).astype(jnp.bfloat16)
    experts = lax.axis_size("lon")
    capacity = 2 * column_count // experts
    targets_all = batch_index.reshape(column_count)
    position = positions(targets_all, experts)
    targets = targets_all * capacity + position
    packed = jnp.zeros((features, experts * capacity), jnp.bfloat16).at[:, targets].set(columns)
    packed = packed.reshape(features, experts, capacity)
    received = lax.all_to_all(packed, "lon", split_axis=1, concat_axis=1, tiled=True)
    layout = received.shape
    flattened = received.reshape(layout[0], layout[1] * layout[2])
    hidden = jax.nn.silu(
        jnp.dot(input_weight[0], flattened, preferred_element_type=jnp.float32)
    ).astype(jnp.bfloat16)
    for layer_index in range(middle_weight.shape[1]):
        hidden = jax.nn.silu(
            jnp.dot(middle_weight[0, layer_index], hidden, preferred_element_type=jnp.float32)
        ).astype(jnp.bfloat16)
    result = jnp.dot(output_weight[0], hidden, preferred_element_type=jnp.float32).astype(
        jnp.bfloat16
    )
    answered = result.reshape(layout)
    returned = lax.all_to_all(answered, "lon", split_axis=1, concat_axis=1, tiled=True)
    tendency = returned.reshape(features, -1)[:, targets]
    return (current + tendency.astype(jnp.float32).reshape(current.shape)).reshape(column_state.shape)


def solution(mesh):
    in_specs = (
        P(None, None, "lat", "lon"),
        P(None, None, "lat", "lon"),
        P(None, "lat", "lon"),
        P("lat", "lon", None),
        P("lon", None, None),
        P("lon", None, None, None),
        P("lon", None, None),
    )
    out_specs = P(None, None, "lat", "lon")
    return jax.shard_map(local, mesh=mesh, in_specs=in_specs, out_specs=out_specs, check_vma=False)
```

time: 238 us -> 197 us (0.83)
  other arithmetic: 39.3 us -> 7.68 us
  local copies, waits for them, and re-layouts: 58.7 us -> 42.8 us
  Pallas kernels: 0 us -> 11.9 us
  blocking collectives: 40.4 us -> 37.8 us
    another operation x3 -> x1, other arithmetic: 18.6 us -> 0.05 us  [positions(): offsets = jnp.cumsum(totals, axis=0) - totals]
    pallas_call x0 -> x2, Pallas kernels: none -> 11.9 us  [sweep(): pl.pallas_call(sweep_kernel, grid=(nb,), in_specs=[big, edge_row, edge_ro...]
    ppermute x4 -> x0, local copies, waits for them, and re-layouts: 11.8 us -> none  [the longest x2 5.91 us: padded(): lax.ppermute(lax.slice_in_dim(block, block.shape[dim] - width, None, axis...]
    slice x9 -> x4, local copies, waits for them, and re-layouts: 18.1 us -> 10.5 us  [the longest x2 7.88 us: step(): hw = lax.ppermute(columns_of(x[:, :, cols - 1]), 'lon', lon_forward)]
    add x2 -> x1, other arithmetic: 9.6 us -> 3.39 us  [local(): current + tendency.astype(jnp.float32).reshape(current.shape)]
    convert_element_type x1, other arithmetic: 6.01 us -> 1.81 us  [local(): columns = current.reshape(features, column_count).astype(jnp.bfloat16)]
    all_to_all x1, blocking collectives: 40.4 us -> 37.8 us  [local(): lax.all_to_all(packed, 'lon', split_axis=1, concat_axis=1, tiled=True)]
  transfers between devices with their start and end apart: 9 -> 9, of which waited for: 4 -> 3; matrix products, arithmetic and copies ran while one was open for 12% -> 4% of each run, Pallas kernels for 0% -> 0%
where the time goes in v2:
time: 197 us; the launch traced here: 196 us
  local copies, waits for them, and re-layouts  42.8 us (22%)
  matrix products  41.1 us (21%)
  blocking collectives  37.8 us (19%)
  waiting for transfers between devices  31.2 us (16%)
  starting transfers between devices  23.5 us (12%)
  Pallas kernels  11.9 us (6%)
  other arithmetic  7.68 us (4%)
    all_to_all x1, blocking collectives, local(): lax.all_to_all(packed, 'lon', split_axis=1, concat_axis=1, tiled=True)  37.8 us
    all_to_all x1, waiting for transfers between devices, local(): lax.all_to_all(answered, 'lon', split_axis=1, concat_axis=1, tiled=True)  28.3 us
    dot_general x2, matrix products, local(): jnp.dot(middle_weight[0, layer_index], hidden, preferred_element_type=jnp...  25.1 us
    dot_general x1, matrix products, local(): jnp.dot(output_weight[0], hidden, preferred_element_type=jnp.float32)  15 us
    gather x1, local copies, waits for them, and re-layouts, local(): tendency = returned.reshape(features, -1)[:, targets]  12.1 us
    pallas_call x2, Pallas kernels, sweep(): pl.pallas_call(sweep_kernel, grid=(nb,), in_specs=[big, edge_row, edge_ro...  11.9 us
    scatter x1, local copies, waits for them, and re-layouts, local(): jnp.zeros((features, experts * capacity), jnp.bfloat16).at[:, targets]  11.6 us
    ppermute x2, starting transfers between devices, step(): hs = lax.ppermute(x[:, rows - 1:, :], 'lat', lat_forward)  8.64 us
  transfers between devices with their start and end apart: 9, of which 3 were waited for; matrix products, arithmetic and copies ran while one was open for 4% of the time, Pallas kernels for 0%

profile of v2, /device:TPU:1, one launch (start us, length us, event | category | flops | bytes accessed | tf_op | source)
XLA Modules:
  0.0 196.3 jit_solution(1350231614135922189)
XLA Ops:
  0.0 1.3 fusion.54
  1.3 4.4 %collective-permute-start.1 = (f32[128,1,128]{2,1,0:T(1,128)S(1)}, f32[128,1,128]{2,1,0:T(1,128)S(1)}, u32[]{:S(2)}, u32[]{:S(2)}) collective-permute-start(f32[128,1,128]{2,1,0:T(1,128)S(1)} %get-tuple-element.11), channel_id=1, source_target_pairs={{0,32},{32,64},{64,96},{1,33},{33,65},{65,97},{2,34},{34,66},{66,9... | collective-permute-start | bytes 196616 | tf_op jit(solution)/shard_map/ppermute | solution.py:68
  5.7 1.3 collective-permute-start
  7.0 3.9 %slice_reduce_fusion.2 = (f32[128,32]{1,0:T(8,128)S(1)}, f32[128,32]{1,0:T(8,128)S(1)}) fusion(f32[128,32,128]{2,1,0:T(8,128)} %bitcast.123), kind=kLoop, calls=%fused_computation.33 | loop fusion | bytes 65536 | tf_op jit(solution)/shard_map/slice | solution.py:70
  14.4 2.2 %slice_bitcast_fusion = (f32[32,32,128]{2,1,0:T(8,128)}, f32[32,32,128]{2,1,0:T(8,128)}) fusion(f32[2,32,32,128]{3,2,1,0:T(8,128)} %param.8), kind=kLoop, calls=%fused_computation.50 | loop fusion | bytes 2097152 | tf_op jit(solution)/shard_map/squeeze | solution.py:98
  18.5 6.0 %shard_map.73.q_ref = f32[128,32,128]{2,1,0:T(8,128)} custom-call(f32[128,32,128]{2,1,0:T(8,128)} %bitcast.124, f32[128,1,128]{2,1,0:T(1,128)} %copy-done.3, f32[128,1,128]{2,1,0:T(1,128)} %copy-done.2, f32[4,32,32]{2,1,0:T(8,128)} %copy-done.4, f32[4,32,32]{2,1,0:T(8,128)} %copy-done.7, f32[32,32,128]{2,1,0:T(8,128)} %get-tuple-element.14.u_ref, ...), custom_call_target="tpu_custom_call" | custom-call | flops 10485760 | bytes 5767168 | tf_op jit(solution)/shard_map/pallas_call | solution.py:48
  24.4 1.3 fusion.53
  25.7 3.9 %slice_reduce_fusion = (f32[128,32]{1,0:T(8,128)S(1)}, f32[128,32]{1,0:T(8,128)S(1)}) fusion(f32[128,32,128]{2,1,0:T(8,128)} %shard_map.73.q_ref), kind=kLoop, calls=%fused_computation.31 | loop fusion | bytes 65536 | tf_op jit(solution)/shard_map/slice | solution.py:70
  29.7 4.3 %collective-permute-start.5 = (f32[128,1,128]{2,1,0:T(1,128)S(1)}, f32[128,1,128]{2,1,0:T(1,128)S(1)}, u32[]{:S(2)}, u32[]{:S(2)}) collective-permute-start(f32[128,1,128]{2,1,0:T(1,128)S(1)} %get-tuple-element.9), channel_id=1, source_target_pairs={{0,32},{32,64},{64,96},{1,33},{33,65},{65,97},{2,34},{34,66},{66,9... | collective-permute-start | bytes 196616 | tf_op jit(solution)/shard_map/ppermute | solution.py:68
  35.4 6.1 %collective-permute-start.6 = (f32[4,32,32]{2,1,0:T(8,128)S(1)}, f32[4,32,32]{2,1,0:T(8,128)S(1)}, u32[]{:S(2)}, u32[]{:S(2)}) collective-permute-start(f32[4,32,32]{2,1,0:T(8,128)S(1)} %bitcast.142), channel_id=1, source_target_pairs={{1,0},{2,1},{3,2},{4,3},{5,4},{6,5},{7,6},{8,7},{9,8},{10,9},{11,1... | collective-permute-start | bytes 49160 | tf_op jit(solution)/shard_map/ppermute | solution.py:69
  42.4 2.0 %collective-permute-done.7.hw_ref = f32[4,32,32]{2,1,0:T(8,128)S(1)} collective-permute-done((f32[4,32,32]{2,1,0:T(8,128)S(1)}, f32[4,32,32]{2,1,0:T(8,128)S(1)}, u32[]{:S(2)}, u32[]{:S(2)}) %collective-permute-start.7) | collective-permute-done | bytes 16416 | tf_op jit(solution)/shard_map/ppermute | solution.py:70
  45.7 6.0 %shard_map.74 = f32[128,32,128]{2,1,0:T(8,128)} custom-call(f32[128,32,128]{2,1,0:T(8,128)} %shard_map.73.q_ref, f32[128,1,128]{2,1,0:T(1,128)} %copy-done.6, f32[128,1,128]{2,1,0:T(1,128)} %copy-done.5, f32[4,32,32]{2,1,0:T(8,128)} %copy-done.8, f32[4,32,32]{2,1,0:T(8,128)} %copy-done.9, f32[32,32,128]{2,1,0:T(8,128)} %get-tuple-element.14.u_ref, ...), custom_call_target="tpu_custom_call" | custom-call | flops 10485760 | bytes 5767168 | tf_op jit(solution)/shard_map/pallas_call | solution.py:48
  51.6 1.8 convert_element_type.57
  54.4 11.6 %scatter_custom_fusion = bf16[128,8192]{0,1:T(8,128)(2,1)S(1)} fusion(s32[4096]{0:T(1024)S(1)} %bitcast.137, bf16[4096,128]{1,0:T(8,128)(2,1)S(1)} %bitcast.129, bf16[]{:T(256)} %constant.7.clone.1), kind=kCustom, calls=%fused_computation.39 | custom fusion | bytes 2097154 | tf_op jit(solution)/shard_map/scatter | solution.py:106
  66.0 37.8 %all_to_all.10 = bf16[128,32,256]{0,2,1:T(8,128)(2,1)} all-to-all(bf16[128,32,256]{0,2,1:T(8,128)(2,1)S(1)} %bitcast.125), channel_id=1, replica_groups=mesh['lat'=4,'lon'=32] {'lon'}, dimensions={1} | all-to-all | bytes 4194304 | tf_op jit(solution)/shard_map/all_to_all | solution.py:108
  103.8 13.5 %fusion.20 = f32[8192,512]{1,0:T(8,128)} fusion(bf16[128,8192]{0,1:T(8,128)(2,1)} %bitcast.128, bf16[1,3,512,512]{3,2,1,0:T(8,128)(2,1)} %param.12, bf16[1,512,128]{2,1,0:T(8,128)(2,1)S(1)} %copy-done), kind=kOutput, calls=%fused_computation.29 | convolution fusion | flops 5389680640 | bytes 19529728 | tf_op jit(solution)/shard_map/dot_general | solution.py:116
  117.3 11.6 %fusion.18 = f32[8192,512]{1,0:T(8,128)} fusion(f32[8192,512]{1,0:T(8,128)} %fusion.20, bf16[1,3,512,512]{3,2,1,0:T(8,128)(2,1)S(1)} %copy-done.11), kind=kOutput, calls=%fused_computation.28 | convolution fusion | flops 4315938816 | bytes 34078720 | tf_op jit(solution)/shard_map/dot_general | solution.py:116
  128.9 15.0 %convolution_convert_fusion = bf16[8192,128]{1,0:T(8,128)(2,1)} fusion(f32[8192,512]{1,0:T(8,128)} %fusion.18, bf16[1,3,512,512]{3,2,1,0:T(8,128)(2,1)S(1)} %copy-done.11, bf16[1,128,512]{2,1,0:T(8,128)(2,1)S(1)} %copy-done.12), kind=kOutput, calls=%fused_computation.26 | convolution fusion | flops 5411700736 | bytes 19529728 | tf_op jit(solution)/shard_map/dot_general | solution.py:118
  143.9 3.9 %all-to-all-start.1 = ((bf16[128,32,256]{0,2,1:T(8,128)(2,1)}), bf16[128,32,256]{0,2,1:T(8,128)(2,1)S(1)}, u32[]{:S(2)}, u32[]{:S(2)}) async-start(bf16[128,32,256]{0,2,1:T(8,128)(2,1)} %bitcast.127), calls=%async_computation.1 | async-start | bytes 4194304 | tf_op jit(solution)/shard_map/all_to_all | solution.py:122
  147.9 28.3 %all-to-all-done.1 = bf16[128,32,256]{0,2,1:T(8,128)(2,1)S(1)} async-done(((bf16[128,32,256]{0,2,1:T(8,128)(2,1)}), bf16[128,32,256]{0,2,1:T(8,128)(2,1)S(1)}, u32[]{:S(2)}, u32[]{:S(2)}) %all-to-all-start.1) | async-done | bytes 2097184 | tf_op jit(solution)/shard_map/all_to_all | solution.py:122
  176.2 12.1 %gather_fusion = bf16[4096,128]{1,0:T(8,128)(2,1)S(1)} fusion(bf16[128,8192]{0,1:T(8,128)(2,1)S(1)} %bitcast.121, s32[4096]{0:T(1024)S(1)} %broadcast_clamp_fusion), kind=kCustom, calls=%fused_computation | custom fusion | bytes 2113536 | tf_op jit(solution)/shard_map/gather | solution.py:123
  188.3 1.5 convert_element_type.68
  189.8 3.1 %copy.29 = f32[128,32,128]{2,1,0:T(8,128)} copy(f32[128,32,128]{0,2,1:T(8,128)} %bitcast.126) | data formatting | bytes 4194304 | tf_op jit(solution)/shard_map/convert_element_type | solution.py:124
  192.9 3.4 %add.57 = f32[128,32,128]{2,1,0:T(8,128)} add(f32[128,32,128]{2,1,0:T(8,128)S(1)} %copy-done.1, f32[128,32,128]{2,1,0:T(8,128)} %copy.29) | non-fusion elementwise | flops 524288 | bytes 6291456 | tf_op jit(solution)/shard_map/add | solution.py:124
  (49 shorter events, 9.8 us)
Async XLA Ops:
  0.0 103.8 %copy-start = (bf16[1,512,128]{2,1,0:T(8,128)(2,1)S(1)}, bf16[1,512,128]{2,1,0:T(8,128)(2,1)}, u32[]{:S(2)}) copy-start(bf16[1,512,128]{2,1,0:T(8,128)(2,1)} %param.11) | copy-start | bytes 393220
  1.3 16.5 %collective-permute-start.1 = (f32[128,1,128]{2,1,0:T(1,128)S(1)}, f32[128,1,128]{2,1,0:T(1,128)S(1)}, u32[]{:S(2)}, u32[]{:S(2)}) collective-permute-start(f32[128,1,128]{2,1,0:T(1,128)S(1)} %get-tuple-element.11), channel_id=1, source_target_pairs={{0,32},{32,64},{64,96},{1,33},{33,65},{65,97},{2,34},{34,66},{66,9... | collective-permute-start | bytes 196616 | tf_op jit(solution)/shard_map/ppermute | solution.py:68
  5.7 35.8 %copy-start.10 = (s32[1,4096,1]{1,2,0:T(1,128)S(1)}, s32[1,4096,1]{1,2,0:T(1,128)}, u32[]{:S(2)}) copy-start(s32[1,4096,1]{1,2,0:T(1,128)} %param.10) | copy-start | bytes 49156
  5.7 12.1 %collective-permute-start = (f32[128,1,128]{2,1,0:T(1,128)S(1)}, f32[128,1,128]{2,1,0:T(1,128)S(1)}, u32[]{:S(2)}, u32[]{:S(2)}) collective-permute-start(f32[128,1,128]{2,1,0:T(1,128)S(1)} %get-tuple-element.12), channel_id=1, source_target_pairs={{32,0},{64,32},{96,64},{33,1},{65,33},{97,65},{34,2},{66,34},{98,6... | collective-permute-start | bytes 196616 | tf_op jit(solution)/shard_map/ppermute | solution.py:67
  11.1 6.7 %collective-permute-start.2 = (f32[4,32,32]{2,1,0:T(8,128)S(1)}, f32[4,32,32]{2,1,0:T(8,128)S(1)}, u32[]{:S(2)}, u32[]{:S(2)}) collective-permute-start(f32[4,32,32]{2,1,0:T(8,128)S(1)} %bitcast.139), channel_id=1, source_target_pairs={{1,0},{2,1},{3,2},{4,3},{5,4},{6,5},{7,6},{8,7},{9,8},{10,9},{11,1... | collective-permute-start | bytes 49160 | tf_op jit(solution)/shard_map/ppermute | solution.py:69
  12.2 5.6 %collective-permute-start.3 = (f32[4,32,32]{2,1,0:T(8,128)S(1)}, f32[4,32,32]{2,1,0:T(8,128)S(1)}, u32[]{:S(2)}, u32[]{:S(2)}) collective-permute-start(f32[4,32,32]{2,1,0:T(8,128)S(1)} %bitcast.140), channel_id=1, source_target_pairs={{0,1},{1,2},{2,3},{3,4},{4,5},{5,6},{6,7},{7,8},{8,9},{9,10},{10,1... | collective-permute-start | bytes 49160 | tf_op jit(solution)/shard_map/ppermute | solution.py:70
  17.8 0.6 copy-start.4
  17.8 0.6 copy-start.7
  17.8 0.6 copy-start.2
  17.8 0.6 copy-start.3
  29.7 14.7 %collective-permute-start.5 = (f32[128,1,128]{2,1,0:T(1,128)S(1)}, f32[128,1,128]{2,1,0:T(1,128)S(1)}, u32[]{:S(2)}, u32[]{:S(2)}) collective-permute-start(f32[128,1,128]{2,1,0:T(1,128)S(1)} %get-tuple-element.9), channel_id=1, source_target_pairs={{0,32},{32,64},{64,96},{1,33},{33,65},{65,97},{2,34},{34,66},{66,9... | collective-permute-start | bytes 196616 | tf_op jit(solution)/shard_map/ppermute | solution.py:68
  34.0 10.4 %collective-permute-start.4 = (f32[128,1,128]{2,1,0:T(1,128)S(1)}, f32[128,1,128]{2,1,0:T(1,128)S(1)}, u32[]{:S(2)}, u32[]{:S(2)}) collective-permute-start(f32[128,1,128]{2,1,0:T(1,128)S(1)} %get-tuple-element.10), channel_id=1, source_target_pairs={{32,0},{64,32},{96,64},{33,1},{65,33},{97,65},{34,2},{66,34},{98,6... | collective-permute-start | bytes 196616 | tf_op jit(solution)/shard_map/ppermute | solution.py:67
  35.4 7.0 %collective-permute-start.6 = (f32[4,32,32]{2,1,0:T(8,128)S(1)}, f32[4,32,32]{2,1,0:T(8,128)S(1)}, u32[]{:S(2)}, u32[]{:S(2)}) collective-permute-start(f32[4,32,32]{2,1,0:T(8,128)S(1)} %bitcast.142), channel_id=1, source_target_pairs={{1,0},{2,1},{3,2},{4,3},{5,4},{6,5},{7,6},{8,7},{9,8},{10,9},{11,1... | collective-permute-start | bytes 49160 | tf_op jit(solution)/shard_map/ppermute | solution.py:69
  41.5 2.9 %collective-permute-start.7 = (f32[4,32,32]{2,1,0:T(8,128)S(1)}, f32[4,32,32]{2,1,0:T(8,128)S(1)}, u32[]{:S(2)}, u32[]{:S(2)}) collective-permute-start(f32[4,32,32]{2,1,0:T(8,128)S(1)} %bitcast.141), channel_id=1, source_target_pairs={{0,1},{1,2},{2,3},{3,4},{4,5},{5,6},{6,7},{7,8},{8,9},{9,10},{10,1... | collective-permute-start | bytes 49160 | tf_op jit(solution)/shard_map/ppermute | solution.py:70
  42.4 2.0 %copy-start.8 = (f32[4,32,32]{2,1,0:T(8,128)}, f32[4,32,32]{2,1,0:T(8,128)S(1)}, u32[]{:S(2)}) copy-start(f32[4,32,32]{2,1,0:T(8,128)S(1)} %collective-permute-done.6.he_ref) | copy-start | bytes 49156
  44.4 0.6 copy-start.9
  44.4 0.6 copy-start.5
  45.0 0.6 copy-start.6
  103.8 13.5 %copy-start.11 = (bf16[1,3,512,512]{3,2,1,0:T(8,128)(2,1)S(1)}, bf16[1,3,512,512]{3,2,1,0:T(8,128)(2,1)}, u32[]{:S(2)}) copy-start(bf16[1,3,512,512]{3,2,1,0:T(8,128)(2,1)} %param.12) | copy-start | bytes 4718596
  117.3 11.6 %copy-start.12 = (bf16[1,128,512]{2,1,0:T(8,128)(2,1)S(1)}, bf16[1,128,512]{2,1,0:T(8,128)(2,1)}, u32[]{:S(2)}) copy-start(bf16[1,128,512]{2,1,0:T(8,128)(2,1)} %param.13) | copy-start | bytes 393220
  143.9 32.2 %all-to-all-start.1 = ((bf16[128,32,256]{0,2,1:T(8,128)(2,1)}), bf16[128,32,256]{0,2,1:T(8,128)(2,1)S(1)}, u32[]{:S(2)}, u32[]{:S(2)}) async-start(bf16[128,32,256]{0,2,1:T(8,128)(2,1)} %bitcast.127), calls=%async_computation.1 | async-start | bytes 4194304 | tf_op jit(solution)/shard_map/all_to_all | solution.py:122
  188.3 4.6 %copy-start.1 = (f32[128,32,128]{2,1,0:T(8,128)S(1)}, f32[128,32,128]{2,1,0:T(8,128)}, u32[]{:S(2)}) copy-start(f32[128,32,128]{2,1,0:T(8,128)} %shard_map.74) | copy-start | bytes 6291460

commit v3 on v2

--- a/solution.py
+++ b/solution.py
@@ -88,6 +88,19 @@
     return position.reshape(count).astype(jnp.int32)
 
 
+def network(flattened, input_weight, middle_weight, output_weight):
+    hidden = jax.nn.silu(
+        jnp.dot(input_weight[0], flattened, preferred_element_type=jnp.float32)
+    ).astype(jnp.bfloat16)
+    for layer_index in range(middle_weight.shape[1]):
+        hidden = jax.nn.silu(
+            jnp.dot(middle_weight[0, layer_index], hidden, preferred_element_type=jnp.float32)
+        ).astype(jnp.bfloat16)
+    return jnp.dot(output_weight[0], hidden, preferred_element_type=jnp.float32).astype(
+        jnp.bfloat16
+    )
+
+
 def local(
     column_state, wind_speed, diffusivity, batch_index, input_weight, middle_weight, output_weight
 ):
@@ -105,21 +118,17 @@
     targets = targets_all * capacity + position
     packed = jnp.zeros((features, experts * capacity), jnp.bfloat16).at[:, targets].set(columns)
     packed = packed.reshape(features, experts, capacity)
-    received = lax.all_to_all(packed, "lon", split_axis=1, concat_axis=1, tiled=True)
-    layout = received.shape
-    flattened = received.reshape(layout[0], layout[1] * layout[2])
-    hidden = jax.nn.silu(
-        jnp.dot(input_weight[0], flattened, preferred_element_type=jnp.float32)
-    ).astype(jnp.bfloat16)
-    for layer_index in range(middle_weight.shape[1]):
-        hidden = jax.nn.silu(
-            jnp.dot(middle_weight[0, layer_index], hidden, preferred_element_type=jnp.float32)
-        ).astype(jnp.bfloat16)
-    result = jnp.dot(output_weight[0], hidden, preferred_element_type=jnp.float32).astype(
-        jnp.bfloat16
-    )
-    answered = result.reshape(layout)
-    returned = lax.all_to_all(answered, "lon", split_axis=1, concat_axis=1, tiled=True)
+    chunks = 2
+    width = capacity // chunks
+    answers = []
+    for chunk in range(chunks):
+        part = packed[:, :, chunk * width:(chunk + 1) * width]
+        received = lax.all_to_all(part, "lon", split_axis=1, concat_axis=1, tiled=True)
+        result = network(received.reshape(features, experts * width), input_weight, middle_weight, output_weight)
+        answers.append(
+            lax.all_to_all(result.reshape(features, experts, width), "lon", split_axis=1, concat_axis=1, tiled=True)
+        )
+    returned = jnp.concatenate(answers, axis=2)
     tendency = returned.reshape(features, -1)[:, targets]
     return (current + tendency.astype(jnp.float32).reshape(current.shape)).reshape(column_state.shape)
 

time: 197 us -> 202 us (1.025)
  starting transfers between devices: 23.5 us -> 38.4 us
  blocking collectives: 37.8 us -> 25.9 us
  waiting for transfers between devices: 31.2 us -> 19.8 us
  matrix products: 41.1 us -> 51.2 us
    all_to_all x1 -> x3, starting transfers between devices: 3.94 us -> 18.8 us  [the longest x2 14.8 us: local(): lax.all_to_all(result.reshape(features, experts, width), 'lon', split_axi...]
    all_to_all x1, blocking collectives: 37.8 us -> 25.9 us  [local(): lax.all_to_all(part, 'lon', split_axis=1, concat_axis=1, tiled=True)]
    all_to_all x1 -> x3, waiting for transfers between devices: 28.3 us -> 17 us  [the longest x2 17 us: local(): lax.all_to_all(result.reshape(features, experts, width), 'lon', split_axi...]
    dot_general x3 -> x6, matrix products: 40.1 us -> 50.1 us  [the longest x4 36.8 us: network(): jnp.dot(middle_weight[0, layer_index], hidden, preferred_element_type=jnp...]
  transfers between devices with their start and end apart: 9 -> 11, of which waited for: 3 -> 3; matrix products, arithmetic and copies ran while one was open for 4% -> 29% of each run, Pallas kernels for 0% -> 0%
where the time goes in v3:
time: 202 us; the launch traced here: 201 us
  matrix products  51.2 us (25%)
  local copies, waits for them, and re-layouts  43.9 us (22%)
  starting transfers between devices  38.4 us (19%)
  blocking collectives  25.9 us (13%)
  waiting for transfers between devices  19.8 us (10%)
  Pallas kernels  11.9 us (6%)
  other arithmetic  9.08 us (4%)
    dot_general x4, matrix products, network(): jnp.dot(middle_weight[0, layer_index], hidden, preferred_element_type=jnp...  36.8 us
    all_to_all x1, blocking collectives, local(): lax.all_to_all(part, 'lon', split_axis=1, concat_axis=1, tiled=True)  25.9 us
    all_to_all x2, waiting for transfers between devices, local(): lax.all_to_all(result.reshape(features, experts, width), 'lon', split_axi...  17 us
    all_to_all x2, starting transfers between devices, local(): lax.all_to_all(result.reshape(features, experts, width), 'lon', split_axi...  14.8 us
    dot_general x2, matrix products, network(): jnp.dot(output_weight[0], hidden, preferred_element_type=jnp.float32)  13.4 us
    gather x1, local copies, waits for them, and re-layouts, local(): tendency = returned.reshape(features, -1)[:, targets]  12.1 us
    pallas_call x2, Pallas kernels, sweep(): pl.pallas_call(sweep_kernel, grid=(nb,), in_specs=[big, edge_row, edge_ro...  11.9 us
    scatter x1, local copies, waits for them, and re-layouts, local(): jnp.zeros((features, experts * capacity), jnp.bfloat16).at[:, targets]  11.6 us
  transfers between devices with their start and end apart: 11, of which 3 were waited for; matrix products, arithmetic and copies ran while one was open for 29% of the time, Pallas kernels for 0%

profile of v3, /device:TPU:1, one launch (start us, length us, event | category | flops | bytes accessed | tf_op | source)
XLA Modules:
  0.0 200.5 jit_solution(13745720435374558672)
XLA Ops:
  1.3 4.4 %collective-permute-start.1 = (f32[128,1,128]{2,1,0:T(1,128)S(1)}, f32[128,1,128]{2,1,0:T(1,128)S(1)}, u32[]{:S(2)}, u32[]{:S(2)}) collective-permute-start(f32[128,1,128]{2,1,0:T(1,128)S(1)} %get-tuple-element.13), channel_id=1, source_target_pairs={{0,32},{32,64},{64,96},{1,33},{33,65},{65,97},{2,34},{34,66},{66,9... | collective-permute-start | bytes 196616 | tf_op jit(solution)/shard_map/ppermute | solution.py:68
  7.0 3.9 %slice_reduce_fusion.2 = (f32[128,32]{1,0:T(8,128)S(1)}, f32[128,32]{1,0:T(8,128)S(1)}) fusion(f32[128,32,128]{2,1,0:T(8,128)} %bitcast.200), kind=kLoop, calls=%fused_computation.62 | loop fusion | bytes 65536 | tf_op jit(solution)/shard_map/slice | solution.py:70
  14.4 2.2 %slice_bitcast_fusion = (f32[32,32,128]{2,1,0:T(8,128)}, f32[32,32,128]{2,1,0:T(8,128)}) fusion(f32[2,32,32,128]{3,2,1,0:T(8,128)} %param.8), kind=kLoop, calls=%fused_computation.80 | loop fusion | bytes 2097152 | tf_op jit(solution)/shard_map/squeeze | solution.py:111
  18.5 6.0 %shard_map.73.q_ref = f32[128,32,128]{2,1,0:T(8,128)} custom-call(f32[128,32,128]{2,1,0:T(8,128)} %bitcast.201, f32[128,1,128]{2,1,0:T(1,128)} %copy-done.4, f32[128,1,128]{2,1,0:T(1,128)} %copy-done.3, f32[4,32,32]{2,1,0:T(8,128)} %copy-done.5, f32[4,32,32]{2,1,0:T(8,128)} %copy-done.8, f32[32,32,128]{2,1,0:T(8,128)} %get-tuple-element.16.u_ref, ...), custom_call_target="tpu_custom_call" | custom-call | flops 10485760 | bytes 5767168 | tf_op jit(solution)/shard_map/pallas_call | solution.py:48
  25.7 3.9 %slice_reduce_fusion = (f32[128,32]{1,0:T(8,128)S(1)}, f32[128,32]{1,0:T(8,128)S(1)}) fusion(f32[128,32,128]{2,1,0:T(8,128)} %shard_map.73.q_ref), kind=kLoop, calls=%fused_computation.60 | loop fusion | bytes 65536 | tf_op jit(solution)/shard_map/slice | solution.py:70
  29.7 4.3 %collective-permute-start.5 = (f32[128,1,128]{2,1,0:T(1,128)S(1)}, f32[128,1,128]{2,1,0:T(1,128)S(1)}, u32[]{:S(2)}, u32[]{:S(2)}) collective-permute-start(f32[128,1,128]{2,1,0:T(1,128)S(1)} %get-tuple-element.11), channel_id=1, source_target_pairs={{0,32},{32,64},{64,96},{1,33},{33,65},{65,97},{2,34},{34,66},{66,9... | collective-permute-start | bytes 196616 | tf_op jit(solution)/shard_map/ppermute | solution.py:68
  35.4 6.1 %collective-permute-start.6 = (f32[4,32,32]{2,1,0:T(8,128)S(1)}, f32[4,32,32]{2,1,0:T(8,128)S(1)}, u32[]{:S(2)}, u32[]{:S(2)}) collective-permute-start(f32[4,32,32]{2,1,0:T(8,128)S(1)} %bitcast.219), channel_id=1, source_target_pairs={{1,0},{2,1},{3,2},{4,3},{5,4},{6,5},{7,6},{8,7},{9,8},{10,9},{11,1... | collective-permute-start | bytes 49160 | tf_op jit(solution)/shard_map/ppermute | solution.py:69
  42.4 2.0 collective-permute-done.7.hw_ref
  45.7 6.0 %shard_map.74 = f32[128,32,128]{2,1,0:T(8,128)} custom-call(f32[128,32,128]{2,1,0:T(8,128)} %shard_map.73.q_ref, f32[128,1,128]{2,1,0:T(1,128)} %copy-done.7, f32[128,1,128]{2,1,0:T(1,128)} %copy-done.6, f32[4,32,32]{2,1,0:T(8,128)} %copy-done.9, f32[4,32,32]{2,1,0:T(8,128)} %copy-done.10, f32[32,32,128]{2,1,0:T(8,128)} %get-tuple-element.16.u_ref, ...), custom_call_target="tpu_custom_call" | custom-call | flops 10485760 | bytes 5767168 | tf_op jit(solution)/shard_map/pallas_call | solution.py:48
  54.5 11.6 %scatter_custom_fusion = bf16[128,8192]{0,1:T(8,128)(2,1)S(1)} fusion(s32[4096]{0:T(1024)S(1)} %bitcast.213, bf16[4096,128]{1,0:T(8,128)(2,1)S(1)} %bitcast.206, bf16[]{:T(256)} %constant.17.clone.1), kind=kCustom, calls=%fused_computation.69 | custom fusion | bytes 2097154 | tf_op jit(solution)/shard_map/scatter | solution.py:119
  67.1 25.9 %all_to_all.20 = bf16[128,32,128]{0,2,1:T(8,128)(2,1)S(1)} all-to-all(bf16[128,32,128]{0,2,1:T(8,128)(2,1)S(1)} %get-tuple-element.10), channel_id=1, replica_groups=mesh['lat'=4,'lon'=32] {'lon'}, dimensions={1} | all-to-all | bytes 2097152 | tf_op jit(solution)/shard_map/all_to_all | solution.py:126
  93.1 3.9 %all-to-all-start = ((bf16[128,32,128]{0,2,1:T(8,128)(2,1)}), bf16[128,32,128]{0,2,1:T(8,128)(2,1)S(1)}, u32[]{:S(2)}, u32[]{:S(2)}) async-start(bf16[128,32,128]{0,2,1:T(8,128)(2,1)} %get-tuple-element.9), calls=%async_computation | async-start | bytes 2097152 | tf_op jit(solution)/shard_map/all_to_all | solution.py:126
  97.0 7.4 %fusion.36 = f32[4096,512]{1,0:T(8,128)} fusion(bf16[128,4096]{0,1:T(8,128)(2,1)S(1)} %bitcast.205, bf16[1,3,512,512]{3,2,1,0:T(8,128)(2,1)} %param.12, bf16[1,512,128]{2,1,0:T(8,128)(2,1)S(1)} %copy-done), kind=kOutput, calls=%fused_computation.54 | convolution fusion | flops 2694840320 | bytes 10092544 | tf_op jit(solution)/shard_map/dot_general | solution.py:97
  104.4 11.0 %fusion.32 = f32[4096,512]{1,0:T(8,128)} fusion(f32[4096,512]{1,0:T(8,128)} %fusion.36, bf16[1,3,512,512]{3,2,1,0:T(8,128)(2,1)} %param.12), kind=kOutput, calls=%fused_computation.52 | convolution fusion | flops 4315938816 | bytes 17825792 | tf_op jit(solution)/shard_map/dot_general | solution.py:97
  115.4 6.7 %convolution_convert_fusion = bf16[4096,128]{1,0:T(8,128)(2,1)} fusion(f32[4096,512]{1,0:T(8,128)} %fusion.32, bf16[1,128,512]{2,1,0:T(8,128)(2,1)S(1)} %copy-done.12), kind=kOutput, calls=%fused_computation.50 | convolution fusion | flops 547880960 | bytes 9568256 | tf_op jit(solution)/shard_map/dot_general | solution.py:99
  122.1 7.4 %all-to-all-start.3 = ((bf16[128,32,128]{0,2,1:T(8,128)(2,1)}), bf16[128,32,128]{0,2,1:T(8,128)(2,1)S(1)}, u32[]{:S(2)}, u32[]{:S(2)}) async-start(bf16[128,32,128]{0,2,1:T(8,128)(2,1)} %bitcast.34), calls=%async_computation.3 | async-start | bytes 2097152 | tf_op jit(solution)/shard_map/all_to_all | solution.py:129
  129.5 7.5 %fusion.42 = f32[4096,512]{1,0:T(8,128)} fusion(bf16[128,4096]{0,1:T(8,128)(2,1)S(1)} %bitcast.204, bf16[1,3,512,512]{3,2,1,0:T(8,128)(2,1)} %param.12, bf16[1,512,128]{2,1,0:T(8,128)(2,1)S(1)} %copy-done), kind=kOutput, calls=%fused_computation.57 | convolution fusion | flops 2694840320 | bytes 10092544 | tf_op jit(solution)/shard_map/dot_general | solution.py:97
  137.0 10.9 %fusion.38 = f32[4096,512]{1,0:T(8,128)} fusion(f32[4096,512]{1,0:T(8,128)} %fusion.42, bf16[1,3,512,512]{3,2,1,0:T(8,128)(2,1)} %param.12), kind=kOutput, calls=%fused_computation.55 | convolution fusion | flops 4315938816 | bytes 17825792 | tf_op jit(solution)/shard_map/dot_general | solution.py:97
  147.9 6.7 %convolution_convert_fusion.1 = bf16[4096,128]{1,0:T(8,128)(2,1)} fusion(f32[4096,512]{1,0:T(8,128)} %fusion.38, bf16[1,128,512]{2,1,0:T(8,128)(2,1)S(1)} %copy-done.12), kind=kOutput, calls=%fused_computation.51 | convolution fusion | flops 547880960 | bytes 9568256 | tf_op jit(solution)/shard_map/dot_general | solution.py:99
  154.5 7.4 %all-to-all-start.1 = ((bf16[128,32,128]{0,2,1:T(8,128)(2,1)}), bf16[128,32,128]{0,2,1:T(8,128)(2,1)}, u32[]{:S(2)}, u32[]{:S(2)}) async-start(bf16[128,32,128]{0,2,1:T(8,128)(2,1)} %bitcast.27), calls=%async_computation.1 | async-start | bytes 2097152 | tf_op jit(solution)/shard_map/all_to_all | solution.py:129
  162.0 16.9 %all-to-all-done.1 = bf16[128,32,128]{0,2,1:T(8,128)(2,1)} async-done(((bf16[128,32,128]{0,2,1:T(8,128)(2,1)}), bf16[128,32,128]{0,2,1:T(8,128)(2,1)}, u32[]{:S(2)}, u32[]{:S(2)}) %all-to-all-start.1) | async-done | bytes 1048608 | tf_op jit(solution)/shard_map/all_to_all | solution.py:129
  180.4 12.1 %gather_fusion = bf16[4096,128]{1,0:T(8,128)(2,1)S(1)} fusion(bf16[128,8192]{0,1:T(8,128)(2,1)S(1)} %bitcast.198, s32[4096]{0:T(1024)S(1)} %broadcast_clamp_fusion), kind=kCustom, calls=%fused_computation | custom fusion | bytes 2113536 | tf_op jit(solution)/shard_map/gather | solution.py:132
  194.0 3.1 %copy.29 = f32[128,32,128]{2,1,0:T(8,128)} copy(f32[128,32,128]{0,2,1:T(8,128)} %bitcast.203) | data formatting | bytes 4194304 | tf_op jit(solution)/shard_map/convert_element_type | solution.py:133
  197.1 3.4 %add.73 = f32[128,32,128]{2,1,0:T(8,128)} add(f32[128,32,128]{2,1,0:T(8,128)S(1)} %copy-done.2, f32[128,32,128]{2,1,0:T(8,128)} %copy.29) | non-fusion elementwise | flops 524288 | bytes 6291456 | tf_op jit(solution)/shard_map/add | solution.py:133
  (58 shorter events, 19.5 us)
Async XLA Ops:
  0.0 97.0 %copy-start = (bf16[1,512,128]{2,1,0:T(8,128)(2,1)S(1)}, bf16[1,512,128]{2,1,0:T(8,128)(2,1)}, u32[]{:S(2)}) copy-start(bf16[1,512,128]{2,1,0:T(8,128)(2,1)} %param.11) | copy-start | bytes 393220
  1.3 16.5 %collective-permute-start.1 = (f32[128,1,128]{2,1,0:T(1,128)S(1)}, f32[128,1,128]{2,1,0:T(1,128)S(1)}, u32[]{:S(2)}, u32[]{:S(2)}) collective-permute-start(f32[128,1,128]{2,1,0:T(1,128)S(1)} %get-tuple-element.13), channel_id=1, source_target_pairs={{0,32},{32,64},{64,96},{1,33},{33,65},{65,97},{2,34},{34,66},{66,9... | collective-permute-start | bytes 196616 | tf_op jit(solution)/shard_map/ppermute | solution.py:68
  5.7 35.8 %copy-start.11 = (s32[1,4096,1]{1,2,0:T(1,128)S(1)}, s32[1,4096,1]{1,2,0:T(1,128)}, u32[]{:S(2)}) copy-start(s32[1,4096,1]{1,2,0:T(1,128)} %param.10) | copy-start | bytes 49156
  5.7 12.1 %collective-permute-start = (f32[128,1,128]{2,1,0:T(1,128)S(1)}, f32[128,1,128]{2,1,0:T(1,128)S(1)}, u32[]{:S(2)}, u32[]{:S(2)}) collective-permute-start(f32[128,1,128]{2,1,0:T(1,128)S(1)} %get-tuple-element.14), channel_id=1, source_target_pairs={{32,0},{64,32},{96,64},{33,1},{65,33},{97,65},{34,2},{66,34},{98,6... | collective-permute-start | bytes 196616 | tf_op jit(solution)/shard_map/ppermute | solution.py:67
  11.1 6.7 %collective-permute-start.2 = (f32[4,32,32]{2,1,0:T(8,128)S(1)}, f32[4,32,32]{2,1,0:T(8,128)S(1)}, u32[]{:S(2)}, u32[]{:S(2)}) collective-permute-start(f32[4,32,32]{2,1,0:T(8,128)S(1)} %bitcast.216), channel_id=1, source_target_pairs={{1,0},{2,1},{3,2},{4,3},{5,4},{6,5},{7,6},{8,7},{9,8},{10,9},{11,1... | collective-permute-start | bytes 49160 | tf_op jit(solution)/shard_map/ppermute | solution.py:69
  12.2 5.6 %collective-permute-start.3 = (f32[4,32,32]{2,1,0:T(8,128)S(1)}, f32[4,32,32]{2,1,0:T(8,128)S(1)}, u32[]{:S(2)}, u32[]{:S(2)}) collective-permute-start(f32[4,32,32]{2,1,0:T(8,128)S(1)} %bitcast.217), channel_id=1, source_target_pairs={{0,1},{1,2},{2,3},{3,4},{4,5},{5,6},{6,7},{7,8},{8,9},{9,10},{10,1... | collective-permute-start | bytes 49160 | tf_op jit(solution)/shard_map/ppermute | solution.py:70
  17.8 0.6 copy-start.5
  17.8 0.6 copy-start.8
  17.8 0.6 copy-start.3
  17.8 0.6 copy-start.4
  29.7 14.7 %collective-permute-start.5 = (f32[128,1,128]{2,1,0:T(1,128)S(1)}, f32[128,1,128]{2,1,0:T(1,128)S(1)}, u32[]{:S(2)}, u32[]{:S(2)}) collective-permute-start(f32[128,1,128]{2,1,0:T(1,128)S(1)} %get-tuple-element.11), channel_id=1, source_target_pairs={{0,32},{32,64},{64,96},{1,33},{33,65},{65,97},{2,34},{34,66},{66,9... | collective-permute-start | bytes 196616 | tf_op jit(solution)/shard_map/ppermute | solution.py:68
  34.0 10.4 %collective-permute-start.4 = (f32[128,1,128]{2,1,0:T(1,128)S(1)}, f32[128,1,128]{2,1,0:T(1,128)S(1)}, u32[]{:S(2)}, u32[]{:S(2)}) collective-permute-start(f32[128,1,128]{2,1,0:T(1,128)S(1)} %get-tuple-element.12), channel_id=1, source_target_pairs={{32,0},{64,32},{96,64},{33,1},{65,33},{97,65},{34,2},{66,34},{98,6... | collective-permute-start | bytes 196616 | tf_op jit(solution)/shard_map/ppermute | solution.py:67
  35.4 7.0 %collective-permute-start.6 = (f32[4,32,32]{2,1,0:T(8,128)S(1)}, f32[4,32,32]{2,1,0:T(8,128)S(1)}, u32[]{:S(2)}, u32[]{:S(2)}) collective-permute-start(f32[4,32,32]{2,1,0:T(8,128)S(1)} %bitcast.219), channel_id=1, source_target_pairs={{1,0},{2,1},{3,2},{4,3},{5,4},{6,5},{7,6},{8,7},{9,8},{10,9},{11,1... | collective-permute-start | bytes 49160 | tf_op jit(solution)/shard_map/ppermute | solution.py:69
  41.5 2.9 %collective-permute-start.7 = (f32[4,32,32]{2,1,0:T(8,128)S(1)}, f32[4,32,32]{2,1,0:T(8,128)S(1)}, u32[]{:S(2)}, u32[]{:S(2)}) collective-permute-start(f32[4,32,32]{2,1,0:T(8,128)S(1)} %bitcast.218), channel_id=1, source_target_pairs={{0,1},{1,2},{2,3},{3,4},{4,5},{5,6},{6,7},{7,8},{8,9},{9,10},{10,1... | collective-permute-start | bytes 49160 | tf_op jit(solution)/shard_map/ppermute | solution.py:70
  42.4 2.0 copy-start.9
  44.4 0.6 copy-start.10
  44.4 0.7 copy-start.6
  45.1 0.6 copy-start.7
  93.1 29.1 %all-to-all-start = ((bf16[128,32,128]{0,2,1:T(8,128)(2,1)}), bf16[128,32,128]{0,2,1:T(8,128)(2,1)S(1)}, u32[]{:S(2)}, u32[]{:S(2)}) async-start(bf16[128,32,128]{0,2,1:T(8,128)(2,1)} %get-tuple-element.9), calls=%async_computation | async-start | bytes 2097152 | tf_op jit(solution)/shard_map/all_to_all | solution.py:126
  104.4 11.0 %copy-start.12 = (bf16[1,128,512]{2,1,0:T(8,128)(2,1)S(1)}, bf16[1,128,512]{2,1,0:T(8,128)(2,1)}, u32[]{:S(2)}) copy-start(bf16[1,128,512]{2,1,0:T(8,128)(2,1)} %param.13) | copy-start | bytes 393220
  122.1 32.4 %all-to-all-start.3 = ((bf16[128,32,128]{0,2,1:T(8,128)(2,1)}), bf16[128,32,128]{0,2,1:T(8,128)(2,1)S(1)}, u32[]{:S(2)}, u32[]{:S(2)}) async-start(bf16[128,32,128]{0,2,1:T(8,128)(2,1)} %bitcast.34), calls=%async_computation.3 | async-start | bytes 2097152 | tf_op jit(solution)/shard_map/all_to_all | solution.py:129
  154.5 24.4 %all-to-all-start.1 = ((bf16[128,32,128]{0,2,1:T(8,128)(2,1)}), bf16[128,32,128]{0,2,1:T(8,128)(2,1)}, u32[]{:S(2)}, u32[]{:S(2)}) async-start(bf16[128,32,128]{0,2,1:T(8,128)(2,1)} %bitcast.27), calls=%async_computation.1 | async-start | bytes 2097152 | tf_op jit(solution)/shard_map/all_to_all | solution.py:129
  180.4 20.1 %copy-start.1 = (bf16[1,512,128]{2,1,0:T(8,128)(2,1)S(1)}, bf16[1,512,128]{2,1,0:T(8,128)(2,1)}, u32[]{:S(2)}) copy-start(bf16[1,512,128]{2,1,0:T(8,128)(2,1)} %param.11) | copy-start | bytes 393220
  192.5 4.6 %copy-start.2 = (f32[128,32,128]{2,1,0:T(8,128)S(1)}, f32[128,32,128]{2,1,0:T(8,128)}, u32[]{:S(2)}) copy-start(f32[128,32,128]{2,1,0:T(8,128)} %shard_map.74) | copy-start | bytes 6291460

commit v4 on v3

--- a/solution.py
+++ b/solution.py
@@ -88,17 +88,68 @@
     return position.reshape(count).astype(jnp.int32)
 
 
-def network(flattened, input_weight, middle_weight, output_weight):
-    hidden = jax.nn.silu(
-        jnp.dot(input_weight[0], flattened, preferred_element_type=jnp.float32)
-    ).astype(jnp.bfloat16)
-    for layer_index in range(middle_weight.shape[1]):
-        hidden = jax.nn.silu(
-            jnp.dot(middle_weight[0, layer_index], hidden, preferred_element_type=jnp.float32)
+ROWS = 256
+HALF = ROWS // 2
+
+
+def silu(t):
+    return t * (0.5 * jnp.tanh(0.5 * t) + 0.5)
+
+
+def layers(x, w_first, w_middle, w_last):
+    nt = (((1,), (1,)), ((), ()))
+    hidden = silu(lax.dot_general(x, w_first, nt, preferred_element_type=jnp.float32)).astype(jnp.bfloat16)
+    for layer_index in range(w_middle.shape[0]):
+        hidden = silu(
+            lax.dot_general(hidden, w_middle[layer_index], nt, preferred_element_type=jnp.float32)
         ).astype(jnp.bfloat16)
-    return jnp.dot(output_weight[0], hidden, preferred_element_type=jnp.float32).astype(
-        jnp.bfloat16
-    )
+    return lax.dot_general(hidden, w_last, nt, preferred_element_type=jnp.float32).astype(jnp.bfloat16)
+
+
+def network_kernel(filled_ref, x_ref, first_ref, middle_ref, last_ref, o_ref):
+    filled = filled_ref[pl.program_id(0)]
+
+    @pl.when(filled == 2)
+    def _():
+        o_ref[...] = layers(x_ref[...], first_ref[0], middle_ref[0], last_ref[0])
+
+    @pl.when(filled == 1)
+    def _():
+        o_ref[:HALF, :] = layers(x_ref[:HALF, :], first_ref[0], middle_ref[0], last_ref[0])
+        o_ref[HALF:, :] = jnp.zeros((ROWS - HALF, o_ref.shape[1]), o_ref.dtype)
+
+    @pl.when(filled == 0)
+    def _():
+        o_ref[...] = jnp.zeros(o_ref.shape, o_ref.dtype)
+
+
+def network(rows_in, input_weight, middle_weight, output_weight):
+    count, feats = rows_in.shape
+    blocks = count // ROWS
+    hid = input_weight.shape[1]
+    nonzero = jnp.any(rows_in.reshape(blocks, 2, HALF * feats) != 0, axis=2)
+    filled = jnp.where(nonzero[:, 1], 2, jnp.where(nonzero[:, 0], 1, 0)).astype(jnp.int32)
+    mats = 2 * (hid * feats * 2 + middle_weight.shape[1] * hid * hid)
+    return pl.pallas_call(
+        network_kernel,
+        grid_spec=pltpu.PrefetchScalarGridSpec(
+            num_scalar_prefetch=1,
+            grid=(blocks,),
+            in_specs=[
+                pl.BlockSpec((ROWS, feats), lambda i, f: (i, 0)),
+                pl.BlockSpec(input_weight.shape, lambda i, f: (0, 0, 0)),
+                pl.BlockSpec(middle_weight.shape, lambda i, f: (0, 0, 0, 0)),
+                pl.BlockSpec(output_weight.shape, lambda i, f: (0, 0, 0)),
+            ],
+            out_specs=pl.BlockSpec((ROWS, feats), lambda i, f: (i, 0)),
+        ),
+        out_shape=jax.ShapeDtypeStruct((count, feats), jnp.bfloat16),
+        cost_estimate=pl.CostEstimate(
+            flops=mats * count,
+            bytes_accessed=4 * count * feats + 2 * (mats // 2),
+            transcendentals=(1 + middle_weight.shape[1]) * hid * count,
+        ),
+    )(filled, rows_in, input_weight, middle_weight, output_weight)
 
 
 def local(
@@ -118,13 +169,14 @@
     targets = targets_all * capacity + position
     packed = jnp.zeros((features, experts * capacity), jnp.bfloat16).at[:, targets].set(columns)
     packed = packed.reshape(features, experts, capacity)
-    chunks = 2
+    chunks = 1
     width = capacity // chunks
     answers = []
     for chunk in range(chunks):
         part = packed[:, :, chunk * width:(chunk + 1) * width]
         received = lax.all_to_all(part, "lon", split_axis=1, concat_axis=1, tiled=True)
-        result = network(received.reshape(features, experts * width), input_weight, middle_weight, output_weight)
+        rows_in = received.reshape(features, experts * width).T
+        result = network(rows_in, input_weight, middle_weight, output_weight).T
         answers.append(
             lax.all_to_all(result.reshape(features, experts, width), "lon", split_axis=1, concat_axis=1, tiled=True)
         )

time: 202 us -> 200 us (0.990)
  matrix products: 51.2 us -> 0.28 us
  Pallas kernels: 11.9 us -> 51.7 us
  starting transfers between devices: 38.4 us -> 24 us
  waiting for transfers between devices: 19.8 us -> 31.9 us
  blocking collectives: 25.9 us -> 36.7 us
    dot_general x6 -> x0, matrix products: 50.1 us -> none  [the longest x4 36.8 us: network(): jnp.dot(middle_weight[0, layer_index], hidden, preferred_element_type=jnp...]
    pallas_call x0 -> x1, Pallas kernels: none -> 39.8 us  [network(): pl.pallas_call(network_kernel, grid_spec=pltpu.PrefetchScalarGridSpec(num...]
    all_to_all x2 -> x1, waiting for transfers between devices: 17 us -> 28.3 us  [local(): lax.all_to_all(result.reshape(features, experts, width), 'lon', split_axi...]
    all_to_all x2 -> x1, starting transfers between devices: 14.8 us -> 3.86 us  [local(): lax.all_to_all(result.reshape(features, experts, width), 'lon', split_axi...]
    all_to_all x1, blocking collectives: 25.9 us -> 36.7 us  [local(): lax.all_to_all(part, 'lon', split_axis=1, concat_axis=1, tiled=True)]
    all_to_all x1 -> x0, starting transfers between devices: 3.94 us -> none  [local(): lax.all_to_all(part, 'lon', split_axis=1, concat_axis=1, tiled=True)]
  transfers between devices with their start and end apart: 11 -> 9, of which waited for: 3 -> 5; matrix products, arithmetic and copies ran while one was open for 29% -> 3% of each run, Pallas kernels for 0% -> 0%
where the time goes in v4:
time: 200 us; the launch traced here: 199 us
  Pallas kernels  51.7 us (26%)
  local copies, waits for them, and re-layouts  44.2 us (22%)
  blocking collectives  36.7 us (18%)
  waiting for transfers between devices  31.9 us (16%)
  starting transfers between devices  24 us (12%)
  other arithmetic  10.2 us (5%)
    pallas_call x1, Pallas kernels, network(): pl.pallas_call(network_kernel, grid_spec=pltpu.PrefetchScalarGridSpec(num...  39.8 us
    all_to_all x1, blocking collectives, local(): lax.all_to_all(part, 'lon', split_axis=1, concat_axis=1, tiled=True)  36.7 us
    all_to_all x1, waiting for transfers between devices, local(): lax.all_to_all(result.reshape(features, experts, width), 'lon', split_axi...  28.3 us
    gather x1, local copies, waits for them, and re-layouts, local(): tendency = returned.reshape(features, -1)[:, targets]  12.1 us
    pallas_call x2, Pallas kernels, sweep(): pl.pallas_call(sweep_kernel, grid=(nb,), in_specs=[big, edge_row, edge_ro...  11.9 us
    scatter x1, local copies, waits for them, and re-layouts, local(): jnp.zeros((features, experts * capacity), jnp.bfloat16).at[:, targets]  11.6 us
    ppermute x2, starting transfers between devices, step(): hs = lax.ppermute(x[:, rows - 1:, :], 'lat', lat_forward)  8.55 us
    slice x2, local copies, waits for them, and re-layouts, step(): hw = lax.ppermute(columns_of(x[:, :, cols - 1]), 'lon', lon_forward)  7.91 us
  transfers between devices with their start and end apart: 9, of which 5 were waited for; matrix products, arithmetic and copies ran while one was open for 3% of the time, Pallas kernels for 0%

profile of v4, /device:TPU:1, one launch (start us, length us, event | category | flops | bytes accessed | tf_op | source)
XLA Modules:
  0.0 199.2 jit_solution(11390033060352015530)
XLA Ops:
  0.0 1.3 fusion.10
  1.3 4.4 %collective-permute-start.1 = (f32[128,1,128]{2,1,0:T(1,128)S(1)}, f32[128,1,128]{2,1,0:T(1,128)S(1)}, u32[]{:S(2)}, u32[]{:S(2)}) collective-permute-start(f32[128,1,128]{2,1,0:T(1,128)S(1)} %get-tuple-element.11), channel_id=1, source_target_pairs={{0,32},{32,64},{64,96},{1,33},{33,65},{65,97},{2,34},{34,66},{66,9... | collective-permute-start | bytes 196616 | tf_op jit(solution)/shard_map/ppermute | solution.py:68
  5.7 1.4 collective-permute-start
  7.1 3.9 %slice_reduce_fusion.2 = (f32[128,32]{1,0:T(8,128)S(1)}, f32[128,32]{1,0:T(8,128)S(1)}) fusion(f32[128,32,128]{2,1,0:T(8,128)} %bitcast.48), kind=kLoop, calls=%fused_computation.4 | loop fusion | bytes 65536 | tf_op jit(solution)/shard_map/slice | solution.py:70
  15.3 2.1 %collective-permute-done.3.hw_ref = f32[4,32,32]{2,1,0:T(8,128)S(1)} collective-permute-done((f32[4,32,32]{2,1,0:T(8,128)S(1)}, f32[4,32,32]{2,1,0:T(8,128)S(1)}, u32[]{:S(2)}, u32[]{:S(2)}) %collective-permute-start.3) | collective-permute-done | bytes 16416 | tf_op jit(solution)/shard_map/ppermute | solution.py:70
  18.1 6.0 %shard_map.73.q_ref = f32[128,32,128]{2,1,0:T(8,128)} custom-call(f32[128,32,128]{2,1,0:T(8,128)} %bitcast.49, f32[128,1,128]{2,1,0:T(1,128)} %copy-done.4, f32[128,1,128]{2,1,0:T(1,128)} %copy-done.3, f32[4,32,32]{2,1,0:T(8,128)} %copy-done.5, f32[4,32,32]{2,1,0:T(8,128)} %copy-done.8, f32[32,32,128]{2,1,0:T(8,128)} %get-tuple-element.14.u_ref, ...), custom_call_target="tpu_custom_call" | custom-call | flops 10485760 | bytes 5767168 | tf_op jit(solution)/shard_map/pallas_call | solution.py:48
  24.1 1.3 fusion.9
  25.4 4.0 %slice_reduce_fusion = (f32[128,32]{1,0:T(8,128)S(1)}, f32[128,32]{1,0:T(8,128)S(1)}) fusion(f32[128,32,128]{2,1,0:T(8,128)} %shard_map.73.q_ref), kind=kLoop, calls=%fused_computation.2 | loop fusion | bytes 65536 | tf_op jit(solution)/shard_map/slice | solution.py:70
  29.4 4.2 %collective-permute-start.5 = (f32[128,1,128]{2,1,0:T(1,128)S(1)}, f32[128,1,128]{2,1,0:T(1,128)S(1)}, u32[]{:S(2)}, u32[]{:S(2)}) collective-permute-start(f32[128,1,128]{2,1,0:T(1,128)S(1)} %get-tuple-element.9), channel_id=1, source_target_pairs={{0,32},{32,64},{64,96},{1,33},{33,65},{65,97},{2,34},{34,66},{66,9... | collective-permute-start | bytes 196616 | tf_op jit(solution)/shard_map/ppermute | solution.py:68
  33.6 1.3 collective-permute-start.4
  35.0 6.6 %collective-permute-start.6 = (f32[4,32,32]{2,1,0:T(8,128)S(1)}, f32[4,32,32]{2,1,0:T(8,128)S(1)}, u32[]{:S(2)}, u32[]{:S(2)}) collective-permute-start(f32[4,32,32]{2,1,0:T(8,128)S(1)} %bitcast.67), channel_id=1, source_target_pairs={{1,0},{2,1},{3,2},{4,3},{5,4},{6,5},{7,6},{8,7},{9,8},{10,9},{11,1... | collective-permute-start | bytes 49160 | tf_op jit(solution)/shard_map/ppermute | solution.py:69
  44.2 6.0 %shard_map.74 = f32[128,32,128]{2,1,0:T(8,128)} custom-call(f32[128,32,128]{2,1,0:T(8,128)} %shard_map.73.q_ref, f32[128,1,128]{2,1,0:T(1,128)} %copy-done.7, f32[128,1,128]{2,1,0:T(1,128)} %copy-done.6, f32[4,32,32]{2,1,0:T(8,128)} %copy-done.9, f32[4,32,32]{2,1,0:T(8,128)} %copy-done.10, f32[32,32,128]{2,1,0:T(8,128)} %get-tuple-element.14.u_ref, ...), custom_call_target="tpu_custom_call" | custom-call | flops 10485760 | bytes 5767168 | tf_op jit(solution)/shard_map/pallas_call | solution.py:48
  50.2 1.8 convert_element_type.39
  53.0 11.6 %scatter_custom_fusion = bf16[128,8192]{0,1:T(8,128)(2,1)S(1)} fusion(s32[4096]{0:T(1024)S(1)} %bitcast.62, bf16[4096,128]{1,0:T(8,128)(2,1)S(1)} %bitcast.54, bf16[]{:T(256)} %constant.8.clone.1), kind=kCustom, calls=%fused_computation.11 | custom fusion | bytes 2097154 | tf_op jit(solution)/shard_map/scatter | solution.py:170
  64.6 36.7 %all_to_all.10 = bf16[128,32,256]{0,2,1:T(8,128)(2,1)S(1)} all-to-all(bf16[128,32,256]{0,2,1:T(8,128)(2,1)S(1)} %bitcast.51), channel_id=1, replica_groups=mesh['lat'=4,'lon'=32] {'lon'}, dimensions={1} | all-to-all | bytes 4194304 | tf_op jit(solution)/shard_map/all_to_all | solution.py:177
  101.3 1.3 copy-done.1
  104.4 1.9 reduce_or.9
  107.0 39.8 %shard_map.75 = bf16[8192,128]{1,0:T(8,128)(2,1)} custom-call(s32[32]{0:T(128)} %select_reduce_fusion.filled_ref, bf16[8192,128]{1,0:T(8,128)(2,1)} %bitcast.50, bf16[1,512,128]{2,1,0:T(8,128)(2,1)} %first_ref.1, bf16[1,3,512,512]{3,2,1,0:T(8,128)(2,1)} %middle_ref.1, bf16[1,128,512]{2,1,0:T(8,128)(2,1)} %last_ref.1), custom_call_target="tpu_custom_call" | custom-call | flops 15032385536 | bytes 6029312 | tf_op jit(solution)/shard_map/pallas_call | solution.py:133
  146.8 3.9 %all-to-all-start.1 = ((bf16[128,32,256]{0,2,1:T(8,128)(2,1)}), bf16[128,32,256]{0,2,1:T(8,128)(2,1)S(1)}, u32[]{:S(2)}, u32[]{:S(2)}) async-start(bf16[128,32,256]{0,2,1:T(8,128)(2,1)} %bitcast.53), calls=%async_computation.1 | async-start | bytes 4194304 | tf_op jit(solution)/shard_map/all_to_all | solution.py:181
  150.7 28.3 %all-to-all-done.1 = bf16[128,32,256]{0,2,1:T(8,128)(2,1)S(1)} async-done(((bf16[128,32,256]{0,2,1:T(8,128)(2,1)}), bf16[128,32,256]{0,2,1:T(8,128)(2,1)S(1)}, u32[]{:S(2)}, u32[]{:S(2)}) %all-to-all-start.1) | async-done | bytes 2097184 | tf_op jit(solution)/shard_map/all_to_all | solution.py:181
  179.0 12.1 %gather_fusion = bf16[4096,128]{1,0:T(8,128)(2,1)S(1)} fusion(bf16[128,8192]{0,1:T(8,128)(2,1)S(1)} %bitcast.46, s32[4096]{0:T(1024)S(1)} %broadcast_clamp_fusion), kind=kCustom, calls=%fused_computation | custom fusion | bytes 2113536 | tf_op jit(solution)/shard_map/gather | solution.py:184
  191.1 1.5 convert_element_type.44
  192.6 3.2 %copy.49 = f32[128,32,128]{2,1,0:T(8,128)} copy(f32[128,32,128]{0,2,1:T(8,128)} %bitcast.52) | data formatting | bytes 4194304 | tf_op jit(solution)/shard_map/convert_element_type | solution.py:185
  195.8 3.4 %add.40 = f32[128,32,128]{2,1,0:T(8,128)} add(f32[128,32,128]{2,1,0:T(8,128)S(1)} %copy-done, f32[128,32,128]{2,1,0:T(8,128)} %copy.49) | non-fusion elementwise | flops 524288 | bytes 6291456 | tf_op jit(solution)/shard_map/add | solution.py:185
  (49 shorter events, 11.2 us)
Async XLA Ops:
  1.3 16.2 %collective-permute-start.1 = (f32[128,1,128]{2,1,0:T(1,128)S(1)}, f32[128,1,128]{2,1,0:T(1,128)S(1)}, u32[]{:S(2)}, u32[]{:S(2)}) collective-permute-start(f32[128,1,128]{2,1,0:T(1,128)S(1)} %get-tuple-element.11), channel_id=1, source_target_pairs={{0,32},{32,64},{64,96},{1,33},{33,65},{65,97},{2,34},{34,66},{66,9... | collective-permute-start | bytes 196616 | tf_op jit(solution)/shard_map/ppermute | solution.py:68
  5.7 7.9 %copy-start.11 = (s32[1,4096,1]{1,2,0:T(1,128)S(1)}, s32[1,4096,1]{1,2,0:T(1,128)}, u32[]{:S(2)}) copy-start(s32[1,4096,1]{1,2,0:T(1,128)} %param.10) | copy-start | bytes 49156
  5.7 8.1 %copy-start.2 = (f32[2,32,32,128]{3,2,1,0:T(8,128)S(1)}, f32[2,32,32,128]{3,2,1,0:T(8,128)}, u32[]{:S(2)}) copy-start(f32[2,32,32,128]{3,2,1,0:T(8,128)} %param.8) | copy-start | bytes 3145732
  5.7 11.8 %collective-permute-start = (f32[128,1,128]{2,1,0:T(1,128)S(1)}, f32[128,1,128]{2,1,0:T(1,128)S(1)}, u32[]{:S(2)}, u32[]{:S(2)}) collective-permute-start(f32[128,1,128]{2,1,0:T(1,128)S(1)} %get-tuple-element.12), channel_id=1, source_target_pairs={{32,0},{64,32},{96,64},{33,1},{65,33},{97,65},{34,2},{66,34},{98,6... | collective-permute-start | bytes 196616 | tf_op jit(solution)/shard_map/ppermute | solution.py:67
  11.2 4.2 %collective-permute-start.2 = (f32[4,32,32]{2,1,0:T(8,128)S(1)}, f32[4,32,32]{2,1,0:T(8,128)S(1)}, u32[]{:S(2)}, u32[]{:S(2)}) collective-permute-start(f32[4,32,32]{2,1,0:T(8,128)S(1)} %bitcast.64), channel_id=1, source_target_pairs={{1,0},{2,1},{3,2},{4,3},{5,4},{6,5},{7,6},{8,7},{9,8},{10,9},{11,1... | collective-permute-start | bytes 49160 | tf_op jit(solution)/shard_map/ppermute | solution.py:69
  12.3 5.2 %collective-permute-start.3 = (f32[4,32,32]{2,1,0:T(8,128)S(1)}, f32[4,32,32]{2,1,0:T(8,128)S(1)}, u32[]{:S(2)}, u32[]{:S(2)}) collective-permute-start(f32[4,32,32]{2,1,0:T(8,128)S(1)} %bitcast.65), channel_id=1, source_target_pairs={{0,1},{1,2},{2,3},{3,4},{4,5},{5,6},{6,7},{7,8},{8,9},{9,10},{10,1... | collective-permute-start | bytes 49160 | tf_op jit(solution)/shard_map/ppermute | solution.py:70
  15.3 2.2 %copy-start.5 = (f32[4,32,32]{2,1,0:T(8,128)}, f32[4,32,32]{2,1,0:T(8,128)S(1)}, u32[]{:S(2)}) copy-start(f32[4,32,32]{2,1,0:T(8,128)S(1)} %collective-permute-done.2.he_ref) | copy-start | bytes 49156
  17.5 0.6 copy-start.8
  17.5 0.6 copy-start.3
  17.5 0.7 copy-start.4
  29.4 13.6 %collective-permute-start.5 = (f32[128,1,128]{2,1,0:T(1,128)S(1)}, f32[128,1,128]{2,1,0:T(1,128)S(1)}, u32[]{:S(2)}, u32[]{:S(2)}) collective-permute-start(f32[128,1,128]{2,1,0:T(1,128)S(1)} %get-tuple-element.9), channel_id=1, source_target_pairs={{0,32},{32,64},{64,96},{1,33},{33,65},{65,97},{2,34},{34,66},{66,9... | collective-permute-start | bytes 196616 | tf_op jit(solution)/shard_map/ppermute | solution.py:68
  33.6 9.4 %collective-permute-start.4 = (f32[128,1,128]{2,1,0:T(1,128)S(1)}, f32[128,1,128]{2,1,0:T(1,128)S(1)}, u32[]{:S(2)}, u32[]{:S(2)}) collective-permute-start(f32[128,1,128]{2,1,0:T(1,128)S(1)} %get-tuple-element.10), channel_id=1, source_target_pairs={{32,0},{64,32},{96,64},{33,1},{65,33},{97,65},{34,2},{66,34},{98,6... | collective-permute-start | bytes 196616 | tf_op jit(solution)/shard_map/ppermute | solution.py:67
  35.0 7.5 %collective-permute-start.6 = (f32[4,32,32]{2,1,0:T(8,128)S(1)}, f32[4,32,32]{2,1,0:T(8,128)S(1)}, u32[]{:S(2)}, u32[]{:S(2)}) collective-permute-start(f32[4,32,32]{2,1,0:T(8,128)S(1)} %bitcast.67), channel_id=1, source_target_pairs={{1,0},{2,1},{3,2},{4,3},{5,4},{6,5},{7,6},{8,7},{9,8},{10,9},{11,1... | collective-permute-start | bytes 49160 | tf_op jit(solution)/shard_map/ppermute | solution.py:69
  41.6 1.3 collective-permute-start.7
  42.5 0.6 copy-start.9
  43.0 0.6 copy-start.10
  43.0 0.6 copy-start.6
  43.6 0.6 copy-start.7
  101.3 1.3 copy-start.1
  146.8 32.2 %all-to-all-start.1 = ((bf16[128,32,256]{0,2,1:T(8,128)(2,1)}), bf16[128,32,256]{0,2,1:T(8,128)(2,1)S(1)}, u32[]{:S(2)}, u32[]{:S(2)}) async-start(bf16[128,32,256]{0,2,1:T(8,128)(2,1)} %bitcast.53), calls=%async_computation.1 | async-start | bytes 4194304 | tf_op jit(solution)/shard_map/all_to_all | solution.py:181
  192.5 3.2 %copy-start = (f32[128,32,128]{2,1,0:T(8,128)S(1)}, f32[128,32,128]{2,1,0:T(8,128)}, u32[]{:S(2)}) copy-start(f32[128,32,128]{2,1,0:T(8,128)} %shard_map.74) | copy-start | bytes 6291460

commit v5 on v4

--- a/solution.py
+++ b/solution.py
@@ -97,13 +97,12 @@
 
 
 def layers(x, w_first, w_middle, w_last):
-    nt = (((1,), (1,)), ((), ()))
-    hidden = silu(lax.dot_general(x, w_first, nt, preferred_element_type=jnp.float32)).astype(jnp.bfloat16)
+    hidden = silu(jnp.dot(x, w_first, preferred_element_type=jnp.float32)).astype(jnp.bfloat16)
     for layer_index in range(w_middle.shape[0]):
         hidden = silu(
-            lax.dot_general(hidden, w_middle[layer_index], nt, preferred_element_type=jnp.float32)
+            jnp.dot(hidden, w_middle[layer_index], preferred_element_type=jnp.float32)
         ).astype(jnp.bfloat16)
-    return lax.dot_general(hidden, w_last, nt, preferred_element_type=jnp.float32).astype(jnp.bfloat16)
+    return jnp.dot(hidden, w_last, preferred_element_type=jnp.float32).astype(jnp.bfloat16)
 
 
 def network_kernel(filled_ref, x_ref, first_ref, middle_ref, last_ref, o_ref):
@@ -111,11 +110,11 @@
 
     @pl.when(filled == 2)
     def _():
-        o_ref[...] = layers(x_ref[...], first_ref[0], middle_ref[0], last_ref[0])
+        o_ref[...] = layers(x_ref[...], first_ref[...], middle_ref[...], last_ref[...])
 
     @pl.when(filled == 1)
     def _():
-        o_ref[:HALF, :] = layers(x_ref[:HALF, :], first_ref[0], middle_ref[0], last_ref[0])
+        o_ref[:HALF, :] = layers(x_ref[:HALF, :], first_ref[...], middle_ref[...], last_ref[...])
         o_ref[HALF:, :] = jnp.zeros((ROWS - HALF, o_ref.shape[1]), o_ref.dtype)
 
     @pl.when(filled == 0)
@@ -127,6 +126,9 @@
     count, feats = rows_in.shape
     blocks = count // ROWS
     hid = input_weight.shape[1]
+    first = input_weight[0].T
+    middle = jnp.swapaxes(middle_weight[0], 1, 2)
+    last = output_weight[0].T
     nonzero = jnp.any(rows_in.reshape(blocks, 2, HALF * feats) != 0, axis=2)
     filled = jnp.where(nonzero[:, 1], 2, jnp.where(nonzero[:, 0], 1, 0)).astype(jnp.int32)
     mats = 2 * (hid * feats * 2 + middle_weight.shape[1] * hid * hid)
@@ -137,9 +139,9 @@
             grid=(blocks,),
             in_specs=[
                 pl.BlockSpec((ROWS, feats), lambda i, f: (i, 0)),
-                pl.BlockSpec(input_weight.shape, lambda i, f: (0, 0, 0)),
-                pl.BlockSpec(middle_weight.shape, lambda i, f: (0, 0, 0, 0)),
-                pl.BlockSpec(output_weight.shape, lambda i, f: (0, 0, 0)),
+                pl.BlockSpec(first.shape, lambda i, f: (0, 0)),
+                pl.BlockSpec(middle.shape, lambda i, f: (0, 0, 0)),
+                pl.BlockSpec(last.shape, lambda i, f: (0, 0)),
             ],
             out_specs=pl.BlockSpec((ROWS, feats), lambda i, f: (i, 0)),
         ),
@@ -149,7 +151,7 @@
             bytes_accessed=4 * count * feats + 2 * (mats // 2),
             transcendentals=(1 + middle_weight.shape[1]) * hid * count,
         ),
-    )(filled, rows_in, input_weight, middle_weight, output_weight)
+    )(filled, rows_in, first, middle, last)
 
 
 def local(

time: 200 us -> 199 us (level)
  blocking collectives: 36.7 us -> 0 us
  waiting for transfers between devices: 31.9 us -> 53.5 us
  starting transfers between devices: 24 us -> 36.5 us
  local copies, waits for them, and re-layouts: 44.2 us -> 48.8 us
  Pallas kernels: 51.7 us -> 47.5 us
    all_to_all x1 -> x0, blocking collectives: 36.7 us -> none  [local(): lax.all_to_all(part, 'lon', split_axis=1, concat_axis=1, tiled=True)]
    all_to_all x0 -> x1, waiting for transfers between devices: none -> 24 us  [local(): lax.all_to_all(part, 'lon', split_axis=1, concat_axis=1, tiled=True)]
    all_to_all x0 -> x1, starting transfers between devices: none -> 10.6 us  [local(): lax.all_to_all(part, 'lon', split_axis=1, concat_axis=1, tiled=True)]
    pallas_call x1, Pallas kernels: 39.8 us -> 35.6 us  [network(): pl.pallas_call(network_kernel, grid_spec=pltpu.PrefetchScalarGridSpec(num...]
    all_to_all x1, starting transfers between devices: 3.86 us -> 7.57 us  [local(): lax.all_to_all(result.reshape(features, experts, width), 'lon', split_axi...]
    unnamed x24 -> x31, local copies, waits for them, and re-layouts: 3.24 us -> 6.86 us
    ppermute x2, waiting for transfers between devices: 2.57 us -> 0.01 us  [step(): hw = lax.ppermute(columns_of(x[:, :, cols - 1]), 'lon', lon_forward)]
    ppermute x2, starting transfers between devices: 7.63 us -> 5.55 us  [step(): he = lax.ppermute(columns_of(x[:, :, 0]), 'lon', lon_backward)]
  transfers between devices with their start and end apart: 9 -> 10, of which waited for: 5 -> 3; matrix products, arithmetic and copies ran while one was open for 3% -> 4% of each run, Pallas kernels for 0% -> 0%
where the time goes in v5:
time: 199 us; the launch traced here: 197 us
  waiting for transfers between devices  53.5 us (27%)
  local copies, waits for them, and re-layouts  48.8 us (25%)
  Pallas kernels  47.5 us (24%)
  starting transfers between devices  36.5 us (18%)
  other arithmetic  10.3 us (5%)
    pallas_call x1, Pallas kernels, network(): pl.pallas_call(network_kernel, grid_spec=pltpu.PrefetchScalarGridSpec(num...  35.6 us
    all_to_all x1, waiting for transfers between devices, local(): lax.all_to_all(result.reshape(features, experts, width), 'lon', split_axi...  28.3 us
    all_to_all x1, waiting for transfers between devices, local(): lax.all_to_all(part, 'lon', split_axis=1, concat_axis=1, tiled=True)  24 us
    scatter x1, local copies, waits for them, and re-layouts, local(): jnp.zeros((features, experts * capacity), jnp.bfloat16).at[:, targets]  12.4 us
    gather x1, local copies, waits for them, and re-layouts, local(): tendency = returned.reshape(features, -1)[:, targets]  12.1 us
    pallas_call x2, Pallas kernels, sweep(): pl.pallas_call(sweep_kernel, grid=(nb,), in_specs=[big, edge_row, edge_ro...  11.9 us
    all_to_all x1, starting transfers between devices, local(): lax.all_to_all(part, 'lon', split_axis=1, concat_axis=1, tiled=True)  10.6 us
    ppermute x2, starting transfers between devices, step(): hs = lax.ppermute(x[:, rows - 1:, :], 'lat', lat_forward)  8.79 us
  transfers between devices with their start and end apart: 10, of which 3 were waited for; matrix products, arithmetic and copies ran while one was open for 4% of the time, Pallas kernels for 0%

profile of v5, /device:TPU:1, one launch (start us, length us, event | category | flops | bytes accessed | tf_op | source)
XLA Modules:
  0.0 197.2 jit_solution(7547084578945980356)
XLA Ops:
  0.0 4.0 %slice_reduce_fusion.2 = (f32[128,32]{1,0:T(8,128)S(1)}, f32[128,32]{1,0:T(8,128)S(1)}) fusion(f32[128,32,128]{2,1,0:T(8,128)} %bitcast.55), kind=kLoop, calls=%fused_computation.4 | loop fusion | bytes 65536 | tf_op jit(solution)/shard_map/slice | solution.py:70
  4.1 1.5 collective-permute-start.2
  5.7 1.3 collective-permute-start.3
  9.7 4.2 %collective-permute-start.1 = (f32[128,1,128]{2,1,0:T(1,128)S(1)}, f32[128,1,128]{2,1,0:T(1,128)S(1)}, u32[]{:S(2)}, u32[]{:S(2)}) collective-permute-start(f32[128,1,128]{2,1,0:T(1,128)S(1)} %get-tuple-element.11), channel_id=1, source_target_pairs={{0,32},{32,64},{64,96},{1,33},{33,65},{65,97},{2,34},{34,66},{66,9... | collective-permute-start | bytes 196616 | tf_op jit(solution)/shard_map/ppermute | solution.py:68
  16.2 6.0 %shard_map.73.q_ref = f32[128,32,128]{2,1,0:T(8,128)} custom-call(f32[128,32,128]{2,1,0:T(8,128)} %bitcast.57, f32[128,1,128]{2,1,0:T(1,128)} %copy-done.7, f32[128,1,128]{2,1,0:T(1,128)} %copy-done.9, f32[4,32,32]{2,1,0:T(8,128)} %copy-done.5, f32[4,32,32]{2,1,0:T(8,128)} %copy-done.6, f32[32,32,128]{2,1,0:T(8,128)} %get-tuple-element.14.u_ref, ...), custom_call_target="tpu_custom_call" | custom-call | flops 10485760 | bytes 5767168 | tf_op jit(solution)/shard_map/pallas_call | solution.py:48
  22.2 3.9 %slice_reduce_fusion = (f32[128,32]{1,0:T(8,128)S(1)}, f32[128,32]{1,0:T(8,128)S(1)}) fusion(f32[128,32,128]{2,1,0:T(8,128)} %shard_map.73.q_ref), kind=kLoop, calls=%fused_computation.2 | loop fusion | bytes 65536 | tf_op jit(solution)/shard_map/slice | solution.py:70
  26.1 1.3 fusion.9
  27.5 4.1 %collective-permute-start.6 = (f32[4,32,32]{2,1,0:T(8,128)S(1)}, f32[4,32,32]{2,1,0:T(8,128)S(1)}, u32[]{:S(2)}, u32[]{:S(2)}) collective-permute-start(f32[4,32,32]{2,1,0:T(8,128)S(1)} %bitcast.77), channel_id=1, source_target_pairs={{1,0},{2,1},{3,2},{4,3},{5,4},{6,5},{7,6},{8,7},{9,8},{10,9},{11,1... | collective-permute-start | bytes 49160 | tf_op jit(solution)/shard_map/ppermute | solution.py:69
  33.0 4.6 %collective-permute-start.5 = (f32[128,1,128]{2,1,0:T(1,128)S(1)}, f32[128,1,128]{2,1,0:T(1,128)S(1)}, u32[]{:S(2)}, u32[]{:S(2)}) collective-permute-start(f32[128,1,128]{2,1,0:T(1,128)S(1)} %get-tuple-element.9), channel_id=1, source_target_pairs={{0,32},{32,64},{64,96},{1,33},{33,65},{65,97},{2,34},{34,66},{66,9... | collective-permute-start | bytes 196616 | tf_op jit(solution)/shard_map/ppermute | solution.py:68
  39.6 6.0 %shard_map.74 = f32[128,32,128]{2,1,0:T(8,128)} custom-call(f32[128,32,128]{2,1,0:T(8,128)} %shard_map.73.q_ref, f32[128,1,128]{2,1,0:T(1,128)} %copy-done.11, f32[128,1,128]{2,1,0:T(1,128)} %copy-done.12, f32[4,32,32]{2,1,0:T(8,128)} %copy-done.8, f32[4,32,32]{2,1,0:T(8,128)} %copy-done.10, f32[32,32,128]{2,1,0:T(8,128)} %get-tuple-element.14.u_ref, ...), custom_call_target="tpu_custom_call" | custom-call | flops 10485760 | bytes 5767168 | tf_op jit(solution)/shard_map/pallas_call | solution.py:48
  45.6 1.8 convert_element_type.39
  48.4 12.4 %scatter_custom_fusion = bf16[128,8192]{0,1:T(8,128)(2,1)} fusion(s32[4096]{0:T(1024)S(1)} %bitcast.72, bf16[4096,128]{1,0:T(8,128)(2,1)S(1)} %bitcast.63, bf16[]{:T(256)} %constant.8.clone.1), kind=kCustom, calls=%fused_computation.11 | custom fusion | bytes 2097154 | tf_op jit(solution)/shard_map/scatter | solution.py:172
  60.8 10.6 %all-to-all-start = ((bf16[128,32,256]{0,2,1:T(8,128)(2,1)}), bf16[128,32,256]{0,2,1:T(8,128)(2,1)S(1)}, u32[]{:S(2)}, u32[]{:S(2)}) async-start(bf16[128,32,256]{0,2,1:T(8,128)(2,1)} %bitcast.59), calls=%async_computation | async-start | bytes 4194304 | tf_op jit(solution)/shard_map/all_to_all | solution.py:179
  71.4 2.7 %copy.49 = bf16[1,3,512,512]{2,3,1,0:T(8,128)(2,1)} copy(bf16[1,3,512,512]{3,2,1,0:T(8,128)(2,1)} %param.12) | data formatting | bytes 3145728 | tf_op args[5]
  75.7 24.0 %all-to-all-done = bf16[128,32,256]{0,2,1:T(8,128)(2,1)S(1)} async-done(((bf16[128,32,256]{0,2,1:T(8,128)(2,1)}), bf16[128,32,256]{0,2,1:T(8,128)(2,1)S(1)}, u32[]{:S(2)}, u32[]{:S(2)}) %all-to-all-start) | async-done | bytes 2097184 | tf_op jit(solution)/shard_map/all_to_all | solution.py:179
  99.7 1.3 copy-done.1
  102.9 1.9 reduce_or.9
  105.5 35.6 %shard_map.75 = bf16[8192,128]{1,0:T(8,128)(2,1)} custom-call(s32[32]{0:T(128)} %select_reduce_fusion.filled_ref, bf16[8192,128]{1,0:T(8,128)(2,1)} %bitcast.58, bf16[128,512]{1,0:T(8,128)(2,1)} %bitcast.68, bf16[3,512,512]{2,1,0:T(8,128)(2,1)} %bitcast.62, bf16[512,128]{1,0:T(8,128)(2,1)} %bitcast.69), custom_call_target="tpu_custom_call" | custom-call | flops 15032385536 | bytes 6029312 | tf_op jit(solution)/shard_map/pallas_call | solution.py:135
  141.1 7.6 %all-to-all-start.1 = ((bf16[128,32,256]{0,2,1:T(8,128)(2,1)}), bf16[128,32,256]{0,2,1:T(8,128)(2,1)S(1)}, u32[]{:S(2)}, u32[]{:S(2)}) async-start(bf16[128,32,256]{0,2,1:T(8,128)(2,1)} %bitcast.61), calls=%async_computation.1 | async-start | bytes 4194304 | tf_op jit(solution)/shard_map/all_to_all | solution.py:183
  148.7 28.3 %all-to-all-done.1 = bf16[128,32,256]{0,2,1:T(8,128)(2,1)S(1)} async-done(((bf16[128,32,256]{0,2,1:T(8,128)(2,1)}), bf16[128,32,256]{0,2,1:T(8,128)(2,1)S(1)}, u32[]{:S(2)}, u32[]{:S(2)}) %all-to-all-start.1) | async-done | bytes 2097184 | tf_op jit(solution)/shard_map/all_to_all | solution.py:183
  177.0 12.1 %gather_fusion = bf16[4096,128]{1,0:T(8,128)(2,1)S(1)} fusion(bf16[128,8192]{0,1:T(8,128)(2,1)S(1)} %bitcast.54, s32[4096]{0:T(1024)S(1)} %broadcast_clamp_fusion), kind=kCustom, calls=%fused_computation | custom fusion | bytes 2113536 | tf_op jit(solution)/shard_map/gather | solution.py:186
  189.1 1.5 convert_element_type.44
  190.6 3.2 %copy.61 = f32[128,32,128]{2,1,0:T(8,128)} copy(f32[128,32,128]{0,2,1:T(8,128)} %bitcast.60) | data formatting | bytes 4194304 | tf_op jit(solution)/shard_map/convert_element_type | solution.py:187
  193.8 3.4 %add.40 = f32[128,32,128]{2,1,0:T(8,128)} add(f32[128,32,128]{2,1,0:T(8,128)S(1)} %copy-done, f32[128,32,128]{2,1,0:T(8,128)} %copy.61) | non-fusion elementwise | flops 524288 | bytes 6291456 | tf_op jit(solution)/shard_map/add | solution.py:187
  (57 shorter events, 13.6 us)
Async XLA Ops:
  0.0 13.8 %copy-start.2 = (f32[2,32,32,128]{3,2,1,0:T(8,128)S(1)}, f32[2,32,32,128]{3,2,1,0:T(8,128)}, u32[]{:S(2)}) copy-start(f32[2,32,32,128]{3,2,1,0:T(8,128)} %param.8) | copy-start | bytes 3145732
  4.0 10.9 %copy-start.13 = (s32[1,4096,1]{1,2,0:T(1,128)S(1)}, s32[1,4096,1]{1,2,0:T(1,128)}, u32[]{:S(2)}) copy-start(s32[1,4096,1]{1,2,0:T(1,128)} %param.10) | copy-start | bytes 49156
  4.1 11.4 %collective-permute-start.2 = (f32[4,32,32]{2,1,0:T(8,128)S(1)}, f32[4,32,32]{2,1,0:T(8,128)S(1)}, u32[]{:S(2)}, u32[]{:S(2)}) collective-permute-start(f32[4,32,32]{2,1,0:T(8,128)S(1)} %bitcast.75), channel_id=1, source_target_pairs={{1,0},{2,1},{3,2},{4,3},{5,4},{6,5},{7,6},{8,7},{9,8},{10,9},{11,1... | collective-permute-start | bytes 49160 | tf_op jit(solution)/shard_map/ppermute | solution.py:69
  5.7 9.8 %collective-permute-start.3 = (f32[4,32,32]{2,1,0:T(8,128)S(1)}, f32[4,32,32]{2,1,0:T(8,128)S(1)}, u32[]{:S(2)}, u32[]{:S(2)}) collective-permute-start(f32[4,32,32]{2,1,0:T(8,128)S(1)} %bitcast.76), channel_id=1, source_target_pairs={{0,1},{1,2},{2,3},{3,4},{4,5},{5,6},{6,7},{7,8},{8,9},{9,10},{10,1... | collective-permute-start | bytes 49160 | tf_op jit(solution)/shard_map/ppermute | solution.py:70
  8.4 7.2 %collective-permute-start = (f32[128,1,128]{2,1,0:T(1,128)S(1)}, f32[128,1,128]{2,1,0:T(1,128)S(1)}, u32[]{:S(2)}, u32[]{:S(2)}) collective-permute-start(f32[128,1,128]{2,1,0:T(1,128)S(1)} %get-tuple-element.12), channel_id=1, source_target_pairs={{32,0},{64,32},{96,64},{33,1},{65,33},{97,65},{34,2},{66,34},{98,6... | collective-permute-start | bytes 196616 | tf_op jit(solution)/shard_map/ppermute | solution.py:67
  9.7 5.9 %collective-permute-start.1 = (f32[128,1,128]{2,1,0:T(1,128)S(1)}, f32[128,1,128]{2,1,0:T(1,128)S(1)}, u32[]{:S(2)}, u32[]{:S(2)}) collective-permute-start(f32[128,1,128]{2,1,0:T(1,128)S(1)} %get-tuple-element.11), channel_id=1, source_target_pairs={{0,32},{32,64},{64,96},{1,33},{33,65},{65,97},{2,34},{34,66},{66,9... | collective-permute-start | bytes 196616 | tf_op jit(solution)/shard_map/ppermute | solution.py:68
  15.5 0.6 copy-start.5
  15.5 0.6 copy-start.6
  15.6 0.6 copy-start.7
  15.6 0.6 copy-start.9
  27.5 10.2 %collective-permute-start.6 = (f32[4,32,32]{2,1,0:T(8,128)S(1)}, f32[4,32,32]{2,1,0:T(8,128)S(1)}, u32[]{:S(2)}, u32[]{:S(2)}) collective-permute-start(f32[4,32,32]{2,1,0:T(8,128)S(1)} %bitcast.77), channel_id=1, source_target_pairs={{1,0},{2,1},{3,2},{4,3},{5,4},{6,5},{7,6},{8,7},{9,8},{10,9},{11,1... | collective-permute-start | bytes 49160 | tf_op jit(solution)/shard_map/ppermute | solution.py:69
  31.7 6.1 %collective-permute-start.7 = (f32[4,32,32]{2,1,0:T(8,128)S(1)}, f32[4,32,32]{2,1,0:T(8,128)S(1)}, u32[]{:S(2)}, u32[]{:S(2)}) collective-permute-start(f32[4,32,32]{2,1,0:T(8,128)S(1)} %bitcast.78), channel_id=1, source_target_pairs={{0,1},{1,2},{2,3},{3,4},{4,5},{5,6},{6,7},{7,8},{8,9},{9,10},{10,1... | collective-permute-start | bytes 49160 | tf_op jit(solution)/shard_map/ppermute | solution.py:70
  31.7 6.0 %collective-permute-start.4 = (f32[128,1,128]{2,1,0:T(1,128)S(1)}, f32[128,1,128]{2,1,0:T(1,128)S(1)}, u32[]{:S(2)}, u32[]{:S(2)}) collective-permute-start(f32[128,1,128]{2,1,0:T(1,128)S(1)} %get-tuple-element.10), channel_id=1, source_target_pairs={{32,0},{64,32},{96,64},{33,1},{65,33},{97,65},{34,2},{66,34},{98,6... | collective-permute-start | bytes 196616 | tf_op jit(solution)/shard_map/ppermute | solution.py:67
  33.0 5.9 %collective-permute-start.5 = (f32[128,1,128]{2,1,0:T(1,128)S(1)}, f32[128,1,128]{2,1,0:T(1,128)S(1)}, u32[]{:S(2)}, u32[]{:S(2)}) collective-permute-start(f32[128,1,128]{2,1,0:T(1,128)S(1)} %get-tuple-element.9), channel_id=1, source_target_pairs={{0,32},{32,64},{64,96},{1,33},{33,65},{65,97},{2,34},{34,66},{66,9... | collective-permute-start | bytes 196616 | tf_op jit(solution)/shard_map/ppermute | solution.py:68
  37.7 1.3 copy-start.8
  37.7 1.2 copy-start.10
  37.7 1.2 copy-start.11
  39.0 0.6 copy-start.12
  60.8 38.9 %all-to-all-start = ((bf16[128,32,256]{0,2,1:T(8,128)(2,1)}), bf16[128,32,256]{0,2,1:T(8,128)(2,1)S(1)}, u32[]{:S(2)}, u32[]{:S(2)}) async-start(bf16[128,32,256]{0,2,1:T(8,128)(2,1)} %bitcast.59), calls=%async_computation | async-start | bytes 4194304 | tf_op jit(solution)/shard_map/all_to_all | solution.py:179
  71.4 2.7 %copy-start.3 = (bf16[1,512,128]{2,1,0:T(8,128)(2,1)S(1)}, bf16[1,512,128]{2,1,0:T(8,128)(2,1)}, u32[]{:S(2)}) copy-start(bf16[1,512,128]{2,1,0:T(8,128)(2,1)} %param.11) | copy-start | bytes 393220
  71.4 3.5 %copy-start.4 = (bf16[1,128,512]{2,1,0:T(8,128)(2,1)S(1)}, bf16[1,128,512]{2,1,0:T(8,128)(2,1)}, u32[]{:S(2)}) copy-start(bf16[1,128,512]{2,1,0:T(8,128)(2,1)} %param.13) | copy-start | bytes 393220
  99.7 1.3 copy-start.1
  141.1 35.9 %all-to-all-start.1 = ((bf16[128,32,256]{0,2,1:T(8,128)(2,1)}), bf16[128,32,256]{0,2,1:T(8,128)(2,1)S(1)}, u32[]{:S(2)}, u32[]{:S(2)}) async-start(bf16[128,32,256]{0,2,1:T(8,128)(2,1)} %bitcast.61), calls=%async_computation.1 | async-start | bytes 4194304 | tf_op jit(solution)/shard_map/all_to_all | solution.py:183
  190.6 3.2 %copy-start = (f32[128,32,128]{2,1,0:T(8,128)S(1)}, f32[128,32,128]{2,1,0:T(8,128)}, u32[]{:S(2)}) copy-start(f32[128,32,128]{2,1,0:T(8,128)} %shard_map.74) | copy-start | bytes 6291460

commit v6 on v5

--- a/solution.py
+++ b/solution.py
@@ -88,8 +88,8 @@
     return position.reshape(count).astype(jnp.int32)
 
 
-ROWS = 256
-HALF = ROWS // 2
+ROWS = 1024
+HALF = 128
 
 
 def silu(t):
@@ -105,45 +105,44 @@
     return jnp.dot(hidden, w_last, preferred_element_type=jnp.float32).astype(jnp.bfloat16)
 
 
-def network_kernel(filled_ref, x_ref, first_ref, middle_ref, last_ref, o_ref):
-    filled = filled_ref[pl.program_id(0)]
-
-    @pl.when(filled == 2)
+def network_kernel(active_ref, x_ref, first_ref, middle_ref, last_ref, o_ref):
+    @pl.when(pl.program_id(0) < active_ref[0])
     def _():
         o_ref[...] = layers(x_ref[...], first_ref[...], middle_ref[...], last_ref[...])
 
-    @pl.when(filled == 1)
-    def _():
-        o_ref[:HALF, :] = layers(x_ref[:HALF, :], first_ref[...], middle_ref[...], last_ref[...])
-        o_ref[HALF:, :] = jnp.zeros((ROWS - HALF, o_ref.shape[1]), o_ref.dtype)
-
-    @pl.when(filled == 0)
+    @pl.when(pl.program_id(0) >= active_ref[0])
     def _():
         o_ref[...] = jnp.zeros(o_ref.shape, o_ref.dtype)
 
 
 def network(rows_in, input_weight, middle_weight, output_weight):
     count, feats = rows_in.shape
-    blocks = count // ROWS
+    groups = count // HALF
     hid = input_weight.shape[1]
     first = input_weight[0].T
     middle = jnp.swapaxes(middle_weight[0], 1, 2)
     last = output_weight[0].T
-    nonzero = jnp.any(rows_in.reshape(blocks, 2, HALF * feats) != 0, axis=2)
-    filled = jnp.where(nonzero[:, 1], 2, jnp.where(nonzero[:, 0], 1, 0)).astype(jnp.int32)
+    grouped = rows_in.reshape(groups, HALF * feats)
+    nonzero = jnp.any(grouped != 0, axis=1).astype(jnp.int32)
+    used = jnp.sum(nonzero)
+    ahead = jnp.cumsum(nonzero) - nonzero
+    place = jnp.where(nonzero > 0, ahead, used + jnp.arange(groups, dtype=jnp.int32) - ahead)
+    source = jnp.zeros((groups,), jnp.int32).at[place].set(jnp.arange(groups, dtype=jnp.int32))
+    packed_rows = grouped[source].reshape(count, feats)
+    active = ((used * HALF + ROWS - 1) // ROWS).reshape(1)
     mats = 2 * (hid * feats * 2 + middle_weight.shape[1] * hid * hid)
-    return pl.pallas_call(
+    out = pl.pallas_call(
         network_kernel,
         grid_spec=pltpu.PrefetchScalarGridSpec(
             num_scalar_prefetch=1,
-            grid=(blocks,),
+            grid=(count // ROWS,),
             in_specs=[
-                pl.BlockSpec((ROWS, feats), lambda i, f: (i, 0)),
-                pl.BlockSpec(first.shape, lambda i, f: (0, 0)),
-                pl.BlockSpec(middle.shape, lambda i, f: (0, 0, 0)),
-                pl.BlockSpec(last.shape, lambda i, f: (0, 0)),
+                pl.BlockSpec((ROWS, feats), lambda i, a: (i, 0)),
+                pl.BlockSpec(first.shape, lambda i, a: (0, 0)),
+                pl.BlockSpec(middle.shape, lambda i, a: (0, 0, 0)),
+                pl.BlockSpec(last.shape, lambda i, a: (0, 0)),
             ],
-            out_specs=pl.BlockSpec((ROWS, feats), lambda i, f: (i, 0)),
+            out_specs=pl.BlockSpec((ROWS, feats), lambda i, a: (i, 0)),
         ),
         out_shape=jax.ShapeDtypeStruct((count, feats), jnp.bfloat16),
         cost_estimate=pl.CostEstimate(
@@ -151,7 +150,8 @@
             bytes_accessed=4 * count * feats + 2 * (mats // 2),
             transcendentals=(1 + middle_weight.shape[1]) * hid * count,
         ),
-    )(filled, rows_in, first, middle, last)
+    )(active, packed_rows, first, middle, last)
+    return out.reshape(groups, HALF * feats)[place].reshape(count, feats)
 
 
 def local(

time: 199 us -> 201 us (1.010)
  local copies, waits for them, and re-layouts: 48.8 us -> 67.5 us
  Pallas kernels: 47.5 us -> 31.2 us
    pallas_call x1, Pallas kernels: 35.6 us -> 19.3 us  [network(): pl.pallas_call(network_kernel, grid_spec=pltpu.PrefetchScalarGridSpec(num...]
    reshape x0 -> x4, local copies, waits for them, and re-layouts: none -> 14.1 us  [the longest x2 7.03 us: network(): return out.reshape(groups, HALF * feats)[place].reshape(count, feats)]
    gather x0 -> x2, local copies, waits for them, and re-layouts: none -> 6.38 us  [the longest x1 3.19 us: network(): packed_rows = grouped[source].reshape(count, feats)]
where the time goes in v6:
time: 201 us
  local copies, waits for them, and re-layouts  67.5 us (34%)
  waiting for transfers between devices  53.7 us (27%)
  starting transfers between devices  37.5 us (19%)
  Pallas kernels  31.2 us (16%)
  other arithmetic  9.73 us (5%)
    all_to_all x1, waiting for transfers between devices, local(): lax.all_to_all(result.reshape(features, experts, width), 'lon', split_axi...  28.4 us
    all_to_all x1, waiting for transfers between devices, local(): lax.all_to_all(part, 'lon', split_axis=1, concat_axis=1, tiled=True)  24.1 us
    pallas_call x1, Pallas kernels, network(): pl.pallas_call(network_kernel, grid_spec=pltpu.PrefetchScalarGridSpec(num...  19.3 us
    scatter x1, local copies, waits for them, and re-layouts, local(): jnp.zeros((features, experts * capacity), jnp.bfloat16).at[:, targets]  12.4 us
    gather x1, local copies, waits for them, and re-layouts, local(): tendency = returned.reshape(features, -1)[:, targets]  12.1 us
    pallas_call x2, Pallas kernels, sweep(): pl.pallas_call(sweep_kernel, grid=(nb,), in_specs=[big, edge_row, edge_ro...  11.9 us
    all_to_all x1, starting transfers between devices, local(): lax.all_to_all(part, 'lon', split_axis=1, concat_axis=1, tiled=True)  10.6 us
    ppermute x2, starting transfers between devices, step(): hs = lax.ppermute(x[:, rows - 1:, :], 'lat', lat_forward)  8.79 us
  transfers between devices with their start and end apart: 10, of which 3 were waited for; matrix products, arithmetic and copies ran while one was open for 4% of the time, Pallas kernels for 0%

profile of v6, /device:TPU:1, one launch (start us, length us, event | category | flops | bytes accessed | tf_op | source)
XLA Modules:
  0.0 201.0 jit_solution(10709738631388061007)
XLA Ops:
  0.0 4.0 %slice_reduce_fusion.2 = (f32[128,32]{1,0:T(8,128)S(1)}, f32[128,32]{1,0:T(8,128)S(1)}) fusion(f32[128,32,128]{2,1,0:T(8,128)} %bitcast.60), kind=kLoop, calls=%fused_computation.8 | loop fusion | bytes 65536 | tf_op jit(solution)/shard_map/slice | solution.py:70
  9.7 4.2 %collective-permute-start.1 = (f32[128,1,128]{2,1,0:T(1,128)S(1)}, f32[128,1,128]{2,1,0:T(1,128)S(1)}, u32[]{:S(2)}, u32[]{:S(2)}) collective-permute-start(f32[128,1,128]{2,1,0:T(1,128)S(1)} %get-tuple-element.11), channel_id=1, source_target_pairs={{0,32},{32,64},{64,96},{1,33},{33,65},{65,97},{2,34},{34,66},{66,9... | collective-permute-start | bytes 196616 | tf_op jit(solution)/shard_map/ppermute | solution.py:68
  16.2 6.0 %shard_map.73.q_ref = f32[128,32,128]{2,1,0:T(8,128)} custom-call(f32[128,32,128]{2,1,0:T(8,128)} %bitcast.62, f32[128,1,128]{2,1,0:T(1,128)} %copy-done.7, f32[128,1,128]{2,1,0:T(1,128)} %copy-done.9, f32[4,32,32]{2,1,0:T(8,128)} %copy-done.5, f32[4,32,32]{2,1,0:T(8,128)} %copy-done.6, f32[32,32,128]{2,1,0:T(8,128)} %get-tuple-element.14.u_ref, ...), custom_call_target="tpu_custom_call" | custom-call | flops 10485760 | bytes 5767168 | tf_op jit(solution)/shard_map/pallas_call | solution.py:48
  22.1 3.9 %slice_reduce_fusion = (f32[128,32]{1,0:T(8,128)S(1)}, f32[128,32]{1,0:T(8,128)S(1)}) fusion(f32[128,32,128]{2,1,0:T(8,128)} %shard_map.73.q_ref), kind=kLoop, calls=%fused_computation.6 | loop fusion | bytes 65536 | tf_op jit(solution)/shard_map/slice | solution.py:70
  27.5 4.1 %collective-permute-start.6 = (f32[4,32,32]{2,1,0:T(8,128)S(1)}, f32[4,32,32]{2,1,0:T(8,128)S(1)}, u32[]{:S(2)}, u32[]{:S(2)}) collective-permute-start(f32[4,32,32]{2,1,0:T(8,128)S(1)} %bitcast.82), channel_id=1, source_target_pairs={{1,0},{2,1},{3,2},{4,3},{5,4},{6,5},{7,6},{8,7},{9,8},{10,9},{11,1... | collective-permute-start | bytes 49160 | tf_op jit(solution)/shard_map/ppermute | solution.py:69
  33.0 4.6 %collective-permute-start.5 = (f32[128,1,128]{2,1,0:T(1,128)S(1)}, f32[128,1,128]{2,1,0:T(1,128)S(1)}, u32[]{:S(2)}, u32[]{:S(2)}) collective-permute-start(f32[128,1,128]{2,1,0:T(1,128)S(1)} %get-tuple-element.9), channel_id=1, source_target_pairs={{0,32},{32,64},{64,96},{1,33},{33,65},{65,97},{2,34},{34,66},{66,9... | collective-permute-start | bytes 196616 | tf_op jit(solution)/shard_map/ppermute | solution.py:68
  39.6 6.0 %shard_map.74 = f32[128,32,128]{2,1,0:T(8,128)} custom-call(f32[128,32,128]{2,1,0:T(8,128)} %shard_map.73.q_ref, f32[128,1,128]{2,1,0:T(1,128)} %copy-done.11, f32[128,1,128]{2,1,0:T(1,128)} %copy-done.12, f32[4,32,32]{2,1,0:T(8,128)} %copy-done.8, f32[4,32,32]{2,1,0:T(8,128)} %copy-done.10, f32[32,32,128]{2,1,0:T(8,128)} %get-tuple-element.14.u_ref, ...), custom_call_target="tpu_custom_call" | custom-call | flops 10485760 | bytes 5767168 | tf_op jit(solution)/shard_map/pallas_call | solution.py:48
  45.6 1.8 convert_element_type.58
  48.4 12.4 %scatter_custom_fusion = bf16[128,8192]{0,1:T(8,128)(2,1)} fusion(s32[4096]{0:T(1024)S(1)} %bitcast.77, bf16[4096,128]{1,0:T(8,128)(2,1)S(1)} %bitcast.68, bf16[]{:T(256)} %constant.15.clone.1), kind=kCustom, calls=%fused_computation.14 | custom fusion | bytes 2097154 | tf_op jit(solution)/shard_map/scatter | solution.py:172
  60.8 10.6 %all-to-all-start = ((bf16[128,32,256]{0,2,1:T(8,128)(2,1)}), bf16[128,32,256]{0,2,1:T(8,128)(2,1)S(1)}, u32[]{:S(2)}, u32[]{:S(2)}) async-start(bf16[128,32,256]{0,2,1:T(8,128)(2,1)} %bitcast.64), calls=%async_computation | async-start | bytes 4194304 | tf_op jit(solution)/shard_map/all_to_all | solution.py:179
  71.4 2.7 %copy.45 = bf16[1,3,512,512]{2,3,1,0:T(8,128)(2,1)} copy(bf16[1,3,512,512]{3,2,1,0:T(8,128)(2,1)} %param.12) | data formatting | bytes 3145728 | tf_op args[5]
  75.6 24.1 %all-to-all-done = bf16[128,32,256]{0,2,1:T(8,128)(2,1)S(1)} async-done(((bf16[128,32,256]{0,2,1:T(8,128)(2,1)}), bf16[128,32,256]{0,2,1:T(8,128)(2,1)S(1)}, u32[]{:S(2)}, u32[]{:S(2)}) %all-to-all-start) | async-done | bytes 2097184 | tf_op jit(solution)/shard_map/all_to_all | solution.py:179
  104.0 2.8 %reshape.154 = bf16[64,16384]{1,0:T(8,128)(2,1)S(1)} reshape(bf16[8192,128]{1,0:T(8,128)(2,1)} %bitcast.63) | data formatting | bytes 4194304 | tf_op jit(solution)/shard_map/reshape | solution.py:125
  106.8 3.2 %gather_fusion = bf16[64,16384]{1,0:T(8,128)(2,1)} fusion(bf16[64,16384]{1,0:T(8,128)(2,1)S(1)} %reshape.154, s32[1024]{0:T(1024)S(1)} %pad_clamp_fusion.1), kind=kCustom, calls=%fused_computation | custom fusion | bytes 4194560 | tf_op jit(solution)/shard_map/gather | solution.py:131
  110.0 4.2 %reshape.155.x_ref = bf16[8192,128]{1,0:T(8,128)(2,1)} reshape(bf16[64,16384]{1,0:T(8,128)(2,1)} %gather_fusion) | data formatting | bytes 4194304 | tf_op jit(solution)/shard_map/reshape | solution.py:131
  114.2 19.3 %shard_map.75 = bf16[8192,128]{1,0:T(8,128)(2,1)} custom-call(s32[1]{0:T(128)} %bitcast.19.active_ref, bf16[8192,128]{1,0:T(8,128)(2,1)} %reshape.155.x_ref, bf16[128,512]{1,0:T(8,128)(2,1)} %bitcast.73, bf16[3,512,512]{2,1,0:T(8,128)(2,1)} %bitcast.67, bf16[512,128]{1,0:T(8,128)(2,1)} %bitcast.74), custom_call_target="tpu_custom_call" | custom-call | flops 15032385536 | bytes 6029312 | tf_op jit(solution)/shard_map/pallas_call | solution.py:134
  133.5 2.8 %reshape.156 = bf16[64,16384]{1,0:T(8,128)(2,1)S(1)} reshape(bf16[8192,128]{1,0:T(8,128)(2,1)} %shard_map.75) | data formatting | bytes 4194304 | tf_op jit(solution)/shard_map/reshape | solution.py:154
  136.3 3.2 %gather_fusion.1 = bf16[64,16384]{1,0:T(8,128)(2,1)} fusion(bf16[64,16384]{1,0:T(8,128)(2,1)S(1)} %reshape.156, s32[1024]{0:T(1024)S(1)} %pad_clamp_fusion), kind=kCustom, calls=%fused_computation.1 | custom fusion | bytes 4194560 | tf_op jit(solution)/shard_map/gather | solution.py:154
  139.5 4.2 %reshape.157 = bf16[8192,128]{1,0:T(8,128)(2,1)} reshape(bf16[64,16384]{1,0:T(8,128)(2,1)} %gather_fusion.1) | data formatting | bytes 4194304 | tf_op jit(solution)/shard_map/reshape | solution.py:154
  143.7 8.6 %all-to-all-start.1 = ((bf16[128,32,256]{0,2,1:T(8,128)(2,1)}), bf16[128,32,256]{0,2,1:T(8,128)(2,1)S(1)}, u32[]{:S(2)}, u32[]{:S(2)}) async-start(bf16[128,32,256]{0,2,1:T(8,128)(2,1)} %bitcast.65), calls=%async_computation.1 | async-start | bytes 4194304 | tf_op jit(solution)/shard_map/all_to_all | solution.py:183
  152.4 28.4 %all-to-all-done.1 = bf16[128,32,256]{0,2,1:T(8,128)(2,1)S(1)} async-done(((bf16[128,32,256]{0,2,1:T(8,128)(2,1)}), bf16[128,32,256]{0,2,1:T(8,128)(2,1)S(1)}, u32[]{:S(2)}, u32[]{:S(2)}) %all-to-all-start.1) | async-done | bytes 2097184 | tf_op jit(solution)/shard_map/all_to_all | solution.py:183
  180.7 12.1 %gather_fusion.2 = bf16[4096,128]{1,0:T(8,128)(2,1)S(1)} fusion(bf16[128,8192]{0,1:T(8,128)(2,1)S(1)} %bitcast.59, s32[4096]{0:T(1024)S(1)} %broadcast_clamp_fusion), kind=kCustom, calls=%fused_computation.2 | custom fusion | bytes 2113536 | tf_op jit(solution)/shard_map/gather | solution.py:186
  194.3 3.2 %copy.57 = f32[128,32,128]{2,1,0:T(8,128)} copy(f32[128,32,128]{0,2,1:T(8,128)} %bitcast.66) | data formatting | bytes 4194304 | tf_op jit(solution)/shard_map/convert_element_type | solution.py:187
  197.6 3.4 %add.76 = f32[128,32,128]{2,1,0:T(8,128)} add(f32[128,32,128]{2,1,0:T(8,128)S(1)} %copy-done, f32[128,32,128]{2,1,0:T(8,128)} %copy.57) | non-fusion elementwise | flops 524288 | bytes 6291456 | tf_op jit(solution)/shard_map/add | solution.py:187
  (71 shorter events, 20.2 us)
Async XLA Ops:
  0.0 13.8 %copy-start.2 = (f32[2,32,32,128]{3,2,1,0:T(8,128)S(1)}, f32[2,32,32,128]{3,2,1,0:T(8,128)}, u32[]{:S(2)}) copy-start(f32[2,32,32,128]{3,2,1,0:T(8,128)} %param.8) | copy-start | bytes 3145732
  4.0 10.9 %copy-start.13 = (s32[1,4096,1]{1,2,0:T(1,128)S(1)}, s32[1,4096,1]{1,2,0:T(1,128)}, u32[]{:S(2)}) copy-start(s32[1,4096,1]{1,2,0:T(1,128)} %param.10) | copy-start | bytes 49156
  4.1 11.4 %collective-permute-start.2 = (f32[4,32,32]{2,1,0:T(8,128)S(1)}, f32[4,32,32]{2,1,0:T(8,128)S(1)}, u32[]{:S(2)}, u32[]{:S(2)}) collective-permute-start(f32[4,32,32]{2,1,0:T(8,128)S(1)} %bitcast.80), channel_id=1, source_target_pairs={{1,0},{2,1},{3,2},{4,3},{5,4},{6,5},{7,6},{8,7},{9,8},{10,9},{11,1... | collective-permute-start | bytes 49160 | tf_op jit(solution)/shard_map/ppermute | solution.py:69
  5.7 9.8 %collective-permute-start.3 = (f32[4,32,32]{2,1,0:T(8,128)S(1)}, f32[4,32,32]{2,1,0:T(8,128)S(1)}, u32[]{:S(2)}, u32[]{:S(2)}) collective-permute-start(f32[4,32,32]{2,1,0:T(8,128)S(1)} %bitcast.81), channel_id=1, source_target_pairs={{0,1},{1,2},{2,3},{3,4},{4,5},{5,6},{6,7},{7,8},{8,9},{9,10},{10,1... | collective-permute-start | bytes 49160 | tf_op jit(solution)/shard_map/ppermute | solution.py:70
  8.4 7.2 %collective-permute-start = (f32[128,1,128]{2,1,0:T(1,128)S(1)}, f32[128,1,128]{2,1,0:T(1,128)S(1)}, u32[]{:S(2)}, u32[]{:S(2)}) collective-permute-start(f32[128,1,128]{2,1,0:T(1,128)S(1)} %get-tuple-element.12), channel_id=1, source_target_pairs={{32,0},{64,32},{96,64},{33,1},{65,33},{97,65},{34,2},{66,34},{98,6... | collective-permute-start | bytes 196616 | tf_op jit(solution)/shard_map/ppermute | solution.py:67
  9.7 5.9 %collective-permute-start.1 = (f32[128,1,128]{2,1,0:T(1,128)S(1)}, f32[128,1,128]{2,1,0:T(1,128)S(1)}, u32[]{:S(2)}, u32[]{:S(2)}) collective-permute-start(f32[128,1,128]{2,1,0:T(1,128)S(1)} %get-tuple-element.11), channel_id=1, source_target_pairs={{0,32},{32,64},{64,96},{1,33},{33,65},{65,97},{2,34},{34,66},{66,9... | collective-permute-start | bytes 196616 | tf_op jit(solution)/shard_map/ppermute | solution.py:68
  15.5 0.6 copy-start.5
  15.5 0.6 copy-start.6
  15.5 0.6 copy-start.7
  15.6 0.6 copy-start.9
  27.5 10.2 %collective-permute-start.6 = (f32[4,32,32]{2,1,0:T(8,128)S(1)}, f32[4,32,32]{2,1,0:T(8,128)S(1)}, u32[]{:S(2)}, u32[]{:S(2)}) collective-permute-start(f32[4,32,32]{2,1,0:T(8,128)S(1)} %bitcast.82), channel_id=1, source_target_pairs={{1,0},{2,1},{3,2},{4,3},{5,4},{6,5},{7,6},{8,7},{9,8},{10,9},{11,1... | collective-permute-start | bytes 49160 | tf_op jit(solution)/shard_map/ppermute | solution.py:69
  31.6 6.1 %collective-permute-start.7 = (f32[4,32,32]{2,1,0:T(8,128)S(1)}, f32[4,32,32]{2,1,0:T(8,128)S(1)}, u32[]{:S(2)}, u32[]{:S(2)}) collective-permute-start(f32[4,32,32]{2,1,0:T(8,128)S(1)} %bitcast.83), channel_id=1, source_target_pairs={{0,1},{1,2},{2,3},{3,4},{4,5},{5,6},{6,7},{7,8},{8,9},{9,10},{10,1... | collective-permute-start | bytes 49160 | tf_op jit(solution)/shard_map/ppermute | solution.py:70
  31.7 6.0 %collective-permute-start.4 = (f32[128,1,128]{2,1,0:T(1,128)S(1)}, f32[128,1,128]{2,1,0:T(1,128)S(1)}, u32[]{:S(2)}, u32[]{:S(2)}) collective-permute-start(f32[128,1,128]{2,1,0:T(1,128)S(1)} %get-tuple-element.10), channel_id=1, source_target_pairs={{32,0},{64,32},{96,64},{33,1},{65,33},{97,65},{34,2},{66,34},{98,6... | collective-permute-start | bytes 196616 | tf_op jit(solution)/shard_map/ppermute | solution.py:67
  33.0 5.9 %collective-permute-start.5 = (f32[128,1,128]{2,1,0:T(1,128)S(1)}, f32[128,1,128]{2,1,0:T(1,128)S(1)}, u32[]{:S(2)}, u32[]{:S(2)}) collective-permute-start(f32[128,1,128]{2,1,0:T(1,128)S(1)} %get-tuple-element.9), channel_id=1, source_target_pairs={{0,32},{32,64},{64,96},{1,33},{33,65},{65,97},{2,34},{34,66},{66,9... | collective-permute-start | bytes 196616 | tf_op jit(solution)/shard_map/ppermute | solution.py:68
  37.7 1.3 copy-start.8
  37.7 1.2 copy-start.10
  37.7 1.2 copy-start.11
  39.0 0.6 copy-start.12
  60.8 38.9 %all-to-all-start = ((bf16[128,32,256]{0,2,1:T(8,128)(2,1)}), bf16[128,32,256]{0,2,1:T(8,128)(2,1)S(1)}, u32[]{:S(2)}, u32[]{:S(2)}) async-start(bf16[128,32,256]{0,2,1:T(8,128)(2,1)} %bitcast.64), calls=%async_computation | async-start | bytes 4194304 | tf_op jit(solution)/shard_map/all_to_all | solution.py:179
  71.4 2.7 %copy-start.3 = (bf16[1,512,128]{2,1,0:T(8,128)(2,1)S(1)}, bf16[1,512,128]{2,1,0:T(8,128)(2,1)}, u32[]{:S(2)}) copy-start(bf16[1,512,128]{2,1,0:T(8,128)(2,1)} %param.11) | copy-start | bytes 393220
  71.4 3.4 %copy-start.4 = (bf16[1,128,512]{2,1,0:T(8,128)(2,1)S(1)}, bf16[1,128,512]{2,1,0:T(8,128)(2,1)}, u32[]{:S(2)}) copy-start(bf16[1,128,512]{2,1,0:T(8,128)(2,1)} %param.13) | copy-start | bytes 393220
  99.7 4.3 %copy-start.1 = (bf16[128,32,256]{0,2,1:T(8,128)(2,1)}, bf16[128,32,256]{0,2,1:T(8,128)(2,1)S(1)}, u32[]{:S(2)}) copy-start(bf16[128,32,256]{0,2,1:T(8,128)(2,1)S(1)} %all-to-all-done) | copy-start | bytes 6291460
  143.7 37.0 %all-to-all-start.1 = ((bf16[128,32,256]{0,2,1:T(8,128)(2,1)}), bf16[128,32,256]{0,2,1:T(8,128)(2,1)S(1)}, u32[]{:S(2)}, u32[]{:S(2)}) async-start(bf16[128,32,256]{0,2,1:T(8,128)(2,1)} %bitcast.65), calls=%async_computation.1 | async-start | bytes 4194304 | tf_op jit(solution)/shard_map/all_to_all | solution.py:183
  194.3 3.2 %copy-start = (f32[128,32,128]{2,1,0:T(8,128)S(1)}, f32[128,32,128]{2,1,0:T(8,128)}, u32[]{:S(2)}) copy-start(f32[128,32,128]{2,1,0:T(8,128)} %shard_map.74) | copy-start | bytes 6291460

commit v7 on v6

--- a/solution.py
+++ b/solution.py
@@ -105,14 +105,38 @@
     return jnp.dot(hidden, w_last, preferred_element_type=jnp.float32).astype(jnp.bfloat16)
 
 
-def network_kernel(active_ref, x_ref, first_ref, middle_ref, last_ref, o_ref):
-    @pl.when(pl.program_id(0) < active_ref[0])
+def network_kernel(active_ref, source_ref, x_hbm, first_ref, middle_ref, last_ref, o_hbm, buf, res, sems):
+    block = pl.program_id(0)
+    per = ROWS // HALF
+
+    @pl.when(block < active_ref[0])
     def _():
-        o_ref[...] = layers(x_ref[...], first_ref[...], middle_ref[...], last_ref[...])
-
-    @pl.when(pl.program_id(0) >= active_ref[0])
+        loads = []
+        for j in range(per):
+            group = source_ref[block * per + j]
+            copy = pltpu.make_async_copy(
+                x_hbm.at[pl.ds(group * HALF, HALF)], buf.at[pl.ds(j * HALF, HALF)], sems.at[j]
+            )
+            copy.start()
+            loads.append(copy)
+        for copy in loads:
+            copy.wait()
+        res[...] = layers(buf[...], first_ref[...], middle_ref[...], last_ref[...])
+
+    @pl.when(block >= active_ref[0])
     def _():
-        o_ref[...] = jnp.zeros(o_ref.shape, o_ref.dtype)
+        res[...] = jnp.zeros(res.shape, res.dtype)
+
+    stores = []
+    for j in range(per):
+        group = source_ref[block * per + j]
+        copy = pltpu.make_async_copy(
+            res.at[pl.ds(j * HALF, HALF)], o_hbm.at[pl.ds(group * HALF, HALF)], sems.at[per + j]
+        )
+        copy.start()
+        stores.append(copy)
+    for copy in stores:
+        copy.wait()
 
 
 def network(rows_in, input_weight, middle_weight, output_weight):
@@ -122,27 +146,32 @@
     first = input_weight[0].T
     middle = jnp.swapaxes(middle_weight[0], 1, 2)
     last = output_weight[0].T
-    grouped = rows_in.reshape(groups, HALF * feats)
-    nonzero = jnp.any(grouped != 0, axis=1).astype(jnp.int32)
+    grouped = rows_in.reshape(groups, HALF, feats)
+    nonzero = jnp.any(grouped != 0, axis=(1, 2)).astype(jnp.int32)
     used = jnp.sum(nonzero)
     ahead = jnp.cumsum(nonzero) - nonzero
     place = jnp.where(nonzero > 0, ahead, used + jnp.arange(groups, dtype=jnp.int32) - ahead)
     source = jnp.zeros((groups,), jnp.int32).at[place].set(jnp.arange(groups, dtype=jnp.int32))
-    packed_rows = grouped[source].reshape(count, feats)
     active = ((used * HALF + ROWS - 1) // ROWS).reshape(1)
     mats = 2 * (hid * feats * 2 + middle_weight.shape[1] * hid * hid)
-    out = pl.pallas_call(
+    per = ROWS // HALF
+    return pl.pallas_call(
         network_kernel,
         grid_spec=pltpu.PrefetchScalarGridSpec(
-            num_scalar_prefetch=1,
+            num_scalar_prefetch=2,
             grid=(count // ROWS,),
             in_specs=[
-                pl.BlockSpec((ROWS, feats), lambda i, a: (i, 0)),
-                pl.BlockSpec(first.shape, lambda i, a: (0, 0)),
-                pl.BlockSpec(middle.shape, lambda i, a: (0, 0, 0)),
-                pl.BlockSpec(last.shape, lambda i, a: (0, 0)),
+                pl.BlockSpec(memory_space=pl.ANY),
+                pl.BlockSpec(first.shape, lambda i, a, s: (0, 0)),
+                pl.BlockSpec(middle.shape, lambda i, a, s: (0, 0, 0)),
+                pl.BlockSpec(last.shape, lambda i, a, s: (0, 0)),
             ],
-            out_specs=pl.BlockSpec((ROWS, feats), lambda i, a: (i, 0)),
+            out_specs=pl.BlockSpec(memory_space=pl.ANY),
+            scratch_shapes=[
+                pltpu.VMEM((ROWS, feats), jnp.bfloat16),
+                pltpu.VMEM((ROWS, feats), jnp.bfloat16),
+                pltpu.SemaphoreType.DMA((2 * per,)),
+            ],
         ),
         out_shape=jax.ShapeDtypeStruct((count, feats), jnp.bfloat16),
         cost_estimate=pl.CostEstimate(
@@ -150,8 +179,7 @@
             bytes_accessed=4 * count * feats + 2 * (mats // 2),
             transcendentals=(1 + middle_weight.shape[1]) * hid * count,
         ),
-    )(active, packed_rows, first, middle, last)
-    return out.reshape(groups, HALF * feats)[place].reshape(count, feats)
+    )(active, source, rows_in, first, middle, last)
 
 
 def local(

time: 201 us -> 194 us (0.965)
  local copies, waits for them, and re-layouts: 67.5 us -> 47.6 us
  starting transfers between devices: 37.5 us -> 43.8 us
  Pallas kernels: 31.2 us -> 37.3 us
    reshape x4 -> x0, local copies, waits for them, and re-layouts: 14.1 us -> none  [the longest x2 7.03 us: network(): return out.reshape(groups, HALF * feats)[place].reshape(count, feats)]
    gather x2 -> x0, local copies, waits for them, and re-layouts: 6.38 us -> none  [the longest x1 3.19 us: network(): packed_rows = grouped[source].reshape(count, feats)]
    all_to_all x1, starting transfers between devices: 8.63 us -> 14.9 us  [local(): lax.all_to_all(result.reshape(features, experts, width), 'lon', split_axi...]
    pallas_call x1, Pallas kernels: 19.3 us -> 25.4 us  [network(): pl.pallas_call(network_kernel, grid_spec=pltpu.PrefetchScalarGridSpec(num...]
where the time goes in v7:
time: 194 us; the launch traced here: 193 us
  waiting for transfers between devices  53.7 us (28%)
  local copies, waits for them, and re-layouts  47.6 us (25%)
  starting transfers between devices  43.8 us (23%)
  Pallas kernels  37.3 us (19%)
  other arithmetic  9.71 us (5%)
    all_to_all x1, waiting for transfers between devices, local(): lax.all_to_all(result.reshape(features, experts, width), 'lon', split_axi...  28.4 us
    pallas_call x1, Pallas kernels, network(): pl.pallas_call(network_kernel, grid_spec=pltpu.PrefetchScalarGridSpec(num...  25.4 us
    all_to_all x1, waiting for transfers between devices, local(): lax.all_to_all(part, 'lon', split_axis=1, concat_axis=1, tiled=True)  24.1 us
    all_to_all x1, starting transfers between devices, local(): lax.all_to_all(result.reshape(features, experts, width), 'lon', split_axi...  14.9 us
    scatter x1, local copies, waits for them, and re-layouts, local(): jnp.zeros((features, experts * capacity), jnp.bfloat16).at[:, targets]  12.4 us
    gather x1, local copies, waits for them, and re-layouts, local(): tendency = returned.reshape(features, -1)[:, targets]  12.1 us
    pallas_call x2, Pallas kernels, sweep(): pl.pallas_call(sweep_kernel, grid=(nb,), in_specs=[big, edge_row, edge_ro...  11.9 us
    all_to_all x1, starting transfers between devices, local(): lax.all_to_all(part, 'lon', split_axis=1, concat_axis=1, tiled=True)  10.6 us
  transfers between devices with their start and end apart: 10, of which 3 were waited for; matrix products, arithmetic and copies ran while one was open for 4% of the time, Pallas kernels for 0%

profile of v7, /device:TPU:1, one launch (start us, length us, event | category | flops | bytes accessed | tf_op | source)
XLA Modules:
  0.0 193.4 jit_solution(5802876755588756532)
XLA Ops:
  0.0 4.0 %slice_reduce_fusion.2 = (f32[128,32]{1,0:T(8,128)S(1)}, f32[128,32]{1,0:T(8,128)S(1)}) fusion(f32[128,32,128]{2,1,0:T(8,128)} %bitcast.60), kind=kLoop, calls=%fused_computation.6 | loop fusion | bytes 65536 | tf_op jit(solution)/shard_map/slice | solution.py:70
  4.1 1.5 collective-permute-start.2
  5.7 1.3 collective-permute-start.3
  7.1 1.3 fusion.13
  8.4 1.3 collective-permute-start
  9.7 4.2 %collective-permute-start.1 = (f32[128,1,128]{2,1,0:T(1,128)S(1)}, f32[128,1,128]{2,1,0:T(1,128)S(1)}, u32[]{:S(2)}, u32[]{:S(2)}) collective-permute-start(f32[128,1,128]{2,1,0:T(1,128)S(1)} %get-tuple-element.11), channel_id=1, source_target_pairs={{0,32},{32,64},{64,96},{1,33},{33,65},{65,97},{2,34},{34,66},{66,9... | collective-permute-start | bytes 196616 | tf_op jit(solution)/shard_map/ppermute | solution.py:68
  16.2 6.0 %shard_map.73.q_ref = f32[128,32,128]{2,1,0:T(8,128)} custom-call(f32[128,32,128]{2,1,0:T(8,128)} %bitcast.62, f32[128,1,128]{2,1,0:T(1,128)} %copy-done.7, f32[128,1,128]{2,1,0:T(1,128)} %copy-done.9, f32[4,32,32]{2,1,0:T(8,128)} %copy-done.5, f32[4,32,32]{2,1,0:T(8,128)} %copy-done.6, f32[32,32,128]{2,1,0:T(8,128)} %get-tuple-element.14.u_ref, ...), custom_call_target="tpu_custom_call" | custom-call | flops 10485760 | bytes 5767168 | tf_op jit(solution)/shard_map/pallas_call | solution.py:48
  22.1 3.9 %slice_reduce_fusion = (f32[128,32]{1,0:T(8,128)S(1)}, f32[128,32]{1,0:T(8,128)S(1)}) fusion(f32[128,32,128]{2,1,0:T(8,128)} %shard_map.73.q_ref), kind=kLoop, calls=%fused_computation.4 | loop fusion | bytes 65536 | tf_op jit(solution)/shard_map/slice | solution.py:70
  26.1 1.3 fusion.12
  27.5 4.1 %collective-permute-start.6 = (f32[4,32,32]{2,1,0:T(8,128)S(1)}, f32[4,32,32]{2,1,0:T(8,128)S(1)}, u32[]{:S(2)}, u32[]{:S(2)}) collective-permute-start(f32[4,32,32]{2,1,0:T(8,128)S(1)} %bitcast.82), channel_id=1, source_target_pairs={{1,0},{2,1},{3,2},{4,3},{5,4},{6,5},{7,6},{8,7},{9,8},{10,9},{11,1... | collective-permute-start | bytes 49160 | tf_op jit(solution)/shard_map/ppermute | solution.py:69
  33.0 4.6 %collective-permute-start.5 = (f32[128,1,128]{2,1,0:T(1,128)S(1)}, f32[128,1,128]{2,1,0:T(1,128)S(1)}, u32[]{:S(2)}, u32[]{:S(2)}) collective-permute-start(f32[128,1,128]{2,1,0:T(1,128)S(1)} %get-tuple-element.9), channel_id=1, source_target_pairs={{0,32},{32,64},{64,96},{1,33},{33,65},{65,97},{2,34},{34,66},{66,9... | collective-permute-start | bytes 196616 | tf_op jit(solution)/shard_map/ppermute | solution.py:68
  39.6 6.0 %shard_map.74 = f32[128,32,128]{2,1,0:T(8,128)} custom-call(f32[128,32,128]{2,1,0:T(8,128)} %shard_map.73.q_ref, f32[128,1,128]{2,1,0:T(1,128)} %copy-done.11, f32[128,1,128]{2,1,0:T(1,128)} %copy-done.12, f32[4,32,32]{2,1,0:T(8,128)} %copy-done.8, f32[4,32,32]{2,1,0:T(8,128)} %copy-done.10, f32[32,32,128]{2,1,0:T(8,128)} %get-tuple-element.14.u_ref, ...), custom_call_target="tpu_custom_call" | custom-call | flops 10485760 | bytes 5767168 | tf_op jit(solution)/shard_map/pallas_call | solution.py:48
  45.6 1.8 convert_element_type.58
  48.4 12.4 %scatter_custom_fusion = bf16[128,8192]{0,1:T(8,128)(2,1)} fusion(s32[4096]{0:T(1024)S(1)} %bitcast.77, bf16[4096,128]{1,0:T(8,128)(2,1)S(1)} %bitcast.68, bf16[]{:T(256)} %constant.15.clone.1), kind=kCustom, calls=%fused_computation.12 | custom fusion | bytes 2097154 | tf_op jit(solution)/shard_map/scatter | solution.py:200
  60.8 10.6 %all-to-all-start = ((bf16[128,32,256]{0,2,1:T(8,128)(2,1)}), bf16[128,32,256]{0,2,1:T(8,128)(2,1)S(1)}, u32[]{:S(2)}, u32[]{:S(2)}) async-start(bf16[128,32,256]{0,2,1:T(8,128)(2,1)} %bitcast.64), calls=%async_computation | async-start | bytes 4194304 | tf_op jit(solution)/shard_map/all_to_all | solution.py:207
  71.4 2.7 %copy.45 = bf16[1,3,512,512]{2,3,1,0:T(8,128)(2,1)} copy(bf16[1,3,512,512]{3,2,1,0:T(8,128)(2,1)} %param.12) | data formatting | bytes 3145728 | tf_op args[5]
  75.6 24.1 %all-to-all-done = bf16[128,32,256]{0,2,1:T(8,128)(2,1)S(1)} async-done(((bf16[128,32,256]{0,2,1:T(8,128)(2,1)}), bf16[128,32,256]{0,2,1:T(8,128)(2,1)S(1)}, u32[]{:S(2)}, u32[]{:S(2)}) %all-to-all-start) | async-done | bytes 2097184 | tf_op jit(solution)/shard_map/all_to_all | solution.py:207
  104.5 25.4 %shard_map.75 = bf16[8192,128]{1,0:T(8,128)(2,1)} custom-call(s32[1]{0:T(128)} %bitcast.19.active_ref, s32[64]{0:T(128)} %scatter_custom_fusion.1.source_ref, bf16[8192,128]{1,0:T(8,128)(2,1)} %bitcast.63, bf16[128,512]{1,0:T(8,128)(2,1)} %bitcast.73, bf16[3,512,512]{2,1,0:T(8,128)(2,1)} %bitcast.67, bf16[512,128]{1,0:T(8,128)(2,1)} %bitcast.74), custom_call_target="tpu_custom_call" | custom-call | flops 15032385536 | bytes 6029312 | tf_op jit(solution)/shard_map/pallas_call | solution.py:158
  129.9 14.9 %all-to-all-start.1 = ((bf16[128,32,256]{0,2,1:T(8,128)(2,1)}), bf16[128,32,256]{0,2,1:T(8,128)(2,1)S(1)}, u32[]{:S(2)}, u32[]{:S(2)}) async-start(bf16[128,32,256]{0,2,1:T(8,128)(2,1)} %bitcast.66), calls=%async_computation.1 | async-start | bytes 4194304 | tf_op jit(solution)/shard_map/all_to_all | solution.py:211
  144.8 28.4 %all-to-all-done.1 = bf16[128,32,256]{0,2,1:T(8,128)(2,1)S(1)} async-done(((bf16[128,32,256]{0,2,1:T(8,128)(2,1)}), bf16[128,32,256]{0,2,1:T(8,128)(2,1)S(1)}, u32[]{:S(2)}, u32[]{:S(2)}) %all-to-all-start.1) | async-done | bytes 2097184 | tf_op jit(solution)/shard_map/all_to_all | solution.py:211
  173.2 12.1 %gather_fusion = bf16[4096,128]{1,0:T(8,128)(2,1)S(1)} fusion(bf16[128,8192]{0,1:T(8,128)(2,1)S(1)} %bitcast.59, s32[4096]{0:T(1024)S(1)} %broadcast_clamp_fusion), kind=kCustom, calls=%fused_computation | custom fusion | bytes 2113536 | tf_op jit(solution)/shard_map/gather | solution.py:214
  185.3 1.5 convert_element_type.67
  186.8 3.2 %copy.57 = f32[128,32,128]{2,1,0:T(8,128)} copy(f32[128,32,128]{0,2,1:T(8,128)} %bitcast.65) | data formatting | bytes 4194304 | tf_op jit(solution)/shard_map/convert_element_type | solution.py:215
  190.0 3.4 %add.75 = f32[128,32,128]{2,1,0:T(8,128)} add(f32[128,32,128]{2,1,0:T(8,128)S(1)} %copy-done, f32[128,32,128]{2,1,0:T(8,128)} %copy.57) | non-fusion elementwise | flops 524288 | bytes 6291456 | tf_op jit(solution)/shard_map/add | solution.py:215
  (62 shorter events, 12.5 us)
Async XLA Ops:
  0.0 13.8 %copy-start.2 = (f32[2,32,32,128]{3,2,1,0:T(8,128)S(1)}, f32[2,32,32,128]{3,2,1,0:T(8,128)}, u32[]{:S(2)}) copy-start(f32[2,32,32,128]{3,2,1,0:T(8,128)} %param.8) | copy-start | bytes 3145732
  4.0 10.9 %copy-start.13 = (s32[1,4096,1]{1,2,0:T(1,128)S(1)}, s32[1,4096,1]{1,2,0:T(1,128)}, u32[]{:S(2)}) copy-start(s32[1,4096,1]{1,2,0:T(1,128)} %param.10) | copy-start | bytes 49156
  4.1 11.4 %collective-permute-start.2 = (f32[4,32,32]{2,1,0:T(8,128)S(1)}, f32[4,32,32]{2,1,0:T(8,128)S(1)}, u32[]{:S(2)}, u32[]{:S(2)}) collective-permute-start(f32[4,32,32]{2,1,0:T(8,128)S(1)} %bitcast.80), channel_id=1, source_target_pairs={{1,0},{2,1},{3,2},{4,3},{5,4},{6,5},{7,6},{8,7},{9,8},{10,9},{11,1... | collective-permute-start | bytes 49160 | tf_op jit(solution)/shard_map/ppermute | solution.py:69
  5.7 9.8 %collective-permute-start.3 = (f32[4,32,32]{2,1,0:T(8,128)S(1)}, f32[4,32,32]{2,1,0:T(8,128)S(1)}, u32[]{:S(2)}, u32[]{:S(2)}) collective-permute-start(f32[4,32,32]{2,1,0:T(8,128)S(1)} %bitcast.81), channel_id=1, source_target_pairs={{0,1},{1,2},{2,3},{3,4},{4,5},{5,6},{6,7},{7,8},{8,9},{9,10},{10,1... | collective-permute-start | bytes 49160 | tf_op jit(solution)/shard_map/ppermute | solution.py:70
  8.4 7.2 %collective-permute-start = (f32[128,1,128]{2,1,0:T(1,128)S(1)}, f32[128,1,128]{2,1,0:T(1,128)S(1)}, u32[]{:S(2)}, u32[]{:S(2)}) collective-permute-start(f32[128,1,128]{2,1,0:T(1,128)S(1)} %get-tuple-element.12), channel_id=1, source_target_pairs={{32,0},{64,32},{96,64},{33,1},{65,33},{97,65},{34,2},{66,34},{98,6... | collective-permute-start | bytes 196616 | tf_op jit(solution)/shard_map/ppermute | solution.py:67
  9.7 5.9 %collective-permute-start.1 = (f32[128,1,128]{2,1,0:T(1,128)S(1)}, f32[128,1,128]{2,1,0:T(1,128)S(1)}, u32[]{:S(2)}, u32[]{:S(2)}) collective-permute-start(f32[128,1,128]{2,1,0:T(1,128)S(1)} %get-tuple-element.11), channel_id=1, source_target_pairs={{0,32},{32,64},{64,96},{1,33},{33,65},{65,97},{2,34},{34,66},{66,9... | collective-permute-start | bytes 196616 | tf_op jit(solution)/shard_map/ppermute | solution.py:68
  15.5 0.6 copy-start.5
  15.5 0.6 copy-start.6
  15.5 0.6 copy-start.7
  15.6 0.6 copy-start.9
  27.5 10.2 %collective-permute-start.6 = (f32[4,32,32]{2,1,0:T(8,128)S(1)}, f32[4,32,32]{2,1,0:T(8,128)S(1)}, u32[]{:S(2)}, u32[]{:S(2)}) collective-permute-start(f32[4,32,32]{2,1,0:T(8,128)S(1)} %bitcast.82), channel_id=1, source_target_pairs={{1,0},{2,1},{3,2},{4,3},{5,4},{6,5},{7,6},{8,7},{9,8},{10,9},{11,1... | collective-permute-start | bytes 49160 | tf_op jit(solution)/shard_map/ppermute | solution.py:69
  31.6 6.1 %collective-permute-start.7 = (f32[4,32,32]{2,1,0:T(8,128)S(1)}, f32[4,32,32]{2,1,0:T(8,128)S(1)}, u32[]{:S(2)}, u32[]{:S(2)}) collective-permute-start(f32[4,32,32]{2,1,0:T(8,128)S(1)} %bitcast.83), channel_id=1, source_target_pairs={{0,1},{1,2},{2,3},{3,4},{4,5},{5,6},{6,7},{7,8},{8,9},{9,10},{10,1... | collective-permute-start | bytes 49160 | tf_op jit(solution)/shard_map/ppermute | solution.py:70
  31.7 6.0 %collective-permute-start.4 = (f32[128,1,128]{2,1,0:T(1,128)S(1)}, f32[128,1,128]{2,1,0:T(1,128)S(1)}, u32[]{:S(2)}, u32[]{:S(2)}) collective-permute-start(f32[128,1,128]{2,1,0:T(1,128)S(1)} %get-tuple-element.10), channel_id=1, source_target_pairs={{32,0},{64,32},{96,64},{33,1},{65,33},{97,65},{34,2},{66,34},{98,6... | collective-permute-start | bytes 196616 | tf_op jit(solution)/shard_map/ppermute | solution.py:67
  33.0 5.9 %collective-permute-start.5 = (f32[128,1,128]{2,1,0:T(1,128)S(1)}, f32[128,1,128]{2,1,0:T(1,128)S(1)}, u32[]{:S(2)}, u32[]{:S(2)}) collective-permute-start(f32[128,1,128]{2,1,0:T(1,128)S(1)} %get-tuple-element.9), channel_id=1, source_target_pairs={{0,32},{32,64},{64,96},{1,33},{33,65},{65,97},{2,34},{34,66},{66,9... | collective-permute-start | bytes 196616 | tf_op jit(solution)/shard_map/ppermute | solution.py:68
  37.7 1.3 copy-start.8
  37.7 1.2 copy-start.10
  37.7 1.2 copy-start.11
  39.0 0.6 copy-start.12
  60.8 38.9 %all-to-all-start = ((bf16[128,32,256]{0,2,1:T(8,128)(2,1)}), bf16[128,32,256]{0,2,1:T(8,128)(2,1)S(1)}, u32[]{:S(2)}, u32[]{:S(2)}) async-start(bf16[128,32,256]{0,2,1:T(8,128)(2,1)} %bitcast.64), calls=%async_computation | async-start | bytes 4194304 | tf_op jit(solution)/shard_map/all_to_all | solution.py:207
  71.4 2.7 %copy-start.3 = (bf16[1,512,128]{2,1,0:T(8,128)(2,1)S(1)}, bf16[1,512,128]{2,1,0:T(8,128)(2,1)}, u32[]{:S(2)}) copy-start(bf16[1,512,128]{2,1,0:T(8,128)(2,1)} %param.11) | copy-start | bytes 393220
  71.4 3.4 %copy-start.4 = (bf16[1,128,512]{2,1,0:T(8,128)(2,1)S(1)}, bf16[1,128,512]{2,1,0:T(8,128)(2,1)}, u32[]{:S(2)}) copy-start(bf16[1,128,512]{2,1,0:T(8,128)(2,1)} %param.13) | copy-start | bytes 393220
  99.7 4.8 %copy-start.1 = (bf16[128,32,256]{0,2,1:T(8,128)(2,1)}, bf16[128,32,256]{0,2,1:T(8,128)(2,1)S(1)}, u32[]{:S(2)}) copy-start(bf16[128,32,256]{0,2,1:T(8,128)(2,1)S(1)} %all-to-all-done) | copy-start | bytes 6291460
  129.9 43.3 %all-to-all-start.1 = ((bf16[128,32,256]{0,2,1:T(8,128)(2,1)}), bf16[128,32,256]{0,2,1:T(8,128)(2,1)S(1)}, u32[]{:S(2)}, u32[]{:S(2)}) async-start(bf16[128,32,256]{0,2,1:T(8,128)(2,1)} %bitcast.66), calls=%async_computation.1 | async-start | bytes 4194304 | tf_op jit(solution)/shard_map/all_to_all | solution.py:211
  186.8 3.2 %copy-start = (f32[128,32,128]{2,1,0:T(8,128)S(1)}, f32[128,32,128]{2,1,0:T(8,128)}, u32[]{:S(2)}) copy-start(f32[128,32,128]{2,1,0:T(8,128)} %shard_map.74) | copy-start | bytes 6291460

commit v8 on v7

--- a/solution.py
+++ b/solution.py
@@ -105,38 +105,67 @@
     return jnp.dot(hidden, w_last, preferred_element_type=jnp.float32).astype(jnp.bfloat16)
 
 
-def network_kernel(active_ref, source_ref, x_hbm, first_ref, middle_ref, last_ref, o_hbm, buf, res, sems):
+def network_kernel(active_ref, source_ref, x_hbm, first_ref, middle_ref, last_ref, o_hbm, buf, res, lsem, ssem):
     block = pl.program_id(0)
+    blocks = pl.num_programs(0)
+    active = active_ref[0]
+    slot = block % 2
     per = ROWS // HALF
 
-    @pl.when(block < active_ref[0])
-    def _():
-        loads = []
-        for j in range(per):
-            group = source_ref[block * per + j]
-            copy = pltpu.make_async_copy(
-                x_hbm.at[pl.ds(group * HALF, HALF)], buf.at[pl.ds(j * HALF, HALF)], sems.at[j]
+    def loads(index, into):
+        return [
+            pltpu.make_async_copy(
+                x_hbm.at[pl.ds(source_ref[index * per + j] * HALF, HALF)],
+                buf.at[into, pl.ds(j * HALF, HALF)],
+                lsem.at[into, j],
             )
+            for j in range(per)
+        ]
+
+    def stores(index, outof):
+        return [
+            pltpu.make_async_copy(
+                res.at[outof, pl.ds(j * HALF, HALF)],
+                o_hbm.at[pl.ds(source_ref[index * per + j] * HALF, HALF)],
+                ssem.at[outof, j],
+            )
+            for j in range(per)
+        ]
+
+    @pl.when((block == 0) & (active > 0))
+    def _():
+        for copy in loads(0, 0):
             copy.start()
-            loads.append(copy)
-        for copy in loads:
-            copy.wait()
-        res[...] = layers(buf[...], first_ref[...], middle_ref[...], last_ref[...])
-
-    @pl.when(block >= active_ref[0])
-    def _():
-        res[...] = jnp.zeros(res.shape, res.dtype)
-
-    stores = []
-    for j in range(per):
-        group = source_ref[block * per + j]
-        copy = pltpu.make_async_copy(
-            res.at[pl.ds(j * HALF, HALF)], o_hbm.at[pl.ds(group * HALF, HALF)], sems.at[per + j]
-        )
+
+    @pl.when(block + 1 < active)
+    def _():
+        for copy in loads(block + 1, 1 - slot):
+            copy.start()
+
+    @pl.when(block >= 2)
+    def _():
+        for copy in stores(block - 2, slot):
+            copy.wait()
+
+    @pl.when(block < active)
+    def _():
+        for copy in loads(block, slot):
+            copy.wait()
+        res[slot] = layers(buf[slot], first_ref[...], middle_ref[...], last_ref[...])
+
+    @pl.when(block >= active)
+    def _():
+        res[slot] = jnp.zeros(res.shape[1:], res.dtype)
+
+    for copy in stores(block, slot):
         copy.start()
-        stores.append(copy)
-    for copy in stores:
-        copy.wait()
+
+    @pl.when(block == blocks - 1)
+    def _():
+        for copy in stores(block - 1, 1 - slot):
+            copy.wait()
+        for copy in stores(block, slot):
+            copy.wait()
 
 
 def network(rows_in, input_weight, middle_weight, output_weight):
@@ -168,9 +197,10 @@
             ],
             out_specs=pl.BlockSpec(memory_space=pl.ANY),
             scratch_shapes=[
-                pltpu.VMEM((ROWS, feats), jnp.bfloat16),
-                pltpu.VMEM((ROWS, feats), jnp.bfloat16),
-                pltpu.SemaphoreType.DMA((2 * per,)),
+                pltpu.VMEM((2, ROWS, feats), jnp.bfloat16),
+                pltpu.VMEM((2, ROWS, feats), jnp.bfloat16),
+                pltpu.SemaphoreType.DMA((2, per)),
+                pltpu.SemaphoreType.DMA((2, per)),
             ],
         ),
         out_shape=jax.ShapeDtypeStruct((count, feats), jnp.bfloat16),

time: 194 us -> 184 us (0.948)
  Pallas kernels: 37.3 us -> 30.4 us
  starting transfers between devices: 43.8 us -> 40.8 us
    pallas_call x1, Pallas kernels: 25.4 us -> 18.5 us  [network(): pl.pallas_call(network_kernel, grid_spec=pltpu.PrefetchScalarGridSpec(num...]
    all_to_all x1, starting transfers between devices: 14.9 us -> 11.9 us  [local(): lax.all_to_all(result.reshape(features, experts, width), 'lon', split_axi...]
where the time goes in v8:
time: 184 us; the launch traced here: 183 us
  waiting for transfers between devices  53.7 us (29%)
  local copies, waits for them, and re-layouts  47.6 us (26%)
  starting transfers between devices  40.8 us (22%)
  Pallas kernels  30.4 us (17%)
  other arithmetic  9.71 us (5%)
    all_to_all x1, waiting for transfers between devices, local(): lax.all_to_all(result.reshape(features, experts, width), 'lon', split_axi...  28.4 us
    all_to_all x1, waiting for transfers between devices, local(): lax.all_to_all(part, 'lon', split_axis=1, concat_axis=1, tiled=True)  24.1 us
    pallas_call x1, Pallas kernels, network(): pl.pallas_call(network_kernel, grid_spec=pltpu.PrefetchScalarGridSpec(num...  18.5 us
    scatter x1, local copies, waits for them, and re-layouts, local(): jnp.zeros((features, experts * capacity), jnp.bfloat16).at[:, targets]  12.4 us
    gather x1, local copies, waits for them, and re-layouts, local(): tendency = returned.reshape(features, -1)[:, targets]  12.1 us
    pallas_call x2, Pallas kernels, sweep(): pl.pallas_call(sweep_kernel, grid=(nb,), in_specs=[big, edge_row, edge_ro...  11.9 us
    all_to_all x1, starting transfers between devices, local(): lax.all_to_all(result.reshape(features, experts, width), 'lon', split_axi...  11.9 us
    all_to_all x1, starting transfers between devices, local(): lax.all_to_all(part, 'lon', split_axis=1, concat_axis=1, tiled=True)  10.6 us
  transfers between devices with their start and end apart: 10, of which 3 were waited for; matrix products, arithmetic and copies ran while one was open for 4% of the time, Pallas kernels for 0%

profile of v8, /device:TPU:1, one launch (start us, length us, event | category | flops | bytes accessed | tf_op | source)
XLA Modules:
  0.0 183.5 jit_solution(16797101613917359209)
XLA Ops:
  0.0 4.0 %slice_reduce_fusion.2 = (f32[128,32]{1,0:T(8,128)S(1)}, f32[128,32]{1,0:T(8,128)S(1)}) fusion(f32[128,32,128]{2,1,0:T(8,128)} %bitcast.60), kind=kLoop, calls=%fused_computation.6 | loop fusion | bytes 65536 | tf_op jit(solution)/shard_map/slice | solution.py:70
  4.1 1.5 collective-permute-start.2
  5.7 1.3 collective-permute-start.3
  7.1 1.3 fusion.13
  9.7 4.2 %collective-permute-start.1 = (f32[128,1,128]{2,1,0:T(1,128)S(1)}, f32[128,1,128]{2,1,0:T(1,128)S(1)}, u32[]{:S(2)}, u32[]{:S(2)}) collective-permute-start(f32[128,1,128]{2,1,0:T(1,128)S(1)} %get-tuple-element.11), channel_id=1, source_target_pairs={{0,32},{32,64},{64,96},{1,33},{33,65},{65,97},{2,34},{34,66},{66,9... | collective-permute-start | bytes 196616 | tf_op jit(solution)/shard_map/ppermute | solution.py:68
  16.2 6.0 %shard_map.73.q_ref = f32[128,32,128]{2,1,0:T(8,128)} custom-call(f32[128,32,128]{2,1,0:T(8,128)} %bitcast.62, f32[128,1,128]{2,1,0:T(1,128)} %copy-done.7, f32[128,1,128]{2,1,0:T(1,128)} %copy-done.9, f32[4,32,32]{2,1,0:T(8,128)} %copy-done.5, f32[4,32,32]{2,1,0:T(8,128)} %copy-done.6, f32[32,32,128]{2,1,0:T(8,128)} %get-tuple-element.14.u_ref, ...), custom_call_target="tpu_custom_call" | custom-call | flops 10485760 | bytes 5767168 | tf_op jit(solution)/shard_map/pallas_call | solution.py:48
  22.1 3.9 %slice_reduce_fusion = (f32[128,32]{1,0:T(8,128)S(1)}, f32[128,32]{1,0:T(8,128)S(1)}) fusion(f32[128,32,128]{2,1,0:T(8,128)} %shard_map.73.q_ref), kind=kLoop, calls=%fused_computation.4 | loop fusion | bytes 65536 | tf_op jit(solution)/shard_map/slice | solution.py:70
  26.1 1.3 fusion.12
  27.5 4.1 %collective-permute-start.6 = (f32[4,32,32]{2,1,0:T(8,128)S(1)}, f32[4,32,32]{2,1,0:T(8,128)S(1)}, u32[]{:S(2)}, u32[]{:S(2)}) collective-permute-start(f32[4,32,32]{2,1,0:T(8,128)S(1)} %bitcast.82), channel_id=1, source_target_pairs={{1,0},{2,1},{3,2},{4,3},{5,4},{6,5},{7,6},{8,7},{9,8},{10,9},{11,1... | collective-permute-start | bytes 49160 | tf_op jit(solution)/shard_map/ppermute | solution.py:69
  31.7 1.3 collective-permute-start.4
  33.0 4.6 %collective-permute-start.5 = (f32[128,1,128]{2,1,0:T(1,128)S(1)}, f32[128,1,128]{2,1,0:T(1,128)S(1)}, u32[]{:S(2)}, u32[]{:S(2)}) collective-permute-start(f32[128,1,128]{2,1,0:T(1,128)S(1)} %get-tuple-element.9), channel_id=1, source_target_pairs={{0,32},{32,64},{64,96},{1,33},{33,65},{65,97},{2,34},{34,66},{66,9... | collective-permute-start | bytes 196616 | tf_op jit(solution)/shard_map/ppermute | solution.py:68
  39.6 6.0 %shard_map.74 = f32[128,32,128]{2,1,0:T(8,128)} custom-call(f32[128,32,128]{2,1,0:T(8,128)} %shard_map.73.q_ref, f32[128,1,128]{2,1,0:T(1,128)} %copy-done.11, f32[128,1,128]{2,1,0:T(1,128)} %copy-done.12, f32[4,32,32]{2,1,0:T(8,128)} %copy-done.8, f32[4,32,32]{2,1,0:T(8,128)} %copy-done.10, f32[32,32,128]{2,1,0:T(8,128)} %get-tuple-element.14.u_ref, ...), custom_call_target="tpu_custom_call" | custom-call | flops 10485760 | bytes 5767168 | tf_op jit(solution)/shard_map/pallas_call | solution.py:48
  45.6 1.8 convert_element_type.58
  48.4 12.4 %scatter_custom_fusion = bf16[128,8192]{0,1:T(8,128)(2,1)} fusion(s32[4096]{0:T(1024)S(1)} %bitcast.77, bf16[4096,128]{1,0:T(8,128)(2,1)S(1)} %bitcast.68, bf16[]{:T(256)} %constant.15.clone.1), kind=kCustom, calls=%fused_computation.12 | custom fusion | bytes 2097154 | tf_op jit(solution)/shard_map/scatter | solution.py:230
  60.8 10.6 %all-to-all-start = ((bf16[128,32,256]{0,2,1:T(8,128)(2,1)}), bf16[128,32,256]{0,2,1:T(8,128)(2,1)S(1)}, u32[]{:S(2)}, u32[]{:S(2)}) async-start(bf16[128,32,256]{0,2,1:T(8,128)(2,1)} %bitcast.64), calls=%async_computation | async-start | bytes 4194304 | tf_op jit(solution)/shard_map/all_to_all | solution.py:237
  71.4 2.7 %copy.45 = bf16[1,3,512,512]{2,3,1,0:T(8,128)(2,1)} copy(bf16[1,3,512,512]{3,2,1,0:T(8,128)(2,1)} %param.12) | data formatting | bytes 3145728 | tf_op args[5]
  75.6 24.1 %all-to-all-done = bf16[128,32,256]{0,2,1:T(8,128)(2,1)S(1)} async-done(((bf16[128,32,256]{0,2,1:T(8,128)(2,1)}), bf16[128,32,256]{0,2,1:T(8,128)(2,1)S(1)}, u32[]{:S(2)}, u32[]{:S(2)}) %all-to-all-start) | async-done | bytes 2097184 | tf_op jit(solution)/shard_map/all_to_all | solution.py:237
  104.5 18.5 %shard_map.75 = bf16[8192,128]{1,0:T(8,128)(2,1)} custom-call(s32[1]{0:T(128)} %bitcast.19.active_ref, s32[64]{0:T(128)} %scatter_custom_fusion.1.source_ref, bf16[8192,128]{1,0:T(8,128)(2,1)} %bitcast.63, bf16[128,512]{1,0:T(8,128)(2,1)} %bitcast.73, bf16[3,512,512]{2,1,0:T(8,128)(2,1)} %bitcast.67, bf16[512,128]{1,0:T(8,128)(2,1)} %bitcast.74), custom_call_target="tpu_custom_call" | custom-call | flops 15032385536 | bytes 6029312 | tf_op jit(solution)/shard_map/pallas_call | solution.py:187
  123.0 11.9 %all-to-all-start.1 = ((bf16[128,32,256]{0,2,1:T(8,128)(2,1)}), bf16[128,32,256]{0,2,1:T(8,128)(2,1)S(1)}, u32[]{:S(2)}, u32[]{:S(2)}) async-start(bf16[128,32,256]{0,2,1:T(8,128)(2,1)} %bitcast.66), calls=%async_computation.1 | async-start | bytes 4194304 | tf_op jit(solution)/shard_map/all_to_all | solution.py:241
  134.9 28.4 %all-to-all-done.1 = bf16[128,32,256]{0,2,1:T(8,128)(2,1)S(1)} async-done(((bf16[128,32,256]{0,2,1:T(8,128)(2,1)}), bf16[128,32,256]{0,2,1:T(8,128)(2,1)S(1)}, u32[]{:S(2)}, u32[]{:S(2)}) %all-to-all-start.1) | async-done | bytes 2097184 | tf_op jit(solution)/shard_map/all_to_all | solution.py:241
  163.3 12.1 %gather_fusion = bf16[4096,128]{1,0:T(8,128)(2,1)S(1)} fusion(bf16[128,8192]{0,1:T(8,128)(2,1)S(1)} %bitcast.59, s32[4096]{0:T(1024)S(1)} %broadcast_clamp_fusion), kind=kCustom, calls=%fused_computation | custom fusion | bytes 2113536 | tf_op jit(solution)/shard_map/gather | solution.py:244
  175.4 1.5 convert_element_type.67
  176.9 3.2 %copy.57 = f32[128,32,128]{2,1,0:T(8,128)} copy(f32[128,32,128]{0,2,1:T(8,128)} %bitcast.65) | data formatting | bytes 4194304 | tf_op jit(solution)/shard_map/convert_element_type | solution.py:245
  180.1 3.4 %add.75 = f32[128,32,128]{2,1,0:T(8,128)} add(f32[128,32,128]{2,1,0:T(8,128)S(1)} %copy-done, f32[128,32,128]{2,1,0:T(8,128)} %copy.57) | non-fusion elementwise | flops 524288 | bytes 6291456 | tf_op jit(solution)/shard_map/add | solution.py:245
  (62 shorter events, 12.5 us)
Async XLA Ops:
  0.0 13.8 %copy-start.2 = (f32[2,32,32,128]{3,2,1,0:T(8,128)S(1)}, f32[2,32,32,128]{3,2,1,0:T(8,128)}, u32[]{:S(2)}) copy-start(f32[2,32,32,128]{3,2,1,0:T(8,128)} %param.8) | copy-start | bytes 3145732
  4.0 10.9 %copy-start.13 = (s32[1,4096,1]{1,2,0:T(1,128)S(1)}, s32[1,4096,1]{1,2,0:T(1,128)}, u32[]{:S(2)}) copy-start(s32[1,4096,1]{1,2,0:T(1,128)} %param.10) | copy-start | bytes 49156
  4.1 11.4 %collective-permute-start.2 = (f32[4,32,32]{2,1,0:T(8,128)S(1)}, f32[4,32,32]{2,1,0:T(8,128)S(1)}, u32[]{:S(2)}, u32[]{:S(2)}) collective-permute-start(f32[4,32,32]{2,1,0:T(8,128)S(1)} %bitcast.80), channel_id=1, source_target_pairs={{1,0},{2,1},{3,2},{4,3},{5,4},{6,5},{7,6},{8,7},{9,8},{10,9},{11,1... | collective-permute-start | bytes 49160 | tf_op jit(solution)/shard_map/ppermute | solution.py:69
  5.7 9.8 %collective-permute-start.3 = (f32[4,32,32]{2,1,0:T(8,128)S(1)}, f32[4,32,32]{2,1,0:T(8,128)S(1)}, u32[]{:S(2)}, u32[]{:S(2)}) collective-permute-start(f32[4,32,32]{2,1,0:T(8,128)S(1)} %bitcast.81), channel_id=1, source_target_pairs={{0,1},{1,2},{2,3},{3,4},{4,5},{5,6},{6,7},{7,8},{8,9},{9,10},{10,1... | collective-permute-start | bytes 49160 | tf_op jit(solution)/shard_map/ppermute | solution.py:70
  8.4 7.2 %collective-permute-start = (f32[128,1,128]{2,1,0:T(1,128)S(1)}, f32[128,1,128]{2,1,0:T(1,128)S(1)}, u32[]{:S(2)}, u32[]{:S(2)}) collective-permute-start(f32[128,1,128]{2,1,0:T(1,128)S(1)} %get-tuple-element.12), channel_id=1, source_target_pairs={{32,0},{64,32},{96,64},{33,1},{65,33},{97,65},{34,2},{66,34},{98,6... | collective-permute-start | bytes 196616 | tf_op jit(solution)/shard_map/ppermute | solution.py:67
  9.7 5.9 %collective-permute-start.1 = (f32[128,1,128]{2,1,0:T(1,128)S(1)}, f32[128,1,128]{2,1,0:T(1,128)S(1)}, u32[]{:S(2)}, u32[]{:S(2)}) collective-permute-start(f32[128,1,128]{2,1,0:T(1,128)S(1)} %get-tuple-element.11), channel_id=1, source_target_pairs={{0,32},{32,64},{64,96},{1,33},{33,65},{65,97},{2,34},{34,66},{66,9... | collective-permute-start | bytes 196616 | tf_op jit(solution)/shard_map/ppermute | solution.py:68
  15.5 0.6 copy-start.5
  15.5 0.6 copy-start.6
  15.5 0.6 copy-start.7
  15.6 0.6 copy-start.9
  27.5 10.2 %collective-permute-start.6 = (f32[4,32,32]{2,1,0:T(8,128)S(1)}, f32[4,32,32]{2,1,0:T(8,128)S(1)}, u32[]{:S(2)}, u32[]{:S(2)}) collective-permute-start(f32[4,32,32]{2,1,0:T(8,128)S(1)} %bitcast.82), channel_id=1, source_target_pairs={{1,0},{2,1},{3,2},{4,3},{5,4},{6,5},{7,6},{8,7},{9,8},{10,9},{11,1... | collective-permute-start | bytes 49160 | tf_op jit(solution)/shard_map/ppermute | solution.py:69
  31.6 6.1 %collective-permute-start.7 = (f32[4,32,32]{2,1,0:T(8,128)S(1)}, f32[4,32,32]{2,1,0:T(8,128)S(1)}, u32[]{:S(2)}, u32[]{:S(2)}) collective-permute-start(f32[4,32,32]{2,1,0:T(8,128)S(1)} %bitcast.83), channel_id=1, source_target_pairs={{0,1},{1,2},{2,3},{3,4},{4,5},{5,6},{6,7},{7,8},{8,9},{9,10},{10,1... | collective-permute-start | bytes 49160 | tf_op jit(solution)/shard_map/ppermute | solution.py:70
  31.7 6.0 %collective-permute-start.4 = (f32[128,1,128]{2,1,0:T(1,128)S(1)}, f32[128,1,128]{2,1,0:T(1,128)S(1)}, u32[]{:S(2)}, u32[]{:S(2)}) collective-permute-start(f32[128,1,128]{2,1,0:T(1,128)S(1)} %get-tuple-element.10), channel_id=1, source_target_pairs={{32,0},{64,32},{96,64},{33,1},{65,33},{97,65},{34,2},{66,34},{98,6... | collective-permute-start | bytes 196616 | tf_op jit(solution)/shard_map/ppermute | solution.py:67
  33.0 5.9 %collective-permute-start.5 = (f32[128,1,128]{2,1,0:T(1,128)S(1)}, f32[128,1,128]{2,1,0:T(1,128)S(1)}, u32[]{:S(2)}, u32[]{:S(2)}) collective-permute-start(f32[128,1,128]{2,1,0:T(1,128)S(1)} %get-tuple-element.9), channel_id=1, source_target_pairs={{0,32},{32,64},{64,96},{1,33},{33,65},{65,97},{2,34},{34,66},{66,9... | collective-permute-start | bytes 196616 | tf_op jit(solution)/shard_map/ppermute | solution.py:68
  37.7 1.3 copy-start.8
  37.7 1.2 copy-start.10
  37.7 1.2 copy-start.11
  39.0 0.6 copy-start.12
  60.8 38.9 %all-to-all-start = ((bf16[128,32,256]{0,2,1:T(8,128)(2,1)}), bf16[128,32,256]{0,2,1:T(8,128)(2,1)S(1)}, u32[]{:S(2)}, u32[]{:S(2)}) async-start(bf16[128,32,256]{0,2,1:T(8,128)(2,1)} %bitcast.64), calls=%async_computation | async-start | bytes 4194304 | tf_op jit(solution)/shard_map/all_to_all | solution.py:237
  71.4 2.7 %copy-start.3 = (bf16[1,512,128]{2,1,0:T(8,128)(2,1)S(1)}, bf16[1,512,128]{2,1,0:T(8,128)(2,1)}, u32[]{:S(2)}) copy-start(bf16[1,512,128]{2,1,0:T(8,128)(2,1)} %param.11) | copy-start | bytes 393220
  71.4 3.4 %copy-start.4 = (bf16[1,128,512]{2,1,0:T(8,128)(2,1)S(1)}, bf16[1,128,512]{2,1,0:T(8,128)(2,1)}, u32[]{:S(2)}) copy-start(bf16[1,128,512]{2,1,0:T(8,128)(2,1)} %param.13) | copy-start | bytes 393220
  99.7 4.8 %copy-start.1 = (bf16[128,32,256]{0,2,1:T(8,128)(2,1)}, bf16[128,32,256]{0,2,1:T(8,128)(2,1)S(1)}, u32[]{:S(2)}) copy-start(bf16[128,32,256]{0,2,1:T(8,128)(2,1)S(1)} %all-to-all-done) | copy-start | bytes 6291460
  123.0 40.3 %all-to-all-start.1 = ((bf16[128,32,256]{0,2,1:T(8,128)(2,1)}), bf16[128,32,256]{0,2,1:T(8,128)(2,1)S(1)}, u32[]{:S(2)}, u32[]{:S(2)}) async-start(bf16[128,32,256]{0,2,1:T(8,128)(2,1)} %bitcast.66), calls=%async_computation.1 | async-start | bytes 4194304 | tf_op jit(solution)/shard_map/all_to_all | solution.py:241
  176.9 3.2 %copy-start = (f32[128,32,128]{2,1,0:T(8,128)S(1)}, f32[128,32,128]{2,1,0:T(8,128)}, u32[]{:S(2)}) copy-start(f32[128,32,128]{2,1,0:T(8,128)} %shard_map.74) | copy-start | bytes 6291460

commit v9 on v8

--- a/solution.py
+++ b/solution.py
@@ -212,6 +212,75 @@
     )(active, source, rows_in, first, middle, last)
 
 
+def pack_kernel(t_ref, cur_ref, o_ref, rows, full):
+    feats, lat_cells, lon_cells = cur_ref.shape
+    for r in range(lat_cells):
+        rows[r * lon_cells:(r + 1) * lon_cells, :] = cur_ref[:, r, :].T
+    full[...] = jnp.zeros(full.shape, full.dtype)
+
+    def body(i, carry):
+        for u in range(8):
+            c = i * 8 + u
+            full[pl.ds(t_ref[c], 1), :] = rows[pl.ds(c, 1), :]
+        return carry
+
+    lax.fori_loop(0, rows.shape[0] // 8, body, 0)
+    o_ref[...] = full[...].astype(o_ref.dtype)
+
+
+def pack(targets, current, slots):
+    feats, lat_cells, lon_cells = current.shape
+    count = lat_cells * lon_cells
+    return pl.pallas_call(
+        pack_kernel,
+        grid_spec=pltpu.PrefetchScalarGridSpec(
+            num_scalar_prefetch=1,
+            grid=(1,),
+            in_specs=[pl.BlockSpec(current.shape, lambda i, t: (0, 0, 0))],
+            out_specs=pl.BlockSpec((slots, feats), lambda i, t: (0, 0)),
+            scratch_shapes=[pltpu.VMEM((count, feats), jnp.float32), pltpu.VMEM((slots, feats), jnp.float32)],
+        ),
+        out_shape=jax.ShapeDtypeStruct((slots, feats), jnp.bfloat16),
+    )(targets, current)
+
+
+def combine_kernel(t_ref, ret_ref, cur_ref, o_ref, full, tend):
+    feats, lat_cells, lon_cells = cur_ref.shape
+    full[...] = ret_ref[...].astype(jnp.float32)
+
+    def body(i, carry):
+        for u in range(8):
+            c = i * 8 + u
+            tend[pl.ds(c, 1), :] = full[pl.ds(t_ref[c], 1), :]
+        return carry
+
+    lax.fori_loop(0, tend.shape[0] // 8, body, 0)
+    for r in range(lat_cells):
+        o_ref[:, r, :] = cur_ref[:, r, :] + tend[r * lon_cells:(r + 1) * lon_cells, :].T
+
+
+def combine(targets, returned_rows, current):
+    feats, lat_cells, lon_cells = current.shape
+    slots = returned_rows.shape[0]
+    return pl.pallas_call(
+        combine_kernel,
+        grid_spec=pltpu.PrefetchScalarGridSpec(
+            num_scalar_prefetch=1,
+            grid=(1,),
+            in_specs=[
+                pl.BlockSpec((slots, feats), lambda i, t: (0, 0)),
+                pl.BlockSpec(current.shape, lambda i, t: (0, 0, 0)),
+            ],
+            out_specs=pl.BlockSpec(current.shape, lambda i, t: (0, 0, 0)),
+            scratch_shapes=[
+                pltpu.VMEM((slots, feats), jnp.float32),
+                pltpu.VMEM((lat_cells * lon_cells, feats), jnp.float32),
+            ],
+        ),
+        out_shape=jax.ShapeDtypeStruct(current.shape, jnp.float32),
+    )(targets, returned_rows, current)
+
+
 def local(
     column_state, wind_speed, diffusivity, batch_index, input_weight, middle_weight, output_weight
 ):
@@ -221,14 +290,12 @@
     for sweep_index in range(2):
         current = step(current, wind_speed[0], wind_speed[1], diffusivity)
     column_count = lat_cells * lon_cells
-    columns = current.reshape(features, column_count).astype(jnp.bfloat16)
     experts = lax.axis_size("lon")
     capacity = 2 * column_count // experts
     targets_all = batch_index.reshape(column_count)
     position = positions(targets_all, experts)
     targets = targets_all * capacity + position
-    packed = jnp.zeros((features, experts * capacity), jnp.bfloat16).at[:, targets].set(columns)
-    packed = packed.reshape(features, experts, capacity)
+    packed = pack(targets, current, experts * capacity).T.reshape(features, experts, capacity)
     chunks = 1
     width = capacity // chunks
     answers = []
@@ -241,8 +308,7 @@
             lax.all_to_all(result.reshape(features, experts, width), "lon", split_axis=1, concat_axis=1, tiled=True)
         )
     returned = jnp.concatenate(answers, axis=2)
-    tendency = returned.reshape(features, -1)[:, targets]
-    return (current + tendency.astype(jnp.float32).reshape(current.shape)).reshape(column_state.shape)
+    return combine(targets, returned.reshape(features, -1).T, current).reshape(column_state.shape)
 
 
 def solution(mesh):

time: 184 us -> 171 us (0.929)
  blocking collectives: 0 us -> 41.1 us
  waiting for transfers between devices: 53.7 us -> 24.8 us
  local copies, waits for them, and re-layouts: 47.6 us -> 18.8 us
  Pallas kernels: 30.4 us -> 51.4 us
  starting transfers between devices: 40.8 us -> 28.9 us
  other arithmetic: 9.71 us -> 3.64 us
    all_to_all x0 -> x1, blocking collectives: none -> 41.1 us  [local(): lax.all_to_all(result.reshape(features, experts, width), 'lon', split_axi...]
    all_to_all x1 -> x0, waiting for transfers between devices: 28.4 us -> none  [local(): lax.all_to_all(result.reshape(features, experts, width), 'lon', split_axi...]
    pallas_call x0 -> x2, Pallas kernels: none -> 23.2 us  [the longest x1 12.3 us: combine(): pl.pallas_call(combine_kernel, grid_spec=pltpu.PrefetchScalarGridSpec(num...]
    scatter x1 -> x0, local copies, waits for them, and re-layouts: 12.4 us -> none  [local(): jnp.zeros((features, experts * capacity), jnp.bfloat16).at[:, targets]]
    gather x1 -> x0, local copies, waits for them, and re-layouts: 12.1 us -> none  [local(): tendency = returned.reshape(features, -1)[:, targets]]
    all_to_all x1 -> x0, starting transfers between devices: 11.9 us -> none  [local(): lax.all_to_all(result.reshape(features, experts, width), 'lon', split_axi...]
    convert_element_type x2 -> x0, local copies, waits for them, and re-layouts: 4.23 us -> none  [the longest x1 3.24 us: local(): tendency.astype(jnp.float32).reshape(current.shape)]
    convert_element_type x3 -> x0, other arithmetic: 3.28 us -> none  [the longest x1 1.81 us: local(): columns = current.reshape(features, column_count).astype(jnp.bfloat16)]
  transfers between devices with their start and end apart: 10 -> 9, of which waited for: 3 -> 2; matrix products, arithmetic and copies ran while one was open for 4% -> 5% of each run, Pallas kernels for 0% -> 0%
where the time goes in v9:
time: 171 us; the launch traced here: 170 us
  Pallas kernels  51.4 us (30%)
  blocking collectives  41.1 us (24%)
  starting transfers between devices  28.9 us (17%)
  waiting for transfers between devices  24.8 us (15%)
  local copies, waits for them, and re-layouts  18.8 us (11%)
  other arithmetic  3.64 us (2%)
    all_to_all x1, blocking collectives, local(): lax.all_to_all(result.reshape(features, experts, width), 'lon', split_axi...  41.1 us
    all_to_all x1, waiting for transfers between devices, local(): lax.all_to_all(part, 'lon', split_axis=1, concat_axis=1, tiled=True)  24.1 us
    pallas_call x1, Pallas kernels, network(): pl.pallas_call(network_kernel, grid_spec=pltpu.PrefetchScalarGridSpec(num...  16.3 us
    pallas_call x1, Pallas kernels, combine(): pl.pallas_call(combine_kernel, grid_spec=pltpu.PrefetchScalarGridSpec(num...  12.3 us
    pallas_call x2, Pallas kernels, sweep(): pl.pallas_call(sweep_kernel, grid=(nb,), in_specs=[big, edge_row, edge_ro...  11.9 us
    pallas_call x1, Pallas kernels, pack(): pl.pallas_call(pack_kernel, grid_spec=pltpu.PrefetchScalarGridSpec(num_sc...  10.8 us
    all_to_all x1, starting transfers between devices, local(): lax.all_to_all(part, 'lon', split_axis=1, concat_axis=1, tiled=True)  10.6 us
    ppermute x2, starting transfers between devices, step(): hs = lax.ppermute(x[:, rows - 1:, :], 'lat', lat_forward)  8.79 us
  transfers between devices with their start and end apart: 9, of which 2 were waited for; matrix products, arithmetic and copies ran while one was open for 5% of the time, Pallas kernels for 0%

profile of v9, /device:TPU:1, one launch (start us, length us, event | category | flops | bytes accessed | tf_op | source)
XLA Modules:
  0.0 169.8 jit_solution(3812181292897047960)
XLA Ops:
  0.0 4.0 %slice_reduce_fusion.2 = (f32[128,32]{1,0:T(8,128)S(1)}, f32[128,32]{1,0:T(8,128)S(1)}) fusion(f32[128,32,128]{2,1,0:T(8,128)} %bitcast.54), kind=kLoop, calls=%fused_computation.4 | loop fusion | bytes 65536 | tf_op jit(solution)/shard_map/slice | solution.py:70
  4.1 1.5 collective-permute-start.2
  5.7 1.3 collective-permute-start.3
  7.1 1.3 fusion.11
  8.4 1.3 collective-permute-start
  9.7 4.2 %collective-permute-start.1 = (f32[128,1,128]{2,1,0:T(1,128)S(1)}, f32[128,1,128]{2,1,0:T(1,128)S(1)}, u32[]{:S(2)}, u32[]{:S(2)}) collective-permute-start(f32[128,1,128]{2,1,0:T(1,128)S(1)} %get-tuple-element.11), channel_id=1, source_target_pairs={{0,32},{32,64},{64,96},{1,33},{33,65},{65,97},{2,34},{34,66},{66,9... | collective-permute-start | bytes 196616 | tf_op jit(solution)/shard_map/ppermute | solution.py:68
  13.8 1.1 slice_bitcast_fusion
  16.2 6.0 %shard_map.73.q_ref = f32[128,32,128]{2,1,0:T(8,128)} custom-call(f32[128,32,128]{2,1,0:T(8,128)} %bitcast.56, f32[128,1,128]{2,1,0:T(1,128)} %copy-done.7, f32[128,1,128]{2,1,0:T(1,128)} %copy-done.8, f32[4,32,32]{2,1,0:T(8,128)} %copy-done.4, f32[4,32,32]{2,1,0:T(8,128)} %copy-done.5, f32[32,32,128]{2,1,0:T(8,128)} %get-tuple-element.14.u_ref, ...), custom_call_target="tpu_custom_call" | custom-call | flops 10485760 | bytes 5767168 | tf_op jit(solution)/shard_map/pallas_call | solution.py:48
  22.2 3.9 %slice_reduce_fusion = (f32[128,32]{1,0:T(8,128)S(1)}, f32[128,32]{1,0:T(8,128)S(1)}) fusion(f32[128,32,128]{2,1,0:T(8,128)} %shard_map.73.q_ref), kind=kLoop, calls=%fused_computation.2 | loop fusion | bytes 65536 | tf_op jit(solution)/shard_map/slice | solution.py:70
  26.1 1.3 fusion.10
  27.5 4.1 %collective-permute-start.6 = (f32[4,32,32]{2,1,0:T(8,128)S(1)}, f32[4,32,32]{2,1,0:T(8,128)S(1)}, u32[]{:S(2)}, u32[]{:S(2)}) collective-permute-start(f32[4,32,32]{2,1,0:T(8,128)S(1)} %bitcast.71), channel_id=1, source_target_pairs={{1,0},{2,1},{3,2},{4,3},{5,4},{6,5},{7,6},{8,7},{9,8},{10,9},{11,1... | collective-permute-start | bytes 49160 | tf_op jit(solution)/shard_map/ppermute | solution.py:69
  31.7 1.3 collective-permute-start.4
  33.0 4.6 %collective-permute-start.5 = (f32[128,1,128]{2,1,0:T(1,128)S(1)}, f32[128,1,128]{2,1,0:T(1,128)S(1)}, u32[]{:S(2)}, u32[]{:S(2)}) collective-permute-start(f32[128,1,128]{2,1,0:T(1,128)S(1)} %get-tuple-element.9), channel_id=1, source_target_pairs={{0,32},{32,64},{64,96},{1,33},{33,65},{65,97},{2,34},{34,66},{66,9... | collective-permute-start | bytes 196616 | tf_op jit(solution)/shard_map/ppermute | solution.py:68
  39.6 6.0 %shard_map.74.cur_ref = f32[128,32,128]{2,1,0:T(8,128)} custom-call(f32[128,32,128]{2,1,0:T(8,128)} %shard_map.73.q_ref, f32[128,1,128]{2,1,0:T(1,128)} %copy-done.10, f32[128,1,128]{2,1,0:T(1,128)} %copy-done.11, f32[4,32,32]{2,1,0:T(8,128)} %copy-done.6, f32[4,32,32]{2,1,0:T(8,128)} %copy-done.9, f32[32,32,128]{2,1,0:T(8,128)} %get-tuple-element.14.u_ref, ...), custom_call_target="tpu_custom_call" | custom-call | flops 10485760 | bytes 5767168 | tf_op jit(solution)/shard_map/pallas_call | solution.py:48
  45.6 10.8 %shard_map.75 = bf16[8192,128]{1,0:T(8,128)(2,1)} custom-call(s32[4096]{0:T(1024)} %bitcast_add_fusion.t_ref, f32[128,32,128]{2,1,0:T(8,128)} %shard_map.74.cur_ref), custom_call_target="tpu_custom_call" | custom-call | tf_op jit(solution)/shard_map/pallas_call | solution.py:234
  56.4 10.6 %all-to-all-start = ((bf16[128,32,256]{0,2,1:T(8,128)(2,1)}), bf16[128,32,256]{0,2,1:T(8,128)(2,1)S(1)}, u32[]{:S(2)}, u32[]{:S(2)}) async-start(bf16[128,32,256]{0,2,1:T(8,128)(2,1)} %bitcast.59), calls=%async_computation | async-start | bytes 4194304 | tf_op jit(solution)/shard_map/all_to_all | solution.py:304
  67.0 2.7 %copy.40 = bf16[1,3,512,512]{2,3,1,0:T(8,128)(2,1)} copy(bf16[1,3,512,512]{3,2,1,0:T(8,128)(2,1)} %param.12) | data formatting | bytes 3145728 | tf_op args[5]
  69.7 0.8 copy.39
  71.2 24.1 %all-to-all-done = bf16[128,32,256]{0,2,1:T(8,128)(2,1)S(1)} async-done(((bf16[128,32,256]{0,2,1:T(8,128)(2,1)}), bf16[128,32,256]{0,2,1:T(8,128)(2,1)S(1)}, u32[]{:S(2)}, u32[]{:S(2)}) %all-to-all-start) | async-done | bytes 2097184 | tf_op jit(solution)/shard_map/all_to_all | solution.py:304
  95.3 1.2 compare_reduce_fusion
  98.8 1.3 scatter_custom_fusion.source_ref
  100.1 16.3 %shard_map.76 = bf16[8192,128]{1,0:T(8,128)(2,1)} custom-call(s32[1]{0:T(128)} %bitcast.17.active_ref, s32[64]{0:T(128)} %scatter_custom_fusion.source_ref, bf16[8192,128]{1,0:T(8,128)(2,1)} %bitcast.58, bf16[128,512]{1,0:T(8,128)(2,1)} %bitcast.66, bf16[3,512,512]{2,1,0:T(8,128)(2,1)} %bitcast.61, bf16[512,128]{1,0:T(8,128)(2,1)} %bitcast.67), custom_call_target="tpu_custom_call" | custom-call | flops 15032385536 | bytes 6029312 | tf_op jit(solution)/shard_map/pallas_call | solution.py:187
  116.4 41.1 %all_to_all.10 = bf16[128,32,256]{0,2,1:T(8,128)(2,1)} all-to-all(bf16[128,32,256]{0,2,1:T(8,128)(2,1)} %bitcast.60), channel_id=1, replica_groups=mesh['lat'=4,'lon'=32] {'lon'}, dimensions={1} | all-to-all | bytes 4194304 | tf_op jit(solution)/shard_map/all_to_all | solution.py:308
  157.5 12.3 %shard_map.77 = f32[128,32,128]{2,1,0:T(8,128)} custom-call(s32[4096]{0:T(1024)} %bitcast_add_fusion.t_ref, bf16[8192,128]{1,0:T(8,128)(2,1)} %bitcast.57, f32[128,32,128]{2,1,0:T(8,128)} %shard_map.74.cur_ref), custom_call_target="tpu_custom_call" | custom-call | tf_op jit(solution)/shard_map/pallas_call | solution.py:265
  (53 shorter events, 6.0 us)
Async XLA Ops:
  0.0 13.8 %copy-start.1 = (f32[2,32,32,128]{3,2,1,0:T(8,128)S(1)}, f32[2,32,32,128]{3,2,1,0:T(8,128)}, u32[]{:S(2)}) copy-start(f32[2,32,32,128]{3,2,1,0:T(8,128)} %param.8) | copy-start | bytes 3145732
  4.0 10.9 %copy-start.12 = (s32[1,4096,1]{1,2,0:T(1,128)S(1)}, s32[1,4096,1]{1,2,0:T(1,128)}, u32[]{:S(2)}) copy-start(s32[1,4096,1]{1,2,0:T(1,128)} %param.10) | copy-start | bytes 49156
  4.1 11.4 %collective-permute-start.2 = (f32[4,32,32]{2,1,0:T(8,128)S(1)}, f32[4,32,32]{2,1,0:T(8,128)S(1)}, u32[]{:S(2)}, u32[]{:S(2)}) collective-permute-start(f32[4,32,32]{2,1,0:T(8,128)S(1)} %bitcast.69), channel_id=1, source_target_pairs={{1,0},{2,1},{3,2},{4,3},{5,4},{6,5},{7,6},{8,7},{9,8},{10,9},{11,1... | collective-permute-start | bytes 49160 | tf_op jit(solution)/shard_map/ppermute | solution.py:69
  5.7 9.8 %collective-permute-start.3 = (f32[4,32,32]{2,1,0:T(8,128)S(1)}, f32[4,32,32]{2,1,0:T(8,128)S(1)}, u32[]{:S(2)}, u32[]{:S(2)}) collective-permute-start(f32[4,32,32]{2,1,0:T(8,128)S(1)} %bitcast.70), channel_id=1, source_target_pairs={{0,1},{1,2},{2,3},{3,4},{4,5},{5,6},{6,7},{7,8},{8,9},{9,10},{10,1... | collective-permute-start | bytes 49160 | tf_op jit(solution)/shard_map/ppermute | solution.py:70
  8.4 7.2 %collective-permute-start = (f32[128,1,128]{2,1,0:T(1,128)S(1)}, f32[128,1,128]{2,1,0:T(1,128)S(1)}, u32[]{:S(2)}, u32[]{:S(2)}) collective-permute-start(f32[128,1,128]{2,1,0:T(1,128)S(1)} %get-tuple-element.12), channel_id=1, source_target_pairs={{32,0},{64,32},{96,64},{33,1},{65,33},{97,65},{34,2},{66,34},{98,6... | collective-permute-start | bytes 196616 | tf_op jit(solution)/shard_map/ppermute | solution.py:67
  9.7 5.9 %collective-permute-start.1 = (f32[128,1,128]{2,1,0:T(1,128)S(1)}, f32[128,1,128]{2,1,0:T(1,128)S(1)}, u32[]{:S(2)}, u32[]{:S(2)}) collective-permute-start(f32[128,1,128]{2,1,0:T(1,128)S(1)} %get-tuple-element.11), channel_id=1, source_target_pairs={{0,32},{32,64},{64,96},{1,33},{33,65},{65,97},{2,34},{34,66},{66,9... | collective-permute-start | bytes 196616 | tf_op jit(solution)/shard_map/ppermute | solution.py:68
  15.5 0.6 copy-start.4
  15.5 0.6 copy-start.5
  15.5 0.6 copy-start.7
  15.6 0.6 copy-start.8
  27.5 10.8 %collective-permute-start.6 = (f32[4,32,32]{2,1,0:T(8,128)S(1)}, f32[4,32,32]{2,1,0:T(8,128)S(1)}, u32[]{:S(2)}, u32[]{:S(2)}) collective-permute-start(f32[4,32,32]{2,1,0:T(8,128)S(1)} %bitcast.71), channel_id=1, source_target_pairs={{1,0},{2,1},{3,2},{4,3},{5,4},{6,5},{7,6},{8,7},{9,8},{10,9},{11,1... | collective-permute-start | bytes 49160 | tf_op jit(solution)/shard_map/ppermute | solution.py:69
  31.6 6.6 %collective-permute-start.7 = (f32[4,32,32]{2,1,0:T(8,128)S(1)}, f32[4,32,32]{2,1,0:T(8,128)S(1)}, u32[]{:S(2)}, u32[]{:S(2)}) collective-permute-start(f32[4,32,32]{2,1,0:T(8,128)S(1)} %bitcast.72), channel_id=1, source_target_pairs={{0,1},{1,2},{2,3},{3,4},{4,5},{5,6},{6,7},{7,8},{8,9},{9,10},{10,1... | collective-permute-start | bytes 49160 | tf_op jit(solution)/shard_map/ppermute | solution.py:70
  31.7 6.5 %collective-permute-start.4 = (f32[128,1,128]{2,1,0:T(1,128)S(1)}, f32[128,1,128]{2,1,0:T(1,128)S(1)}, u32[]{:S(2)}, u32[]{:S(2)}) collective-permute-start(f32[128,1,128]{2,1,0:T(1,128)S(1)} %get-tuple-element.10), channel_id=1, source_target_pairs={{32,0},{64,32},{96,64},{33,1},{65,33},{97,65},{34,2},{66,34},{98,6... | collective-permute-start | bytes 196616 | tf_op jit(solution)/shard_map/ppermute | solution.py:67
  33.0 5.9 %collective-permute-start.5 = (f32[128,1,128]{2,1,0:T(1,128)S(1)}, f32[128,1,128]{2,1,0:T(1,128)S(1)}, u32[]{:S(2)}, u32[]{:S(2)}) collective-permute-start(f32[128,1,128]{2,1,0:T(1,128)S(1)} %get-tuple-element.9), channel_id=1, source_target_pairs={{0,32},{32,64},{64,96},{1,33},{33,65},{65,97},{2,34},{34,66},{66,9... | collective-permute-start | bytes 196616 | tf_op jit(solution)/shard_map/ppermute | solution.py:68
  38.2 0.7 copy-start.6
  38.3 0.7 copy-start.9
  38.3 0.7 copy-start.10
  39.0 0.6 copy-start.11
  56.4 38.9 %all-to-all-start = ((bf16[128,32,256]{0,2,1:T(8,128)(2,1)}), bf16[128,32,256]{0,2,1:T(8,128)(2,1)S(1)}, u32[]{:S(2)}, u32[]{:S(2)}) async-start(bf16[128,32,256]{0,2,1:T(8,128)(2,1)} %bitcast.59), calls=%async_computation | async-start | bytes 4194304 | tf_op jit(solution)/shard_map/all_to_all | solution.py:304
  67.0 2.7 %copy-start.2 = (bf16[1,512,128]{2,1,0:T(8,128)(2,1)S(1)}, bf16[1,512,128]{2,1,0:T(8,128)(2,1)}, u32[]{:S(2)}) copy-start(bf16[1,512,128]{2,1,0:T(8,128)(2,1)} %param.11) | copy-start | bytes 393220
  67.0 3.4 %copy-start.3 = (bf16[1,128,512]{2,1,0:T(8,128)(2,1)S(1)}, bf16[1,128,512]{2,1,0:T(8,128)(2,1)}, u32[]{:S(2)}) copy-start(bf16[1,128,512]{2,1,0:T(8,128)(2,1)} %param.13) | copy-start | bytes 393220
  95.3 4.8 %copy-start = (bf16[128,32,256]{0,2,1:T(8,128)(2,1)}, bf16[128,32,256]{0,2,1:T(8,128)(2,1)S(1)}, u32[]{:S(2)}) copy-start(bf16[128,32,256]{0,2,1:T(8,128)(2,1)S(1)} %all-to-all-done) | copy-start | bytes 6291460

commit v10 on v9

--- a/solution.py
+++ b/solution.py
@@ -15,14 +15,39 @@
     return forward, backward
 
 
-FB = 32
-
-def sweep_kernel(q_ref, hn_ref, hs_ref, he_ref, hw_ref, u_ref, v_ref, k_ref, o_ref):
+FB = 8
+
+
+def keep_edges(f, s, top_ref, bottom_ref, lanes, first, last):
+    rows, cols = s.shape
+    top_ref[f] = s[0:1, :]
+    bottom_ref[f] = s[rows - 1:rows, :]
+    first = jnp.where(lanes == f, jnp.broadcast_to(s[:, 0:1], first.shape), first)
+    last = jnp.where(lanes == f, jnp.broadcast_to(s[:, cols - 1:cols], last.shape), last)
+    return first, last
+
+
+def edges_kernel(q_ref, top_ref, bottom_ref, first_ref, last_ref):
+    rows = q_ref.shape[1]
+    lanes = lax.broadcasted_iota(jnp.int32, (rows, FB), 1)
+    first = jnp.zeros((rows, FB), jnp.float32)
+    last = jnp.zeros((rows, FB), jnp.float32)
+    for f in range(FB):
+        first, last = keep_edges(f, q_ref[f], top_ref, bottom_ref, lanes, first, last)
+    first_ref[0] = first
+    last_ref[0] = last
+
+
+def sweep_kernel(q_ref, hn_ref, hs_ref, he_ref, hw_ref, u_ref, v_ref, k_ref,
+                 o_ref, top_ref, bottom_ref, first_ref, last_ref):
     rows, cols = q_ref.shape[1], q_ref.shape[2]
     row = lax.broadcasted_iota(jnp.int32, (rows, cols), 0)
     lane = lax.broadcasted_iota(jnp.int32, (rows, cols), 1)
+    lanes = lax.broadcasted_iota(jnp.int32, (rows, FB), 1)
     he = he_ref[0]
     hw = hw_ref[0]
+    first = jnp.zeros((rows, FB), jnp.float32)
+    last = jnp.zeros((rows, FB), jnp.float32)
     for f in range(FB):
         q = q_ref[f]
         north = jnp.where(row == rows - 1, jnp.broadcast_to(hn_ref[f], (rows, cols)), pltpu.roll(q, rows - 1, 0))
@@ -32,43 +57,65 @@
         u = u_ref[f]
         v = v_ref[f]
         k = k_ref[f]
-        o_ref[f] = (q - 0.5 * u * (east - west) - 0.5 * v * (north - south)
-                    + k * (east + west + north + south - 4.0 * q))
-
-
-def sweep(q, hn, hs, he, hw, u, v, k):
+        s = (q - 0.5 * u * (east - west) - 0.5 * v * (north - south)
+             + k * (east + west + north + south - 4.0 * q))
+        o_ref[f] = s
+        first, last = keep_edges(f, s, top_ref, bottom_ref, lanes, first, last)
+    first_ref[0] = first
+    last_ref[0] = last
+
+
+def edge_specs(feats, rows, cols):
+    nb = feats // FB
+    edge_row = pl.BlockSpec((FB, 1, cols), lambda i: (i, 0, 0))
+    edge_col = pl.BlockSpec((1, rows, FB), lambda i: (i, 0, 0))
+    shapes = [
+        jax.ShapeDtypeStruct((feats, 1, cols), jnp.float32),
+        jax.ShapeDtypeStruct((feats, 1, cols), jnp.float32),
+        jax.ShapeDtypeStruct((nb, rows, FB), jnp.float32),
+        jax.ShapeDtypeStruct((nb, rows, FB), jnp.float32),
+    ]
+    return [edge_row, edge_row, edge_col, edge_col], shapes
+
+
+def edges(q):
+    feats, rows, cols = q.shape
+    specs, shapes = edge_specs(feats, rows, cols)
+    return pl.pallas_call(
+        edges_kernel,
+        grid=(feats // FB,),
+        in_specs=[pl.BlockSpec((FB, rows, cols), lambda i: (i, 0, 0))],
+        out_specs=specs,
+        out_shape=shapes,
+    )(q)
+
+
+def sweep(q, halos, u, v, k):
     feats, rows, cols = q.shape
     levels = u.shape[0]
     nb = feats // FB
     per = levels // FB
     big = pl.BlockSpec((FB, rows, cols), lambda i: (i, 0, 0))
     field = pl.BlockSpec((FB, rows, cols), lambda i: (i % per, 0, 0))
-    edge_row = pl.BlockSpec((FB, 1, cols), lambda i: (i, 0, 0))
-    edge_col = pl.BlockSpec((1, rows, FB), lambda i: (i, 0, 0))
+    specs, shapes = edge_specs(feats, rows, cols)
     return pl.pallas_call(
         sweep_kernel,
         grid=(nb,),
-        in_specs=[big, edge_row, edge_row, edge_col, edge_col, field, field, field],
-        out_specs=big,
-        out_shape=jax.ShapeDtypeStruct(q.shape, q.dtype),
+        in_specs=[big] + specs + [field, field, field],
+        out_specs=[big] + specs,
+        out_shape=[jax.ShapeDtypeStruct(q.shape, q.dtype)] + shapes,
         cost_estimate=pl.CostEstimate(flops=20 * q.size, bytes_accessed=8 * q.size + 12 * u.size, transcendentals=0),
-    )(q, hn, hs, he, hw, u, v, k)
-
-
-def columns_of(edge):
-    feats, rows = edge.shape
-    return jnp.swapaxes(edge.reshape(feats // FB, FB, rows), 1, 2)
-
-
-def step(x, u, v, k):
-    feats, rows, cols = x.shape
+    )(q, *halos, u, v, k)
+
+
+def exchange(top, bottom, first, last):
     lat_forward, lat_backward = neighbours("lat", False)
     lon_forward, lon_backward = neighbours("lon", True)
-    hn = lax.ppermute(x[:, :1, :], "lat", lat_backward)
-    hs = lax.ppermute(x[:, rows - 1:, :], "lat", lat_forward)
-    he = lax.ppermute(columns_of(x[:, :, 0]), "lon", lon_backward)
-    hw = lax.ppermute(columns_of(x[:, :, cols - 1]), "lon", lon_forward)
-    return sweep(x, hn, hs, he, hw, u, v, k)
+    hn = lax.ppermute(top, "lat", lat_backward)
+    hs = lax.ppermute(bottom, "lat", lat_forward)
+    he = lax.ppermute(first, "lon", lon_backward)
+    hw = lax.ppermute(last, "lon", lon_forward)
+    return hn, hs, he, hw
 
 
 def positions(targets_all, experts):
@@ -287,8 +334,9 @@
     num_vars, levels, lat_cells, lon_cells = column_state.shape
     features = num_vars * levels
     current = column_state.reshape(features, lat_cells, lon_cells)
+    sides = edges(current)
     for sweep_index in range(2):
-        current = step(current, wind_speed[0], wind_speed[1], diffusivity)
+        current, *sides = sweep(current, exchange(*sides), wind_speed[0], wind_speed[1], diffusivity)
     column_count = lat_cells * lon_cells
     experts = lax.axis_size("lon")
     capacity = 2 * column_count // experts

time: 171 us -> 191 us (1.12)
  Pallas kernels: 51.4 us -> 85.9 us
  local copies, waits for them, and re-layouts: 18.8 us -> 8.13 us
  blocking collectives: 41.1 us -> 36.8 us
    pallas_call x2 -> x3, Pallas kernels: 11.9 us -> 41.6 us  [the longest x2 31.5 us: sweep(): pl.pallas_call(sweep_kernel, grid=(nb,), in_specs=[big] + specs + [field,...]
    slice x4 -> x0, local copies, waits for them, and re-layouts: 10.6 us -> none  [the longest x2 7.96 us: step(): hw = lax.ppermute(columns_of(x[:, :, cols - 1]), 'lon', lon_forward)]
    pallas_call x1, Pallas kernels: 16.3 us -> 21.1 us  [network(): pl.pallas_call(network_kernel, grid_spec=pltpu.PrefetchScalarGridSpec(num...]
    all_to_all x1, blocking collectives: 41.1 us -> 36.8 us  [local(): lax.all_to_all(result.reshape(features, experts, width), 'lon', split_axi...]
  transfers between devices with their start and end apart: 9 -> 9, of which waited for: 2 -> 2; matrix products, arithmetic and copies ran while one was open for 5% -> 3% of each run, Pallas kernels for 0% -> 0%
where the time goes in v10:
time: 191 us; the launch traced here: 189 us
  Pallas kernels  85.9 us (45%)
  blocking collectives  36.8 us (19%)
  starting transfers between devices  28.7 us (15%)
  waiting for transfers between devices  25.1 us (13%)
  local copies, waits for them, and re-layouts  8.13 us (4%)
  other arithmetic  3.57 us (2%)
    all_to_all x1, blocking collectives, local(): lax.all_to_all(result.reshape(features, experts, width), 'lon', split_axi...  36.8 us
    pallas_call x2, Pallas kernels, sweep(): pl.pallas_call(sweep_kernel, grid=(nb,), in_specs=[big] + specs + [field,...  31.5 us
    all_to_all x1, waiting for transfers between devices, local(): lax.all_to_all(part, 'lon', split_axis=1, concat_axis=1, tiled=True)  24.1 us
    pallas_call x1, Pallas kernels, network(): pl.pallas_call(network_kernel, grid_spec=pltpu.PrefetchScalarGridSpec(num...  21.1 us
    pallas_call x1, Pallas kernels, combine(): pl.pallas_call(combine_kernel, grid_spec=pltpu.PrefetchScalarGridSpec(num...  12.3 us
    pallas_call x1, Pallas kernels, pack(): pl.pallas_call(pack_kernel, grid_spec=pltpu.PrefetchScalarGridSpec(num_sc...  10.8 us
    pallas_call x1, Pallas kernels, edges(): pl.pallas_call(edges_kernel, grid=(feats // FB,), in_specs=[pl.BlockSpec(...  10.1 us
    all_to_all x1, starting transfers between devices, local(): lax.all_to_all(part, 'lon', split_axis=1, concat_axis=1, tiled=True)  9.47 us
  transfers between devices with their start and end apart: 9, of which 2 were waited for; matrix products, arithmetic and copies ran while one was open for 3% of the time, Pallas kernels for 0%

profile of v10, /device:TPU:1, one launch (start us, length us, event | category | flops | bytes accessed | tf_op | source)
XLA Modules:
  0.0 189.2 jit_solution(14097205206798023557)
XLA Ops:
  0.0 10.1 %shard_map.73 = (f32[128,1,128]{2,1,0:T(1,128)}, f32[128,1,128]{2,1,0:T(1,128)}, f32[16,32,8]{2,1,0:T(8,128)}, f32[16,32,8]{2,1,0:T(8,128)}) custom-call(f32[128,32,128]{2,1,0:T(8,128)} %bitcast.47), custom_call_target="tpu_custom_call" | custom-call | tf_op jit(solution)/shard_map/pallas_call | solution.py:84
  10.1 1.4 collective-permute-start.2
  11.6 1.3 collective-permute-start.3
  12.9 1.3 collective-permute-start
  14.2 4.2 %collective-permute-start.1 = (f32[128,1,128]{2,1,0:T(1,128)}, f32[128,1,128]{2,1,0:T(1,128)S(1)}, u32[]{:S(2)}, u32[]{:S(2)}) collective-permute-start(f32[128,1,128]{2,1,0:T(1,128)} %get-tuple-element.16), channel_id=1, source_target_pairs={{0,32},{32,64},{64,96},{1,33},{33,65},{65,97},{2,34},{34,66},{66,9... | collective-permute-start | bytes 196616 | tf_op jit(solution)/shard_map/ppermute | solution.py:115
  18.4 1.1 slice_bitcast_fusion
  20.9 15.7 %shard_map.74 = (f32[128,32,128]{2,1,0:T(8,128)}, f32[128,1,128]{2,1,0:T(1,128)}, f32[128,1,128]{2,1,0:T(1,128)}, f32[16,32,8]{2,1,0:T(8,128)}, f32[16,32,8]{2,1,0:T(8,128)}) custom-call(f32[128,32,128]{2,1,0:T(8,128)} %bitcast.48, f32[128,1,128]{2,1,0:T(1,128)} %copy-done.8, f32[128,1,128]{2,1,0:T(1,128)} %copy-done.9, f32[16,32,8]{2,1,0:T(8,128)} %copy-done.2, ...), custom_call_target="tpu_custom_call" | custom-call | flops 10485760 | bytes 5767168 | tf_op jit(solution)/shard_map/pallas_call | solution.py:101
  36.6 5.6 %collective-permute-start.6 = (f32[16,32,8]{2,1,0:T(8,128)}, f32[16,32,8]{2,1,0:T(8,128)S(1)}, u32[]{:S(2)}, u32[]{:S(2)}) collective-permute-start(f32[16,32,8]{2,1,0:T(8,128)} %get-tuple-element.22), channel_id=1, source_target_pairs={{1,0},{2,1},{3,2},{4,3},{5,4},{6,5},{7,6},{8,7},{9,8},{10,9},{11,1... | collective-permute-start | bytes 49160 | tf_op jit(solution)/shard_map/ppermute | solution.py:116
  42.2 1.3 collective-permute-start.4
  43.5 4.2 %collective-permute-start.5 = (f32[128,1,128]{2,1,0:T(1,128)}, f32[128,1,128]{2,1,0:T(1,128)S(1)}, u32[]{:S(2)}, u32[]{:S(2)}) collective-permute-start(f32[128,1,128]{2,1,0:T(1,128)} %get-tuple-element.21), channel_id=1, source_target_pairs={{0,32},{32,64},{64,96},{1,33},{33,65},{65,97},{2,34},{34,66},{66,9... | collective-permute-start | bytes 196616 | tf_op jit(solution)/shard_map/ppermute | solution.py:115
  48.3 1.0 collective-permute-done.5.hs_ref
  49.9 15.7 %shard_map.75 = (f32[128,32,128]{2,1,0:T(8,128)}, f32[128,1,128]{2,1,0:T(1,128)}, f32[128,1,128]{2,1,0:T(1,128)}, f32[16,32,8]{2,1,0:T(8,128)}, f32[16,32,8]{2,1,0:T(8,128)}) custom-call(f32[128,32,128]{2,1,0:T(8,128)} %get-tuple-element.19.q_ref, f32[128,1,128]{2,1,0:T(1,128)} %copy-done.10, f32[128,1,128]{2,1,0:T(1,128)} %copy-done.11, ...), custom_call_target="tpu_custom_call" | custom-call | flops 10485760 | bytes 5767168 | tf_op jit(solution)/shard_map/pallas_call | solution.py:101
  65.6 10.8 %shard_map.76 = bf16[8192,128]{1,0:T(8,128)(2,1)} custom-call(s32[4096]{0:T(1024)} %bitcast_add_fusion.t_ref, f32[128,32,128]{2,1,0:T(8,128)} %get-tuple-element.24.cur_ref), custom_call_target="tpu_custom_call" | custom-call | tf_op jit(solution)/shard_map/pallas_call | solution.py:281
  76.5 9.5 %all-to-all-start = ((bf16[128,32,256]{0,2,1:T(8,128)(2,1)}), bf16[128,32,256]{0,2,1:T(8,128)(2,1)S(1)}, u32[]{:S(2)}, u32[]{:S(2)}) async-start(bf16[128,32,256]{0,2,1:T(8,128)(2,1)} %bitcast.50), calls=%async_computation | async-start | bytes 4194304 | tf_op jit(solution)/shard_map/all_to_all | solution.py:352
  86.0 2.7 %copy.24 = bf16[1,3,512,512]{2,3,1,0:T(8,128)(2,1)} copy(bf16[1,3,512,512]{3,2,1,0:T(8,128)(2,1)} %param.12) | data formatting | bytes 3145728 | tf_op args[5]
  88.7 0.8 copy.23
  89.4 0.8 copy.25
  90.2 24.1 %all-to-all-done = bf16[128,32,256]{0,2,1:T(8,128)(2,1)S(1)} async-done(((bf16[128,32,256]{0,2,1:T(8,128)(2,1)}), bf16[128,32,256]{0,2,1:T(8,128)(2,1)S(1)}, u32[]{:S(2)}, u32[]{:S(2)}) %all-to-all-start) | async-done | bytes 2097184 | tf_op jit(solution)/shard_map/all_to_all | solution.py:352
  114.3 1.2 compare_reduce_fusion
  117.0 0.7 fusion.7
  117.7 1.3 scatter_custom_fusion.source_ref
  119.0 21.1 %shard_map.77 = bf16[8192,128]{1,0:T(8,128)(2,1)} custom-call(s32[1]{0:T(128)} %bitcast.13.active_ref, s32[64]{0:T(128)} %scatter_custom_fusion.source_ref, bf16[8192,128]{1,0:T(8,128)(2,1)} %bitcast.49, bf16[128,512]{1,0:T(8,128)(2,1)} %bitcast.53, bf16[3,512,512]{2,1,0:T(8,128)(2,1)} %bitcast.52, bf16[512,128]{1,0:T(8,128)(2,1)} %bitcast.54), custom_call_target="tpu_custom_call" | custom-call | flops 15032385536 | bytes 6029312 | tf_op jit(solution)/shard_map/pallas_call | solution.py:234
  140.1 36.8 %all_to_all.10 = bf16[128,32,256]{0,2,1:T(8,128)(2,1)} all-to-all(bf16[128,32,256]{0,2,1:T(8,128)(2,1)} %bitcast.51), channel_id=1, replica_groups=mesh['lat'=4,'lon'=32] {'lon'}, dimensions={1} | all-to-all | bytes 4194304 | tf_op jit(solution)/shard_map/all_to_all | solution.py:356
  176.9 12.3 %shard_map.78 = f32[128,32,128]{2,1,0:T(8,128)} custom-call(s32[4096]{0:T(1024)} %bitcast_add_fusion.t_ref, bf16[8192,128]{1,0:T(8,128)(2,1)} %bitcast.46, f32[128,32,128]{2,1,0:T(8,128)} %get-tuple-element.24.cur_ref), custom_call_target="tpu_custom_call" | custom-call | tf_op jit(solution)/shard_map/pallas_call | solution.py:312
  (46 shorter events, 3.6 us)
Async XLA Ops:
  0.0 18.4 %copy-start.1 = (f32[2,32,32,128]{3,2,1,0:T(8,128)S(1)}, f32[2,32,32,128]{3,2,1,0:T(8,128)}, u32[]{:S(2)}) copy-start(f32[2,32,32,128]{3,2,1,0:T(8,128)} %param.8) | copy-start | bytes 3145732
  0.0 19.4 %copy-start.12 = (s32[1,4096,1]{1,2,0:T(1,128)S(1)}, s32[1,4096,1]{1,2,0:T(1,128)}, u32[]{:S(2)}) copy-start(s32[1,4096,1]{1,2,0:T(1,128)} %param.10) | copy-start | bytes 49156
  10.1 9.9 %collective-permute-start.2 = (f32[16,32,8]{2,1,0:T(8,128)}, f32[16,32,8]{2,1,0:T(8,128)S(1)}, u32[]{:S(2)}, u32[]{:S(2)}) collective-permute-start(f32[16,32,8]{2,1,0:T(8,128)} %get-tuple-element.17), channel_id=1, source_target_pairs={{1,0},{2,1},{3,2},{4,3},{5,4},{6,5},{7,6},{8,7},{9,8},{10,9},{11,1... | collective-permute-start | bytes 49160 | tf_op jit(solution)/shard_map/ppermute | solution.py:116
  11.6 8.5 %collective-permute-start.3 = (f32[16,32,8]{2,1,0:T(8,128)}, f32[16,32,8]{2,1,0:T(8,128)S(1)}, u32[]{:S(2)}, u32[]{:S(2)}) collective-permute-start(f32[16,32,8]{2,1,0:T(8,128)} %get-tuple-element.18), channel_id=1, source_target_pairs={{0,1},{1,2},{2,3},{3,4},{4,5},{5,6},{6,7},{7,8},{8,9},{9,10},{10,1... | collective-permute-start | bytes 49160 | tf_op jit(solution)/shard_map/ppermute | solution.py:117
  12.9 7.2 %collective-permute-start = (f32[128,1,128]{2,1,0:T(1,128)}, f32[128,1,128]{2,1,0:T(1,128)S(1)}, u32[]{:S(2)}, u32[]{:S(2)}) collective-permute-start(f32[128,1,128]{2,1,0:T(1,128)} %get-tuple-element.15), channel_id=1, source_target_pairs={{32,0},{64,32},{96,64},{33,1},{65,33},{97,65},{34,2},{66,34},{98,6... | collective-permute-start | bytes 196616 | tf_op jit(solution)/shard_map/ppermute | solution.py:114
  14.2 5.9 %collective-permute-start.1 = (f32[128,1,128]{2,1,0:T(1,128)}, f32[128,1,128]{2,1,0:T(1,128)S(1)}, u32[]{:S(2)}, u32[]{:S(2)}) collective-permute-start(f32[128,1,128]{2,1,0:T(1,128)} %get-tuple-element.16), channel_id=1, source_target_pairs={{0,32},{32,64},{64,96},{1,33},{33,65},{65,97},{2,34},{34,66},{66,9... | collective-permute-start | bytes 196616 | tf_op jit(solution)/shard_map/ppermute | solution.py:115
  20.0 0.7 copy-start.2
  20.0 0.8 copy-start.3
  20.1 0.8 copy-start.8
  20.1 0.8 copy-start.9
  36.6 11.6 %collective-permute-start.6 = (f32[16,32,8]{2,1,0:T(8,128)}, f32[16,32,8]{2,1,0:T(8,128)S(1)}, u32[]{:S(2)}, u32[]{:S(2)}) collective-permute-start(f32[16,32,8]{2,1,0:T(8,128)} %get-tuple-element.22), channel_id=1, source_target_pairs={{1,0},{2,1},{3,2},{4,3},{5,4},{6,5},{7,6},{8,7},{9,8},{10,9},{11,1... | collective-permute-start | bytes 49160 | tf_op jit(solution)/shard_map/ppermute | solution.py:116
  42.2 6.1 %collective-permute-start.7 = (f32[16,32,8]{2,1,0:T(8,128)}, f32[16,32,8]{2,1,0:T(8,128)S(1)}, u32[]{:S(2)}, u32[]{:S(2)}) collective-permute-start(f32[16,32,8]{2,1,0:T(8,128)} %get-tuple-element.23), channel_id=1, source_target_pairs={{0,1},{1,2},{2,3},{3,4},{4,5},{5,6},{6,7},{7,8},{8,9},{9,10},{10,1... | collective-permute-start | bytes 49160 | tf_op jit(solution)/shard_map/ppermute | solution.py:117
  42.2 6.1 %collective-permute-start.4 = (f32[128,1,128]{2,1,0:T(1,128)}, f32[128,1,128]{2,1,0:T(1,128)S(1)}, u32[]{:S(2)}, u32[]{:S(2)}) collective-permute-start(f32[128,1,128]{2,1,0:T(1,128)} %get-tuple-element.20), channel_id=1, source_target_pairs={{32,0},{64,32},{96,64},{33,1},{65,33},{97,65},{34,2},{66,34},{98,6... | collective-permute-start | bytes 196616 | tf_op jit(solution)/shard_map/ppermute | solution.py:114
  43.5 5.8 %collective-permute-start.5 = (f32[128,1,128]{2,1,0:T(1,128)}, f32[128,1,128]{2,1,0:T(1,128)S(1)}, u32[]{:S(2)}, u32[]{:S(2)}) collective-permute-start(f32[128,1,128]{2,1,0:T(1,128)} %get-tuple-element.21), channel_id=1, source_target_pairs={{0,32},{32,64},{64,96},{1,33},{33,65},{65,97},{2,34},{34,66},{66,9... | collective-permute-start | bytes 196616 | tf_op jit(solution)/shard_map/ppermute | solution.py:115
  48.3 1.0 copy-start.4
  48.3 1.0 copy-start.5
  48.3 1.0 copy-start.10
  49.3 0.6 copy-start.11
  76.5 37.8 %all-to-all-start = ((bf16[128,32,256]{0,2,1:T(8,128)(2,1)}), bf16[128,32,256]{0,2,1:T(8,128)(2,1)S(1)}, u32[]{:S(2)}, u32[]{:S(2)}) async-start(bf16[128,32,256]{0,2,1:T(8,128)(2,1)} %bitcast.50), calls=%async_computation | async-start | bytes 4194304 | tf_op jit(solution)/shard_map/all_to_all | solution.py:352
  86.0 2.7 %copy-start.6 = (bf16[1,512,128]{2,1,0:T(8,128)(2,1)S(1)}, bf16[1,512,128]{2,1,0:T(8,128)(2,1)}, u32[]{:S(2)}) copy-start(bf16[1,512,128]{2,1,0:T(8,128)(2,1)} %param.11) | copy-start | bytes 393220
  86.0 3.5 %copy-start.7 = (bf16[1,128,512]{2,1,0:T(8,128)(2,1)S(1)}, bf16[1,128,512]{2,1,0:T(8,128)(2,1)}, u32[]{:S(2)}) copy-start(bf16[1,128,512]{2,1,0:T(8,128)(2,1)} %param.13) | copy-start | bytes 393220
  114.3 4.7 %copy-start = (bf16[128,32,256]{0,2,1:T(8,128)(2,1)}, bf16[128,32,256]{0,2,1:T(8,128)(2,1)S(1)}, u32[]{:S(2)}) copy-start(bf16[128,32,256]{0,2,1:T(8,128)(2,1)S(1)} %all-to-all-done) | copy-start | bytes 6291460

commit v11 on v9

--- a/solution.py
+++ b/solution.py
@@ -66,8 +66,12 @@
     lon_forward, lon_backward = neighbours("lon", True)
     hn = lax.ppermute(x[:, :1, :], "lat", lat_backward)
     hs = lax.ppermute(x[:, rows - 1:, :], "lat", lat_forward)
-    he = lax.ppermute(columns_of(x[:, :, 0]), "lon", lon_backward)
-    hw = lax.ppermute(columns_of(x[:, :, cols - 1]), "lon", lon_forward)
+    lane = lax.broadcasted_iota(jnp.int32, (cols, 2), 0)
+    which = lax.broadcasted_iota(jnp.int32, (cols, 2), 1)
+    pick = (lane == which * (cols - 1)).astype(jnp.float32)
+    ends = jnp.dot(x.reshape(feats * rows, cols), pick, precision=lax.Precision.HIGHEST)
+    he = lax.ppermute(columns_of(ends[:, 0].reshape(feats, rows)), "lon", lon_backward)
+    hw = lax.ppermute(columns_of(ends[:, 1].reshape(feats, rows)), "lon", lon_forward)
     return sweep(x, hn, hs, he, hw, u, v, k)
 
 

time: 171 us -> 169 us (0.988)
  local copies, waits for them, and re-layouts: 18.8 us -> 11.3 us
  matrix products: 0.28 us -> 5.64 us
  Pallas kernels: 51.4 us -> 53.6 us
  blocking collectives: 41.1 us -> 39 us
    slice x2, local copies, waits for them, and re-layouts: 7.96 us -> 0.18 us  [step(): ends[:, 1].reshape(feats, rows)]
    dot_general x0 -> x2, matrix products: none -> 5.36 us  [step(): jnp.dot(x.reshape(feats * rows, cols), pick, precision=lax.Precision.HIGH...]
    pallas_call x1, Pallas kernels: 16.3 us -> 18.5 us  [network(): pl.pallas_call(network_kernel, grid_spec=pltpu.PrefetchScalarGridSpec(num...]
    all_to_all x1, blocking collectives: 41.1 us -> 39 us  [local(): lax.all_to_all(result.reshape(features, experts, width), 'lon', split_axi...]
where the time goes in v11:
time: 169 us; the launch traced here: 168 us
  Pallas kernels  53.6 us (32%)
  blocking collectives  39 us (23%)
  starting transfers between devices  28.9 us (17%)
  waiting for transfers between devices  24.8 us (15%)
  local copies, waits for them, and re-layouts  11.3 us (7%)
  matrix products  5.64 us (3%)
  other arithmetic  3.65 us (2%)
    all_to_all x1, blocking collectives, local(): lax.all_to_all(result.reshape(features, experts, width), 'lon', split_axi...  39 us
    all_to_all x1, waiting for transfers between devices, local(): lax.all_to_all(part, 'lon', split_axis=1, concat_axis=1, tiled=True)  24.1 us
    pallas_call x1, Pallas kernels, network(): pl.pallas_call(network_kernel, grid_spec=pltpu.PrefetchScalarGridSpec(num...  18.5 us
    pallas_call x1, Pallas kernels, combine(): pl.pallas_call(combine_kernel, grid_spec=pltpu.PrefetchScalarGridSpec(num...  12.3 us
    pallas_call x2, Pallas kernels, sweep(): pl.pallas_call(sweep_kernel, grid=(nb,), in_specs=[big, edge_row, edge_ro...  11.9 us
    pallas_call x1, Pallas kernels, pack(): pl.pallas_call(pack_kernel, grid_spec=pltpu.PrefetchScalarGridSpec(num_sc...  10.8 us
    all_to_all x1, starting transfers between devices, local(): lax.all_to_all(part, 'lon', split_axis=1, concat_axis=1, tiled=True)  10.6 us
    ppermute x2, starting transfers between devices, step(): hs = lax.ppermute(x[:, rows - 1:, :], 'lat', lat_forward)  8.79 us
  transfers between devices with their start and end apart: 9, of which 2 were waited for; matrix products, arithmetic and copies ran while one was open for 5% of the time, Pallas kernels for 0%

profile of v11, /device:TPU:1, one launch (start us, length us, event | category | flops | bytes accessed | tf_op | source)
XLA Modules:
  0.0 167.8 jit_solution(15156172764373124219)
XLA Ops:
  0.0 2.7 %convolution_bitcast_fusion = f32[4096,2]{0,1:T(2,128)S(1)} fusion(f32[4096,128]{1,0:T(8,128)} %bitcast.57, s32[2]{0:T(128)S(1)} %iota_multiply_fusion), kind=kOutput, calls=%fused_computation.1 | convolution fusion | flops 12583424 | bytes 2129928 | tf_op jit(solution)/shard_map/dot_general | solution.py:72
  3.0 1.5 collective-permute-start.2
  4.7 1.4 collective-permute-start.3
  6.0 1.3 fusion.16
  7.3 1.3 collective-permute-start
  8.6 4.2 %collective-permute-start.1 = (f32[128,1,128]{2,1,0:T(1,128)S(1)}, f32[128,1,128]{2,1,0:T(1,128)S(1)}, u32[]{:S(2)}, u32[]{:S(2)}) collective-permute-start(f32[128,1,128]{2,1,0:T(1,128)S(1)} %get-tuple-element.11), channel_id=1, source_target_pairs={{0,32},{32,64},{64,96},{1,33},{33,65},{65,97},{2,34},{34,66},{66,9... | collective-permute-start | bytes 196616 | tf_op jit(solution)/shard_map/ppermute | solution.py:68
  12.8 1.1 slice_bitcast_fusion
  15.1 6.0 %shard_map.73.q_ref = f32[128,32,128]{2,1,0:T(8,128)} custom-call(f32[128,32,128]{2,1,0:T(8,128)} %bitcast.59, f32[128,1,128]{2,1,0:T(1,128)} %copy-done.7, f32[128,1,128]{2,1,0:T(1,128)} %copy-done.8, f32[4,32,32]{2,1,0:T(8,128)} %copy-done.4, f32[4,32,32]{2,1,0:T(8,128)} %copy-done.5, f32[32,32,128]{2,1,0:T(8,128)} %get-tuple-element.14.u_ref, ...), custom_call_target="tpu_custom_call" | custom-call | flops 10485760 | bytes 5767168 | tf_op jit(solution)/shard_map/pallas_call | solution.py:48
  21.1 1.3 fusion.15
  22.4 2.6 %fusion.5 = f32[4096,2]{0,1:T(2,128)S(1)} fusion(f32[4096,128]{1,0:T(8,128)} %bitcast.56, s32[2]{0:T(128)S(1)} %iota_multiply_fusion), kind=kOutput, calls=%fused_computation.15 | convolution fusion | flops 12583168 | bytes 2129928 | tf_op jit(solution)/shard_map/dot_general | solution.py:72
  25.3 4.1 %collective-permute-start.6 = (f32[4,32,32]{2,1,0:T(8,128)S(1)}, f32[4,32,32]{2,1,0:T(8,128)S(1)}, u32[]{:S(2)}, u32[]{:S(2)}) collective-permute-start(f32[4,32,32]{2,1,0:T(8,128)S(1)} %bitcast.70), channel_id=1, source_target_pairs={{1,0},{2,1},{3,2},{4,3},{5,4},{6,5},{7,6},{8,7},{9,8},{10,9},{11,1... | collective-permute-start | bytes 49160 | tf_op jit(solution)/shard_map/ppermute | solution.py:73
  29.6 1.3 collective-permute-start.4
  30.9 4.6 %collective-permute-start.5 = (f32[128,1,128]{2,1,0:T(1,128)S(1)}, f32[128,1,128]{2,1,0:T(1,128)S(1)}, u32[]{:S(2)}, u32[]{:S(2)}) collective-permute-start(f32[128,1,128]{2,1,0:T(1,128)S(1)} %get-tuple-element.9), channel_id=1, source_target_pairs={{0,32},{32,64},{64,96},{1,33},{33,65},{65,97},{2,34},{34,66},{66,9... | collective-permute-start | bytes 196616 | tf_op jit(solution)/shard_map/ppermute | solution.py:68
  37.5 6.0 %shard_map.74.cur_ref = f32[128,32,128]{2,1,0:T(8,128)} custom-call(f32[128,32,128]{2,1,0:T(8,128)} %shard_map.73.q_ref, f32[128,1,128]{2,1,0:T(1,128)} %copy-done.10, f32[128,1,128]{2,1,0:T(1,128)} %copy-done.11, f32[4,32,32]{2,1,0:T(8,128)} %copy-done.6, f32[4,32,32]{2,1,0:T(8,128)} %copy-done.9, f32[32,32,128]{2,1,0:T(8,128)} %get-tuple-element.14.u_ref, ...), custom_call_target="tpu_custom_call" | custom-call | flops 10485760 | bytes 5767168 | tf_op jit(solution)/shard_map/pallas_call | solution.py:48
  43.5 10.8 %shard_map.75 = bf16[8192,128]{1,0:T(8,128)(2,1)} custom-call(s32[4096]{0:T(1024)} %bitcast_add_fusion.t_ref, f32[128,32,128]{2,1,0:T(8,128)} %shard_map.74.cur_ref), custom_call_target="tpu_custom_call" | custom-call | tf_op jit(solution)/shard_map/pallas_call | solution.py:238
  54.3 10.6 %all-to-all-start = ((bf16[128,32,256]{0,2,1:T(8,128)(2,1)}), bf16[128,32,256]{0,2,1:T(8,128)(2,1)S(1)}, u32[]{:S(2)}, u32[]{:S(2)}) async-start(bf16[128,32,256]{0,2,1:T(8,128)(2,1)} %bitcast.62), calls=%async_computation | async-start | bytes 4194304 | tf_op jit(solution)/shard_map/all_to_all | solution.py:308
  64.9 2.7 %copy.32 = bf16[1,3,512,512]{2,3,1,0:T(8,128)(2,1)} copy(bf16[1,3,512,512]{3,2,1,0:T(8,128)(2,1)} %param.12) | data formatting | bytes 3145728 | tf_op args[5]
  67.6 0.8 copy.31
  69.1 24.1 %all-to-all-done = bf16[128,32,256]{0,2,1:T(8,128)(2,1)S(1)} async-done(((bf16[128,32,256]{0,2,1:T(8,128)(2,1)}), bf16[128,32,256]{0,2,1:T(8,128)(2,1)S(1)}, u32[]{:S(2)}, u32[]{:S(2)}) %all-to-all-start) | async-done | bytes 2097184 | tf_op jit(solution)/shard_map/all_to_all | solution.py:308
  93.2 1.2 compare_reduce_fusion
  96.7 1.3 scatter_custom_fusion.source_ref
  98.0 18.5 %shard_map.76 = bf16[8192,128]{1,0:T(8,128)(2,1)} custom-call(s32[1]{0:T(128)} %bitcast.20.active_ref, s32[64]{0:T(128)} %scatter_custom_fusion.source_ref, bf16[8192,128]{1,0:T(8,128)(2,1)} %bitcast.61, bf16[128,512]{1,0:T(8,128)(2,1)} %bitcast.65, bf16[3,512,512]{2,1,0:T(8,128)(2,1)} %bitcast.64, bf16[512,128]{1,0:T(8,128)(2,1)} %bitcast.66), custom_call_target="tpu_custom_call" | custom-call | flops 15032385536 | bytes 6029312 | tf_op jit(solution)/shard_map/pallas_call | solution.py:191
  116.5 39.0 %all_to_all.10 = bf16[128,32,256]{0,2,1:T(8,128)(2,1)} all-to-all(bf16[128,32,256]{0,2,1:T(8,128)(2,1)} %bitcast.63), channel_id=1, replica_groups=mesh['lat'=4,'lon'=32] {'lon'}, dimensions={1} | all-to-all | bytes 4194304 | tf_op jit(solution)/shard_map/all_to_all | solution.py:312
  155.5 12.3 %shard_map.77 = f32[128,32,128]{2,1,0:T(8,128)} custom-call(s32[4096]{0:T(1024)} %bitcast_add_fusion.t_ref, bf16[8192,128]{1,0:T(8,128)(2,1)} %bitcast.60, f32[128,32,128]{2,1,0:T(8,128)} %shard_map.74.cur_ref), custom_call_target="tpu_custom_call" | custom-call | tf_op jit(solution)/shard_map/pallas_call | solution.py:269
  (60 shorter events, 6.5 us)
Async XLA Ops:
  0.0 12.8 %copy-start.1 = (f32[2,32,32,128]{3,2,1,0:T(8,128)S(1)}, f32[2,32,32,128]{3,2,1,0:T(8,128)}, u32[]{:S(2)}) copy-start(f32[2,32,32,128]{3,2,1,0:T(8,128)} %param.8) | copy-start | bytes 3145732
  0.0 13.9 %copy-start.12 = (s32[1,4096,1]{1,2,0:T(1,128)S(1)}, s32[1,4096,1]{1,2,0:T(1,128)}, u32[]{:S(2)}) copy-start(s32[1,4096,1]{1,2,0:T(1,128)} %param.10) | copy-start | bytes 49156
  3.0 11.4 %collective-permute-start.2 = (f32[4,32,32]{2,1,0:T(8,128)S(1)}, f32[4,32,32]{2,1,0:T(8,128)S(1)}, u32[]{:S(2)}, u32[]{:S(2)}) collective-permute-start(f32[4,32,32]{2,1,0:T(8,128)S(1)} %bitcast.68), channel_id=1, source_target_pairs={{1,0},{2,1},{3,2},{4,3},{5,4},{6,5},{7,6},{8,7},{9,8},{10,9},{11,1... | collective-permute-start | bytes 49160 | tf_op jit(solution)/shard_map/ppermute | solution.py:73
  4.7 9.8 %collective-permute-start.3 = (f32[4,32,32]{2,1,0:T(8,128)S(1)}, f32[4,32,32]{2,1,0:T(8,128)S(1)}, u32[]{:S(2)}, u32[]{:S(2)}) collective-permute-start(f32[4,32,32]{2,1,0:T(8,128)S(1)} %bitcast.69), channel_id=1, source_target_pairs={{0,1},{1,2},{2,3},{3,4},{4,5},{5,6},{6,7},{7,8},{8,9},{9,10},{10,1... | collective-permute-start | bytes 49160 | tf_op jit(solution)/shard_map/ppermute | solution.py:74
  7.3 7.2 %collective-permute-start = (f32[128,1,128]{2,1,0:T(1,128)S(1)}, f32[128,1,128]{2,1,0:T(1,128)S(1)}, u32[]{:S(2)}, u32[]{:S(2)}) collective-permute-start(f32[128,1,128]{2,1,0:T(1,128)S(1)} %get-tuple-element.12), channel_id=1, source_target_pairs={{32,0},{64,32},{96,64},{33,1},{65,33},{97,65},{34,2},{66,34},{98,6... | collective-permute-start | bytes 196616 | tf_op jit(solution)/shard_map/ppermute | solution.py:67
  8.6 5.9 %collective-permute-start.1 = (f32[128,1,128]{2,1,0:T(1,128)S(1)}, f32[128,1,128]{2,1,0:T(1,128)S(1)}, u32[]{:S(2)}, u32[]{:S(2)}) collective-permute-start(f32[128,1,128]{2,1,0:T(1,128)S(1)} %get-tuple-element.11), channel_id=1, source_target_pairs={{0,32},{32,64},{64,96},{1,33},{33,65},{65,97},{2,34},{34,66},{66,9... | collective-permute-start | bytes 196616 | tf_op jit(solution)/shard_map/ppermute | solution.py:68
  14.5 0.6 copy-start.4
  14.5 0.6 copy-start.5
  14.5 0.6 copy-start.7
  14.5 0.6 copy-start.8
  25.3 10.8 %collective-permute-start.6 = (f32[4,32,32]{2,1,0:T(8,128)S(1)}, f32[4,32,32]{2,1,0:T(8,128)S(1)}, u32[]{:S(2)}, u32[]{:S(2)}) collective-permute-start(f32[4,32,32]{2,1,0:T(8,128)S(1)} %bitcast.70), channel_id=1, source_target_pairs={{1,0},{2,1},{3,2},{4,3},{5,4},{6,5},{7,6},{8,7},{9,8},{10,9},{11,1... | collective-permute-start | bytes 49160 | tf_op jit(solution)/shard_map/ppermute | solution.py:73
  29.5 6.6 %collective-permute-start.7 = (f32[4,32,32]{2,1,0:T(8,128)S(1)}, f32[4,32,32]{2,1,0:T(8,128)S(1)}, u32[]{:S(2)}, u32[]{:S(2)}) collective-permute-start(f32[4,32,32]{2,1,0:T(8,128)S(1)} %bitcast.71), channel_id=1, source_target_pairs={{0,1},{1,2},{2,3},{3,4},{4,5},{5,6},{6,7},{7,8},{8,9},{9,10},{10,1... | collective-permute-start | bytes 49160 | tf_op jit(solution)/shard_map/ppermute | solution.py:74
  29.6 6.5 %collective-permute-start.4 = (f32[128,1,128]{2,1,0:T(1,128)S(1)}, f32[128,1,128]{2,1,0:T(1,128)S(1)}, u32[]{:S(2)}, u32[]{:S(2)}) collective-permute-start(f32[128,1,128]{2,1,0:T(1,128)S(1)} %get-tuple-element.10), channel_id=1, source_target_pairs={{32,0},{64,32},{96,64},{33,1},{65,33},{97,65},{34,2},{66,34},{98,6... | collective-permute-start | bytes 196616 | tf_op jit(solution)/shard_map/ppermute | solution.py:67
  30.9 5.9 %collective-permute-start.5 = (f32[128,1,128]{2,1,0:T(1,128)S(1)}, f32[128,1,128]{2,1,0:T(1,128)S(1)}, u32[]{:S(2)}, u32[]{:S(2)}) collective-permute-start(f32[128,1,128]{2,1,0:T(1,128)S(1)} %get-tuple-element.9), channel_id=1, source_target_pairs={{0,32},{32,64},{64,96},{1,33},{33,65},{65,97},{2,34},{34,66},{66,9... | collective-permute-start | bytes 196616 | tf_op jit(solution)/shard_map/ppermute | solution.py:68
  36.2 0.7 copy-start.6
  36.2 0.7 copy-start.9
  36.2 0.7 copy-start.10
  36.9 0.6 copy-start.11
  54.3 38.9 %all-to-all-start = ((bf16[128,32,256]{0,2,1:T(8,128)(2,1)}), bf16[128,32,256]{0,2,1:T(8,128)(2,1)S(1)}, u32[]{:S(2)}, u32[]{:S(2)}) async-start(bf16[128,32,256]{0,2,1:T(8,128)(2,1)} %bitcast.62), calls=%async_computation | async-start | bytes 4194304 | tf_op jit(solution)/shard_map/all_to_all | solution.py:308
  64.9 2.7 %copy-start.2 = (bf16[1,512,128]{2,1,0:T(8,128)(2,1)S(1)}, bf16[1,512,128]{2,1,0:T(8,128)(2,1)}, u32[]{:S(2)}) copy-start(bf16[1,512,128]{2,1,0:T(8,128)(2,1)} %param.11) | copy-start | bytes 393220
  64.9 3.4 %copy-start.3 = (bf16[1,128,512]{2,1,0:T(8,128)(2,1)S(1)}, bf16[1,128,512]{2,1,0:T(8,128)(2,1)}, u32[]{:S(2)}) copy-start(bf16[1,128,512]{2,1,0:T(8,128)(2,1)} %param.13) | copy-start | bytes 393220
  93.2 4.8 %copy-start = (bf16[128,32,256]{0,2,1:T(8,128)(2,1)}, bf16[128,32,256]{0,2,1:T(8,128)(2,1)S(1)}, u32[]{:S(2)}) copy-start(bf16[128,32,256]{0,2,1:T(8,128)(2,1)S(1)} %all-to-all-done) | copy-start | bytes 6291460

commit v12 on v11

--- a/solution.py
+++ b/solution.py
@@ -216,6 +216,9 @@
     )(active, source, rows_in, first, middle, last)
 
 
+UNROLL = 32
+
+
 def pack_kernel(t_ref, cur_ref, o_ref, rows, full):
     feats, lat_cells, lon_cells = cur_ref.shape
     for r in range(lat_cells):
@@ -223,12 +226,12 @@
     full[...] = jnp.zeros(full.shape, full.dtype)
 
     def body(i, carry):
-        for u in range(8):
-            c = i * 8 + u
+        for u in range(UNROLL):
+            c = i * UNROLL + u
             full[pl.ds(t_ref[c], 1), :] = rows[pl.ds(c, 1), :]
         return carry
 
-    lax.fori_loop(0, rows.shape[0] // 8, body, 0)
+    lax.fori_loop(0, rows.shape[0] // UNROLL, body, 0)
     o_ref[...] = full[...].astype(o_ref.dtype)
 
 
@@ -253,12 +256,12 @@
     full[...] = ret_ref[...].astype(jnp.float32)
 
     def body(i, carry):
-        for u in range(8):
-            c = i * 8 + u
+        for u in range(UNROLL):
+            c = i * UNROLL + u
             tend[pl.ds(c, 1), :] = full[pl.ds(t_ref[c], 1), :]
         return carry
 
-    lax.fori_loop(0, tend.shape[0] // 8, body, 0)
+    lax.fori_loop(0, tend.shape[0] // UNROLL, body, 0)
     for r in range(lat_cells):
         o_ref[:, r, :] = cur_ref[:, r, :] + tend[r * lon_cells:(r + 1) * lon_cells, :].T
 

time: 169 us -> 166 us (0.982)
  blocking collectives: 39 us -> 32.1 us
  Pallas kernels: 53.6 us -> 57.8 us
    pallas_call x1, Pallas kernels: 18.5 us -> 25.8 us  [network(): pl.pallas_call(network_kernel, grid_spec=pltpu.PrefetchScalarGridSpec(num...]
    all_to_all x1, blocking collectives: 39 us -> 32.1 us  [local(): lax.all_to_all(result.reshape(features, experts, width), 'lon', split_axi...]
where the time goes in v12:
time: 166 us; the launch traced here: 165 us
  Pallas kernels  57.8 us (35%)
  blocking collectives  32.1 us (19%)
  starting transfers between devices  28.9 us (17%)
  waiting for transfers between devices  24.8 us (15%)
  local copies, waits for them, and re-layouts  11.3 us (7%)
  matrix products  5.64 us (3%)
  other arithmetic  3.65 us (2%)
    all_to_all x1, blocking collectives, local(): lax.all_to_all(result.reshape(features, experts, width), 'lon', split_axi...  32.1 us
    pallas_call x1, Pallas kernels, network(): pl.pallas_call(network_kernel, grid_spec=pltpu.PrefetchScalarGridSpec(num...  25.8 us
    all_to_all x1, waiting for transfers between devices, local(): lax.all_to_all(part, 'lon', split_axis=1, concat_axis=1, tiled=True)  24.1 us
    pallas_call x2, Pallas kernels, sweep(): pl.pallas_call(sweep_kernel, grid=(nb,), in_specs=[big, edge_row, edge_ro...  11.9 us
    pallas_call x1, Pallas kernels, combine(): pl.pallas_call(combine_kernel, grid_spec=pltpu.PrefetchScalarGridSpec(num...  10.7 us
    all_to_all x1, starting transfers between devices, local(): lax.all_to_all(part, 'lon', split_axis=1, concat_axis=1, tiled=True)  10.6 us
    pallas_call x1, Pallas kernels, pack(): pl.pallas_call(pack_kernel, grid_spec=pltpu.PrefetchScalarGridSpec(num_sc...  9.29 us
    ppermute x2, starting transfers between devices, step(): hs = lax.ppermute(x[:, rows - 1:, :], 'lat', lat_forward)  8.79 us
  transfers between devices with their start and end apart: 9, of which 2 were waited for; matrix products, arithmetic and copies ran while one was open for 5% of the time, Pallas kernels for 0%

profile of v12, /device:TPU:1, one launch (start us, length us, event | category | flops | bytes accessed | tf_op | source)
XLA Modules:
  0.0 165.1 jit_solution(9924974454298293972)
XLA Ops:
  0.0 2.7 %convolution_bitcast_fusion = f32[4096,2]{0,1:T(2,128)S(1)} fusion(f32[4096,128]{1,0:T(8,128)} %bitcast.57, s32[2]{0:T(128)S(1)} %iota_multiply_fusion), kind=kOutput, calls=%fused_computation.1 | convolution fusion | flops 12583424 | bytes 2129928 | tf_op jit(solution)/shard_map/dot_general | solution.py:72
  3.0 1.5 collective-permute-start.2
  4.7 1.4 collective-permute-start.3
  6.0 1.3 fusion.16
  7.3 1.3 collective-permute-start
  8.6 4.2 %collective-permute-start.1 = (f32[128,1,128]{2,1,0:T(1,128)S(1)}, f32[128,1,128]{2,1,0:T(1,128)S(1)}, u32[]{:S(2)}, u32[]{:S(2)}) collective-permute-start(f32[128,1,128]{2,1,0:T(1,128)S(1)} %get-tuple-element.11), channel_id=1, source_target_pairs={{0,32},{32,64},{64,96},{1,33},{33,65},{65,97},{2,34},{34,66},{66,9... | collective-permute-start | bytes 196616 | tf_op jit(solution)/shard_map/ppermute | solution.py:68
  12.8 1.1 slice_bitcast_fusion
  15.1 6.0 %shard_map.73.q_ref = f32[128,32,128]{2,1,0:T(8,128)} custom-call(f32[128,32,128]{2,1,0:T(8,128)} %bitcast.59, f32[128,1,128]{2,1,0:T(1,128)} %copy-done.7, f32[128,1,128]{2,1,0:T(1,128)} %copy-done.8, f32[4,32,32]{2,1,0:T(8,128)} %copy-done.4, f32[4,32,32]{2,1,0:T(8,128)} %copy-done.5, f32[32,32,128]{2,1,0:T(8,128)} %get-tuple-element.14.u_ref, ...), custom_call_target="tpu_custom_call" | custom-call | flops 10485760 | bytes 5767168 | tf_op jit(solution)/shard_map/pallas_call | solution.py:48
  21.1 1.3 fusion.15
  22.4 2.6 %fusion.5 = f32[4096,2]{0,1:T(2,128)S(1)} fusion(f32[4096,128]{1,0:T(8,128)} %bitcast.56, s32[2]{0:T(128)S(1)} %iota_multiply_fusion), kind=kOutput, calls=%fused_computation.15 | convolution fusion | flops 12583168 | bytes 2129928 | tf_op jit(solution)/shard_map/dot_general | solution.py:72
  25.3 4.1 %collective-permute-start.6 = (f32[4,32,32]{2,1,0:T(8,128)S(1)}, f32[4,32,32]{2,1,0:T(8,128)S(1)}, u32[]{:S(2)}, u32[]{:S(2)}) collective-permute-start(f32[4,32,32]{2,1,0:T(8,128)S(1)} %bitcast.70), channel_id=1, source_target_pairs={{1,0},{2,1},{3,2},{4,3},{5,4},{6,5},{7,6},{8,7},{9,8},{10,9},{11,1... | collective-permute-start | bytes 49160 | tf_op jit(solution)/shard_map/ppermute | solution.py:73
  29.6 1.3 collective-permute-start.4
  30.9 4.6 %collective-permute-start.5 = (f32[128,1,128]{2,1,0:T(1,128)S(1)}, f32[128,1,128]{2,1,0:T(1,128)S(1)}, u32[]{:S(2)}, u32[]{:S(2)}) collective-permute-start(f32[128,1,128]{2,1,0:T(1,128)S(1)} %get-tuple-element.9), channel_id=1, source_target_pairs={{0,32},{32,64},{64,96},{1,33},{33,65},{65,97},{2,34},{34,66},{66,9... | collective-permute-start | bytes 196616 | tf_op jit(solution)/shard_map/ppermute | solution.py:68
  37.5 6.0 %shard_map.74.cur_ref = f32[128,32,128]{2,1,0:T(8,128)} custom-call(f32[128,32,128]{2,1,0:T(8,128)} %shard_map.73.q_ref, f32[128,1,128]{2,1,0:T(1,128)} %copy-done.10, f32[128,1,128]{2,1,0:T(1,128)} %copy-done.11, f32[4,32,32]{2,1,0:T(8,128)} %copy-done.6, f32[4,32,32]{2,1,0:T(8,128)} %copy-done.9, f32[32,32,128]{2,1,0:T(8,128)} %get-tuple-element.14.u_ref, ...), custom_call_target="tpu_custom_call" | custom-call | flops 10485760 | bytes 5767168 | tf_op jit(solution)/shard_map/pallas_call | solution.py:48
  43.5 9.3 %shard_map.75 = bf16[8192,128]{1,0:T(8,128)(2,1)} custom-call(s32[4096]{0:T(1024)} %bitcast_add_fusion.t_ref, f32[128,32,128]{2,1,0:T(8,128)} %shard_map.74.cur_ref), custom_call_target="tpu_custom_call" | custom-call | tf_op jit(solution)/shard_map/pallas_call | solution.py:241
  52.8 10.6 %all-to-all-start = ((bf16[128,32,256]{0,2,1:T(8,128)(2,1)}), bf16[128,32,256]{0,2,1:T(8,128)(2,1)S(1)}, u32[]{:S(2)}, u32[]{:S(2)}) async-start(bf16[128,32,256]{0,2,1:T(8,128)(2,1)} %bitcast.62), calls=%async_computation | async-start | bytes 4194304 | tf_op jit(solution)/shard_map/all_to_all | solution.py:311
  63.3 2.7 %copy.32 = bf16[1,3,512,512]{2,3,1,0:T(8,128)(2,1)} copy(bf16[1,3,512,512]{3,2,1,0:T(8,128)(2,1)} %param.12) | data formatting | bytes 3145728 | tf_op args[5]
  66.0 0.8 copy.31
  67.5 24.1 %all-to-all-done = bf16[128,32,256]{0,2,1:T(8,128)(2,1)S(1)} async-done(((bf16[128,32,256]{0,2,1:T(8,128)(2,1)}), bf16[128,32,256]{0,2,1:T(8,128)(2,1)S(1)}, u32[]{:S(2)}, u32[]{:S(2)}) %all-to-all-start) | async-done | bytes 2097184 | tf_op jit(solution)/shard_map/all_to_all | solution.py:311
  91.6 1.2 compare_reduce_fusion
  95.1 1.3 scatter_custom_fusion.source_ref
  96.4 25.8 %shard_map.76 = bf16[8192,128]{1,0:T(8,128)(2,1)} custom-call(s32[1]{0:T(128)} %bitcast.20.active_ref, s32[64]{0:T(128)} %scatter_custom_fusion.source_ref, bf16[8192,128]{1,0:T(8,128)(2,1)} %bitcast.61, bf16[128,512]{1,0:T(8,128)(2,1)} %bitcast.65, bf16[3,512,512]{2,1,0:T(8,128)(2,1)} %bitcast.64, bf16[512,128]{1,0:T(8,128)(2,1)} %bitcast.66), custom_call_target="tpu_custom_call" | custom-call | flops 15032385536 | bytes 6029312 | tf_op jit(solution)/shard_map/pallas_call | solution.py:191
  122.3 32.1 %all_to_all.10 = bf16[128,32,256]{0,2,1:T(8,128)(2,1)} all-to-all(bf16[128,32,256]{0,2,1:T(8,128)(2,1)} %bitcast.63), channel_id=1, replica_groups=mesh['lat'=4,'lon'=32] {'lon'}, dimensions={1} | all-to-all | bytes 4194304 | tf_op jit(solution)/shard_map/all_to_all | solution.py:315
  154.4 10.7 %shard_map.77 = f32[128,32,128]{2,1,0:T(8,128)} custom-call(s32[4096]{0:T(1024)} %bitcast_add_fusion.t_ref, bf16[8192,128]{1,0:T(8,128)(2,1)} %bitcast.60, f32[128,32,128]{2,1,0:T(8,128)} %shard_map.74.cur_ref), custom_call_target="tpu_custom_call" | custom-call | tf_op jit(solution)/shard_map/pallas_call | solution.py:272
  (60 shorter events, 6.5 us)
Async XLA Ops:
  0.0 12.8 %copy-start.1 = (f32[2,32,32,128]{3,2,1,0:T(8,128)S(1)}, f32[2,32,32,128]{3,2,1,0:T(8,128)}, u32[]{:S(2)}) copy-start(f32[2,32,32,128]{3,2,1,0:T(8,128)} %param.8) | copy-start | bytes 3145732
  0.0 13.9 %copy-start.12 = (s32[1,4096,1]{1,2,0:T(1,128)S(1)}, s32[1,4096,1]{1,2,0:T(1,128)}, u32[]{:S(2)}) copy-start(s32[1,4096,1]{1,2,0:T(1,128)} %param.10) | copy-start | bytes 49156
  3.0 11.4 %collective-permute-start.2 = (f32[4,32,32]{2,1,0:T(8,128)S(1)}, f32[4,32,32]{2,1,0:T(8,128)S(1)}, u32[]{:S(2)}, u32[]{:S(2)}) collective-permute-start(f32[4,32,32]{2,1,0:T(8,128)S(1)} %bitcast.68), channel_id=1, source_target_pairs={{1,0},{2,1},{3,2},{4,3},{5,4},{6,5},{7,6},{8,7},{9,8},{10,9},{11,1... | collective-permute-start | bytes 49160 | tf_op jit(solution)/shard_map/ppermute | solution.py:73
  4.7 9.8 %collective-permute-start.3 = (f32[4,32,32]{2,1,0:T(8,128)S(1)}, f32[4,32,32]{2,1,0:T(8,128)S(1)}, u32[]{:S(2)}, u32[]{:S(2)}) collective-permute-start(f32[4,32,32]{2,1,0:T(8,128)S(1)} %bitcast.69), channel_id=1, source_target_pairs={{0,1},{1,2},{2,3},{3,4},{4,5},{5,6},{6,7},{7,8},{8,9},{9,10},{10,1... | collective-permute-start | bytes 49160 | tf_op jit(solution)/shard_map/ppermute | solution.py:74
  7.3 7.2 %collective-permute-start = (f32[128,1,128]{2,1,0:T(1,128)S(1)}, f32[128,1,128]{2,1,0:T(1,128)S(1)}, u32[]{:S(2)}, u32[]{:S(2)}) collective-permute-start(f32[128,1,128]{2,1,0:T(1,128)S(1)} %get-tuple-element.12), channel_id=1, source_target_pairs={{32,0},{64,32},{96,64},{33,1},{65,33},{97,65},{34,2},{66,34},{98,6... | collective-permute-start | bytes 196616 | tf_op jit(solution)/shard_map/ppermute | solution.py:67
  8.6 5.9 %collective-permute-start.1 = (f32[128,1,128]{2,1,0:T(1,128)S(1)}, f32[128,1,128]{2,1,0:T(1,128)S(1)}, u32[]{:S(2)}, u32[]{:S(2)}) collective-permute-start(f32[128,1,128]{2,1,0:T(1,128)S(1)} %get-tuple-element.11), channel_id=1, source_target_pairs={{0,32},{32,64},{64,96},{1,33},{33,65},{65,97},{2,34},{34,66},{66,9... | collective-permute-start | bytes 196616 | tf_op jit(solution)/shard_map/ppermute | solution.py:68
  14.5 0.6 copy-start.4
  14.5 0.6 copy-start.5
  14.5 0.6 copy-start.7
  14.5 0.6 copy-start.8
  25.3 10.8 %collective-permute-start.6 = (f32[4,32,32]{2,1,0:T(8,128)S(1)}, f32[4,32,32]{2,1,0:T(8,128)S(1)}, u32[]{:S(2)}, u32[]{:S(2)}) collective-permute-start(f32[4,32,32]{2,1,0:T(8,128)S(1)} %bitcast.70), channel_id=1, source_target_pairs={{1,0},{2,1},{3,2},{4,3},{5,4},{6,5},{7,6},{8,7},{9,8},{10,9},{11,1... | collective-permute-start | bytes 49160 | tf_op jit(solution)/shard_map/ppermute | solution.py:73
  29.5 6.6 %collective-permute-start.7 = (f32[4,32,32]{2,1,0:T(8,128)S(1)}, f32[4,32,32]{2,1,0:T(8,128)S(1)}, u32[]{:S(2)}, u32[]{:S(2)}) collective-permute-start(f32[4,32,32]{2,1,0:T(8,128)S(1)} %bitcast.71), channel_id=1, source_target_pairs={{0,1},{1,2},{2,3},{3,4},{4,5},{5,6},{6,7},{7,8},{8,9},{9,10},{10,1... | collective-permute-start | bytes 49160 | tf_op jit(solution)/shard_map/ppermute | solution.py:74
  29.6 6.5 %collective-permute-start.4 = (f32[128,1,128]{2,1,0:T(1,128)S(1)}, f32[128,1,128]{2,1,0:T(1,128)S(1)}, u32[]{:S(2)}, u32[]{:S(2)}) collective-permute-start(f32[128,1,128]{2,1,0:T(1,128)S(1)} %get-tuple-element.10), channel_id=1, source_target_pairs={{32,0},{64,32},{96,64},{33,1},{65,33},{97,65},{34,2},{66,34},{98,6... | collective-permute-start | bytes 196616 | tf_op jit(solution)/shard_map/ppermute | solution.py:67
  30.9 5.9 %collective-permute-start.5 = (f32[128,1,128]{2,1,0:T(1,128)S(1)}, f32[128,1,128]{2,1,0:T(1,128)S(1)}, u32[]{:S(2)}, u32[]{:S(2)}) collective-permute-start(f32[128,1,128]{2,1,0:T(1,128)S(1)} %get-tuple-element.9), channel_id=1, source_target_pairs={{0,32},{32,64},{64,96},{1,33},{33,65},{65,97},{2,34},{34,66},{66,9... | collective-permute-start | bytes 196616 | tf_op jit(solution)/shard_map/ppermute | solution.py:68
  36.2 0.7 copy-start.6
  36.2 0.7 copy-start.9
  36.2 0.7 copy-start.10
  36.9 0.6 copy-start.11
  52.8 38.9 %all-to-all-start = ((bf16[128,32,256]{0,2,1:T(8,128)(2,1)}), bf16[128,32,256]{0,2,1:T(8,128)(2,1)S(1)}, u32[]{:S(2)}, u32[]{:S(2)}) async-start(bf16[128,32,256]{0,2,1:T(8,128)(2,1)} %bitcast.62), calls=%async_computation | async-start | bytes 4194304 | tf_op jit(solution)/shard_map/all_to_all | solution.py:311
  63.3 2.7 %copy-start.2 = (bf16[1,512,128]{2,1,0:T(8,128)(2,1)S(1)}, bf16[1,512,128]{2,1,0:T(8,128)(2,1)}, u32[]{:S(2)}) copy-start(bf16[1,512,128]{2,1,0:T(8,128)(2,1)} %param.11) | copy-start | bytes 393220
  63.3 3.4 %copy-start.3 = (bf16[1,128,512]{2,1,0:T(8,128)(2,1)S(1)}, bf16[1,128,512]{2,1,0:T(8,128)(2,1)}, u32[]{:S(2)}) copy-start(bf16[1,128,512]{2,1,0:T(8,128)(2,1)} %param.13) | copy-start | bytes 393220
  91.6 4.8 %copy-start = (bf16[128,32,256]{0,2,1:T(8,128)(2,1)}, bf16[128,32,256]{0,2,1:T(8,128)(2,1)S(1)}, u32[]{:S(2)}) copy-start(bf16[128,32,256]{0,2,1:T(8,128)(2,1)S(1)} %all-to-all-done) | copy-start | bytes 6291460

commit v13 on v12

--- a/solution.py
+++ b/solution.py
@@ -17,7 +17,26 @@
 
 FB = 32
 
-def sweep_kernel(q_ref, hn_ref, hs_ref, he_ref, hw_ref, u_ref, v_ref, k_ref, o_ref):
+
+def keep_edges(block_ref, top_ref, bottom_ref, ends_ref):
+    feats, rows, cols = block_ref.shape
+    for f in range(feats):
+        top_ref[f] = block_ref[f, 0:1, :]
+        bottom_ref[f] = block_ref[f, rows - 1:rows, :]
+    lane = lax.broadcasted_iota(jnp.int32, (2, cols), 1)
+    which = lax.broadcasted_iota(jnp.int32, (2, cols), 0)
+    pick = (lane == which * (cols - 1)).astype(jnp.float32)
+    ends_ref[...] = lax.dot_general(
+        pick, block_ref[...].reshape(feats * rows, cols), (((1,), (1,)), ((), ())),
+        precision=lax.Precision.HIGHEST, preferred_element_type=jnp.float32,
+    )
+
+
+def edges_kernel(q_ref, top_ref, bottom_ref, ends_ref):
+    keep_edges(q_ref, top_ref, bottom_ref, ends_ref)
+
+
+def sweep_kernel(q_ref, hn_ref, hs_ref, he_ref, hw_ref, u_ref, v_ref, k_ref, o_ref, top_ref, bottom_ref, ends_ref):
     rows, cols = q_ref.shape[1], q_ref.shape[2]
     row = lax.broadcasted_iota(jnp.int32, (rows, cols), 0)
     lane = lax.broadcasted_iota(jnp.int32, (rows, cols), 1)
@@ -34,9 +53,33 @@
         k = k_ref[f]
         o_ref[f] = (q - 0.5 * u * (east - west) - 0.5 * v * (north - south)
                     + k * (east + west + north + south - 4.0 * q))
-
-
-def sweep(q, hn, hs, he, hw, u, v, k):
+    keep_edges(o_ref, top_ref, bottom_ref, ends_ref)
+
+
+def edge_specs(feats, rows, cols):
+    edge_row = pl.BlockSpec((FB, 1, cols), lambda i: (i, 0, 0))
+    ends = pl.BlockSpec((2, FB * rows), lambda i: (0, i))
+    shapes = [
+        jax.ShapeDtypeStruct((feats, 1, cols), jnp.float32),
+        jax.ShapeDtypeStruct((feats, 1, cols), jnp.float32),
+        jax.ShapeDtypeStruct((2, feats * rows), jnp.float32),
+    ]
+    return [edge_row, edge_row, ends], shapes
+
+
+def edges(q):
+    feats, rows, cols = q.shape
+    specs, shapes = edge_specs(feats, rows, cols)
+    return pl.pallas_call(
+        edges_kernel,
+        grid=(feats // FB,),
+        in_specs=[pl.BlockSpec((FB, rows, cols), lambda i: (i, 0, 0))],
+        out_specs=specs,
+        out_shape=shapes,
+    )(q)
+
+
+def sweep(q, halos, u, v, k):
     feats, rows, cols = q.shape
     levels = u.shape[0]
     nb = feats // FB
@@ -45,14 +88,15 @@
     field = pl.BlockSpec((FB, rows, cols), lambda i: (i % per, 0, 0))
     edge_row = pl.BlockSpec((FB, 1, cols), lambda i: (i, 0, 0))
     edge_col = pl.BlockSpec((1, rows, FB), lambda i: (i, 0, 0))
+    specs, shapes = edge_specs(feats, rows, cols)
     return pl.pallas_call(
         sweep_kernel,
         grid=(nb,),
         in_specs=[big, edge_row, edge_row, edge_col, edge_col, field, field, field],
-        out_specs=big,
-        out_shape=jax.ShapeDtypeStruct(q.shape, q.dtype),
+        out_specs=[big] + specs,
+        out_shape=[jax.ShapeDtypeStruct(q.shape, q.dtype)] + shapes,
         cost_estimate=pl.CostEstimate(flops=20 * q.size, bytes_accessed=8 * q.size + 12 * u.size, transcendentals=0),
-    )(q, hn, hs, he, hw, u, v, k)
+    )(q, *halos, u, v, k)
 
 
 def columns_of(edge):
@@ -60,19 +104,14 @@
     return jnp.swapaxes(edge.reshape(feats // FB, FB, rows), 1, 2)
 
 
-def step(x, u, v, k):
-    feats, rows, cols = x.shape
+def exchange(top, bottom, ends, feats, rows):
     lat_forward, lat_backward = neighbours("lat", False)
     lon_forward, lon_backward = neighbours("lon", True)
-    hn = lax.ppermute(x[:, :1, :], "lat", lat_backward)
-    hs = lax.ppermute(x[:, rows - 1:, :], "lat", lat_forward)
-    lane = lax.broadcasted_iota(jnp.int32, (cols, 2), 0)
-    which = lax.broadcasted_iota(jnp.int32, (cols, 2), 1)
-    pick = (lane == which * (cols - 1)).astype(jnp.float32)
-    ends = jnp.dot(x.reshape(feats * rows, cols), pick, precision=lax.Precision.HIGHEST)
-    he = lax.ppermute(columns_of(ends[:, 0].reshape(feats, rows)), "lon", lon_backward)
-    hw = lax.ppermute(columns_of(ends[:, 1].reshape(feats, rows)), "lon", lon_forward)
-    return sweep(x, hn, hs, he, hw, u, v, k)
+    hn = lax.ppermute(top, "lat", lat_backward)
+    hs = lax.ppermute(bottom, "lat", lat_forward)
+    he = lax.ppermute(columns_of(ends[0].reshape(feats, rows)), "lon", lon_backward)
+    hw = lax.ppermute(columns_of(ends[1].reshape(feats, rows)), "lon", lon_forward)
+    return hn, hs, he, hw
 
 
 def positions(targets_all, experts):
@@ -294,8 +333,10 @@
     num_vars, levels, lat_cells, lon_cells = column_state.shape
     features = num_vars * levels
     current = column_state.reshape(features, lat_cells, lon_cells)
+    sides = edges(current)
     for sweep_index in range(2):
-        current = step(current, wind_speed[0], wind_speed[1], diffusivity)
+        halos = exchange(*sides, features, lat_cells)
+        current, *sides = sweep(current, halos, wind_speed[0], wind_speed[1], diffusivity)
     column_count = lat_cells * lon_cells
     experts = lax.axis_size("lon")
     capacity = 2 * column_count // experts

time: 166 us -> 166 us (level)
  Pallas kernels: 57.8 us -> 63.8 us
  matrix products: 5.64 us -> 0.28 us
    dot_general x2 -> x0, matrix products: 5.36 us -> none  [step(): jnp.dot(x.reshape(feats * rows, cols), pick, precision=lax.Precision.HIGH...]
    pallas_call x0 -> x1, Pallas kernels: none -> 4.46 us  [edges(): pl.pallas_call(edges_kernel, grid=(feats // FB,), in_specs=[pl.BlockSpec(...]
  transfers between devices with their start and end apart: 9 -> 9, of which waited for: 2 -> 2; matrix products, arithmetic and copies ran while one was open for 5% -> 4% of each run, Pallas kernels for 0% -> 0%
where the time goes in v13:
time: 166 us; the launch traced here: 165 us
  Pallas kernels  63.8 us (38%)
  blocking collectives  32.3 us (19%)
  starting transfers between devices  28.9 us (17%)
  waiting for transfers between devices  25.1 us (15%)
  local copies, waits for them, and re-layouts  10.4 us (6%)
  other arithmetic  3.64 us (2%)
    all_to_all x1, blocking collectives, local(): lax.all_to_all(result.reshape(features, experts, width), 'lon', split_axi...  32.3 us
    pallas_call x1, Pallas kernels, network(): pl.pallas_call(network_kernel, grid_spec=pltpu.PrefetchScalarGridSpec(num...  25.9 us
    all_to_all x1, waiting for transfers between devices, local(): lax.all_to_all(part, 'lon', split_axis=1, concat_axis=1, tiled=True)  24.1 us
    pallas_call x2, Pallas kernels, sweep(): pl.pallas_call(sweep_kernel, grid=(nb,), in_specs=[big, edge_row, edge_ro...  13.5 us
    pallas_call x1, Pallas kernels, combine(): pl.pallas_call(combine_kernel, grid_spec=pltpu.PrefetchScalarGridSpec(num...  10.7 us
    all_to_all x1, starting transfers between devices, local(): lax.all_to_all(part, 'lon', split_axis=1, concat_axis=1, tiled=True)  10.3 us
    pallas_call x1, Pallas kernels, pack(): pl.pallas_call(pack_kernel, grid_spec=pltpu.PrefetchScalarGridSpec(num_sc...  9.29 us
    ppermute x2, starting transfers between devices, exchange(): hs = lax.ppermute(bottom, 'lat', lat_forward)  8.68 us
  transfers between devices with their start and end apart: 9, of which 2 were waited for; matrix products, arithmetic and copies ran while one was open for 4% of the time, Pallas kernels for 0%

profile of v13, /device:TPU:1, one launch (start us, length us, event | category | flops | bytes accessed | tf_op | source)
XLA Modules:
  0.0 165.3 jit_solution(5850094777362917491)
XLA Ops:
  0.0 4.5 %shard_map.73 = (f32[128,1,128]{2,1,0:T(1,128)}, f32[128,1,128]{2,1,0:T(1,128)}, f32[2,4096]{1,0:T(2,128)}) custom-call(f32[128,32,128]{2,1,0:T(8,128)} %bitcast.51), custom_call_target="tpu_custom_call" | custom-call | tf_op jit(solution)/shard_map/pallas_call | solution.py:73
  4.5 0.9 slice_reduce_fusion.2
  5.6 1.5 collective-permute-start.2
  7.2 1.4 collective-permute-start.3
  8.6 1.3 collective-permute-start
  9.9 4.2 %collective-permute-start.1 = (f32[128,1,128]{2,1,0:T(1,128)}, f32[128,1,128]{2,1,0:T(1,128)S(1)}, u32[]{:S(2)}, u32[]{:S(2)}) collective-permute-start(f32[128,1,128]{2,1,0:T(1,128)} %get-tuple-element.14), channel_id=1, source_target_pairs={{0,32},{32,64},{64,96},{1,33},{33,65},{65,97},{2,34},{34,66},{66,9... | collective-permute-start | bytes 196616 | tf_op jit(solution)/shard_map/ppermute | solution.py:111
  14.0 1.1 slice_bitcast_fusion
  16.4 6.7 %shard_map.74 = (f32[128,32,128]{2,1,0:T(8,128)}, f32[128,1,128]{2,1,0:T(1,128)}, f32[128,1,128]{2,1,0:T(1,128)}, f32[2,4096]{1,0:T(2,128)}) custom-call(f32[128,32,128]{2,1,0:T(8,128)} %bitcast.52, f32[128,1,128]{2,1,0:T(1,128)} %copy-done.7, f32[128,1,128]{2,1,0:T(1,128)} %copy-done.8, f32[4,32,32]{2,1,0:T(8,128)} %copy-done.4, f32[4,32,32]{2,1,0:T(8,128)} %copy-done.6, ...), custom_call_target="tpu_custom_call" | custom-call | flops 10485760 | bytes 5767168 | tf_op jit(solution)/shard_map/pallas_call | solution.py:92
  23.1 0.9 slice_reduce_fusion
  24.2 4.4 %collective-permute-start.6 = (f32[4,32,32]{2,1,0:T(8,128)S(1)}, f32[4,32,32]{2,1,0:T(8,128)S(1)}, u32[]{:S(2)}, u32[]{:S(2)}) collective-permute-start(f32[4,32,32]{2,1,0:T(8,128)S(1)} %bitcast.62), channel_id=1, source_target_pairs={{1,0},{2,1},{3,2},{4,3},{5,4},{6,5},{7,6},{8,7},{9,8},{10,9},{11,1... | collective-permute-start | bytes 49160 | tf_op jit(solution)/shard_map/ppermute | solution.py:112
  28.9 1.3 collective-permute-start.4
  30.2 4.5 %collective-permute-start.5 = (f32[128,1,128]{2,1,0:T(1,128)}, f32[128,1,128]{2,1,0:T(1,128)S(1)}, u32[]{:S(2)}, u32[]{:S(2)}) collective-permute-start(f32[128,1,128]{2,1,0:T(1,128)} %get-tuple-element.18), channel_id=1, source_target_pairs={{0,32},{32,64},{64,96},{1,33},{33,65},{65,97},{2,34},{34,66},{66,9... | collective-permute-start | bytes 196616 | tf_op jit(solution)/shard_map/ppermute | solution.py:111
  35.3 1.0 collective-permute-done.5.hs_ref
  36.9 6.7 %shard_map.75 = (f32[128,32,128]{2,1,0:T(8,128)}, f32[128,1,128]{2,1,0:T(1,128)}, f32[128,1,128]{2,1,0:T(1,128)}, f32[2,4096]{1,0:T(2,128)}) custom-call(f32[128,32,128]{2,1,0:T(8,128)} %get-tuple-element.16.q_ref, f32[128,1,128]{2,1,0:T(1,128)} %copy-done.10, f32[128,1,128]{2,1,0:T(1,128)} %copy-done.11, f32[4,32,32]{2,1,0:T(8,128)} %copy-done.5, ...), custom_call_target="tpu_custom_call" | custom-call | flops 10485760 | bytes 5767168 | tf_op jit(solution)/shard_map/pallas_call | solution.py:92
  43.7 9.3 %shard_map.76 = bf16[8192,128]{1,0:T(8,128)(2,1)} custom-call(s32[4096]{0:T(1024)} %bitcast_add_fusion.t_ref, f32[128,32,128]{2,1,0:T(8,128)} %get-tuple-element.20.cur_ref), custom_call_target="tpu_custom_call" | custom-call | tf_op jit(solution)/shard_map/pallas_call | solution.py:280
  53.0 10.3 %all-to-all-start = ((bf16[128,32,256]{0,2,1:T(8,128)(2,1)}), bf16[128,32,256]{0,2,1:T(8,128)(2,1)S(1)}, u32[]{:S(2)}, u32[]{:S(2)}) async-start(bf16[128,32,256]{0,2,1:T(8,128)(2,1)} %bitcast.54), calls=%async_computation | async-start | bytes 4194304 | tf_op jit(solution)/shard_map/all_to_all | solution.py:352
  63.3 2.7 %copy.32 = bf16[1,3,512,512]{2,3,1,0:T(8,128)(2,1)} copy(bf16[1,3,512,512]{3,2,1,0:T(8,128)(2,1)} %param.12) | data formatting | bytes 3145728 | tf_op args[5]
  66.0 0.8 copy.31
  67.5 24.1 %all-to-all-done = bf16[128,32,256]{0,2,1:T(8,128)(2,1)S(1)} async-done(((bf16[128,32,256]{0,2,1:T(8,128)(2,1)}), bf16[128,32,256]{0,2,1:T(8,128)(2,1)S(1)}, u32[]{:S(2)}, u32[]{:S(2)}) %all-to-all-start) | async-done | bytes 2097184 | tf_op jit(solution)/shard_map/all_to_all | solution.py:352
  91.6 1.2 compare_reduce_fusion
  95.1 1.3 scatter_custom_fusion.source_ref
  96.4 25.9 %shard_map.77 = bf16[8192,128]{1,0:T(8,128)(2,1)} custom-call(s32[1]{0:T(128)} %bitcast.17.active_ref, s32[64]{0:T(128)} %scatter_custom_fusion.source_ref, bf16[8192,128]{1,0:T(8,128)(2,1)} %bitcast.53, bf16[128,512]{1,0:T(8,128)(2,1)} %bitcast.57, bf16[3,512,512]{2,1,0:T(8,128)(2,1)} %bitcast.56, bf16[512,128]{1,0:T(8,128)(2,1)} %bitcast.58), custom_call_target="tpu_custom_call" | custom-call | flops 15032385536 | bytes 6029312 | tf_op jit(solution)/shard_map/pallas_call | solution.py:230
  122.3 32.3 %all_to_all.10 = bf16[128,32,256]{0,2,1:T(8,128)(2,1)} all-to-all(bf16[128,32,256]{0,2,1:T(8,128)(2,1)} %bitcast.55), channel_id=1, replica_groups=mesh['lat'=4,'lon'=32] {'lon'}, dimensions={1} | all-to-all | bytes 4194304 | tf_op jit(solution)/shard_map/all_to_all | solution.py:356
  154.6 10.7 %shard_map.78 = f32[128,32,128]{2,1,0:T(8,128)} custom-call(s32[4096]{0:T(1024)} %bitcast_add_fusion.t_ref, bf16[8192,128]{1,0:T(8,128)(2,1)} %bitcast.50, f32[128,32,128]{2,1,0:T(8,128)} %get-tuple-element.20.cur_ref), custom_call_target="tpu_custom_call" | custom-call | tf_op jit(solution)/shard_map/pallas_call | solution.py:311
  (56 shorter events, 5.6 us)
Async XLA Ops:
  0.0 14.0 %copy-start.1 = (f32[2,32,32,128]{3,2,1,0:T(8,128)S(1)}, f32[2,32,32,128]{3,2,1,0:T(8,128)}, u32[]{:S(2)}) copy-start(f32[2,32,32,128]{3,2,1,0:T(8,128)} %param.8) | copy-start | bytes 3145732
  0.0 15.1 %copy-start.12 = (s32[1,4096,1]{1,2,0:T(1,128)S(1)}, s32[1,4096,1]{1,2,0:T(1,128)}, u32[]{:S(2)}) copy-start(s32[1,4096,1]{1,2,0:T(1,128)} %param.10) | copy-start | bytes 49156
  5.6 10.1 %collective-permute-start.2 = (f32[4,32,32]{2,1,0:T(8,128)S(1)}, f32[4,32,32]{2,1,0:T(8,128)S(1)}, u32[]{:S(2)}, u32[]{:S(2)}) collective-permute-start(f32[4,32,32]{2,1,0:T(8,128)S(1)} %bitcast.60), channel_id=1, source_target_pairs={{1,0},{2,1},{3,2},{4,3},{5,4},{6,5},{7,6},{8,7},{9,8},{10,9},{11,1... | collective-permute-start | bytes 49160 | tf_op jit(solution)/shard_map/ppermute | solution.py:112
  7.2 8.5 %collective-permute-start.3 = (f32[4,32,32]{2,1,0:T(8,128)S(1)}, f32[4,32,32]{2,1,0:T(8,128)S(1)}, u32[]{:S(2)}, u32[]{:S(2)}) collective-permute-start(f32[4,32,32]{2,1,0:T(8,128)S(1)} %bitcast.61), channel_id=1, source_target_pairs={{0,1},{1,2},{2,3},{3,4},{4,5},{5,6},{6,7},{7,8},{8,9},{9,10},{10,1... | collective-permute-start | bytes 49160 | tf_op jit(solution)/shard_map/ppermute | solution.py:113
  8.6 7.2 %collective-permute-start = (f32[128,1,128]{2,1,0:T(1,128)}, f32[128,1,128]{2,1,0:T(1,128)S(1)}, u32[]{:S(2)}, u32[]{:S(2)}) collective-permute-start(f32[128,1,128]{2,1,0:T(1,128)} %get-tuple-element.13), channel_id=1, source_target_pairs={{32,0},{64,32},{96,64},{33,1},{65,33},{97,65},{34,2},{66,34},{98,6... | collective-permute-start | bytes 196616 | tf_op jit(solution)/shard_map/ppermute | solution.py:110
  9.9 5.9 %collective-permute-start.1 = (f32[128,1,128]{2,1,0:T(1,128)}, f32[128,1,128]{2,1,0:T(1,128)S(1)}, u32[]{:S(2)}, u32[]{:S(2)}) collective-permute-start(f32[128,1,128]{2,1,0:T(1,128)} %get-tuple-element.14), channel_id=1, source_target_pairs={{0,32},{32,64},{64,96},{1,33},{33,65},{65,97},{2,34},{34,66},{66,9... | collective-permute-start | bytes 196616 | tf_op jit(solution)/shard_map/ppermute | solution.py:111
  15.7 0.6 copy-start.4
  15.7 0.6 copy-start.6
  15.7 0.6 copy-start.7
  15.8 0.6 copy-start.8
  24.2 11.1 %collective-permute-start.6 = (f32[4,32,32]{2,1,0:T(8,128)S(1)}, f32[4,32,32]{2,1,0:T(8,128)S(1)}, u32[]{:S(2)}, u32[]{:S(2)}) collective-permute-start(f32[4,32,32]{2,1,0:T(8,128)S(1)} %bitcast.62), channel_id=1, source_target_pairs={{1,0},{2,1},{3,2},{4,3},{5,4},{6,5},{7,6},{8,7},{9,8},{10,9},{11,1... | collective-permute-start | bytes 49160 | tf_op jit(solution)/shard_map/ppermute | solution.py:112
  28.8 6.5 %collective-permute-start.7 = (f32[4,32,32]{2,1,0:T(8,128)S(1)}, f32[4,32,32]{2,1,0:T(8,128)S(1)}, u32[]{:S(2)}, u32[]{:S(2)}) collective-permute-start(f32[4,32,32]{2,1,0:T(8,128)S(1)} %bitcast.63), channel_id=1, source_target_pairs={{0,1},{1,2},{2,3},{3,4},{4,5},{5,6},{6,7},{7,8},{8,9},{9,10},{10,1... | collective-permute-start | bytes 49160 | tf_op jit(solution)/shard_map/ppermute | solution.py:113
  28.9 6.4 %collective-permute-start.4 = (f32[128,1,128]{2,1,0:T(1,128)}, f32[128,1,128]{2,1,0:T(1,128)S(1)}, u32[]{:S(2)}, u32[]{:S(2)}) collective-permute-start(f32[128,1,128]{2,1,0:T(1,128)} %get-tuple-element.17), channel_id=1, source_target_pairs={{32,0},{64,32},{96,64},{33,1},{65,33},{97,65},{34,2},{66,34},{98,6... | collective-permute-start | bytes 196616 | tf_op jit(solution)/shard_map/ppermute | solution.py:110
  30.2 6.1 %collective-permute-start.5 = (f32[128,1,128]{2,1,0:T(1,128)}, f32[128,1,128]{2,1,0:T(1,128)S(1)}, u32[]{:S(2)}, u32[]{:S(2)}) collective-permute-start(f32[128,1,128]{2,1,0:T(1,128)} %get-tuple-element.18), channel_id=1, source_target_pairs={{0,32},{32,64},{64,96},{1,33},{33,65},{65,97},{2,34},{34,66},{66,9... | collective-permute-start | bytes 196616 | tf_op jit(solution)/shard_map/ppermute | solution.py:111
  35.3 1.0 copy-start.5
  35.3 1.0 copy-start.9
  35.3 1.0 copy-start.10
  36.3 0.6 copy-start.11
  53.0 38.6 %all-to-all-start = ((bf16[128,32,256]{0,2,1:T(8,128)(2,1)}), bf16[128,32,256]{0,2,1:T(8,128)(2,1)S(1)}, u32[]{:S(2)}, u32[]{:S(2)}) async-start(bf16[128,32,256]{0,2,1:T(8,128)(2,1)} %bitcast.54), calls=%async_computation | async-start | bytes 4194304 | tf_op jit(solution)/shard_map/all_to_all | solution.py:352
  63.3 2.7 %copy-start.2 = (bf16[1,512,128]{2,1,0:T(8,128)(2,1)S(1)}, bf16[1,512,128]{2,1,0:T(8,128)(2,1)}, u32[]{:S(2)}) copy-start(bf16[1,512,128]{2,1,0:T(8,128)(2,1)} %param.11) | copy-start | bytes 393220
  63.3 3.4 %copy-start.3 = (bf16[1,128,512]{2,1,0:T(8,128)(2,1)S(1)}, bf16[1,128,512]{2,1,0:T(8,128)(2,1)}, u32[]{:S(2)}) copy-start(bf16[1,128,512]{2,1,0:T(8,128)(2,1)} %param.13) | copy-start | bytes 393220
  91.6 4.8 %copy-start = (bf16[128,32,256]{0,2,1:T(8,128)(2,1)}, bf16[128,32,256]{0,2,1:T(8,128)(2,1)S(1)}, u32[]{:S(2)}) copy-start(bf16[128,32,256]{0,2,1:T(8,128)(2,1)S(1)} %all-to-all-done) | copy-start | bytes 6291460

commit v14 on v12

--- a/solution.py
+++ b/solution.py
@@ -109,12 +109,35 @@
     return jnp.dot(hidden, w_last, preferred_element_type=jnp.float32).astype(jnp.bfloat16)
 
 
-def network_kernel(active_ref, source_ref, x_hbm, first_ref, middle_ref, last_ref, o_hbm, buf, res, lsem, ssem):
+def network_kernel(nonzero_ref, x_hbm, first_ref, middle_ref, last_ref, o_hbm, buf, res, lsem, ssem, source_ref, used_ref):
     block = pl.program_id(0)
     blocks = pl.num_programs(0)
-    active = active_ref[0]
+    per = ROWS // HALF
+    groups = source_ref.shape[0]
+
+    @pl.when(block == 0)
+    def _():
+        def nonempty(g, used):
+            @pl.when(nonzero_ref[g] > 0)
+            def _():
+                source_ref[used] = g
+
+            return used + nonzero_ref[g]
+
+        used = lax.fori_loop(0, groups, nonempty, 0)
+        used_ref[0] = used
+
+        def empty(g, at):
+            @pl.when(nonzero_ref[g] == 0)
+            def _():
+                source_ref[at] = g
+
+            return at + 1 - nonzero_ref[g]
+
+        lax.fori_loop(0, groups, empty, used)
+
+    active = (used_ref[0] * HALF + ROWS - 1) // ROWS
     slot = block % 2
-    per = ROWS // HALF
 
     def loads(index, into):
         return [
@@ -181,23 +204,18 @@
     last = output_weight[0].T
     grouped = rows_in.reshape(groups, HALF, feats)
     nonzero = jnp.any(grouped != 0, axis=(1, 2)).astype(jnp.int32)
-    used = jnp.sum(nonzero)
-    ahead = jnp.cumsum(nonzero) - nonzero
-    place = jnp.where(nonzero > 0, ahead, used + jnp.arange(groups, dtype=jnp.int32) - ahead)
-    source = jnp.zeros((groups,), jnp.int32).at[place].set(jnp.arange(groups, dtype=jnp.int32))
-    active = ((used * HALF + ROWS - 1) // ROWS).reshape(1)
     mats = 2 * (hid * feats * 2 + middle_weight.shape[1] * hid * hid)
     per = ROWS // HALF
     return pl.pallas_call(
         network_kernel,
         grid_spec=pltpu.PrefetchScalarGridSpec(
-            num_scalar_prefetch=2,
+            num_scalar_prefetch=1,
             grid=(count // ROWS,),
             in_specs=[
                 pl.BlockSpec(memory_space=pl.ANY),
-                pl.BlockSpec(first.shape, lambda i, a, s: (0, 0)),
-                pl.BlockSpec(middle.shape, lambda i, a, s: (0, 0, 0)),
-                pl.BlockSpec(last.shape, lambda i, a, s: (0, 0)),
+                pl.BlockSpec(first.shape, lambda i, n: (0, 0)),
+                pl.BlockSpec(middle.shape, lambda i, n: (0, 0, 0)),
+                pl.BlockSpec(last.shape, lambda i, n: (0, 0)),
             ],
             out_specs=pl.BlockSpec(memory_space=pl.ANY),
             scratch_shapes=[
@@ -205,6 +223,8 @@
                 pltpu.VMEM((2, ROWS, feats), jnp.bfloat16),
                 pltpu.SemaphoreType.DMA((2, per)),
                 pltpu.SemaphoreType.DMA((2, per)),
+                pltpu.SMEM((groups,), jnp.int32),
+                pltpu.SMEM((1,), jnp.int32),
             ],
         ),
         out_shape=jax.ShapeDtypeStruct((count, feats), jnp.bfloat16),
@@ -213,7 +233,7 @@
             bytes_accessed=4 * count * feats + 2 * (mats // 2),
             transcendentals=(1 + middle_weight.shape[1]) * hid * count,
         ),
-    )(active, source, rows_in, first, middle, last)
+    )(nonzero, rows_in, first, middle, last)
 
 
 UNROLL = 32

time: 166 us -> 163 us (0.982)
  Pallas kernels: 57.8 us -> 55.2 us
  blocking collectives: 32.1 us -> 34.6 us
    pallas_call x1, Pallas kernels: 25.8 us -> 23.3 us  [network(): pl.pallas_call(network_kernel, grid_spec=pltpu.PrefetchScalarGridSpec(num...]
    all_to_all x1, blocking collectives: 32.1 us -> 34.6 us  [local(): lax.all_to_all(result.reshape(features, experts, width), 'lon', split_axi...]
where the time goes in v14:
time: 163 us; the launch traced here: 162 us
  Pallas kernels  55.2 us (34%)
  blocking collectives  34.6 us (21%)
  starting transfers between devices  28.9 us (18%)
  waiting for transfers between devices  24.7 us (15%)
  local copies, waits for them, and re-layouts  9.94 us (6%)
  matrix products  5.64 us (3%)
  other arithmetic  2.69 us (2%)
    all_to_all x1, blocking collectives, local(): lax.all_to_all(result.reshape(features, experts, width), 'lon', split_axi...  34.6 us
    all_to_all x1, waiting for transfers between devices, local(): lax.all_to_all(part, 'lon', split_axis=1, concat_axis=1, tiled=True)  24.1 us
    pallas_call x1, Pallas kernels, network(): pl.pallas_call(network_kernel, grid_spec=pltpu.PrefetchScalarGridSpec(num...  23.3 us
    pallas_call x2, Pallas kernels, sweep(): pl.pallas_call(sweep_kernel, grid=(nb,), in_specs=[big, edge_row, edge_ro...  11.9 us
    pallas_call x1, Pallas kernels, combine(): pl.pallas_call(combine_kernel, grid_spec=pltpu.PrefetchScalarGridSpec(num...  10.7 us
    all_to_all x1, starting transfers between devices, local(): lax.all_to_all(part, 'lon', split_axis=1, concat_axis=1, tiled=True)  10.6 us
    pallas_call x1, Pallas kernels, pack(): pl.pallas_call(pack_kernel, grid_spec=pltpu.PrefetchScalarGridSpec(num_sc...  9.29 us
    ppermute x2, starting transfers between devices, step(): hs = lax.ppermute(x[:, rows - 1:, :], 'lat', lat_forward)  8.79 us
  transfers between devices with their start and end apart: 9, of which 2 were waited for; matrix products, arithmetic and copies ran while one was open for 5% of the time, Pallas kernels for 0%

profile of v14, /device:TPU:1, one launch (start us, length us, event | category | flops | bytes accessed | tf_op | source)
XLA Modules:
  0.0 162.1 jit_solution(18264459892847321319)
XLA Ops:
  0.0 2.7 %convolution_bitcast_fusion = f32[4096,2]{0,1:T(2,128)S(1)} fusion(f32[4096,128]{1,0:T(8,128)} %bitcast.54, s32[2]{0:T(128)S(1)} %iota_multiply_fusion), kind=kOutput, calls=%fused_computation | convolution fusion | flops 12583424 | bytes 2129928 | tf_op jit(solution)/shard_map/dot_general | solution.py:72
  3.0 1.5 collective-permute-start.2
  4.7 1.4 collective-permute-start.3
  6.0 1.3 fusion.13
  7.3 1.3 collective-permute-start
  8.6 4.2 %collective-permute-start.1 = (f32[128,1,128]{2,1,0:T(1,128)S(1)}, f32[128,1,128]{2,1,0:T(1,128)S(1)}, u32[]{:S(2)}, u32[]{:S(2)}) collective-permute-start(f32[128,1,128]{2,1,0:T(1,128)S(1)} %get-tuple-element.11), channel_id=1, source_target_pairs={{0,32},{32,64},{64,96},{1,33},{33,65},{65,97},{2,34},{34,66},{66,9... | collective-permute-start | bytes 196616 | tf_op jit(solution)/shard_map/ppermute | solution.py:68
  12.8 1.1 slice_bitcast_fusion
  15.2 6.0 %shard_map.73.q_ref = f32[128,32,128]{2,1,0:T(8,128)} custom-call(f32[128,32,128]{2,1,0:T(8,128)} %bitcast.56, f32[128,1,128]{2,1,0:T(1,128)} %copy-done.7, f32[128,1,128]{2,1,0:T(1,128)} %copy-done.8, f32[4,32,32]{2,1,0:T(8,128)} %copy-done.4, f32[4,32,32]{2,1,0:T(8,128)} %copy-done.5, f32[32,32,128]{2,1,0:T(8,128)} %get-tuple-element.14.u_ref, ...), custom_call_target="tpu_custom_call" | custom-call | flops 10485760 | bytes 5767168 | tf_op jit(solution)/shard_map/pallas_call | solution.py:48
  21.1 1.3 fusion.12
  22.4 2.6 %fusion.5 = f32[4096,2]{0,1:T(2,128)S(1)} fusion(f32[4096,128]{1,0:T(8,128)} %bitcast.53, s32[2]{0:T(128)S(1)} %iota_multiply_fusion), kind=kOutput, calls=%fused_computation.13 | convolution fusion | flops 12583168 | bytes 2129928 | tf_op jit(solution)/shard_map/dot_general | solution.py:72
  25.3 4.1 %collective-permute-start.6 = (f32[4,32,32]{2,1,0:T(8,128)S(1)}, f32[4,32,32]{2,1,0:T(8,128)S(1)}, u32[]{:S(2)}, u32[]{:S(2)}) collective-permute-start(f32[4,32,32]{2,1,0:T(8,128)S(1)} %bitcast.67), channel_id=1, source_target_pairs={{1,0},{2,1},{3,2},{4,3},{5,4},{6,5},{7,6},{8,7},{9,8},{10,9},{11,1... | collective-permute-start | bytes 49160 | tf_op jit(solution)/shard_map/ppermute | solution.py:73
  29.6 1.3 collective-permute-start.4
  30.9 4.6 %collective-permute-start.5 = (f32[128,1,128]{2,1,0:T(1,128)S(1)}, f32[128,1,128]{2,1,0:T(1,128)S(1)}, u32[]{:S(2)}, u32[]{:S(2)}) collective-permute-start(f32[128,1,128]{2,1,0:T(1,128)S(1)} %get-tuple-element.9), channel_id=1, source_target_pairs={{0,32},{32,64},{64,96},{1,33},{33,65},{65,97},{2,34},{34,66},{66,9... | collective-permute-start | bytes 196616 | tf_op jit(solution)/shard_map/ppermute | solution.py:68
  37.5 6.0 %shard_map.74.cur_ref = f32[128,32,128]{2,1,0:T(8,128)} custom-call(f32[128,32,128]{2,1,0:T(8,128)} %shard_map.73.q_ref, f32[128,1,128]{2,1,0:T(1,128)} %copy-done.10, f32[128,1,128]{2,1,0:T(1,128)} %copy-done.11, f32[4,32,32]{2,1,0:T(8,128)} %copy-done.6, f32[4,32,32]{2,1,0:T(8,128)} %copy-done.9, f32[32,32,128]{2,1,0:T(8,128)} %get-tuple-element.14.u_ref, ...), custom_call_target="tpu_custom_call" | custom-call | flops 10485760 | bytes 5767168 | tf_op jit(solution)/shard_map/pallas_call | solution.py:48
  43.4 9.3 %shard_map.75 = bf16[8192,128]{1,0:T(8,128)(2,1)} custom-call(s32[4096]{0:T(1024)} %bitcast_add_fusion.t_ref, f32[128,32,128]{2,1,0:T(8,128)} %shard_map.74.cur_ref), custom_call_target="tpu_custom_call" | custom-call | tf_op jit(solution)/shard_map/pallas_call | solution.py:261
  52.7 10.6 %all-to-all-start = ((bf16[128,32,256]{0,2,1:T(8,128)(2,1)}), bf16[128,32,256]{0,2,1:T(8,128)(2,1)S(1)}, u32[]{:S(2)}, u32[]{:S(2)}) async-start(bf16[128,32,256]{0,2,1:T(8,128)(2,1)} %bitcast.59), calls=%async_computation | async-start | bytes 4194304 | tf_op jit(solution)/shard_map/all_to_all | solution.py:331
  63.3 2.7 %copy.23 = bf16[1,3,512,512]{2,3,1,0:T(8,128)(2,1)} copy(bf16[1,3,512,512]{3,2,1,0:T(8,128)(2,1)} %param.12) | data formatting | bytes 3145728 | tf_op args[5]
  66.0 0.8 copy.22
  66.8 0.8 copy.24
  67.5 24.1 %all-to-all-done = bf16[128,32,256]{0,2,1:T(8,128)(2,1)S(1)} async-done(((bf16[128,32,256]{0,2,1:T(8,128)(2,1)}), bf16[128,32,256]{0,2,1:T(8,128)(2,1)S(1)}, u32[]{:S(2)}, u32[]{:S(2)}) %all-to-all-start) | async-done | bytes 2097184 | tf_op jit(solution)/shard_map/all_to_all | solution.py:331
  91.6 1.2 compare_reduce_fusion
  93.4 23.3 %shard_map.76 = bf16[8192,128]{1,0:T(8,128)(2,1)} custom-call(s32[64]{0:T(128)} %convert_element_type.24.nonzero_ref, bf16[8192,128]{1,0:T(8,128)(2,1)} %bitcast.58, bf16[128,512]{1,0:T(8,128)(2,1)} %bitcast.62, bf16[3,512,512]{2,1,0:T(8,128)(2,1)} %bitcast.61, bf16[512,128]{1,0:T(8,128)(2,1)} %bitcast.63), custom_call_target="tpu_custom_call" | custom-call | flops 15032385536 | bytes 6029312 | tf_op jit(solution)/shard_map/pallas_call | solution.py:209
  116.7 34.6 %all_to_all.10 = bf16[128,32,256]{0,2,1:T(8,128)(2,1)} all-to-all(bf16[128,32,256]{0,2,1:T(8,128)(2,1)} %bitcast.60), channel_id=1, replica_groups=mesh['lat'=4,'lon'=32] {'lon'}, dimensions={1} | all-to-all | bytes 4194304 | tf_op jit(solution)/shard_map/all_to_all | solution.py:335
  151.4 10.7 %shard_map.77 = f32[128,32,128]{2,1,0:T(8,128)} custom-call(s32[4096]{0:T(1024)} %bitcast_add_fusion.t_ref, bf16[8192,128]{1,0:T(8,128)(2,1)} %bitcast.57, f32[128,32,128]{2,1,0:T(8,128)} %shard_map.74.cur_ref), custom_call_target="tpu_custom_call" | custom-call | tf_op jit(solution)/shard_map/pallas_call | solution.py:292
  (54 shorter events, 4.7 us)
Async XLA Ops:
  0.0 12.8 %copy-start.1 = (f32[2,32,32,128]{3,2,1,0:T(8,128)S(1)}, f32[2,32,32,128]{3,2,1,0:T(8,128)}, u32[]{:S(2)}) copy-start(f32[2,32,32,128]{3,2,1,0:T(8,128)} %param.8) | copy-start | bytes 3145732
  0.0 13.9 %copy-start.12 = (s32[1,4096,1]{1,2,0:T(1,128)S(1)}, s32[1,4096,1]{1,2,0:T(1,128)}, u32[]{:S(2)}) copy-start(s32[1,4096,1]{1,2,0:T(1,128)} %param.10) | copy-start | bytes 49156
  3.0 11.4 %collective-permute-start.2 = (f32[4,32,32]{2,1,0:T(8,128)S(1)}, f32[4,32,32]{2,1,0:T(8,128)S(1)}, u32[]{:S(2)}, u32[]{:S(2)}) collective-permute-start(f32[4,32,32]{2,1,0:T(8,128)S(1)} %bitcast.65), channel_id=1, source_target_pairs={{1,0},{2,1},{3,2},{4,3},{5,4},{6,5},{7,6},{8,7},{9,8},{10,9},{11,1... | collective-permute-start | bytes 49160 | tf_op jit(solution)/shard_map/ppermute | solution.py:73
  4.7 9.8 %collective-permute-start.3 = (f32[4,32,32]{2,1,0:T(8,128)S(1)}, f32[4,32,32]{2,1,0:T(8,128)S(1)}, u32[]{:S(2)}, u32[]{:S(2)}) collective-permute-start(f32[4,32,32]{2,1,0:T(8,128)S(1)} %bitcast.66), channel_id=1, source_target_pairs={{0,1},{1,2},{2,3},{3,4},{4,5},{5,6},{6,7},{7,8},{8,9},{9,10},{10,1... | collective-permute-start | bytes 49160 | tf_op jit(solution)/shard_map/ppermute | solution.py:74
  7.3 7.2 %collective-permute-start = (f32[128,1,128]{2,1,0:T(1,128)S(1)}, f32[128,1,128]{2,1,0:T(1,128)S(1)}, u32[]{:S(2)}, u32[]{:S(2)}) collective-permute-start(f32[128,1,128]{2,1,0:T(1,128)S(1)} %get-tuple-element.12), channel_id=1, source_target_pairs={{32,0},{64,32},{96,64},{33,1},{65,33},{97,65},{34,2},{66,34},{98,6... | collective-permute-start | bytes 196616 | tf_op jit(solution)/shard_map/ppermute | solution.py:67
  8.6 5.9 %collective-permute-start.1 = (f32[128,1,128]{2,1,0:T(1,128)S(1)}, f32[128,1,128]{2,1,0:T(1,128)S(1)}, u32[]{:S(2)}, u32[]{:S(2)}) collective-permute-start(f32[128,1,128]{2,1,0:T(1,128)S(1)} %get-tuple-element.11), channel_id=1, source_target_pairs={{0,32},{32,64},{64,96},{1,33},{33,65},{65,97},{2,34},{34,66},{66,9... | collective-permute-start | bytes 196616 | tf_op jit(solution)/shard_map/ppermute | solution.py:68
  14.5 0.6 copy-start.4
  14.5 0.6 copy-start.5
  14.5 0.6 copy-start.7
  14.5 0.6 copy-start.8
  25.3 10.8 %collective-permute-start.6 = (f32[4,32,32]{2,1,0:T(8,128)S(1)}, f32[4,32,32]{2,1,0:T(8,128)S(1)}, u32[]{:S(2)}, u32[]{:S(2)}) collective-permute-start(f32[4,32,32]{2,1,0:T(8,128)S(1)} %bitcast.67), channel_id=1, source_target_pairs={{1,0},{2,1},{3,2},{4,3},{5,4},{6,5},{7,6},{8,7},{9,8},{10,9},{11,1... | collective-permute-start | bytes 49160 | tf_op jit(solution)/shard_map/ppermute | solution.py:73
  29.5 6.6 %collective-permute-start.7 = (f32[4,32,32]{2,1,0:T(8,128)S(1)}, f32[4,32,32]{2,1,0:T(8,128)S(1)}, u32[]{:S(2)}, u32[]{:S(2)}) collective-permute-start(f32[4,32,32]{2,1,0:T(8,128)S(1)} %bitcast.68), channel_id=1, source_target_pairs={{0,1},{1,2},{2,3},{3,4},{4,5},{5,6},{6,7},{7,8},{8,9},{9,10},{10,1... | collective-permute-start | bytes 49160 | tf_op jit(solution)/shard_map/ppermute | solution.py:74
  29.6 6.6 %collective-permute-start.4 = (f32[128,1,128]{2,1,0:T(1,128)S(1)}, f32[128,1,128]{2,1,0:T(1,128)S(1)}, u32[]{:S(2)}, u32[]{:S(2)}) collective-permute-start(f32[128,1,128]{2,1,0:T(1,128)S(1)} %get-tuple-element.10), channel_id=1, source_target_pairs={{32,0},{64,32},{96,64},{33,1},{65,33},{97,65},{34,2},{66,34},{98,6... | collective-permute-start | bytes 196616 | tf_op jit(solution)/shard_map/ppermute | solution.py:67
  30.9 5.9 %collective-permute-start.5 = (f32[128,1,128]{2,1,0:T(1,128)S(1)}, f32[128,1,128]{2,1,0:T(1,128)S(1)}, u32[]{:S(2)}, u32[]{:S(2)}) collective-permute-start(f32[128,1,128]{2,1,0:T(1,128)S(1)} %get-tuple-element.9), channel_id=1, source_target_pairs={{0,32},{32,64},{64,96},{1,33},{33,65},{65,97},{2,34},{34,66},{66,9... | collective-permute-start | bytes 196616 | tf_op jit(solution)/shard_map/ppermute | solution.py:68
  36.2 0.7 copy-start.6
  36.2 0.7 copy-start.9
  36.2 0.7 copy-start.10
  36.9 0.6 copy-start.11
  52.7 38.9 %all-to-all-start = ((bf16[128,32,256]{0,2,1:T(8,128)(2,1)}), bf16[128,32,256]{0,2,1:T(8,128)(2,1)S(1)}, u32[]{:S(2)}, u32[]{:S(2)}) async-start(bf16[128,32,256]{0,2,1:T(8,128)(2,1)} %bitcast.59), calls=%async_computation | async-start | bytes 4194304 | tf_op jit(solution)/shard_map/all_to_all | solution.py:331
  63.3 2.7 %copy-start.2 = (bf16[1,512,128]{2,1,0:T(8,128)(2,1)S(1)}, bf16[1,512,128]{2,1,0:T(8,128)(2,1)}, u32[]{:S(2)}) copy-start(bf16[1,512,128]{2,1,0:T(8,128)(2,1)} %param.11) | copy-start | bytes 393220
  63.3 3.5 %copy-start.3 = (bf16[1,128,512]{2,1,0:T(8,128)(2,1)S(1)}, bf16[1,128,512]{2,1,0:T(8,128)(2,1)}, u32[]{:S(2)}) copy-start(bf16[1,128,512]{2,1,0:T(8,128)(2,1)} %param.13) | copy-start | bytes 393220
  91.6 1.8 %copy-start = (bf16[128,32,256]{0,2,1:T(8,128)(2,1)}, bf16[128,32,256]{0,2,1:T(8,128)(2,1)S(1)}, u32[]{:S(2)}) copy-start(bf16[128,32,256]{0,2,1:T(8,128)(2,1)S(1)} %all-to-all-done) | copy-start | bytes 6291460

commit v15 on v14

--- a/solution.py
+++ b/solution.py
@@ -17,7 +17,21 @@
 
 FB = 32
 
-def sweep_kernel(q_ref, hn_ref, hs_ref, he_ref, hw_ref, u_ref, v_ref, k_ref, o_ref):
+def keep_edges(block_ref, top_ref, bottom_ref, ends_ref):
+    feats, rows, cols = block_ref.shape
+    for f in range(feats):
+        top_ref[f] = block_ref[f, 0:1, :]
+        bottom_ref[f] = block_ref[f, rows - 1:rows, :]
+    lane = lax.broadcasted_iota(jnp.int32, (2, cols), 1)
+    which = lax.broadcasted_iota(jnp.int32, (2, cols), 0)
+    pick = (lane == which * (cols - 1)).astype(jnp.float32)
+    ends_ref[...] = lax.dot_general(
+        pick, block_ref[...].reshape(feats * rows, cols), (((1,), (1,)), ((), ())),
+        precision=lax.Precision.HIGHEST, preferred_element_type=jnp.float32,
+    )
+
+
+def sweep_kernel(q_ref, hn_ref, hs_ref, he_ref, hw_ref, u_ref, v_ref, k_ref, o_ref, *edge_refs):
     rows, cols = q_ref.shape[1], q_ref.shape[2]
     row = lax.broadcasted_iota(jnp.int32, (rows, cols), 0)
     lane = lax.broadcasted_iota(jnp.int32, (rows, cols), 1)
@@ -34,9 +48,11 @@
         k = k_ref[f]
         o_ref[f] = (q - 0.5 * u * (east - west) - 0.5 * v * (north - south)
                     + k * (east + west + north + south - 4.0 * q))
-
-
-def sweep(q, hn, hs, he, hw, u, v, k):
+    if edge_refs:
+        keep_edges(o_ref, *edge_refs)
+
+
+def sweep(q, halos, u, v, k, emit_edges):
     feats, rows, cols = q.shape
     levels = u.shape[0]
     nb = feats // FB
@@ -45,14 +61,22 @@
     field = pl.BlockSpec((FB, rows, cols), lambda i: (i % per, 0, 0))
     edge_row = pl.BlockSpec((FB, 1, cols), lambda i: (i, 0, 0))
     edge_col = pl.BlockSpec((1, rows, FB), lambda i: (i, 0, 0))
+    out_specs, out_shape = [big], [jax.ShapeDtypeStruct(q.shape, q.dtype)]
+    if emit_edges:
+        out_specs += [edge_row, edge_row, pl.BlockSpec((2, FB * rows), lambda i: (0, i))]
+        out_shape += [
+            jax.ShapeDtypeStruct((feats, 1, cols), jnp.float32),
+            jax.ShapeDtypeStruct((feats, 1, cols), jnp.float32),
+            jax.ShapeDtypeStruct((2, feats * rows), jnp.float32),
+        ]
     return pl.pallas_call(
         sweep_kernel,
         grid=(nb,),
         in_specs=[big, edge_row, edge_row, edge_col, edge_col, field, field, field],
-        out_specs=big,
-        out_shape=jax.ShapeDtypeStruct(q.shape, q.dtype),
+        out_specs=out_specs,
+        out_shape=out_shape,
         cost_estimate=pl.CostEstimate(flops=20 * q.size, bytes_accessed=8 * q.size + 12 * u.size, transcendentals=0),
-    )(q, hn, hs, he, hw, u, v, k)
+    )(q, *halos, u, v, k)
 
 
 def columns_of(edge):
@@ -60,19 +84,23 @@
     return jnp.swapaxes(edge.reshape(feats // FB, FB, rows), 1, 2)
 
 
-def step(x, u, v, k):
-    feats, rows, cols = x.shape
+def exchange(top, bottom, ends, feats, rows):
     lat_forward, lat_backward = neighbours("lat", False)
     lon_forward, lon_backward = neighbours("lon", True)
-    hn = lax.ppermute(x[:, :1, :], "lat", lat_backward)
-    hs = lax.ppermute(x[:, rows - 1:, :], "lat", lat_forward)
+    hn = lax.ppermute(top, "lat", lat_backward)
+    hs = lax.ppermute(bottom, "lat", lat_forward)
+    he = lax.ppermute(columns_of(ends[0].reshape(feats, rows)), "lon", lon_backward)
+    hw = lax.ppermute(columns_of(ends[1].reshape(feats, rows)), "lon", lon_forward)
+    return hn, hs, he, hw
+
+
+def edges(x):
+    feats, rows, cols = x.shape
     lane = lax.broadcasted_iota(jnp.int32, (cols, 2), 0)
     which = lax.broadcasted_iota(jnp.int32, (cols, 2), 1)
     pick = (lane == which * (cols - 1)).astype(jnp.float32)
     ends = jnp.dot(x.reshape(feats * rows, cols), pick, precision=lax.Precision.HIGHEST)
-    he = lax.ppermute(columns_of(ends[:, 0].reshape(feats, rows)), "lon", lon_backward)
-    hw = lax.ppermute(columns_of(ends[:, 1].reshape(feats, rows)), "lon", lon_forward)
-    return sweep(x, hn, hs, he, hw, u, v, k)
+    return x[:, :1, :], x[:, rows - 1:, :], ends.T
 
 
 def positions(targets_all, experts):
@@ -314,8 +342,10 @@
     num_vars, levels, lat_cells, lon_cells = column_state.shape
     features = num_vars * levels
     current = column_state.reshape(features, lat_cells, lon_cells)
+    sides = edges(current)
     for sweep_index in range(2):
-        current = step(current, wind_speed[0], wind_speed[1], diffusivity)
+        halos = exchange(*sides, features, lat_cells)
+        current, *sides = sweep(current, halos, wind_speed[0], wind_speed[1], diffusivity, sweep_index == 0)
     column_count = lat_cells * lon_cells
     experts = lax.axis_size("lon")
     capacity = 2 * column_count // experts

time: 163 us -> 161 us (0.988)
  blocking collectives: 34.6 us -> 39 us
  Pallas kernels: 55.2 us -> 51.3 us
  matrix products: 5.64 us -> 2.92 us
  waiting for transfers between devices: 24.7 us -> 27.2 us
  starting transfers between devices: 28.9 us -> 27 us
    pallas_call x1, Pallas kernels: 23.3 us -> 18.6 us  [network(): pl.pallas_call(network_kernel, grid_spec=pltpu.PrefetchScalarGridSpec(num...]
    all_to_all x1, blocking collectives: 34.6 us -> 39 us  [local(): lax.all_to_all(result.reshape(features, experts, width), 'lon', split_axi...]
    all_to_all x1, starting transfers between devices: 10.6 us -> 6.49 us  [local(): lax.all_to_all(part, 'lon', split_axis=1, concat_axis=1, tiled=True)]
    dot_general x2 -> x1, matrix products: 5.36 us -> 2.64 us  [edges(): jnp.dot(x.reshape(feats * rows, cols), pick, precision=lax.Precision.HIGH...]
    ppermute x8, waiting for transfers between devices: 0.68 us -> 3.17 us  [the longest x2 2.13 us: exchange(): lax.ppermute(columns_of(ends[1].reshape(feats, rows)), 'lon', lon_forward)]
    ppermute x8, starting transfers between devices: 18.3 us -> 20.5 us  [the longest x2 9.18 us: exchange(): hs = lax.ppermute(bottom, 'lat', lat_forward)]
  transfers between devices with their start and end apart: 9 -> 9, of which waited for: 2 -> 4; matrix products, arithmetic and copies ran while one was open for 5% -> 6% of each run, Pallas kernels for 0% -> 0%
where the time goes in v15:
time: 161 us; the launch traced here: 160 us
  Pallas kernels  51.3 us (32%)
  blocking collectives  39 us (24%)
  waiting for transfers between devices  27.2 us (17%)
  starting transfers between devices  27 us (17%)
  local copies, waits for them, and re-layouts  9.58 us (6%)
  matrix products  2.92 us (2%)
  other arithmetic  2.69 us (2%)
    all_to_all x1, blocking collectives, local(): lax.all_to_all(result.reshape(features, experts, width), 'lon', split_axi...  39 us
    all_to_all x1, waiting for transfers between devices, local(): lax.all_to_all(part, 'lon', split_axis=1, concat_axis=1, tiled=True)  24.1 us
    pallas_call x1, Pallas kernels, network(): pl.pallas_call(network_kernel, grid_spec=pltpu.PrefetchScalarGridSpec(num...  18.6 us
    pallas_call x2, Pallas kernels, sweep(): pl.pallas_call(sweep_kernel, grid=(nb,), in_specs=[big, edge_row, edge_ro...  12.7 us
    pallas_call x1, Pallas kernels, combine(): pl.pallas_call(combine_kernel, grid_spec=pltpu.PrefetchScalarGridSpec(num...  10.7 us
    pallas_call x1, Pallas kernels, pack(): pl.pallas_call(pack_kernel, grid_spec=pltpu.PrefetchScalarGridSpec(num_sc...  9.29 us
    ppermute x2, starting transfers between devices, exchange(): hs = lax.ppermute(bottom, 'lat', lat_forward)  9.18 us
    ppermute x2, starting transfers between devices, exchange(): lax.ppermute(columns_of(ends[0].reshape(feats, rows)), 'lon', lon_backward)  7.37 us
  transfers between devices with their start and end apart: 9, of which 4 were waited for; matrix products, arithmetic and copies ran while one was open for 6% of the time, Pallas kernels for 0%

profile of v15, /device:TPU:1, one launch (start us, length us, event | category | flops | bytes accessed | tf_op | source)
XLA Modules:
  0.0 160.0 jit_solution(15003205265661818865)
XLA Ops:
  0.0 1.4 fusion.11
  1.4 1.3 collective-permute-start
  2.7 5.0 %collective-permute-start.1 = (f32[128,1,128]{2,1,0:T(1,128)S(1)}, f32[128,1,128]{2,1,0:T(1,128)S(1)}, u32[]{:S(2)}, u32[]{:S(2)}) collective-permute-start(f32[128,1,128]{2,1,0:T(1,128)S(1)} %get-tuple-element.17), channel_id=1, source_target_pairs={{0,32},{32,64},{64,96},{1,33},{33,65},{65,97},{2,34},{34,66},{66,9... | collective-permute-start | bytes 196616 | tf_op jit(solution)/shard_map/ppermute | solution.py:91
  7.7 2.6 %fusion.8 = f32[2,4096]{1,0:T(2,128)S(1)} fusion(f32[4096,128]{1,0:T(8,128)} %bitcast.50, s32[2]{0:T(128)S(1)} %iota_multiply_fusion), kind=kOutput, calls=%fused_computation.15 | convolution fusion | flops 12583424 | bytes 2129928 | tf_op jit(solution)/shard_map/dot_general | solution.py:102
  10.6 1.0 collective-permute-start.2
  11.8 1.3 collective-permute-start.3
  13.2 1.1 slice_bitcast_fusion
  14.9 2.1 %collective-permute-done.3.hw_ref = f32[4,32,32]{2,1,0:T(8,128)S(1)} collective-permute-done((f32[4,32,32]{2,1,0:T(8,128)S(1)}, f32[4,32,32]{2,1,0:T(8,128)S(1)}, u32[]{:S(2)}, u32[]{:S(2)}) %collective-permute-start.3) | collective-permute-done | bytes 16416 | tf_op jit(solution)/shard_map/ppermute | solution.py:93
  17.7 6.7 %shard_map.73 = (f32[128,32,128]{2,1,0:T(8,128)}, f32[128,1,128]{2,1,0:T(1,128)}, f32[128,1,128]{2,1,0:T(1,128)}, f32[2,4096]{1,0:T(2,128)}) custom-call(f32[128,32,128]{2,1,0:T(8,128)} %bitcast.51, f32[128,1,128]{2,1,0:T(1,128)} %copy-done.4, f32[128,1,128]{2,1,0:T(1,128)} %copy-done.5, f32[4,32,32]{2,1,0:T(8,128)} %copy-done.6, f32[4,32,32]{2,1,0:T(8,128)} %copy-done.8, ...), custom_call_target="tpu_custom_call" | custom-call | flops 10485760 | bytes 5767168 | tf_op jit(solution)/shard_map/pallas_call | solution.py:72
  24.4 0.9 slice_reduce_fusion.2
  25.5 6.3 %collective-permute-start.6 = (f32[4,32,32]{2,1,0:T(8,128)S(1)}, f32[4,32,32]{2,1,0:T(8,128)S(1)}, u32[]{:S(2)}, u32[]{:S(2)}) collective-permute-start(f32[4,32,32]{2,1,0:T(8,128)S(1)} %bitcast.61), channel_id=1, source_target_pairs={{1,0},{2,1},{3,2},{4,3},{5,4},{6,5},{7,6},{8,7},{9,8},{10,9},{11,1... | collective-permute-start | bytes 49160 | tf_op jit(solution)/shard_map/ppermute | solution.py:92
  32.1 1.3 collective-permute-start.4
  33.4 4.2 %collective-permute-start.5 = (f32[128,1,128]{2,1,0:T(1,128)}, f32[128,1,128]{2,1,0:T(1,128)S(1)}, u32[]{:S(2)}, u32[]{:S(2)}) collective-permute-start(f32[128,1,128]{2,1,0:T(1,128)} %get-tuple-element.11), channel_id=1, source_target_pairs={{0,32},{32,64},{64,96},{1,33},{33,65},{65,97},{2,34},{34,66},{66,9... | collective-permute-start | bytes 196616 | tf_op jit(solution)/shard_map/ppermute | solution.py:91
  38.2 1.0 collective-permute-done.5.hs_ref
  39.8 6.0 %shard_map.74.cur_ref = f32[128,32,128]{2,1,0:T(8,128)} custom-call(f32[128,32,128]{2,1,0:T(8,128)} %get-tuple-element.9.q_ref, f32[128,1,128]{2,1,0:T(1,128)} %copy-done.10, f32[128,1,128]{2,1,0:T(1,128)} %copy-done.11, f32[4,32,32]{2,1,0:T(8,128)} %copy-done.7, f32[4,32,32]{2,1,0:T(8,128)} %copy-done.9, f32[32,32,128]{2,1,0:T(8,128)} %get-tuple-element.20.u_ref, ...), custom_call_target="tpu_custom_call" | custom-call | flops 10485760 | bytes 5767168 | tf_op jit(solution)/shard_map/pallas_call | solution.py:72
  45.8 9.3 %shard_map.75 = bf16[8192,128]{1,0:T(8,128)(2,1)} custom-call(s32[4096]{0:T(1024)} %bitcast_add_fusion.t_ref, f32[128,32,128]{2,1,0:T(8,128)} %shard_map.74.cur_ref), custom_call_target="tpu_custom_call" | custom-call | tf_op jit(solution)/shard_map/pallas_call | solution.py:289
  55.1 6.5 %all-to-all-start = ((bf16[128,32,256]{0,2,1:T(8,128)(2,1)}), bf16[128,32,256]{0,2,1:T(8,128)(2,1)S(1)}, u32[]{:S(2)}, u32[]{:S(2)}) async-start(bf16[128,32,256]{0,2,1:T(8,128)(2,1)} %bitcast.54), calls=%async_computation | async-start | bytes 4194304 | tf_op jit(solution)/shard_map/all_to_all | solution.py:361
  61.6 2.7 %copy.23 = bf16[1,3,512,512]{2,3,1,0:T(8,128)(2,1)} copy(bf16[1,3,512,512]{3,2,1,0:T(8,128)(2,1)} %param.12) | data formatting | bytes 3145728 | tf_op args[5]
  64.3 0.8 copy.22
  65.8 24.1 %all-to-all-done = bf16[128,32,256]{0,2,1:T(8,128)(2,1)S(1)} async-done(((bf16[128,32,256]{0,2,1:T(8,128)(2,1)}), bf16[128,32,256]{0,2,1:T(8,128)(2,1)S(1)}, u32[]{:S(2)}, u32[]{:S(2)}) %all-to-all-start) | async-done | bytes 2097184 | tf_op jit(solution)/shard_map/all_to_all | solution.py:361
  89.9 1.2 compare_reduce_fusion
  91.7 18.6 %shard_map.76 = bf16[8192,128]{1,0:T(8,128)(2,1)} custom-call(s32[64]{0:T(128)} %convert_element_type.23.nonzero_ref, bf16[8192,128]{1,0:T(8,128)(2,1)} %bitcast.53, bf16[128,512]{1,0:T(8,128)(2,1)} %bitcast.57, bf16[3,512,512]{2,1,0:T(8,128)(2,1)} %bitcast.56, bf16[512,128]{1,0:T(8,128)(2,1)} %bitcast.58), custom_call_target="tpu_custom_call" | custom-call | flops 15032385536 | bytes 6029312 | tf_op jit(solution)/shard_map/pallas_call | solution.py:237
  110.2 39.0 %all_to_all.10 = bf16[128,32,256]{0,2,1:T(8,128)(2,1)} all-to-all(bf16[128,32,256]{0,2,1:T(8,128)(2,1)} %bitcast.55), channel_id=1, replica_groups=mesh['lat'=4,'lon'=32] {'lon'}, dimensions={1} | all-to-all | bytes 4194304 | tf_op jit(solution)/shard_map/all_to_all | solution.py:365
  149.2 10.7 %shard_map.77 = f32[128,32,128]{2,1,0:T(8,128)} custom-call(s32[4096]{0:T(1024)} %bitcast_add_fusion.t_ref, bf16[8192,128]{1,0:T(8,128)(2,1)} %bitcast.52, f32[128,32,128]{2,1,0:T(8,128)} %shard_map.74.cur_ref), custom_call_target="tpu_custom_call" | custom-call | tf_op jit(solution)/shard_map/pallas_call | solution.py:320
  (52 shorter events, 4.7 us)
Async XLA Ops:
  0.0 13.2 %copy-start.1 = (f32[2,32,32,128]{3,2,1,0:T(8,128)S(1)}, f32[2,32,32,128]{3,2,1,0:T(8,128)}, u32[]{:S(2)}) copy-start(f32[2,32,32,128]{3,2,1,0:T(8,128)} %param.8) | copy-start | bytes 3145732
  1.4 15.6 %collective-permute-start = (f32[128,1,128]{2,1,0:T(1,128)S(1)}, f32[128,1,128]{2,1,0:T(1,128)S(1)}, u32[]{:S(2)}, u32[]{:S(2)}) collective-permute-start(f32[128,1,128]{2,1,0:T(1,128)S(1)} %get-tuple-element.18), channel_id=1, source_target_pairs={{32,0},{64,32},{96,64},{33,1},{65,33},{97,65},{34,2},{66,34},{98,6... | collective-permute-start | bytes 196616 | tf_op jit(solution)/shard_map/ppermute | solution.py:90
  2.7 14.3 %collective-permute-start.1 = (f32[128,1,128]{2,1,0:T(1,128)S(1)}, f32[128,1,128]{2,1,0:T(1,128)S(1)}, u32[]{:S(2)}, u32[]{:S(2)}) collective-permute-start(f32[128,1,128]{2,1,0:T(1,128)S(1)} %get-tuple-element.17), channel_id=1, source_target_pairs={{0,32},{32,64},{64,96},{1,33},{33,65},{65,97},{2,34},{34,66},{66,9... | collective-permute-start | bytes 196616 | tf_op jit(solution)/shard_map/ppermute | solution.py:91
  7.7 6.5 %copy-start.12 = (s32[1,4096,1]{1,2,0:T(1,128)S(1)}, s32[1,4096,1]{1,2,0:T(1,128)}, u32[]{:S(2)}) copy-start(s32[1,4096,1]{1,2,0:T(1,128)} %param.10) | copy-start | bytes 49156
  10.6 4.3 %collective-permute-start.2 = (f32[4,32,32]{2,1,0:T(8,128)S(1)}, f32[4,32,32]{2,1,0:T(8,128)S(1)}, u32[]{:S(2)}, u32[]{:S(2)}) collective-permute-start(f32[4,32,32]{2,1,0:T(8,128)S(1)} %bitcast.60), channel_id=1, source_target_pairs={{1,0},{2,1},{3,2},{4,3},{5,4},{6,5},{7,6},{8,7},{9,8},{10,9},{11,1... | collective-permute-start | bytes 49160 | tf_op jit(solution)/shard_map/ppermute | solution.py:92
  11.8 5.2 %collective-permute-start.3 = (f32[4,32,32]{2,1,0:T(8,128)S(1)}, f32[4,32,32]{2,1,0:T(8,128)S(1)}, u32[]{:S(2)}, u32[]{:S(2)}) collective-permute-start(f32[4,32,32]{2,1,0:T(8,128)S(1)} %bitcast.62), channel_id=1, source_target_pairs={{0,1},{1,2},{2,3},{3,4},{4,5},{5,6},{6,7},{7,8},{8,9},{9,10},{10,1... | collective-permute-start | bytes 49160 | tf_op jit(solution)/shard_map/ppermute | solution.py:93
  14.9 2.2 %copy-start.6 = (f32[4,32,32]{2,1,0:T(8,128)}, f32[4,32,32]{2,1,0:T(8,128)S(1)}, u32[]{:S(2)}) copy-start(f32[4,32,32]{2,1,0:T(8,128)S(1)} %collective-permute-done.2.he_ref) | copy-start | bytes 49156
  17.0 0.6 copy-start.8
  17.0 0.6 copy-start.4
  17.0 0.7 copy-start.5
  25.5 12.7 %collective-permute-start.6 = (f32[4,32,32]{2,1,0:T(8,128)S(1)}, f32[4,32,32]{2,1,0:T(8,128)S(1)}, u32[]{:S(2)}, u32[]{:S(2)}) collective-permute-start(f32[4,32,32]{2,1,0:T(8,128)S(1)} %bitcast.61), channel_id=1, source_target_pairs={{1,0},{2,1},{3,2},{4,3},{5,4},{6,5},{7,6},{8,7},{9,8},{10,9},{11,1... | collective-permute-start | bytes 49160 | tf_op jit(solution)/shard_map/ppermute | solution.py:92
  32.0 6.2 %collective-permute-start.7 = (f32[4,32,32]{2,1,0:T(8,128)S(1)}, f32[4,32,32]{2,1,0:T(8,128)S(1)}, u32[]{:S(2)}, u32[]{:S(2)}) collective-permute-start(f32[4,32,32]{2,1,0:T(8,128)S(1)} %bitcast.63), channel_id=1, source_target_pairs={{0,1},{1,2},{2,3},{3,4},{4,5},{5,6},{6,7},{7,8},{8,9},{9,10},{10,1... | collective-permute-start | bytes 49160 | tf_op jit(solution)/shard_map/ppermute | solution.py:93
  32.1 6.1 %collective-permute-start.4 = (f32[128,1,128]{2,1,0:T(1,128)}, f32[128,1,128]{2,1,0:T(1,128)S(1)}, u32[]{:S(2)}, u32[]{:S(2)}) collective-permute-start(f32[128,1,128]{2,1,0:T(1,128)} %get-tuple-element.10), channel_id=1, source_target_pairs={{32,0},{64,32},{96,64},{33,1},{65,33},{97,65},{34,2},{66,34},{98,6... | collective-permute-start | bytes 196616 | tf_op jit(solution)/shard_map/ppermute | solution.py:90
  33.4 5.8 %collective-permute-start.5 = (f32[128,1,128]{2,1,0:T(1,128)}, f32[128,1,128]{2,1,0:T(1,128)S(1)}, u32[]{:S(2)}, u32[]{:S(2)}) collective-permute-start(f32[128,1,128]{2,1,0:T(1,128)} %get-tuple-element.11), channel_id=1, source_target_pairs={{0,32},{32,64},{64,96},{1,33},{33,65},{65,97},{2,34},{34,66},{66,9... | collective-permute-start | bytes 196616 | tf_op jit(solution)/shard_map/ppermute | solution.py:91
  38.2 1.0 copy-start.7
  38.2 1.0 copy-start.9
  38.2 1.0 copy-start.10
  39.2 0.6 copy-start.11
  55.1 34.8 %all-to-all-start = ((bf16[128,32,256]{0,2,1:T(8,128)(2,1)}), bf16[128,32,256]{0,2,1:T(8,128)(2,1)S(1)}, u32[]{:S(2)}, u32[]{:S(2)}) async-start(bf16[128,32,256]{0,2,1:T(8,128)(2,1)} %bitcast.54), calls=%async_computation | async-start | bytes 4194304 | tf_op jit(solution)/shard_map/all_to_all | solution.py:361
  61.6 2.7 %copy-start.2 = (bf16[1,512,128]{2,1,0:T(8,128)(2,1)S(1)}, bf16[1,512,128]{2,1,0:T(8,128)(2,1)}, u32[]{:S(2)}) copy-start(bf16[1,512,128]{2,1,0:T(8,128)(2,1)} %param.11) | copy-start | bytes 393220
  61.6 3.5 %copy-start.3 = (bf16[1,128,512]{2,1,0:T(8,128)(2,1)S(1)}, bf16[1,128,512]{2,1,0:T(8,128)(2,1)}, u32[]{:S(2)}) copy-start(bf16[1,128,512]{2,1,0:T(8,128)(2,1)} %param.13) | copy-start | bytes 393220
  89.9 1.8 %copy-start = (bf16[128,32,256]{0,2,1:T(8,128)(2,1)}, bf16[128,32,256]{0,2,1:T(8,128)(2,1)S(1)}, u32[]{:S(2)}) copy-start(bf16[128,32,256]{0,2,1:T(8,128)(2,1)S(1)} %all-to-all-done) | copy-start | bytes 6291460

commit v16 on v15

--- a/solution.py
+++ b/solution.py
@@ -15,7 +15,7 @@
     return forward, backward
 
 
-FB = 32
+FB = 16
 
 def keep_edges(block_ref, top_ref, bottom_ref, ends_ref):
     feats, rows, cols = block_ref.shape

time: 161 us -> 168 us (1.043)
  Pallas kernels: 51.3 us -> 56.6 us
    pallas_call x2, Pallas kernels: 12.7 us -> 18 us  [sweep(): pl.pallas_call(sweep_kernel, grid=(nb,), in_specs=[big, edge_row, edge_ro...]
where the time goes in v16:
time: 168 us; the launch traced here: 166 us
  Pallas kernels  56.6 us (34%)
  blocking collectives  39.4 us (23%)
  starting transfers between devices  27.6 us (16%)
  waiting for transfers between devices  27.3 us (16%)
  local copies, waits for them, and re-layouts  9.64 us (6%)
  matrix products  2.92 us (2%)
  other arithmetic  2.69 us (2%)
    all_to_all x1, blocking collectives, local(): lax.all_to_all(result.reshape(features, experts, width), 'lon', split_axi...  39.4 us
    all_to_all x1, waiting for transfers between devices, local(): lax.all_to_all(part, 'lon', split_axis=1, concat_axis=1, tiled=True)  24.1 us
    pallas_call x1, Pallas kernels, network(): pl.pallas_call(network_kernel, grid_spec=pltpu.PrefetchScalarGridSpec(num...  18.6 us
    pallas_call x2, Pallas kernels, sweep(): pl.pallas_call(sweep_kernel, grid=(nb,), in_specs=[big, edge_row, edge_ro...  18 us
    pallas_call x1, Pallas kernels, combine(): pl.pallas_call(combine_kernel, grid_spec=pltpu.PrefetchScalarGridSpec(num...  10.7 us
    pallas_call x1, Pallas kernels, pack(): pl.pallas_call(pack_kernel, grid_spec=pltpu.PrefetchScalarGridSpec(num_sc...  9.29 us
    ppermute x2, starting transfers between devices, exchange(): hs = lax.ppermute(bottom, 'lat', lat_forward)  9.18 us
    ppermute x2, starting transfers between devices, exchange(): lax.ppermute(columns_of(ends[0].reshape(feats, rows)), 'lon', lon_backward)  7.98 us
  transfers between devices with their start and end apart: 9, of which 4 were waited for; matrix products, arithmetic and copies ran while one was open for 6% of the time, Pallas kernels for 0%

profile of v16, /device:TPU:1, one launch (start us, length us, event | category | flops | bytes accessed | tf_op | source)
XLA Modules:
  0.0 166.5 jit_solution(13700829576586263161)
XLA Ops:
  0.0 1.4 fusion.11
  1.4 1.3 collective-permute-start
  2.7 5.0 %collective-permute-start.1 = (f32[128,1,128]{2,1,0:T(1,128)S(1)}, f32[128,1,128]{2,1,0:T(1,128)S(1)}, u32[]{:S(2)}, u32[]{:S(2)}) collective-permute-start(f32[128,1,128]{2,1,0:T(1,128)S(1)} %get-tuple-element.17), channel_id=1, source_target_pairs={{0,32},{32,64},{64,96},{1,33},{33,65},{65,97},{2,34},{34,66},{66,9... | collective-permute-start | bytes 196616 | tf_op jit(solution)/shard_map/ppermute | solution.py:91
  7.7 2.6 %fusion.8 = f32[2,4096]{1,0:T(2,128)S(1)} fusion(f32[4096,128]{1,0:T(8,128)} %bitcast.50, s32[2]{0:T(128)S(1)} %iota_multiply_fusion), kind=kOutput, calls=%fused_computation.15 | convolution fusion | flops 12583424 | bytes 2129928 | tf_op jit(solution)/shard_map/dot_general | solution.py:102
  10.6 1.0 collective-permute-start.2
  11.9 1.3 collective-permute-start.3
  13.2 1.1 slice_bitcast_fusion
  15.6 1.5 collective-permute-done.3.hw_ref
  17.8 9.6 %shard_map.73 = (f32[128,32,128]{2,1,0:T(8,128)}, f32[128,1,128]{2,1,0:T(1,128)}, f32[128,1,128]{2,1,0:T(1,128)}, f32[2,4096]{1,0:T(2,128)}) custom-call(f32[128,32,128]{2,1,0:T(8,128)} %bitcast.51, f32[128,1,128]{2,1,0:T(1,128)} %copy-done.8, f32[128,1,128]{2,1,0:T(1,128)} %copy-done.9, f32[8,32,16]{2,1,0:T(8,128)} %copy-done.2, f32[8,32,16]{2,1,0:T(8,128)} %copy-done.4, ...), custom_call_target="tpu_custom_call" | custom-call | flops 10485760 | bytes 5767168 | tf_op jit(solution)/shard_map/pallas_call | solution.py:72
  27.4 0.9 slice_reduce_fusion.2
  28.5 6.9 %collective-permute-start.6 = (f32[8,32,16]{2,1,0:T(8,128)S(1)}, f32[8,32,16]{2,1,0:T(8,128)S(1)}, u32[]{:S(2)}, u32[]{:S(2)}) collective-permute-start(f32[8,32,16]{2,1,0:T(8,128)S(1)} %bitcast.58), channel_id=1, source_target_pairs={{1,0},{2,1},{3,2},{4,3},{5,4},{6,5},{7,6},{8,7},{9,8},{10,9},{11,1... | collective-permute-start | bytes 49160 | tf_op jit(solution)/shard_map/ppermute | solution.py:92
  35.7 1.3 collective-permute-start.4
  37.0 4.2 %collective-permute-start.5 = (f32[128,1,128]{2,1,0:T(1,128)}, f32[128,1,128]{2,1,0:T(1,128)S(1)}, u32[]{:S(2)}, u32[]{:S(2)}) collective-permute-start(f32[128,1,128]{2,1,0:T(1,128)} %get-tuple-element.11), channel_id=1, source_target_pairs={{0,32},{32,64},{64,96},{1,33},{33,65},{65,97},{2,34},{34,66},{66,9... | collective-permute-start | bytes 196616 | tf_op jit(solution)/shard_map/ppermute | solution.py:91
  41.9 1.0 collective-permute-done.5.hs_ref
  43.5 8.4 %shard_map.74.cur_ref = f32[128,32,128]{2,1,0:T(8,128)} custom-call(f32[128,32,128]{2,1,0:T(8,128)} %get-tuple-element.9.q_ref, f32[128,1,128]{2,1,0:T(1,128)} %copy-done.10, f32[128,1,128]{2,1,0:T(1,128)} %copy-done.11, f32[8,32,16]{2,1,0:T(8,128)} %copy-done.3, f32[8,32,16]{2,1,0:T(8,128)} %copy-done.5, f32[32,32,128]{2,1,0:T(8,128)} %get-tuple-element.20.u_ref, ...), custom_call_target="tpu_custom_call" | custom-call | flops 10485760 | bytes 5767168 | tf_op jit(solution)/shard_map/pallas_call | solution.py:72
  51.9 9.3 %shard_map.75 = bf16[8192,128]{1,0:T(8,128)(2,1)} custom-call(s32[4096]{0:T(1024)} %bitcast_add_fusion.t_ref, f32[128,32,128]{2,1,0:T(8,128)} %shard_map.74.cur_ref), custom_call_target="tpu_custom_call" | custom-call | tf_op jit(solution)/shard_map/pallas_call | solution.py:289
  61.2 6.5 %all-to-all-start = ((bf16[128,32,256]{0,2,1:T(8,128)(2,1)}), bf16[128,32,256]{0,2,1:T(8,128)(2,1)S(1)}, u32[]{:S(2)}, u32[]{:S(2)}) async-start(bf16[128,32,256]{0,2,1:T(8,128)(2,1)} %bitcast.54), calls=%async_computation | async-start | bytes 4194304 | tf_op jit(solution)/shard_map/all_to_all | solution.py:361
  67.7 2.7 %copy.23 = bf16[1,3,512,512]{2,3,1,0:T(8,128)(2,1)} copy(bf16[1,3,512,512]{3,2,1,0:T(8,128)(2,1)} %param.12) | data formatting | bytes 3145728 | tf_op args[5]
  70.4 0.8 copy.22
  71.9 24.1 %all-to-all-done = bf16[128,32,256]{0,2,1:T(8,128)(2,1)S(1)} async-done(((bf16[128,32,256]{0,2,1:T(8,128)(2,1)}), bf16[128,32,256]{0,2,1:T(8,128)(2,1)S(1)}, u32[]{:S(2)}, u32[]{:S(2)}) %all-to-all-start) | async-done | bytes 2097184 | tf_op jit(solution)/shard_map/all_to_all | solution.py:361
  96.0 1.2 compare_reduce_fusion
  97.8 18.6 %shard_map.76 = bf16[8192,128]{1,0:T(8,128)(2,1)} custom-call(s32[64]{0:T(128)} %convert_element_type.23.nonzero_ref, bf16[8192,128]{1,0:T(8,128)(2,1)} %bitcast.53, bf16[128,512]{1,0:T(8,128)(2,1)} %bitcast.61, bf16[3,512,512]{2,1,0:T(8,128)(2,1)} %bitcast.56, bf16[512,128]{1,0:T(8,128)(2,1)} %bitcast.62), custom_call_target="tpu_custom_call" | custom-call | flops 15032385536 | bytes 6029312 | tf_op jit(solution)/shard_map/pallas_call | solution.py:237
  116.4 39.4 %all_to_all.10 = bf16[128,32,256]{0,2,1:T(8,128)(2,1)} all-to-all(bf16[128,32,256]{0,2,1:T(8,128)(2,1)} %bitcast.55), channel_id=1, replica_groups=mesh['lat'=4,'lon'=32] {'lon'}, dimensions={1} | all-to-all | bytes 4194304 | tf_op jit(solution)/shard_map/all_to_all | solution.py:365
  155.7 10.7 %shard_map.77 = f32[128,32,128]{2,1,0:T(8,128)} custom-call(s32[4096]{0:T(1024)} %bitcast_add_fusion.t_ref, bf16[8192,128]{1,0:T(8,128)(2,1)} %bitcast.52, f32[128,32,128]{2,1,0:T(8,128)} %shard_map.74.cur_ref), custom_call_target="tpu_custom_call" | custom-call | tf_op jit(solution)/shard_map/pallas_call | solution.py:320
  (52 shorter events, 5.5 us)
Async XLA Ops:
  0.0 13.2 %copy-start.1 = (f32[2,32,32,128]{3,2,1,0:T(8,128)S(1)}, f32[2,32,32,128]{3,2,1,0:T(8,128)}, u32[]{:S(2)}) copy-start(f32[2,32,32,128]{3,2,1,0:T(8,128)} %param.8) | copy-start | bytes 3145732
  1.4 15.7 %collective-permute-start = (f32[128,1,128]{2,1,0:T(1,128)S(1)}, f32[128,1,128]{2,1,0:T(1,128)S(1)}, u32[]{:S(2)}, u32[]{:S(2)}) collective-permute-start(f32[128,1,128]{2,1,0:T(1,128)S(1)} %get-tuple-element.18), channel_id=1, source_target_pairs={{32,0},{64,32},{96,64},{33,1},{65,33},{97,65},{34,2},{66,34},{98,6... | collective-permute-start | bytes 196616 | tf_op jit(solution)/shard_map/ppermute | solution.py:90
  2.7 14.4 %collective-permute-start.1 = (f32[128,1,128]{2,1,0:T(1,128)S(1)}, f32[128,1,128]{2,1,0:T(1,128)S(1)}, u32[]{:S(2)}, u32[]{:S(2)}) collective-permute-start(f32[128,1,128]{2,1,0:T(1,128)S(1)} %get-tuple-element.17), channel_id=1, source_target_pairs={{0,32},{32,64},{64,96},{1,33},{33,65},{65,97},{2,34},{34,66},{66,9... | collective-permute-start | bytes 196616 | tf_op jit(solution)/shard_map/ppermute | solution.py:91
  7.7 6.6 %copy-start.12 = (s32[1,4096,1]{1,2,0:T(1,128)S(1)}, s32[1,4096,1]{1,2,0:T(1,128)}, u32[]{:S(2)}) copy-start(s32[1,4096,1]{1,2,0:T(1,128)} %param.10) | copy-start | bytes 49156
  10.6 5.0 %collective-permute-start.2 = (f32[8,32,16]{2,1,0:T(8,128)S(1)}, f32[8,32,16]{2,1,0:T(8,128)S(1)}, u32[]{:S(2)}, u32[]{:S(2)}) collective-permute-start(f32[8,32,16]{2,1,0:T(8,128)S(1)} %bitcast.57), channel_id=1, source_target_pairs={{1,0},{2,1},{3,2},{4,3},{5,4},{6,5},{7,6},{8,7},{9,8},{10,9},{11,1... | collective-permute-start | bytes 49160 | tf_op jit(solution)/shard_map/ppermute | solution.py:92
  11.9 5.3 %collective-permute-start.3 = (f32[8,32,16]{2,1,0:T(8,128)S(1)}, f32[8,32,16]{2,1,0:T(8,128)S(1)}, u32[]{:S(2)}, u32[]{:S(2)}) collective-permute-start(f32[8,32,16]{2,1,0:T(8,128)S(1)} %bitcast.59), channel_id=1, source_target_pairs={{0,1},{1,2},{2,3},{3,4},{4,5},{5,6},{6,7},{7,8},{8,9},{9,10},{10,1... | collective-permute-start | bytes 49160 | tf_op jit(solution)/shard_map/ppermute | solution.py:93
  15.6 1.6 copy-start.2
  17.1 0.6 copy-start.4
  17.1 0.7 copy-start.8
  17.1 0.7 copy-start.9
  28.5 13.3 %collective-permute-start.6 = (f32[8,32,16]{2,1,0:T(8,128)S(1)}, f32[8,32,16]{2,1,0:T(8,128)S(1)}, u32[]{:S(2)}, u32[]{:S(2)}) collective-permute-start(f32[8,32,16]{2,1,0:T(8,128)S(1)} %bitcast.58), channel_id=1, source_target_pairs={{1,0},{2,1},{3,2},{4,3},{5,4},{6,5},{7,6},{8,7},{9,8},{10,9},{11,1... | collective-permute-start | bytes 49160 | tf_op jit(solution)/shard_map/ppermute | solution.py:92
  35.7 6.2 %collective-permute-start.7 = (f32[8,32,16]{2,1,0:T(8,128)S(1)}, f32[8,32,16]{2,1,0:T(8,128)S(1)}, u32[]{:S(2)}, u32[]{:S(2)}) collective-permute-start(f32[8,32,16]{2,1,0:T(8,128)S(1)} %bitcast.60), channel_id=1, source_target_pairs={{0,1},{1,2},{2,3},{3,4},{4,5},{5,6},{6,7},{7,8},{8,9},{9,10},{10,1... | collective-permute-start | bytes 49160 | tf_op jit(solution)/shard_map/ppermute | solution.py:93
  35.7 6.1 %collective-permute-start.4 = (f32[128,1,128]{2,1,0:T(1,128)}, f32[128,1,128]{2,1,0:T(1,128)S(1)}, u32[]{:S(2)}, u32[]{:S(2)}) collective-permute-start(f32[128,1,128]{2,1,0:T(1,128)} %get-tuple-element.10), channel_id=1, source_target_pairs={{32,0},{64,32},{96,64},{33,1},{65,33},{97,65},{34,2},{66,34},{98,6... | collective-permute-start | bytes 196616 | tf_op jit(solution)/shard_map/ppermute | solution.py:90
  37.0 5.8 %collective-permute-start.5 = (f32[128,1,128]{2,1,0:T(1,128)}, f32[128,1,128]{2,1,0:T(1,128)S(1)}, u32[]{:S(2)}, u32[]{:S(2)}) collective-permute-start(f32[128,1,128]{2,1,0:T(1,128)} %get-tuple-element.11), channel_id=1, source_target_pairs={{0,32},{32,64},{64,96},{1,33},{33,65},{65,97},{2,34},{34,66},{66,9... | collective-permute-start | bytes 196616 | tf_op jit(solution)/shard_map/ppermute | solution.py:91
  41.8 1.0 copy-start.3
  41.8 1.0 copy-start.5
  41.9 1.0 copy-start.10
  42.8 0.6 copy-start.11
  61.2 34.8 %all-to-all-start = ((bf16[128,32,256]{0,2,1:T(8,128)(2,1)}), bf16[128,32,256]{0,2,1:T(8,128)(2,1)S(1)}, u32[]{:S(2)}, u32[]{:S(2)}) async-start(bf16[128,32,256]{0,2,1:T(8,128)(2,1)} %bitcast.54), calls=%async_computation | async-start | bytes 4194304 | tf_op jit(solution)/shard_map/all_to_all | solution.py:361
  67.7 2.7 %copy-start.6 = (bf16[1,512,128]{2,1,0:T(8,128)(2,1)S(1)}, bf16[1,512,128]{2,1,0:T(8,128)(2,1)}, u32[]{:S(2)}) copy-start(bf16[1,512,128]{2,1,0:T(8,128)(2,1)} %param.11) | copy-start | bytes 393220
  67.7 3.5 %copy-start.7 = (bf16[1,128,512]{2,1,0:T(8,128)(2,1)S(1)}, bf16[1,128,512]{2,1,0:T(8,128)(2,1)}, u32[]{:S(2)}) copy-start(bf16[1,128,512]{2,1,0:T(8,128)(2,1)} %param.13) | copy-start | bytes 393220
  96.0 1.8 %copy-start = (bf16[128,32,256]{0,2,1:T(8,128)(2,1)}, bf16[128,32,256]{0,2,1:T(8,128)(2,1)S(1)}, u32[]{:S(2)}) copy-start(bf16[128,32,256]{0,2,1:T(8,128)(2,1)S(1)} %all-to-all-done) | copy-start | bytes 6291460

commit v17 on v15

--- a/solution.py
+++ b/solution.py
@@ -353,7 +353,7 @@
     position = positions(targets_all, experts)
     targets = targets_all * capacity + position
     packed = pack(targets, current, experts * capacity).T.reshape(features, experts, capacity)
-    chunks = 1
+    chunks = 2
     width = capacity // chunks
     answers = []
     for chunk in range(chunks):

time: 161 us -> 166 us (1.031)
  waiting for transfers between devices: 27.2 us -> 11.2 us
  blocking collectives: 39 us -> 46.3 us
  starting transfers between devices: 27 us -> 31.9 us
  Pallas kernels: 51.3 us -> 55.1 us
  local copies, waits for them, and re-layouts: 9.58 us -> 12.2 us
  other arithmetic: 2.69 us -> 5.03 us
    all_to_all x1, waiting for transfers between devices: 24.1 us -> 0.01 us  [local(): lax.all_to_all(part, 'lon', split_axis=1, concat_axis=1, tiled=True)]
    all_to_all x0 -> x1, blocking collectives: none -> 23.2 us  [local(): lax.all_to_all(part, 'lon', split_axis=1, concat_axis=1, tiled=True)]
    all_to_all x1, blocking collectives: 39 us -> 23.1 us  [local(): lax.all_to_all(result.reshape(features, experts, width), 'lon', split_axi...]
    all_to_all x0 -> x1, waiting for transfers between devices: none -> 8.07 us  [local(): lax.all_to_all(result.reshape(features, experts, width), 'lon', split_axi...]
    all_to_all x0 -> x1, starting transfers between devices: none -> 7.39 us  [local(): lax.all_to_all(result.reshape(features, experts, width), 'lon', split_axi...]
    pallas_call x1 -> x2, Pallas kernels: 18.6 us -> 22.4 us  [network(): pl.pallas_call(network_kernel, grid_spec=pltpu.PrefetchScalarGridSpec(num...]
    slice x0 -> x1, local copies, waits for them, and re-layouts: none -> 2.71 us  [local(): part = packed[:, :, chunk * width:(chunk + 1) * width]]
    all_to_all x1, starting transfers between devices: 6.49 us -> 3.96 us  [local(): lax.all_to_all(part, 'lon', split_axis=1, concat_axis=1, tiled=True)]
  transfers between devices with their start and end apart: 9 -> 10, of which waited for: 4 -> 4; matrix products, arithmetic and copies ran while one was open for 6% -> 7% of each run, Pallas kernels for 0% -> 14%
where the time goes in v17:
time: 166 us; the launch traced here: 165 us
  Pallas kernels  55.1 us (33%)
  blocking collectives  46.3 us (28%)
  starting transfers between devices  31.9 us (19%)
  local copies, waits for them, and re-layouts  12.2 us (7%)
  waiting for transfers between devices  11.2 us (7%)
  other arithmetic  5.03 us (3%)
  matrix products  2.92 us (2%)
    all_to_all x1, blocking collectives, local(): lax.all_to_all(part, 'lon', split_axis=1, concat_axis=1, tiled=True)  23.2 us
    all_to_all x1, blocking collectives, local(): lax.all_to_all(result.reshape(features, experts, width), 'lon', split_axi...  23.1 us
    pallas_call x2, Pallas kernels, network(): pl.pallas_call(network_kernel, grid_spec=pltpu.PrefetchScalarGridSpec(num...  22.4 us
    pallas_call x2, Pallas kernels, sweep(): pl.pallas_call(sweep_kernel, grid=(nb,), in_specs=[big, edge_row, edge_ro...  12.7 us
    pallas_call x1, Pallas kernels, combine(): pl.pallas_call(combine_kernel, grid_spec=pltpu.PrefetchScalarGridSpec(num...  10.7 us
    pallas_call x1, Pallas kernels, pack(): pl.pallas_call(pack_kernel, grid_spec=pltpu.PrefetchScalarGridSpec(num_sc...  9.29 us
    ppermute x2, starting transfers between devices, exchange(): hs = lax.ppermute(bottom, 'lat', lat_forward)  9.18 us
    all_to_all x1, waiting for transfers between devices, local(): lax.all_to_all(result.reshape(features, experts, width), 'lon', split_axi...  8.07 us
  transfers between devices with their start and end apart: 10, of which 4 were waited for; matrix products, arithmetic and copies ran while one was open for 7% of the time, Pallas kernels for 14%

profile of v17, /device:TPU:1, one launch (start us, length us, event | category | flops | bytes accessed | tf_op | source)
XLA Modules:
  0.0 165.0 jit_solution(4735478204241519401)
XLA Ops:
  0.0 1.4 fusion.12
  1.4 1.3 collective-permute-start
  2.7 5.0 %collective-permute-start.1 = (f32[128,1,128]{2,1,0:T(1,128)S(1)}, f32[128,1,128]{2,1,0:T(1,128)S(1)}, u32[]{:S(2)}, u32[]{:S(2)}) collective-permute-start(f32[128,1,128]{2,1,0:T(1,128)S(1)} %get-tuple-element.19), channel_id=1, source_target_pairs={{0,32},{32,64},{64,96},{1,33},{33,65},{65,97},{2,34},{34,66},{66,9... | collective-permute-start | bytes 196616 | tf_op jit(solution)/shard_map/ppermute | solution.py:91
  7.7 2.6 %fusion.8 = f32[2,4096]{1,0:T(2,128)S(1)} fusion(f32[4096,128]{1,0:T(8,128)} %bitcast.59, s32[2]{0:T(128)S(1)} %iota_multiply_fusion), kind=kOutput, calls=%fused_computation.17 | convolution fusion | flops 12583424 | bytes 2129928 | tf_op jit(solution)/shard_map/dot_general | solution.py:102
  11.8 1.3 collective-permute-start.3
  13.2 1.1 slice_bitcast_fusion
  14.9 2.1 %collective-permute-done.3.hw_ref = f32[4,32,32]{2,1,0:T(8,128)S(1)} collective-permute-done((f32[4,32,32]{2,1,0:T(8,128)S(1)}, f32[4,32,32]{2,1,0:T(8,128)S(1)}, u32[]{:S(2)}, u32[]{:S(2)}) %collective-permute-start.3) | collective-permute-done | bytes 16416 | tf_op jit(solution)/shard_map/ppermute | solution.py:93
  17.7 6.7 %shard_map.73 = (f32[128,32,128]{2,1,0:T(8,128)}, f32[128,1,128]{2,1,0:T(1,128)}, f32[128,1,128]{2,1,0:T(1,128)}, f32[2,4096]{1,0:T(2,128)}) custom-call(f32[128,32,128]{2,1,0:T(8,128)} %bitcast.60, f32[128,1,128]{2,1,0:T(1,128)} %copy-done.5, f32[128,1,128]{2,1,0:T(1,128)} %copy-done.6, f32[4,32,32]{2,1,0:T(8,128)} %copy-done.7, f32[4,32,32]{2,1,0:T(8,128)} %copy-done.9, ...), custom_call_target="tpu_custom_call" | custom-call | flops 10485760 | bytes 5767168 | tf_op jit(solution)/shard_map/pallas_call | solution.py:72
  25.5 6.3 %collective-permute-start.6 = (f32[4,32,32]{2,1,0:T(8,128)S(1)}, f32[4,32,32]{2,1,0:T(8,128)S(1)}, u32[]{:S(2)}, u32[]{:S(2)}) collective-permute-start(f32[4,32,32]{2,1,0:T(8,128)S(1)} %bitcast.75), channel_id=1, source_target_pairs={{1,0},{2,1},{3,2},{4,3},{5,4},{6,5},{7,6},{8,7},{9,8},{10,9},{11,1... | collective-permute-start | bytes 49160 | tf_op jit(solution)/shard_map/ppermute | solution.py:92
  32.1 1.3 collective-permute-start.4
  33.4 4.2 %collective-permute-start.5 = (f32[128,1,128]{2,1,0:T(1,128)}, f32[128,1,128]{2,1,0:T(1,128)S(1)}, u32[]{:S(2)}, u32[]{:S(2)}) collective-permute-start(f32[128,1,128]{2,1,0:T(1,128)} %get-tuple-element.11), channel_id=1, source_target_pairs={{0,32},{32,64},{64,96},{1,33},{33,65},{65,97},{2,34},{34,66},{66,9... | collective-permute-start | bytes 196616 | tf_op jit(solution)/shard_map/ppermute | solution.py:91
  39.8 6.0 %shard_map.74.cur_ref = f32[128,32,128]{2,1,0:T(8,128)} custom-call(f32[128,32,128]{2,1,0:T(8,128)} %get-tuple-element.9.q_ref, f32[128,1,128]{2,1,0:T(1,128)} %copy-done.11, f32[128,1,128]{2,1,0:T(1,128)} %copy-done.12, f32[4,32,32]{2,1,0:T(8,128)} %copy-done.8, f32[4,32,32]{2,1,0:T(8,128)} %copy-done.10, f32[32,32,128]{2,1,0:T(8,128)} %get-tuple-element.22.u_ref, ...), custom_call_target="tpu_custom_call" | custom-call | flops 10485760 | bytes 5767168 | tf_op jit(solution)/shard_map/pallas_call | solution.py:72
  45.8 9.3 %shard_map.75 = bf16[8192,128]{1,0:T(8,128)(2,1)} custom-call(s32[4096]{0:T(1024)} %bitcast_add_fusion.t_ref, f32[128,32,128]{2,1,0:T(8,128)} %shard_map.74.cur_ref), custom_call_target="tpu_custom_call" | custom-call | tf_op jit(solution)/shard_map/pallas_call | solution.py:289
  55.1 2.7 %fusion.11 = (bf16[128,32,128]{0,2,1:T(8,128)(2,1)S(1)}, bf16[128,32,128]{0,2,1:T(8,128)(2,1)}) fusion(bf16[128,32,256]{0,2,1:T(8,128)(2,1)} %bitcast.62), kind=kLoop, calls=%fused_computation.28 | loop fusion | bytes 4194304 | tf_op jit(solution)/shard_map/slice | solution.py:360
  57.8 23.2 %all_to_all.20 = bf16[128,32,128]{0,2,1:T(8,128)(2,1)S(1)} all-to-all(bf16[128,32,128]{0,2,1:T(8,128)(2,1)S(1)} %get-tuple-element.17), channel_id=1, replica_groups=mesh['lat'=4,'lon'=32] {'lon'}, dimensions={1} | all-to-all | bytes 2097152 | tf_op jit(solution)/shard_map/all_to_all | solution.py:361
  81.0 4.0 %all-to-all-start.2 = ((bf16[128,32,128]{0,2,1:T(8,128)(2,1)}), bf16[128,32,128]{0,2,1:T(8,128)(2,1)S(1)}, u32[]{:S(2)}, u32[]{:S(2)}) async-start(bf16[128,32,128]{0,2,1:T(8,128)(2,1)} %get-tuple-element.18), calls=%async_computation.2 | async-start | bytes 2097152 | tf_op jit(solution)/shard_map/all_to_all | solution.py:361
  85.0 2.6 %copy.23 = bf16[1,3,512,512]{2,3,1,0:T(8,128)(2,1)} copy(bf16[1,3,512,512]{3,2,1,0:T(8,128)(2,1)} %param.12) | data formatting | bytes 3145728 | tf_op args[5]
  90.5 14.9 %shard_map.76 = bf16[4096,128]{1,0:T(8,128)(2,1)} custom-call(s32[32]{0:T(128)} %convert_element_type.26.nonzero_ref, bf16[4096,128]{1,0:T(8,128)(2,1)} %bitcast.64, bf16[128,512]{1,0:T(8,128)(2,1)} %bitcast.69, bf16[3,512,512]{2,1,0:T(8,128)(2,1)} %bitcast.65, bf16[512,128]{1,0:T(8,128)(2,1)} %bitcast.71), custom_call_target="tpu_custom_call" | custom-call | flops 7516192768 | bytes 3932160 | tf_op jit(solution)/shard_map/pallas_call | solution.py:237
  105.4 7.4 %all-to-all-start.1 = ((bf16[128,32,128]{0,2,1:T(8,128)(2,1)}), bf16[128,32,128]{0,2,1:T(8,128)(2,1)S(1)}, u32[]{:S(2)}, u32[]{:S(2)}) async-start(bf16[128,32,128]{0,2,1:T(8,128)(2,1)} %bitcast.67), calls=%async_computation.1 | async-start | bytes 2097152 | tf_op jit(solution)/shard_map/all_to_all | solution.py:365
  114.1 7.5 %shard_map.77 = bf16[4096,128]{1,0:T(8,128)(2,1)} custom-call(s32[32]{0:T(128)} %convert_element_type.27.nonzero_ref, bf16[4096,128]{1,0:T(8,128)(2,1)} %bitcast.63, bf16[128,512]{1,0:T(8,128)(2,1)} %bitcast.70, bf16[3,512,512]{2,1,0:T(8,128)(2,1)} %bitcast.66, bf16[512,128]{1,0:T(8,128)(2,1)} %bitcast.72), custom_call_target="tpu_custom_call" | custom-call | flops 7516192768 | bytes 3932160 | tf_op jit(solution)/shard_map/pallas_call | solution.py:237
  121.6 8.1 %all-to-all-done.1 = bf16[128,32,128]{0,2,1:T(8,128)(2,1)S(1)} async-done(((bf16[128,32,128]{0,2,1:T(8,128)(2,1)}), bf16[128,32,128]{0,2,1:T(8,128)(2,1)S(1)}, u32[]{:S(2)}, u32[]{:S(2)}) %all-to-all-start.1) | async-done | bytes 1048608 | tf_op jit(solution)/shard_map/all_to_all | solution.py:365
  129.7 23.1 %all_to_all.21 = bf16[128,32,128]{0,2,1:T(8,128)(2,1)S(1)} all-to-all(bf16[128,32,128]{0,2,1:T(8,128)(2,1)} %bitcast.68), channel_id=1, replica_groups=mesh['lat'=4,'lon'=32] {'lon'}, dimensions={1} | all-to-all | bytes 2097152 | tf_op jit(solution)/shard_map/all_to_all | solution.py:365
  152.8 1.5 pad_maximum_fusion
  154.3 10.7 %shard_map.78 = f32[128,32,128]{2,1,0:T(8,128)} custom-call(s32[4096]{0:T(1024)} %bitcast_add_fusion.t_ref, bf16[8192,128]{1,0:T(8,128)(2,1)} %bitcast.61, f32[128,32,128]{2,1,0:T(8,128)} %shard_map.74.cur_ref), custom_call_target="tpu_custom_call" | custom-call | tf_op jit(solution)/shard_map/pallas_call | solution.py:320
  (63 shorter events, 10.5 us)
Async XLA Ops:
  0.0 13.2 %copy-start.2 = (f32[2,32,32,128]{3,2,1,0:T(8,128)S(1)}, f32[2,32,32,128]{3,2,1,0:T(8,128)}, u32[]{:S(2)}) copy-start(f32[2,32,32,128]{3,2,1,0:T(8,128)} %param.8) | copy-start | bytes 3145732
  1.4 15.6 %collective-permute-start = (f32[128,1,128]{2,1,0:T(1,128)S(1)}, f32[128,1,128]{2,1,0:T(1,128)S(1)}, u32[]{:S(2)}, u32[]{:S(2)}) collective-permute-start(f32[128,1,128]{2,1,0:T(1,128)S(1)} %get-tuple-element.20), channel_id=1, source_target_pairs={{32,0},{64,32},{96,64},{33,1},{65,33},{97,65},{34,2},{66,34},{98,6... | collective-permute-start | bytes 196616 | tf_op jit(solution)/shard_map/ppermute | solution.py:90
  2.7 14.3 %collective-permute-start.1 = (f32[128,1,128]{2,1,0:T(1,128)S(1)}, f32[128,1,128]{2,1,0:T(1,128)S(1)}, u32[]{:S(2)}, u32[]{:S(2)}) collective-permute-start(f32[128,1,128]{2,1,0:T(1,128)S(1)} %get-tuple-element.19), channel_id=1, source_target_pairs={{0,32},{32,64},{64,96},{1,33},{33,65},{65,97},{2,34},{34,66},{66,9... | collective-permute-start | bytes 196616 | tf_op jit(solution)/shard_map/ppermute | solution.py:91
  7.7 6.5 %copy-start.13 = (s32[1,4096,1]{1,2,0:T(1,128)S(1)}, s32[1,4096,1]{1,2,0:T(1,128)}, u32[]{:S(2)}) copy-start(s32[1,4096,1]{1,2,0:T(1,128)} %param.10) | copy-start | bytes 49156
  10.6 4.3 %collective-permute-start.2 = (f32[4,32,32]{2,1,0:T(8,128)S(1)}, f32[4,32,32]{2,1,0:T(8,128)S(1)}, u32[]{:S(2)}, u32[]{:S(2)}) collective-permute-start(f32[4,32,32]{2,1,0:T(8,128)S(1)} %bitcast.74), channel_id=1, source_target_pairs={{1,0},{2,1},{3,2},{4,3},{5,4},{6,5},{7,6},{8,7},{9,8},{10,9},{11,1... | collective-permute-start | bytes 49160 | tf_op jit(solution)/shard_map/ppermute | solution.py:92
  11.8 5.2 %collective-permute-start.3 = (f32[4,32,32]{2,1,0:T(8,128)S(1)}, f32[4,32,32]{2,1,0:T(8,128)S(1)}, u32[]{:S(2)}, u32[]{:S(2)}) collective-permute-start(f32[4,32,32]{2,1,0:T(8,128)S(1)} %bitcast.76), channel_id=1, source_target_pairs={{0,1},{1,2},{2,3},{3,4},{4,5},{5,6},{6,7},{7,8},{8,9},{9,10},{10,1... | collective-permute-start | bytes 49160 | tf_op jit(solution)/shard_map/ppermute | solution.py:93
  14.9 2.2 %copy-start.7 = (f32[4,32,32]{2,1,0:T(8,128)}, f32[4,32,32]{2,1,0:T(8,128)S(1)}, u32[]{:S(2)}) copy-start(f32[4,32,32]{2,1,0:T(8,128)S(1)} %collective-permute-done.2.he_ref) | copy-start | bytes 49156
  17.0 0.6 copy-start.9
  17.0 0.6 copy-start.5
  17.0 0.7 copy-start.6
  25.5 12.7 %collective-permute-start.6 = (f32[4,32,32]{2,1,0:T(8,128)S(1)}, f32[4,32,32]{2,1,0:T(8,128)S(1)}, u32[]{:S(2)}, u32[]{:S(2)}) collective-permute-start(f32[4,32,32]{2,1,0:T(8,128)S(1)} %bitcast.75), channel_id=1, source_target_pairs={{1,0},{2,1},{3,2},{4,3},{5,4},{6,5},{7,6},{8,7},{9,8},{10,9},{11,1... | collective-permute-start | bytes 49160 | tf_op jit(solution)/shard_map/ppermute | solution.py:92
  32.0 6.2 %collective-permute-start.7 = (f32[4,32,32]{2,1,0:T(8,128)S(1)}, f32[4,32,32]{2,1,0:T(8,128)S(1)}, u32[]{:S(2)}, u32[]{:S(2)}) collective-permute-start(f32[4,32,32]{2,1,0:T(8,128)S(1)} %bitcast.77), channel_id=1, source_target_pairs={{0,1},{1,2},{2,3},{3,4},{4,5},{5,6},{6,7},{7,8},{8,9},{9,10},{10,1... | collective-permute-start | bytes 49160 | tf_op jit(solution)/shard_map/ppermute | solution.py:93
  32.1 6.1 %collective-permute-start.4 = (f32[128,1,128]{2,1,0:T(1,128)}, f32[128,1,128]{2,1,0:T(1,128)S(1)}, u32[]{:S(2)}, u32[]{:S(2)}) collective-permute-start(f32[128,1,128]{2,1,0:T(1,128)} %get-tuple-element.10), channel_id=1, source_target_pairs={{32,0},{64,32},{96,64},{33,1},{65,33},{97,65},{34,2},{66,34},{98,6... | collective-permute-start | bytes 196616 | tf_op jit(solution)/shard_map/ppermute | solution.py:90
  33.4 5.8 %collective-permute-start.5 = (f32[128,1,128]{2,1,0:T(1,128)}, f32[128,1,128]{2,1,0:T(1,128)S(1)}, u32[]{:S(2)}, u32[]{:S(2)}) collective-permute-start(f32[128,1,128]{2,1,0:T(1,128)} %get-tuple-element.11), channel_id=1, source_target_pairs={{0,32},{32,64},{64,96},{1,33},{33,65},{65,97},{2,34},{34,66},{66,9... | collective-permute-start | bytes 196616 | tf_op jit(solution)/shard_map/ppermute | solution.py:91
  38.2 1.0 copy-start.8
  38.2 1.0 copy-start.10
  38.2 1.0 copy-start.11
  39.2 0.6 copy-start.12
  81.0 8.1 %copy-start.1 = (bf16[128,32,128]{0,2,1:T(8,128)(2,1)}, bf16[128,32,128]{0,2,1:T(8,128)(2,1)S(1)}, u32[]{:S(2)}) copy-start(bf16[128,32,128]{0,2,1:T(8,128)(2,1)S(1)} %all_to_all.20) | copy-start | bytes 3145732
  81.0 24.4 %all-to-all-start.2 = ((bf16[128,32,128]{0,2,1:T(8,128)(2,1)}), bf16[128,32,128]{0,2,1:T(8,128)(2,1)S(1)}, u32[]{:S(2)}, u32[]{:S(2)}) async-start(bf16[128,32,128]{0,2,1:T(8,128)(2,1)} %get-tuple-element.18), calls=%async_computation.2 | async-start | bytes 2097152 | tf_op jit(solution)/shard_map/all_to_all | solution.py:361
  85.0 2.7 %copy-start.3 = (bf16[1,512,128]{2,1,0:T(8,128)(2,1)S(1)}, bf16[1,512,128]{2,1,0:T(8,128)(2,1)}, u32[]{:S(2)}) copy-start(bf16[1,512,128]{2,1,0:T(8,128)(2,1)} %param.11) | copy-start | bytes 393220
  85.0 3.4 %copy-start.4 = (bf16[1,128,512]{2,1,0:T(8,128)(2,1)S(1)}, bf16[1,128,512]{2,1,0:T(8,128)(2,1)}, u32[]{:S(2)}) copy-start(bf16[1,128,512]{2,1,0:T(8,128)(2,1)} %param.13) | copy-start | bytes 393220
  105.4 8.7 %copy-start = (bf16[128,32,128]{0,2,1:T(8,128)(2,1)}, bf16[128,32,128]{0,2,1:T(8,128)(2,1)S(1)}, u32[]{:S(2)}) copy-start(bf16[128,32,128]{0,2,1:T(8,128)(2,1)S(1)} %all-to-all-done.2) | copy-start | bytes 3145732
  105.4 24.3 %all-to-all-start.1 = ((bf16[128,32,128]{0,2,1:T(8,128)(2,1)}), bf16[128,32,128]{0,2,1:T(8,128)(2,1)S(1)}, u32[]{:S(2)}, u32[]{:S(2)}) async-start(bf16[128,32,128]{0,2,1:T(8,128)(2,1)} %bitcast.67), calls=%async_computation.1 | async-start | bytes 2097152 | tf_op jit(solution)/shard_map/all_to_all | solution.py:365

commit v18 on v15

--- a/solution.py
+++ b/solution.py
@@ -100,7 +100,8 @@
     which = lax.broadcasted_iota(jnp.int32, (cols, 2), 1)
     pick = (lane == which * (cols - 1)).astype(jnp.float32)
     ends = jnp.dot(x.reshape(feats * rows, cols), pick, precision=lax.Precision.HIGHEST)
-    return x[:, :1, :], x[:, rows - 1:, :], ends.T
+    ends_t, top, bottom = lax.optimization_barrier((ends.T, x[:, :1, :], x[:, rows - 1:, :]))
+    return top, bottom, ends_t
 
 
 def positions(targets_all, experts):

time: 161 us -> 162 us (level)
  blocking collectives: 39 us -> 43 us
  Pallas kernels: 51.3 us -> 49.1 us
  waiting for transfers between devices: 27.2 us -> 25.1 us
  starting transfers between devices: 27 us -> 28.9 us
    all_to_all x1, starting transfers between devices: 6.49 us -> 10.6 us  [local(): lax.all_to_all(part, 'lon', split_axis=1, concat_axis=1, tiled=True)]
    all_to_all x1, blocking collectives: 39 us -> 43 us  [local(): lax.all_to_all(result.reshape(features, experts, width), 'lon', split_axi...]
    pallas_call x1, Pallas kernels: 18.6 us -> 16.4 us  [network(): pl.pallas_call(network_kernel, grid_spec=pltpu.PrefetchScalarGridSpec(num...]
    ppermute x2, waiting for transfers between devices: 2.13 us -> 0.01 us  [exchange(): lax.ppermute(columns_of(ends[1].reshape(feats, rows)), 'lon', lon_forward)]
    ppermute x2, starting transfers between devices: 7.37 us -> 5.56 us  [exchange(): lax.ppermute(columns_of(ends[0].reshape(feats, rows)), 'lon', lon_backward)]
  transfers between devices with their start and end apart: 9 -> 9, of which waited for: 4 -> 2; matrix products, arithmetic and copies ran while one was open for 6% -> 4% of each run, Pallas kernels for 0% -> 0%
where the time goes in v18:
time: 162 us
  Pallas kernels  49.1 us (30%)
  blocking collectives  43 us (27%)
  starting transfers between devices  28.9 us (18%)
  waiting for transfers between devices  25.1 us (15%)
  local copies, waits for them, and re-layouts  9.56 us (6%)
  matrix products  2.92 us (2%)
  other arithmetic  2.69 us (2%)
    all_to_all x1, blocking collectives, local(): lax.all_to_all(result.reshape(features, experts, width), 'lon', split_axi...  43 us
    all_to_all x1, waiting for transfers between devices, local(): lax.all_to_all(part, 'lon', split_axis=1, concat_axis=1, tiled=True)  24.1 us
    pallas_call x1, Pallas kernels, network(): pl.pallas_call(network_kernel, grid_spec=pltpu.PrefetchScalarGridSpec(num...  16.4 us
    pallas_call x2, Pallas kernels, sweep(): pl.pallas_call(sweep_kernel, grid=(nb,), in_specs=[big, edge_row, edge_ro...  12.7 us
    pallas_call x1, Pallas kernels, combine(): pl.pallas_call(combine_kernel, grid_spec=pltpu.PrefetchScalarGridSpec(num...  10.7 us
    all_to_all x1, starting transfers between devices, local(): lax.all_to_all(part, 'lon', split_axis=1, concat_axis=1, tiled=True)  10.6 us
    pallas_call x1, Pallas kernels, pack(): pl.pallas_call(pack_kernel, grid_spec=pltpu.PrefetchScalarGridSpec(num_sc...  9.29 us
    ppermute x2, starting transfers between devices, exchange(): hs = lax.ppermute(bottom, 'lat', lat_forward)  8.79 us
  transfers between devices with their start and end apart: 9, of which 2 were waited for; matrix products, arithmetic and copies ran while one was open for 4% of the time, Pallas kernels for 0%

profile of v18, /device:TPU:1, one launch (start us, length us, event | category | flops | bytes accessed | tf_op | source)
XLA Modules:
  0.0 161.5 jit_solution(18270168932432932849)
XLA Ops:
  0.0 1.4 fusion.11
  1.4 2.6 %fusion.8 = f32[2,4096]{1,0:T(2,128)S(1)} fusion(f32[4096,128]{1,0:T(8,128)} %bitcast.50, s32[2]{0:T(128)S(1)} %iota_multiply_fusion), kind=kOutput, calls=%fused_computation.15 | convolution fusion | flops 12583424 | bytes 2129928 | tf_op jit(solution)/shard_map/dot_general | solution.py:102
  4.3 1.5 collective-permute-start.2
  6.0 1.3 collective-permute-start.3
  7.3 1.3 collective-permute-start
  8.6 4.2 %collective-permute-start.1 = (f32[128,1,128]{2,1,0:T(1,128)S(1)}, f32[128,1,128]{2,1,0:T(1,128)S(1)}, u32[]{:S(2)}, u32[]{:S(2)}) collective-permute-start(f32[128,1,128]{2,1,0:T(1,128)S(1)} %get-tuple-element.13), channel_id=1, source_target_pairs={{0,32},{32,64},{64,96},{1,33},{33,65},{65,97},{2,34},{34,66},{66,9... | collective-permute-start | bytes 196616 | tf_op jit(solution)/shard_map/ppermute | solution.py:91
  12.8 1.1 slice_bitcast_fusion
  15.1 6.7 %shard_map.73 = (f32[128,32,128]{2,1,0:T(8,128)}, f32[128,1,128]{2,1,0:T(1,128)}, f32[128,1,128]{2,1,0:T(1,128)}, f32[2,4096]{1,0:T(2,128)}) custom-call(f32[128,32,128]{2,1,0:T(8,128)} %bitcast.51, f32[128,1,128]{2,1,0:T(1,128)} %copy-done.7, f32[128,1,128]{2,1,0:T(1,128)} %copy-done.8, f32[4,32,32]{2,1,0:T(8,128)} %copy-done.4, f32[4,32,32]{2,1,0:T(8,128)} %copy-done.5, ...), custom_call_target="tpu_custom_call" | custom-call | flops 10485760 | bytes 5767168 | tf_op jit(solution)/shard_map/pallas_call | solution.py:72
  21.9 0.9 slice_reduce_fusion
  23.0 4.1 %collective-permute-start.6 = (f32[4,32,32]{2,1,0:T(8,128)S(1)}, f32[4,32,32]{2,1,0:T(8,128)S(1)}, u32[]{:S(2)}, u32[]{:S(2)}) collective-permute-start(f32[4,32,32]{2,1,0:T(8,128)S(1)} %bitcast.62), channel_id=1, source_target_pairs={{1,0},{2,1},{3,2},{4,3},{5,4},{6,5},{7,6},{8,7},{9,8},{10,9},{11,1... | collective-permute-start | bytes 49160 | tf_op jit(solution)/shard_map/ppermute | solution.py:92
  27.3 1.3 collective-permute-start.4
  28.6 4.6 %collective-permute-start.5 = (f32[128,1,128]{2,1,0:T(1,128)}, f32[128,1,128]{2,1,0:T(1,128)S(1)}, u32[]{:S(2)}, u32[]{:S(2)}) collective-permute-start(f32[128,1,128]{2,1,0:T(1,128)} %get-tuple-element.17), channel_id=1, source_target_pairs={{0,32},{32,64},{64,96},{1,33},{33,65},{65,97},{2,34},{34,66},{66,9... | collective-permute-start | bytes 196616 | tf_op jit(solution)/shard_map/ppermute | solution.py:91
  33.9 1.0 collective-permute-done.5.hs_ref
  35.5 6.0 %shard_map.74.cur_ref = f32[128,32,128]{2,1,0:T(8,128)} custom-call(f32[128,32,128]{2,1,0:T(8,128)} %get-tuple-element.15.q_ref, f32[128,1,128]{2,1,0:T(1,128)} %copy-done.10, f32[128,1,128]{2,1,0:T(1,128)} %copy-done.11, f32[4,32,32]{2,1,0:T(8,128)} %copy-done.6, f32[4,32,32]{2,1,0:T(8,128)} %copy-done.9, f32[32,32,128]{2,1,0:T(8,128)} %get-tuple-element.26.u_ref, ...), custom_call_target="tpu_custom_call" | custom-call | flops 10485760 | bytes 5767168 | tf_op jit(solution)/shard_map/pallas_call | solution.py:72
  41.4 9.3 %shard_map.75 = bf16[8192,128]{1,0:T(8,128)(2,1)} custom-call(s32[4096]{0:T(1024)} %bitcast_add_fusion.t_ref, f32[128,32,128]{2,1,0:T(8,128)} %shard_map.74.cur_ref), custom_call_target="tpu_custom_call" | custom-call | tf_op jit(solution)/shard_map/pallas_call | solution.py:290
  50.7 10.6 %all-to-all-start = ((bf16[128,32,256]{0,2,1:T(8,128)(2,1)}), bf16[128,32,256]{0,2,1:T(8,128)(2,1)S(1)}, u32[]{:S(2)}, u32[]{:S(2)}) async-start(bf16[128,32,256]{0,2,1:T(8,128)(2,1)} %bitcast.54), calls=%async_computation | async-start | bytes 4194304 | tf_op jit(solution)/shard_map/all_to_all | solution.py:362
  61.3 2.7 %copy.23 = bf16[1,3,512,512]{2,3,1,0:T(8,128)(2,1)} copy(bf16[1,3,512,512]{3,2,1,0:T(8,128)(2,1)} %param.12) | data formatting | bytes 3145728 | tf_op args[5]
  64.0 0.8 copy.22
  64.8 0.8 copy.24
  65.5 24.1 %all-to-all-done = bf16[128,32,256]{0,2,1:T(8,128)(2,1)S(1)} async-done(((bf16[128,32,256]{0,2,1:T(8,128)(2,1)}), bf16[128,32,256]{0,2,1:T(8,128)(2,1)S(1)}, u32[]{:S(2)}, u32[]{:S(2)}) %all-to-all-start) | async-done | bytes 2097184 | tf_op jit(solution)/shard_map/all_to_all | solution.py:362
  89.6 1.2 compare_reduce_fusion
  91.4 16.4 %shard_map.76 = bf16[8192,128]{1,0:T(8,128)(2,1)} custom-call(s32[64]{0:T(128)} %convert_element_type.23.nonzero_ref, bf16[8192,128]{1,0:T(8,128)(2,1)} %bitcast.53, bf16[128,512]{1,0:T(8,128)(2,1)} %bitcast.57, bf16[3,512,512]{2,1,0:T(8,128)(2,1)} %bitcast.56, bf16[512,128]{1,0:T(8,128)(2,1)} %bitcast.58), custom_call_target="tpu_custom_call" | custom-call | flops 15032385536 | bytes 6029312 | tf_op jit(solution)/shard_map/pallas_call | solution.py:238
  107.8 43.0 %all_to_all.10 = bf16[128,32,256]{0,2,1:T(8,128)(2,1)} all-to-all(bf16[128,32,256]{0,2,1:T(8,128)(2,1)} %bitcast.55), channel_id=1, replica_groups=mesh['lat'=4,'lon'=32] {'lon'}, dimensions={1} | all-to-all | bytes 4194304 | tf_op jit(solution)/shard_map/all_to_all | solution.py:366
  150.8 10.7 %shard_map.77 = f32[128,32,128]{2,1,0:T(8,128)} custom-call(s32[4096]{0:T(1024)} %bitcast_add_fusion.t_ref, bf16[8192,128]{1,0:T(8,128)(2,1)} %bitcast.52, f32[128,32,128]{2,1,0:T(8,128)} %shard_map.74.cur_ref), custom_call_target="tpu_custom_call" | custom-call | tf_op jit(solution)/shard_map/pallas_call | solution.py:321
  (52 shorter events, 3.9 us)
Async XLA Ops:
  0.0 12.8 %copy-start.1 = (f32[2,32,32,128]{3,2,1,0:T(8,128)S(1)}, f32[2,32,32,128]{3,2,1,0:T(8,128)}, u32[]{:S(2)}) copy-start(f32[2,32,32,128]{3,2,1,0:T(8,128)} %param.8) | copy-start | bytes 3145732
  1.4 12.5 %copy-start.12 = (s32[1,4096,1]{1,2,0:T(1,128)S(1)}, s32[1,4096,1]{1,2,0:T(1,128)}, u32[]{:S(2)}) copy-start(s32[1,4096,1]{1,2,0:T(1,128)} %param.10) | copy-start | bytes 49156
  4.3 10.1 %collective-permute-start.2 = (f32[4,32,32]{2,1,0:T(8,128)S(1)}, f32[4,32,32]{2,1,0:T(8,128)S(1)}, u32[]{:S(2)}, u32[]{:S(2)}) collective-permute-start(f32[4,32,32]{2,1,0:T(8,128)S(1)} %bitcast.60), channel_id=1, source_target_pairs={{1,0},{2,1},{3,2},{4,3},{5,4},{6,5},{7,6},{8,7},{9,8},{10,9},{11,1... | collective-permute-start | bytes 49160 | tf_op jit(solution)/shard_map/ppermute | solution.py:92
  6.0 8.5 %collective-permute-start.3 = (f32[4,32,32]{2,1,0:T(8,128)S(1)}, f32[4,32,32]{2,1,0:T(8,128)S(1)}, u32[]{:S(2)}, u32[]{:S(2)}) collective-permute-start(f32[4,32,32]{2,1,0:T(8,128)S(1)} %bitcast.61), channel_id=1, source_target_pairs={{0,1},{1,2},{2,3},{3,4},{4,5},{5,6},{6,7},{7,8},{8,9},{9,10},{10,1... | collective-permute-start | bytes 49160 | tf_op jit(solution)/shard_map/ppermute | solution.py:93
  7.3 7.2 %collective-permute-start = (f32[128,1,128]{2,1,0:T(1,128)S(1)}, f32[128,1,128]{2,1,0:T(1,128)S(1)}, u32[]{:S(2)}, u32[]{:S(2)}) collective-permute-start(f32[128,1,128]{2,1,0:T(1,128)S(1)} %get-tuple-element.12), channel_id=1, source_target_pairs={{32,0},{64,32},{96,64},{33,1},{65,33},{97,65},{34,2},{66,34},{98,6... | collective-permute-start | bytes 196616 | tf_op jit(solution)/shard_map/ppermute | solution.py:90
  8.6 5.9 %collective-permute-start.1 = (f32[128,1,128]{2,1,0:T(1,128)S(1)}, f32[128,1,128]{2,1,0:T(1,128)S(1)}, u32[]{:S(2)}, u32[]{:S(2)}) collective-permute-start(f32[128,1,128]{2,1,0:T(1,128)S(1)} %get-tuple-element.13), channel_id=1, source_target_pairs={{0,32},{32,64},{64,96},{1,33},{33,65},{65,97},{2,34},{34,66},{66,9... | collective-permute-start | bytes 196616 | tf_op jit(solution)/shard_map/ppermute | solution.py:91
  14.5 0.6 copy-start.4
  14.5 0.6 copy-start.5
  14.5 0.6 copy-start.7
  14.5 0.6 copy-start.8
  23.0 10.8 %collective-permute-start.6 = (f32[4,32,32]{2,1,0:T(8,128)S(1)}, f32[4,32,32]{2,1,0:T(8,128)S(1)}, u32[]{:S(2)}, u32[]{:S(2)}) collective-permute-start(f32[4,32,32]{2,1,0:T(8,128)S(1)} %bitcast.62), channel_id=1, source_target_pairs={{1,0},{2,1},{3,2},{4,3},{5,4},{6,5},{7,6},{8,7},{9,8},{10,9},{11,1... | collective-permute-start | bytes 49160 | tf_op jit(solution)/shard_map/ppermute | solution.py:92
  27.2 6.6 %collective-permute-start.7 = (f32[4,32,32]{2,1,0:T(8,128)S(1)}, f32[4,32,32]{2,1,0:T(8,128)S(1)}, u32[]{:S(2)}, u32[]{:S(2)}) collective-permute-start(f32[4,32,32]{2,1,0:T(8,128)S(1)} %bitcast.63), channel_id=1, source_target_pairs={{0,1},{1,2},{2,3},{3,4},{4,5},{5,6},{6,7},{7,8},{8,9},{9,10},{10,1... | collective-permute-start | bytes 49160 | tf_op jit(solution)/shard_map/ppermute | solution.py:93
  27.3 6.6 %collective-permute-start.4 = (f32[128,1,128]{2,1,0:T(1,128)}, f32[128,1,128]{2,1,0:T(1,128)S(1)}, u32[]{:S(2)}, u32[]{:S(2)}) collective-permute-start(f32[128,1,128]{2,1,0:T(1,128)} %get-tuple-element.16), channel_id=1, source_target_pairs={{32,0},{64,32},{96,64},{33,1},{65,33},{97,65},{34,2},{66,34},{98,6... | collective-permute-start | bytes 196616 | tf_op jit(solution)/shard_map/ppermute | solution.py:90
  28.6 6.2 %collective-permute-start.5 = (f32[128,1,128]{2,1,0:T(1,128)}, f32[128,1,128]{2,1,0:T(1,128)S(1)}, u32[]{:S(2)}, u32[]{:S(2)}) collective-permute-start(f32[128,1,128]{2,1,0:T(1,128)} %get-tuple-element.17), channel_id=1, source_target_pairs={{0,32},{32,64},{64,96},{1,33},{33,65},{65,97},{2,34},{34,66},{66,9... | collective-permute-start | bytes 196616 | tf_op jit(solution)/shard_map/ppermute | solution.py:91
  33.8 1.0 copy-start.6
  33.8 1.0 copy-start.9
  33.9 1.0 copy-start.10
  34.9 0.6 copy-start.11
  50.7 38.9 %all-to-all-start = ((bf16[128,32,256]{0,2,1:T(8,128)(2,1)}), bf16[128,32,256]{0,2,1:T(8,128)(2,1)S(1)}, u32[]{:S(2)}, u32[]{:S(2)}) async-start(bf16[128,32,256]{0,2,1:T(8,128)(2,1)} %bitcast.54), calls=%async_computation | async-start | bytes 4194304 | tf_op jit(solution)/shard_map/all_to_all | solution.py:362
  61.3 2.7 %copy-start.2 = (bf16[1,512,128]{2,1,0:T(8,128)(2,1)S(1)}, bf16[1,512,128]{2,1,0:T(8,128)(2,1)}, u32[]{:S(2)}) copy-start(bf16[1,512,128]{2,1,0:T(8,128)(2,1)} %param.11) | copy-start | bytes 393220
  61.3 3.5 %copy-start.3 = (bf16[1,128,512]{2,1,0:T(8,128)(2,1)S(1)}, bf16[1,128,512]{2,1,0:T(8,128)(2,1)}, u32[]{:S(2)}) copy-start(bf16[1,128,512]{2,1,0:T(8,128)(2,1)} %param.13) | copy-start | bytes 393220
  89.6 1.8 %copy-start = (bf16[128,32,256]{0,2,1:T(8,128)(2,1)}, bf16[128,32,256]{0,2,1:T(8,128)(2,1)S(1)}, u32[]{:S(2)}) copy-start(bf16[128,32,256]{0,2,1:T(8,128)(2,1)S(1)} %all-to-all-done) | copy-start | bytes 6291460

commit v19 on v18

--- a/solution.py
+++ b/solution.py
@@ -121,7 +121,7 @@
     return position.reshape(count).astype(jnp.int32)
 
 
-ROWS = 1024
+ROWS = 2048
 HALF = 128
 
 

time: 162 us -> 161 us (level)
  blocking collectives: 43 us -> 37.3 us
  Pallas kernels: 49.1 us -> 53.4 us
    all_to_all x1, blocking collectives: 43 us -> 37.3 us  [local(): lax.all_to_all(result.reshape(features, experts, width), 'lon', split_axi...]
    pallas_call x1, Pallas kernels: 16.4 us -> 20.7 us  [network(): pl.pallas_call(network_kernel, grid_spec=pltpu.PrefetchScalarGridSpec(num...]
where the time goes in v19:
time: 161 us; the launch traced here: 160 us
  Pallas kernels  53.4 us (33%)
  blocking collectives  37.3 us (23%)
  starting transfers between devices  28.9 us (18%)
  waiting for transfers between devices  25.1 us (16%)
  local copies, waits for them, and re-layouts  9.56 us (6%)
  matrix products  2.92 us (2%)
  other arithmetic  2.69 us (2%)
    all_to_all x1, blocking collectives, local(): lax.all_to_all(result.reshape(features, experts, width), 'lon', split_axi...  37.3 us
    all_to_all x1, waiting for transfers between devices, local(): lax.all_to_all(part, 'lon', split_axis=1, concat_axis=1, tiled=True)  24.1 us
    pallas_call x1, Pallas kernels, network(): pl.pallas_call(network_kernel, grid_spec=pltpu.PrefetchScalarGridSpec(num...  20.7 us
    pallas_call x2, Pallas kernels, sweep(): pl.pallas_call(sweep_kernel, grid=(nb,), in_specs=[big, edge_row, edge_ro...  12.7 us
    pallas_call x1, Pallas kernels, combine(): pl.pallas_call(combine_kernel, grid_spec=pltpu.PrefetchScalarGridSpec(num...  10.7 us
    all_to_all x1, starting transfers between devices, local(): lax.all_to_all(part, 'lon', split_axis=1, concat_axis=1, tiled=True)  10.6 us
    pallas_call x1, Pallas kernels, pack(): pl.pallas_call(pack_kernel, grid_spec=pltpu.PrefetchScalarGridSpec(num_sc...  9.29 us
    ppermute x2, starting transfers between devices, exchange(): hs = lax.ppermute(bottom, 'lat', lat_forward)  8.79 us
  transfers between devices with their start and end apart: 9, of which 2 were waited for; matrix products, arithmetic and copies ran while one was open for 4% of the time, Pallas kernels for 0%

profile of v19, /device:TPU:1, one launch (start us, length us, event | category | flops | bytes accessed | tf_op | source)
XLA Modules:
  0.0 160.2 jit_solution(2033403618934964970)
XLA Ops:
  0.0 1.4 fusion.11
  1.4 2.6 %fusion.8 = f32[2,4096]{1,0:T(2,128)S(1)} fusion(f32[4096,128]{1,0:T(8,128)} %bitcast.50, s32[2]{0:T(128)S(1)} %iota_multiply_fusion), kind=kOutput, calls=%fused_computation.15 | convolution fusion | flops 12583424 | bytes 2129928 | tf_op jit(solution)/shard_map/dot_general | solution.py:102
  4.3 1.5 collective-permute-start.2
  6.0 1.3 collective-permute-start.3
  7.3 1.3 collective-permute-start
  8.6 4.2 %collective-permute-start.1 = (f32[128,1,128]{2,1,0:T(1,128)S(1)}, f32[128,1,128]{2,1,0:T(1,128)S(1)}, u32[]{:S(2)}, u32[]{:S(2)}) collective-permute-start(f32[128,1,128]{2,1,0:T(1,128)S(1)} %get-tuple-element.13), channel_id=1, source_target_pairs={{0,32},{32,64},{64,96},{1,33},{33,65},{65,97},{2,34},{34,66},{66,9... | collective-permute-start | bytes 196616 | tf_op jit(solution)/shard_map/ppermute | solution.py:91
  12.8 1.1 slice_bitcast_fusion
  15.1 6.7 %shard_map.73 = (f32[128,32,128]{2,1,0:T(8,128)}, f32[128,1,128]{2,1,0:T(1,128)}, f32[128,1,128]{2,1,0:T(1,128)}, f32[2,4096]{1,0:T(2,128)}) custom-call(f32[128,32,128]{2,1,0:T(8,128)} %bitcast.51, f32[128,1,128]{2,1,0:T(1,128)} %copy-done.7, f32[128,1,128]{2,1,0:T(1,128)} %copy-done.8, f32[4,32,32]{2,1,0:T(8,128)} %copy-done.4, f32[4,32,32]{2,1,0:T(8,128)} %copy-done.5, ...), custom_call_target="tpu_custom_call" | custom-call | flops 10485760 | bytes 5767168 | tf_op jit(solution)/shard_map/pallas_call | solution.py:72
  21.9 0.9 slice_reduce_fusion
  23.0 4.1 %collective-permute-start.6 = (f32[4,32,32]{2,1,0:T(8,128)S(1)}, f32[4,32,32]{2,1,0:T(8,128)S(1)}, u32[]{:S(2)}, u32[]{:S(2)}) collective-permute-start(f32[4,32,32]{2,1,0:T(8,128)S(1)} %bitcast.62), channel_id=1, source_target_pairs={{1,0},{2,1},{3,2},{4,3},{5,4},{6,5},{7,6},{8,7},{9,8},{10,9},{11,1... | collective-permute-start | bytes 49160 | tf_op jit(solution)/shard_map/ppermute | solution.py:92
  27.3 1.3 collective-permute-start.4
  28.6 4.6 %collective-permute-start.5 = (f32[128,1,128]{2,1,0:T(1,128)}, f32[128,1,128]{2,1,0:T(1,128)S(1)}, u32[]{:S(2)}, u32[]{:S(2)}) collective-permute-start(f32[128,1,128]{2,1,0:T(1,128)} %get-tuple-element.17), channel_id=1, source_target_pairs={{0,32},{32,64},{64,96},{1,33},{33,65},{65,97},{2,34},{34,66},{66,9... | collective-permute-start | bytes 196616 | tf_op jit(solution)/shard_map/ppermute | solution.py:91
  33.9 1.0 collective-permute-done.5.hs_ref
  35.5 6.0 %shard_map.74.cur_ref = f32[128,32,128]{2,1,0:T(8,128)} custom-call(f32[128,32,128]{2,1,0:T(8,128)} %get-tuple-element.15.q_ref, f32[128,1,128]{2,1,0:T(1,128)} %copy-done.10, f32[128,1,128]{2,1,0:T(1,128)} %copy-done.11, f32[4,32,32]{2,1,0:T(8,128)} %copy-done.6, f32[4,32,32]{2,1,0:T(8,128)} %copy-done.9, f32[32,32,128]{2,1,0:T(8,128)} %get-tuple-element.26.u_ref, ...), custom_call_target="tpu_custom_call" | custom-call | flops 10485760 | bytes 5767168 | tf_op jit(solution)/shard_map/pallas_call | solution.py:72
  41.4 9.3 %shard_map.75 = bf16[8192,128]{1,0:T(8,128)(2,1)} custom-call(s32[4096]{0:T(1024)} %bitcast_add_fusion.t_ref, f32[128,32,128]{2,1,0:T(8,128)} %shard_map.74.cur_ref), custom_call_target="tpu_custom_call" | custom-call | tf_op jit(solution)/shard_map/pallas_call | solution.py:290
  50.7 10.6 %all-to-all-start = ((bf16[128,32,256]{0,2,1:T(8,128)(2,1)}), bf16[128,32,256]{0,2,1:T(8,128)(2,1)S(1)}, u32[]{:S(2)}, u32[]{:S(2)}) async-start(bf16[128,32,256]{0,2,1:T(8,128)(2,1)} %bitcast.54), calls=%async_computation | async-start | bytes 4194304 | tf_op jit(solution)/shard_map/all_to_all | solution.py:362
  61.3 2.7 %copy.23 = bf16[1,3,512,512]{2,3,1,0:T(8,128)(2,1)} copy(bf16[1,3,512,512]{3,2,1,0:T(8,128)(2,1)} %param.12) | data formatting | bytes 3145728 | tf_op args[5]
  64.0 0.8 copy.22
  64.8 0.8 copy.24
  65.5 24.1 %all-to-all-done = bf16[128,32,256]{0,2,1:T(8,128)(2,1)S(1)} async-done(((bf16[128,32,256]{0,2,1:T(8,128)(2,1)}), bf16[128,32,256]{0,2,1:T(8,128)(2,1)S(1)}, u32[]{:S(2)}, u32[]{:S(2)}) %all-to-all-start) | async-done | bytes 2097184 | tf_op jit(solution)/shard_map/all_to_all | solution.py:362
  89.6 1.2 compare_reduce_fusion
  91.4 20.7 %shard_map.76 = bf16[8192,128]{1,0:T(8,128)(2,1)} custom-call(s32[64]{0:T(128)} %convert_element_type.23.nonzero_ref, bf16[8192,128]{1,0:T(8,128)(2,1)} %bitcast.53, bf16[128,512]{1,0:T(8,128)(2,1)} %bitcast.57, bf16[3,512,512]{2,1,0:T(8,128)(2,1)} %bitcast.56, bf16[512,128]{1,0:T(8,128)(2,1)} %bitcast.58), custom_call_target="tpu_custom_call" | custom-call | flops 15032385536 | bytes 6029312 | tf_op jit(solution)/shard_map/pallas_call | solution.py:238
  112.1 37.3 %all_to_all.10 = bf16[128,32,256]{0,2,1:T(8,128)(2,1)} all-to-all(bf16[128,32,256]{0,2,1:T(8,128)(2,1)} %bitcast.55), channel_id=1, replica_groups=mesh['lat'=4,'lon'=32] {'lon'}, dimensions={1} | all-to-all | bytes 4194304 | tf_op jit(solution)/shard_map/all_to_all | solution.py:366
  149.4 10.7 %shard_map.77 = f32[128,32,128]{2,1,0:T(8,128)} custom-call(s32[4096]{0:T(1024)} %bitcast_add_fusion.t_ref, bf16[8192,128]{1,0:T(8,128)(2,1)} %bitcast.52, f32[128,32,128]{2,1,0:T(8,128)} %shard_map.74.cur_ref), custom_call_target="tpu_custom_call" | custom-call | tf_op jit(solution)/shard_map/pallas_call | solution.py:321
  (52 shorter events, 3.9 us)
Async XLA Ops:
  0.0 12.8 %copy-start.1 = (f32[2,32,32,128]{3,2,1,0:T(8,128)S(1)}, f32[2,32,32,128]{3,2,1,0:T(8,128)}, u32[]{:S(2)}) copy-start(f32[2,32,32,128]{3,2,1,0:T(8,128)} %param.8) | copy-start | bytes 3145732
  1.4 12.5 %copy-start.12 = (s32[1,4096,1]{1,2,0:T(1,128)S(1)}, s32[1,4096,1]{1,2,0:T(1,128)}, u32[]{:S(2)}) copy-start(s32[1,4096,1]{1,2,0:T(1,128)} %param.10) | copy-start | bytes 49156
  4.3 10.1 %collective-permute-start.2 = (f32[4,32,32]{2,1,0:T(8,128)S(1)}, f32[4,32,32]{2,1,0:T(8,128)S(1)}, u32[]{:S(2)}, u32[]{:S(2)}) collective-permute-start(f32[4,32,32]{2,1,0:T(8,128)S(1)} %bitcast.60), channel_id=1, source_target_pairs={{1,0},{2,1},{3,2},{4,3},{5,4},{6,5},{7,6},{8,7},{9,8},{10,9},{11,1... | collective-permute-start | bytes 49160 | tf_op jit(solution)/shard_map/ppermute | solution.py:92
  6.0 8.5 %collective-permute-start.3 = (f32[4,32,32]{2,1,0:T(8,128)S(1)}, f32[4,32,32]{2,1,0:T(8,128)S(1)}, u32[]{:S(2)}, u32[]{:S(2)}) collective-permute-start(f32[4,32,32]{2,1,0:T(8,128)S(1)} %bitcast.61), channel_id=1, source_target_pairs={{0,1},{1,2},{2,3},{3,4},{4,5},{5,6},{6,7},{7,8},{8,9},{9,10},{10,1... | collective-permute-start | bytes 49160 | tf_op jit(solution)/shard_map/ppermute | solution.py:93
  7.3 7.2 %collective-permute-start = (f32[128,1,128]{2,1,0:T(1,128)S(1)}, f32[128,1,128]{2,1,0:T(1,128)S(1)}, u32[]{:S(2)}, u32[]{:S(2)}) collective-permute-start(f32[128,1,128]{2,1,0:T(1,128)S(1)} %get-tuple-element.12), channel_id=1, source_target_pairs={{32,0},{64,32},{96,64},{33,1},{65,33},{97,65},{34,2},{66,34},{98,6... | collective-permute-start | bytes 196616 | tf_op jit(solution)/shard_map/ppermute | solution.py:90
  8.6 5.9 %collective-permute-start.1 = (f32[128,1,128]{2,1,0:T(1,128)S(1)}, f32[128,1,128]{2,1,0:T(1,128)S(1)}, u32[]{:S(2)}, u32[]{:S(2)}) collective-permute-start(f32[128,1,128]{2,1,0:T(1,128)S(1)} %get-tuple-element.13), channel_id=1, source_target_pairs={{0,32},{32,64},{64,96},{1,33},{33,65},{65,97},{2,34},{34,66},{66,9... | collective-permute-start | bytes 196616 | tf_op jit(solution)/shard_map/ppermute | solution.py:91
  14.5 0.6 copy-start.4
  14.5 0.6 copy-start.5
  14.5 0.6 copy-start.7
  14.5 0.6 copy-start.8
  23.0 10.8 %collective-permute-start.6 = (f32[4,32,32]{2,1,0:T(8,128)S(1)}, f32[4,32,32]{2,1,0:T(8,128)S(1)}, u32[]{:S(2)}, u32[]{:S(2)}) collective-permute-start(f32[4,32,32]{2,1,0:T(8,128)S(1)} %bitcast.62), channel_id=1, source_target_pairs={{1,0},{2,1},{3,2},{4,3},{5,4},{6,5},{7,6},{8,7},{9,8},{10,9},{11,1... | collective-permute-start | bytes 49160 | tf_op jit(solution)/shard_map/ppermute | solution.py:92
  27.2 6.6 %collective-permute-start.7 = (f32[4,32,32]{2,1,0:T(8,128)S(1)}, f32[4,32,32]{2,1,0:T(8,128)S(1)}, u32[]{:S(2)}, u32[]{:S(2)}) collective-permute-start(f32[4,32,32]{2,1,0:T(8,128)S(1)} %bitcast.63), channel_id=1, source_target_pairs={{0,1},{1,2},{2,3},{3,4},{4,5},{5,6},{6,7},{7,8},{8,9},{9,10},{10,1... | collective-permute-start | bytes 49160 | tf_op jit(solution)/shard_map/ppermute | solution.py:93
  27.3 6.6 %collective-permute-start.4 = (f32[128,1,128]{2,1,0:T(1,128)}, f32[128,1,128]{2,1,0:T(1,128)S(1)}, u32[]{:S(2)}, u32[]{:S(2)}) collective-permute-start(f32[128,1,128]{2,1,0:T(1,128)} %get-tuple-element.16), channel_id=1, source_target_pairs={{32,0},{64,32},{96,64},{33,1},{65,33},{97,65},{34,2},{66,34},{98,6... | collective-permute-start | bytes 196616 | tf_op jit(solution)/shard_map/ppermute | solution.py:90
  28.6 6.2 %collective-permute-start.5 = (f32[128,1,128]{2,1,0:T(1,128)}, f32[128,1,128]{2,1,0:T(1,128)S(1)}, u32[]{:S(2)}, u32[]{:S(2)}) collective-permute-start(f32[128,1,128]{2,1,0:T(1,128)} %get-tuple-element.17), channel_id=1, source_target_pairs={{0,32},{32,64},{64,96},{1,33},{33,65},{65,97},{2,34},{34,66},{66,9... | collective-permute-start | bytes 196616 | tf_op jit(solution)/shard_map/ppermute | solution.py:91
  33.8 1.0 copy-start.6
  33.8 1.0 copy-start.9
  33.9 1.0 copy-start.10
  34.9 0.6 copy-start.11
  50.7 38.9 %all-to-all-start = ((bf16[128,32,256]{0,2,1:T(8,128)(2,1)}), bf16[128,32,256]{0,2,1:T(8,128)(2,1)S(1)}, u32[]{:S(2)}, u32[]{:S(2)}) async-start(bf16[128,32,256]{0,2,1:T(8,128)(2,1)} %bitcast.54), calls=%async_computation | async-start | bytes 4194304 | tf_op jit(solution)/shard_map/all_to_all | solution.py:362
  61.3 2.7 %copy-start.2 = (bf16[1,512,128]{2,1,0:T(8,128)(2,1)S(1)}, bf16[1,512,128]{2,1,0:T(8,128)(2,1)}, u32[]{:S(2)}) copy-start(bf16[1,512,128]{2,1,0:T(8,128)(2,1)} %param.11) | copy-start | bytes 393220
  61.3 3.5 %copy-start.3 = (bf16[1,128,512]{2,1,0:T(8,128)(2,1)S(1)}, bf16[1,128,512]{2,1,0:T(8,128)(2,1)}, u32[]{:S(2)}) copy-start(bf16[1,128,512]{2,1,0:T(8,128)(2,1)} %param.13) | copy-start | bytes 393220
  89.6 1.8 %copy-start = (bf16[128,32,256]{0,2,1:T(8,128)(2,1)}, bf16[128,32,256]{0,2,1:T(8,128)(2,1)S(1)}, u32[]{:S(2)}) copy-start(bf16[128,32,256]{0,2,1:T(8,128)(2,1)S(1)} %all-to-all-done) | copy-start | bytes 6291460

commit v20 on v18

--- a/solution.py
+++ b/solution.py
@@ -122,7 +122,7 @@
 
 
 ROWS = 1024
-HALF = 128
+HALF = 256
 
 
 def silu(t):

time: 162 us -> 162 us (level)
  blocking collectives: 43 us -> 33.7 us
  Pallas kernels: 49.1 us -> 58.1 us
    all_to_all x1, blocking collectives: 43 us -> 33.7 us  [local(): lax.all_to_all(result.reshape(features, experts, width), 'lon', split_axi...]
    pallas_call x1, Pallas kernels: 16.4 us -> 25.4 us  [network(): pl.pallas_call(network_kernel, grid_spec=pltpu.PrefetchScalarGridSpec(num...]
where the time goes in v20:
time: 162 us; the launch traced here: 161 us
  Pallas kernels  58.1 us (36%)
  blocking collectives  33.7 us (21%)
  starting transfers between devices  28.9 us (18%)
  waiting for transfers between devices  25.1 us (15%)
  local copies, waits for them, and re-layouts  9.57 us (6%)
  matrix products  2.92 us (2%)
  other arithmetic  2.69 us (2%)
    all_to_all x1, blocking collectives, local(): lax.all_to_all(result.reshape(features, experts, width), 'lon', split_axi...  33.7 us
    pallas_call x1, Pallas kernels, network(): pl.pallas_call(network_kernel, grid_spec=pltpu.PrefetchScalarGridSpec(num...  25.4 us
    all_to_all x1, waiting for transfers between devices, local(): lax.all_to_all(part, 'lon', split_axis=1, concat_axis=1, tiled=True)  24.1 us
    pallas_call x2, Pallas kernels, sweep(): pl.pallas_call(sweep_kernel, grid=(nb,), in_specs=[big, edge_row, edge_ro...  12.7 us
    pallas_call x1, Pallas kernels, combine(): pl.pallas_call(combine_kernel, grid_spec=pltpu.PrefetchScalarGridSpec(num...  10.7 us
    all_to_all x1, starting transfers between devices, local(): lax.all_to_all(part, 'lon', split_axis=1, concat_axis=1, tiled=True)  10.6 us
    pallas_call x1, Pallas kernels, pack(): pl.pallas_call(pack_kernel, grid_spec=pltpu.PrefetchScalarGridSpec(num_sc...  9.29 us
    ppermute x2, starting transfers between devices, exchange(): hs = lax.ppermute(bottom, 'lat', lat_forward)  8.79 us
  transfers between devices with their start and end apart: 9, of which 2 were waited for; matrix products, arithmetic and copies ran while one was open for 4% of the time, Pallas kernels for 0%

profile of v20, /device:TPU:1, one launch (start us, length us, event | category | flops | bytes accessed | tf_op | source)
XLA Modules:
  0.0 161.2 jit_solution(10587724894580907849)
XLA Ops:
  0.0 1.4 fusion.11
  1.4 2.6 %fusion.8 = f32[2,4096]{1,0:T(2,128)S(1)} fusion(f32[4096,128]{1,0:T(8,128)} %bitcast.48, s32[2]{0:T(128)S(1)} %iota_multiply_fusion), kind=kOutput, calls=%fused_computation.15 | convolution fusion | flops 12583424 | bytes 2129928 | tf_op jit(solution)/shard_map/dot_general | solution.py:102
  4.3 1.5 collective-permute-start.2
  6.0 1.3 collective-permute-start.3
  7.3 1.3 collective-permute-start
  8.6 4.2 %collective-permute-start.1 = (f32[128,1,128]{2,1,0:T(1,128)S(1)}, f32[128,1,128]{2,1,0:T(1,128)S(1)}, u32[]{:S(2)}, u32[]{:S(2)}) collective-permute-start(f32[128,1,128]{2,1,0:T(1,128)S(1)} %get-tuple-element.13), channel_id=1, source_target_pairs={{0,32},{32,64},{64,96},{1,33},{33,65},{65,97},{2,34},{34,66},{66,9... | collective-permute-start | bytes 196616 | tf_op jit(solution)/shard_map/ppermute | solution.py:91
  12.8 1.1 slice_bitcast_fusion
  15.1 6.7 %shard_map.73 = (f32[128,32,128]{2,1,0:T(8,128)}, f32[128,1,128]{2,1,0:T(1,128)}, f32[128,1,128]{2,1,0:T(1,128)}, f32[2,4096]{1,0:T(2,128)}) custom-call(f32[128,32,128]{2,1,0:T(8,128)} %bitcast.49, f32[128,1,128]{2,1,0:T(1,128)} %copy-done.7, f32[128,1,128]{2,1,0:T(1,128)} %copy-done.8, f32[4,32,32]{2,1,0:T(8,128)} %copy-done.4, f32[4,32,32]{2,1,0:T(8,128)} %copy-done.5, ...), custom_call_target="tpu_custom_call" | custom-call | flops 10485760 | bytes 5767168 | tf_op jit(solution)/shard_map/pallas_call | solution.py:72
  21.9 0.9 slice_reduce_fusion
  23.0 4.1 %collective-permute-start.6 = (f32[4,32,32]{2,1,0:T(8,128)S(1)}, f32[4,32,32]{2,1,0:T(8,128)S(1)}, u32[]{:S(2)}, u32[]{:S(2)}) collective-permute-start(f32[4,32,32]{2,1,0:T(8,128)S(1)} %bitcast.60), channel_id=1, source_target_pairs={{1,0},{2,1},{3,2},{4,3},{5,4},{6,5},{7,6},{8,7},{9,8},{10,9},{11,1... | collective-permute-start | bytes 49160 | tf_op jit(solution)/shard_map/ppermute | solution.py:92
  27.3 1.3 collective-permute-start.4
  28.6 4.6 %collective-permute-start.5 = (f32[128,1,128]{2,1,0:T(1,128)}, f32[128,1,128]{2,1,0:T(1,128)S(1)}, u32[]{:S(2)}, u32[]{:S(2)}) collective-permute-start(f32[128,1,128]{2,1,0:T(1,128)} %get-tuple-element.17), channel_id=1, source_target_pairs={{0,32},{32,64},{64,96},{1,33},{33,65},{65,97},{2,34},{34,66},{66,9... | collective-permute-start | bytes 196616 | tf_op jit(solution)/shard_map/ppermute | solution.py:91
  33.9 1.0 collective-permute-done.5.hs_ref
  35.5 6.0 %shard_map.74.cur_ref = f32[128,32,128]{2,1,0:T(8,128)} custom-call(f32[128,32,128]{2,1,0:T(8,128)} %get-tuple-element.15.q_ref, f32[128,1,128]{2,1,0:T(1,128)} %copy-done.10, f32[128,1,128]{2,1,0:T(1,128)} %copy-done.11, f32[4,32,32]{2,1,0:T(8,128)} %copy-done.6, f32[4,32,32]{2,1,0:T(8,128)} %copy-done.9, f32[32,32,128]{2,1,0:T(8,128)} %get-tuple-element.26.u_ref, ...), custom_call_target="tpu_custom_call" | custom-call | flops 10485760 | bytes 5767168 | tf_op jit(solution)/shard_map/pallas_call | solution.py:72
  41.4 9.3 %shard_map.75 = bf16[8192,128]{1,0:T(8,128)(2,1)} custom-call(s32[4096]{0:T(1024)} %bitcast_add_fusion.t_ref, f32[128,32,128]{2,1,0:T(8,128)} %shard_map.74.cur_ref), custom_call_target="tpu_custom_call" | custom-call | tf_op jit(solution)/shard_map/pallas_call | solution.py:290
  50.7 10.6 %all-to-all-start = ((bf16[128,32,256]{0,2,1:T(8,128)(2,1)}), bf16[128,32,256]{0,2,1:T(8,128)(2,1)S(1)}, u32[]{:S(2)}, u32[]{:S(2)}) async-start(bf16[128,32,256]{0,2,1:T(8,128)(2,1)} %bitcast.52), calls=%async_computation | async-start | bytes 4194304 | tf_op jit(solution)/shard_map/all_to_all | solution.py:362
  61.3 2.7 %copy.23 = bf16[1,3,512,512]{2,3,1,0:T(8,128)(2,1)} copy(bf16[1,3,512,512]{3,2,1,0:T(8,128)(2,1)} %param.12) | data formatting | bytes 3145728 | tf_op args[5]
  64.0 0.8 copy.22
  64.8 0.8 copy.24
  65.5 24.1 %all-to-all-done = bf16[128,32,256]{0,2,1:T(8,128)(2,1)S(1)} async-done(((bf16[128,32,256]{0,2,1:T(8,128)(2,1)}), bf16[128,32,256]{0,2,1:T(8,128)(2,1)S(1)}, u32[]{:S(2)}, u32[]{:S(2)}) %all-to-all-start) | async-done | bytes 2097184 | tf_op jit(solution)/shard_map/all_to_all | solution.py:362
  89.6 1.2 compare_reduce_fusion
  91.4 25.4 %shard_map.76 = bf16[8192,128]{1,0:T(8,128)(2,1)} custom-call(s32[32]{0:T(128)} %convert_element_type.23.nonzero_ref, bf16[8192,128]{1,0:T(8,128)(2,1)} %bitcast.51, bf16[128,512]{1,0:T(8,128)(2,1)} %bitcast.55, bf16[3,512,512]{2,1,0:T(8,128)(2,1)} %bitcast.54, bf16[512,128]{1,0:T(8,128)(2,1)} %bitcast.56), custom_call_target="tpu_custom_call" | custom-call | flops 15032385536 | bytes 6029312 | tf_op jit(solution)/shard_map/pallas_call | solution.py:238
  116.8 33.7 %all_to_all.10 = bf16[128,32,256]{0,2,1:T(8,128)(2,1)} all-to-all(bf16[128,32,256]{0,2,1:T(8,128)(2,1)} %bitcast.53), channel_id=1, replica_groups=mesh['lat'=4,'lon'=32] {'lon'}, dimensions={1} | all-to-all | bytes 4194304 | tf_op jit(solution)/shard_map/all_to_all | solution.py:366
  150.5 10.7 %shard_map.77 = f32[128,32,128]{2,1,0:T(8,128)} custom-call(s32[4096]{0:T(1024)} %bitcast_add_fusion.t_ref, bf16[8192,128]{1,0:T(8,128)(2,1)} %bitcast.50, f32[128,32,128]{2,1,0:T(8,128)} %shard_map.74.cur_ref), custom_call_target="tpu_custom_call" | custom-call | tf_op jit(solution)/shard_map/pallas_call | solution.py:321
  (53 shorter events, 3.9 us)
Async XLA Ops:
  0.0 12.8 %copy-start.1 = (f32[2,32,32,128]{3,2,1,0:T(8,128)S(1)}, f32[2,32,32,128]{3,2,1,0:T(8,128)}, u32[]{:S(2)}) copy-start(f32[2,32,32,128]{3,2,1,0:T(8,128)} %param.8) | copy-start | bytes 3145732
  1.4 12.5 %copy-start.12 = (s32[1,4096,1]{1,2,0:T(1,128)S(1)}, s32[1,4096,1]{1,2,0:T(1,128)}, u32[]{:S(2)}) copy-start(s32[1,4096,1]{1,2,0:T(1,128)} %param.10) | copy-start | bytes 49156
  4.3 10.1 %collective-permute-start.2 = (f32[4,32,32]{2,1,0:T(8,128)S(1)}, f32[4,32,32]{2,1,0:T(8,128)S(1)}, u32[]{:S(2)}, u32[]{:S(2)}) collective-permute-start(f32[4,32,32]{2,1,0:T(8,128)S(1)} %bitcast.58), channel_id=1, source_target_pairs={{1,0},{2,1},{3,2},{4,3},{5,4},{6,5},{7,6},{8,7},{9,8},{10,9},{11,1... | collective-permute-start | bytes 49160 | tf_op jit(solution)/shard_map/ppermute | solution.py:92
  6.0 8.5 %collective-permute-start.3 = (f32[4,32,32]{2,1,0:T(8,128)S(1)}, f32[4,32,32]{2,1,0:T(8,128)S(1)}, u32[]{:S(2)}, u32[]{:S(2)}) collective-permute-start(f32[4,32,32]{2,1,0:T(8,128)S(1)} %bitcast.59), channel_id=1, source_target_pairs={{0,1},{1,2},{2,3},{3,4},{4,5},{5,6},{6,7},{7,8},{8,9},{9,10},{10,1... | collective-permute-start | bytes 49160 | tf_op jit(solution)/shard_map/ppermute | solution.py:93
  7.3 7.2 %collective-permute-start = (f32[128,1,128]{2,1,0:T(1,128)S(1)}, f32[128,1,128]{2,1,0:T(1,128)S(1)}, u32[]{:S(2)}, u32[]{:S(2)}) collective-permute-start(f32[128,1,128]{2,1,0:T(1,128)S(1)} %get-tuple-element.12), channel_id=1, source_target_pairs={{32,0},{64,32},{96,64},{33,1},{65,33},{97,65},{34,2},{66,34},{98,6... | collective-permute-start | bytes 196616 | tf_op jit(solution)/shard_map/ppermute | solution.py:90
  8.6 5.9 %collective-permute-start.1 = (f32[128,1,128]{2,1,0:T(1,128)S(1)}, f32[128,1,128]{2,1,0:T(1,128)S(1)}, u32[]{:S(2)}, u32[]{:S(2)}) collective-permute-start(f32[128,1,128]{2,1,0:T(1,128)S(1)} %get-tuple-element.13), channel_id=1, source_target_pairs={{0,32},{32,64},{64,96},{1,33},{33,65},{65,97},{2,34},{34,66},{66,9... | collective-permute-start | bytes 196616 | tf_op jit(solution)/shard_map/ppermute | solution.py:91
  14.5 0.6 copy-start.4
  14.5 0.6 copy-start.5
  14.5 0.6 copy-start.7
  14.5 0.6 copy-start.8
  23.0 10.8 %collective-permute-start.6 = (f32[4,32,32]{2,1,0:T(8,128)S(1)}, f32[4,32,32]{2,1,0:T(8,128)S(1)}, u32[]{:S(2)}, u32[]{:S(2)}) collective-permute-start(f32[4,32,32]{2,1,0:T(8,128)S(1)} %bitcast.60), channel_id=1, source_target_pairs={{1,0},{2,1},{3,2},{4,3},{5,4},{6,5},{7,6},{8,7},{9,8},{10,9},{11,1... | collective-permute-start | bytes 49160 | tf_op jit(solution)/shard_map/ppermute | solution.py:92
  27.2 6.6 %collective-permute-start.7 = (f32[4,32,32]{2,1,0:T(8,128)S(1)}, f32[4,32,32]{2,1,0:T(8,128)S(1)}, u32[]{:S(2)}, u32[]{:S(2)}) collective-permute-start(f32[4,32,32]{2,1,0:T(8,128)S(1)} %bitcast.61), channel_id=1, source_target_pairs={{0,1},{1,2},{2,3},{3,4},{4,5},{5,6},{6,7},{7,8},{8,9},{9,10},{10,1... | collective-permute-start | bytes 49160 | tf_op jit(solution)/shard_map/ppermute | solution.py:93
  27.3 6.6 %collective-permute-start.4 = (f32[128,1,128]{2,1,0:T(1,128)}, f32[128,1,128]{2,1,0:T(1,128)S(1)}, u32[]{:S(2)}, u32[]{:S(2)}) collective-permute-start(f32[128,1,128]{2,1,0:T(1,128)} %get-tuple-element.16), channel_id=1, source_target_pairs={{32,0},{64,32},{96,64},{33,1},{65,33},{97,65},{34,2},{66,34},{98,6... | collective-permute-start | bytes 196616 | tf_op jit(solution)/shard_map/ppermute | solution.py:90
  28.6 6.2 %collective-permute-start.5 = (f32[128,1,128]{2,1,0:T(1,128)}, f32[128,1,128]{2,1,0:T(1,128)S(1)}, u32[]{:S(2)}, u32[]{:S(2)}) collective-permute-start(f32[128,1,128]{2,1,0:T(1,128)} %get-tuple-element.17), channel_id=1, source_target_pairs={{0,32},{32,64},{64,96},{1,33},{33,65},{65,97},{2,34},{34,66},{66,9... | collective-permute-start | bytes 196616 | tf_op jit(solution)/shard_map/ppermute | solution.py:91
  33.8 1.0 copy-start.6
  33.8 1.0 copy-start.9
  33.9 1.0 copy-start.10
  34.9 0.6 copy-start.11
  50.7 38.9 %all-to-all-start = ((bf16[128,32,256]{0,2,1:T(8,128)(2,1)}), bf16[128,32,256]{0,2,1:T(8,128)(2,1)S(1)}, u32[]{:S(2)}, u32[]{:S(2)}) async-start(bf16[128,32,256]{0,2,1:T(8,128)(2,1)} %bitcast.52), calls=%async_computation | async-start | bytes 4194304 | tf_op jit(solution)/shard_map/all_to_all | solution.py:362
  61.3 2.7 %copy-start.2 = (bf16[1,512,128]{2,1,0:T(8,128)(2,1)S(1)}, bf16[1,512,128]{2,1,0:T(8,128)(2,1)}, u32[]{:S(2)}) copy-start(bf16[1,512,128]{2,1,0:T(8,128)(2,1)} %param.11) | copy-start | bytes 393220
  61.3 3.5 %copy-start.3 = (bf16[1,128,512]{2,1,0:T(8,128)(2,1)S(1)}, bf16[1,128,512]{2,1,0:T(8,128)(2,1)}, u32[]{:S(2)}) copy-start(bf16[1,128,512]{2,1,0:T(8,128)(2,1)} %param.13) | copy-start | bytes 393220
  89.6 1.8 %copy-start = (bf16[128,32,256]{0,2,1:T(8,128)(2,1)}, bf16[128,32,256]{0,2,1:T(8,128)(2,1)S(1)}, u32[]{:S(2)}) copy-start(bf16[128,32,256]{0,2,1:T(8,128)(2,1)S(1)} %all-to-all-done) | copy-start | bytes 6291460

commit v21 on v18

--- a/solution.py
+++ b/solution.py
@@ -265,7 +265,7 @@
     )(nonzero, rows_in, first, middle, last)
 
 
-UNROLL = 32
+UNROLL = 64
 
 
 def pack_kernel(t_ref, cur_ref, o_ref, rows, full):

time: 162 us -> 161 us (level)
  blocking collectives: 43 us -> 33.5 us
  Pallas kernels: 49.1 us -> 58 us
    pallas_call x1, Pallas kernels: 16.4 us -> 25.9 us  [network(): pl.pallas_call(network_kernel, grid_spec=pltpu.PrefetchScalarGridSpec(num...]
    all_to_all x1, blocking collectives: 43 us -> 33.5 us  [local(): lax.all_to_all(result.reshape(features, experts, width), 'lon', split_axi...]
where the time goes in v21:
time: 161 us
  Pallas kernels  58 us (36%)
  blocking collectives  33.5 us (21%)
  starting transfers between devices  28.9 us (18%)
  waiting for transfers between devices  25.1 us (16%)
  local copies, waits for them, and re-layouts  9.56 us (6%)
  matrix products  2.92 us (2%)
  other arithmetic  2.69 us (2%)
    all_to_all x1, blocking collectives, local(): lax.all_to_all(result.reshape(features, experts, width), 'lon', split_axi...  33.5 us
    pallas_call x1, Pallas kernels, network(): pl.pallas_call(network_kernel, grid_spec=pltpu.PrefetchScalarGridSpec(num...  25.9 us
    all_to_all x1, waiting for transfers between devices, local(): lax.all_to_all(part, 'lon', split_axis=1, concat_axis=1, tiled=True)  24.1 us
    pallas_call x2, Pallas kernels, sweep(): pl.pallas_call(sweep_kernel, grid=(nb,), in_specs=[big, edge_row, edge_ro...  12.7 us
    all_to_all x1, starting transfers between devices, local(): lax.all_to_all(part, 'lon', split_axis=1, concat_axis=1, tiled=True)  10.6 us
    pallas_call x1, Pallas kernels, combine(): pl.pallas_call(combine_kernel, grid_spec=pltpu.PrefetchScalarGridSpec(num...  10.4 us
    pallas_call x1, Pallas kernels, pack(): pl.pallas_call(pack_kernel, grid_spec=pltpu.PrefetchScalarGridSpec(num_sc...  8.99 us
    ppermute x2, starting transfers between devices, exchange(): hs = lax.ppermute(bottom, 'lat', lat_forward)  8.79 us
  transfers between devices with their start and end apart: 9, of which 2 were waited for; matrix products, arithmetic and copies ran while one was open for 4% of the time, Pallas kernels for 0%

profile of v21, /device:TPU:1, one launch (start us, length us, event | category | flops | bytes accessed | tf_op | source)
XLA Modules:
  0.0 160.9 jit_solution(16382544122707305124)
XLA Ops:
  0.0 1.4 fusion.11
  1.4 2.6 %fusion.8 = f32[2,4096]{1,0:T(2,128)S(1)} fusion(f32[4096,128]{1,0:T(8,128)} %bitcast.50, s32[2]{0:T(128)S(1)} %iota_multiply_fusion), kind=kOutput, calls=%fused_computation.15 | convolution fusion | flops 12583424 | bytes 2129928 | tf_op jit(solution)/shard_map/dot_general | solution.py:102
  4.3 1.5 collective-permute-start.2
  6.0 1.3 collective-permute-start.3
  7.3 1.3 collective-permute-start
  8.6 4.2 %collective-permute-start.1 = (f32[128,1,128]{2,1,0:T(1,128)S(1)}, f32[128,1,128]{2,1,0:T(1,128)S(1)}, u32[]{:S(2)}, u32[]{:S(2)}) collective-permute-start(f32[128,1,128]{2,1,0:T(1,128)S(1)} %get-tuple-element.13), channel_id=1, source_target_pairs={{0,32},{32,64},{64,96},{1,33},{33,65},{65,97},{2,34},{34,66},{66,9... | collective-permute-start | bytes 196616 | tf_op jit(solution)/shard_map/ppermute | solution.py:91
  12.8 1.1 slice_bitcast_fusion
  15.1 6.7 %shard_map.73 = (f32[128,32,128]{2,1,0:T(8,128)}, f32[128,1,128]{2,1,0:T(1,128)}, f32[128,1,128]{2,1,0:T(1,128)}, f32[2,4096]{1,0:T(2,128)}) custom-call(f32[128,32,128]{2,1,0:T(8,128)} %bitcast.51, f32[128,1,128]{2,1,0:T(1,128)} %copy-done.7, f32[128,1,128]{2,1,0:T(1,128)} %copy-done.8, f32[4,32,32]{2,1,0:T(8,128)} %copy-done.4, f32[4,32,32]{2,1,0:T(8,128)} %copy-done.5, ...), custom_call_target="tpu_custom_call" | custom-call | flops 10485760 | bytes 5767168 | tf_op jit(solution)/shard_map/pallas_call | solution.py:72
  21.9 0.9 slice_reduce_fusion
  23.0 4.1 %collective-permute-start.6 = (f32[4,32,32]{2,1,0:T(8,128)S(1)}, f32[4,32,32]{2,1,0:T(8,128)S(1)}, u32[]{:S(2)}, u32[]{:S(2)}) collective-permute-start(f32[4,32,32]{2,1,0:T(8,128)S(1)} %bitcast.62), channel_id=1, source_target_pairs={{1,0},{2,1},{3,2},{4,3},{5,4},{6,5},{7,6},{8,7},{9,8},{10,9},{11,1... | collective-permute-start | bytes 49160 | tf_op jit(solution)/shard_map/ppermute | solution.py:92
  27.3 1.3 collective-permute-start.4
  28.6 4.6 %collective-permute-start.5 = (f32[128,1,128]{2,1,0:T(1,128)}, f32[128,1,128]{2,1,0:T(1,128)S(1)}, u32[]{:S(2)}, u32[]{:S(2)}) collective-permute-start(f32[128,1,128]{2,1,0:T(1,128)} %get-tuple-element.17), channel_id=1, source_target_pairs={{0,32},{32,64},{64,96},{1,33},{33,65},{65,97},{2,34},{34,66},{66,9... | collective-permute-start | bytes 196616 | tf_op jit(solution)/shard_map/ppermute | solution.py:91
  33.9 1.0 collective-permute-done.5.hs_ref
  35.5 6.0 %shard_map.74.cur_ref = f32[128,32,128]{2,1,0:T(8,128)} custom-call(f32[128,32,128]{2,1,0:T(8,128)} %get-tuple-element.15.q_ref, f32[128,1,128]{2,1,0:T(1,128)} %copy-done.10, f32[128,1,128]{2,1,0:T(1,128)} %copy-done.11, f32[4,32,32]{2,1,0:T(8,128)} %copy-done.6, f32[4,32,32]{2,1,0:T(8,128)} %copy-done.9, f32[32,32,128]{2,1,0:T(8,128)} %get-tuple-element.26.u_ref, ...), custom_call_target="tpu_custom_call" | custom-call | flops 10485760 | bytes 5767168 | tf_op jit(solution)/shard_map/pallas_call | solution.py:72
  41.4 9.0 %shard_map.75 = bf16[8192,128]{1,0:T(8,128)(2,1)} custom-call(s32[4096]{0:T(1024)} %bitcast_add_fusion.t_ref, f32[128,32,128]{2,1,0:T(8,128)} %shard_map.74.cur_ref), custom_call_target="tpu_custom_call" | custom-call | tf_op jit(solution)/shard_map/pallas_call | solution.py:290
  50.4 10.6 %all-to-all-start = ((bf16[128,32,256]{0,2,1:T(8,128)(2,1)}), bf16[128,32,256]{0,2,1:T(8,128)(2,1)S(1)}, u32[]{:S(2)}, u32[]{:S(2)}) async-start(bf16[128,32,256]{0,2,1:T(8,128)(2,1)} %bitcast.54), calls=%async_computation | async-start | bytes 4194304 | tf_op jit(solution)/shard_map/all_to_all | solution.py:362
  61.0 2.7 %copy.23 = bf16[1,3,512,512]{2,3,1,0:T(8,128)(2,1)} copy(bf16[1,3,512,512]{3,2,1,0:T(8,128)(2,1)} %param.12) | data formatting | bytes 3145728 | tf_op args[5]
  63.7 0.8 copy.22
  64.5 0.8 copy.24
  65.2 24.1 %all-to-all-done = bf16[128,32,256]{0,2,1:T(8,128)(2,1)S(1)} async-done(((bf16[128,32,256]{0,2,1:T(8,128)(2,1)}), bf16[128,32,256]{0,2,1:T(8,128)(2,1)S(1)}, u32[]{:S(2)}, u32[]{:S(2)}) %all-to-all-start) | async-done | bytes 2097184 | tf_op jit(solution)/shard_map/all_to_all | solution.py:362
  89.3 1.2 compare_reduce_fusion
  91.1 25.9 %shard_map.76 = bf16[8192,128]{1,0:T(8,128)(2,1)} custom-call(s32[64]{0:T(128)} %convert_element_type.23.nonzero_ref, bf16[8192,128]{1,0:T(8,128)(2,1)} %bitcast.53, bf16[128,512]{1,0:T(8,128)(2,1)} %bitcast.57, bf16[3,512,512]{2,1,0:T(8,128)(2,1)} %bitcast.56, bf16[512,128]{1,0:T(8,128)(2,1)} %bitcast.58), custom_call_target="tpu_custom_call" | custom-call | flops 15032385536 | bytes 6029312 | tf_op jit(solution)/shard_map/pallas_call | solution.py:238
  117.0 33.5 %all_to_all.10 = bf16[128,32,256]{0,2,1:T(8,128)(2,1)} all-to-all(bf16[128,32,256]{0,2,1:T(8,128)(2,1)} %bitcast.55), channel_id=1, replica_groups=mesh['lat'=4,'lon'=32] {'lon'}, dimensions={1} | all-to-all | bytes 4194304 | tf_op jit(solution)/shard_map/all_to_all | solution.py:366
  150.5 10.4 %shard_map.77 = f32[128,32,128]{2,1,0:T(8,128)} custom-call(s32[4096]{0:T(1024)} %bitcast_add_fusion.t_ref, bf16[8192,128]{1,0:T(8,128)(2,1)} %bitcast.52, f32[128,32,128]{2,1,0:T(8,128)} %shard_map.74.cur_ref), custom_call_target="tpu_custom_call" | custom-call | tf_op jit(solution)/shard_map/pallas_call | solution.py:321
  (52 shorter events, 3.9 us)
Async XLA Ops:
  0.0 12.8 %copy-start.1 = (f32[2,32,32,128]{3,2,1,0:T(8,128)S(1)}, f32[2,32,32,128]{3,2,1,0:T(8,128)}, u32[]{:S(2)}) copy-start(f32[2,32,32,128]{3,2,1,0:T(8,128)} %param.8) | copy-start | bytes 3145732
  1.4 12.5 %copy-start.12 = (s32[1,4096,1]{1,2,0:T(1,128)S(1)}, s32[1,4096,1]{1,2,0:T(1,128)}, u32[]{:S(2)}) copy-start(s32[1,4096,1]{1,2,0:T(1,128)} %param.10) | copy-start | bytes 49156
  4.3 10.1 %collective-permute-start.2 = (f32[4,32,32]{2,1,0:T(8,128)S(1)}, f32[4,32,32]{2,1,0:T(8,128)S(1)}, u32[]{:S(2)}, u32[]{:S(2)}) collective-permute-start(f32[4,32,32]{2,1,0:T(8,128)S(1)} %bitcast.60), channel_id=1, source_target_pairs={{1,0},{2,1},{3,2},{4,3},{5,4},{6,5},{7,6},{8,7},{9,8},{10,9},{11,1... | collective-permute-start | bytes 49160 | tf_op jit(solution)/shard_map/ppermute | solution.py:92
  6.0 8.5 %collective-permute-start.3 = (f32[4,32,32]{2,1,0:T(8,128)S(1)}, f32[4,32,32]{2,1,0:T(8,128)S(1)}, u32[]{:S(2)}, u32[]{:S(2)}) collective-permute-start(f32[4,32,32]{2,1,0:T(8,128)S(1)} %bitcast.61), channel_id=1, source_target_pairs={{0,1},{1,2},{2,3},{3,4},{4,5},{5,6},{6,7},{7,8},{8,9},{9,10},{10,1... | collective-permute-start | bytes 49160 | tf_op jit(solution)/shard_map/ppermute | solution.py:93
  7.3 7.2 %collective-permute-start = (f32[128,1,128]{2,1,0:T(1,128)S(1)}, f32[128,1,128]{2,1,0:T(1,128)S(1)}, u32[]{:S(2)}, u32[]{:S(2)}) collective-permute-start(f32[128,1,128]{2,1,0:T(1,128)S(1)} %get-tuple-element.12), channel_id=1, source_target_pairs={{32,0},{64,32},{96,64},{33,1},{65,33},{97,65},{34,2},{66,34},{98,6... | collective-permute-start | bytes 196616 | tf_op jit(solution)/shard_map/ppermute | solution.py:90
  8.6 5.9 %collective-permute-start.1 = (f32[128,1,128]{2,1,0:T(1,128)S(1)}, f32[128,1,128]{2,1,0:T(1,128)S(1)}, u32[]{:S(2)}, u32[]{:S(2)}) collective-permute-start(f32[128,1,128]{2,1,0:T(1,128)S(1)} %get-tuple-element.13), channel_id=1, source_target_pairs={{0,32},{32,64},{64,96},{1,33},{33,65},{65,97},{2,34},{34,66},{66,9... | collective-permute-start | bytes 196616 | tf_op jit(solution)/shard_map/ppermute | solution.py:91
  14.5 0.6 copy-start.4
  14.5 0.6 copy-start.5
  14.5 0.6 copy-start.7
  14.5 0.6 copy-start.8
  23.0 10.8 %collective-permute-start.6 = (f32[4,32,32]{2,1,0:T(8,128)S(1)}, f32[4,32,32]{2,1,0:T(8,128)S(1)}, u32[]{:S(2)}, u32[]{:S(2)}) collective-permute-start(f32[4,32,32]{2,1,0:T(8,128)S(1)} %bitcast.62), channel_id=1, source_target_pairs={{1,0},{2,1},{3,2},{4,3},{5,4},{6,5},{7,6},{8,7},{9,8},{10,9},{11,1... | collective-permute-start | bytes 49160 | tf_op jit(solution)/shard_map/ppermute | solution.py:92
  27.2 6.6 %collective-permute-start.7 = (f32[4,32,32]{2,1,0:T(8,128)S(1)}, f32[4,32,32]{2,1,0:T(8,128)S(1)}, u32[]{:S(2)}, u32[]{:S(2)}) collective-permute-start(f32[4,32,32]{2,1,0:T(8,128)S(1)} %bitcast.63), channel_id=1, source_target_pairs={{0,1},{1,2},{2,3},{3,4},{4,5},{5,6},{6,7},{7,8},{8,9},{9,10},{10,1... | collective-permute-start | bytes 49160 | tf_op jit(solution)/shard_map/ppermute | solution.py:93
  27.3 6.6 %collective-permute-start.4 = (f32[128,1,128]{2,1,0:T(1,128)}, f32[128,1,128]{2,1,0:T(1,128)S(1)}, u32[]{:S(2)}, u32[]{:S(2)}) collective-permute-start(f32[128,1,128]{2,1,0:T(1,128)} %get-tuple-element.16), channel_id=1, source_target_pairs={{32,0},{64,32},{96,64},{33,1},{65,33},{97,65},{34,2},{66,34},{98,6... | collective-permute-start | bytes 196616 | tf_op jit(solution)/shard_map/ppermute | solution.py:90
  28.6 6.2 %collective-permute-start.5 = (f32[128,1,128]{2,1,0:T(1,128)}, f32[128,1,128]{2,1,0:T(1,128)S(1)}, u32[]{:S(2)}, u32[]{:S(2)}) collective-permute-start(f32[128,1,128]{2,1,0:T(1,128)} %get-tuple-element.17), channel_id=1, source_target_pairs={{0,32},{32,64},{64,96},{1,33},{33,65},{65,97},{2,34},{34,66},{66,9... | collective-permute-start | bytes 196616 | tf_op jit(solution)/shard_map/ppermute | solution.py:91
  33.8 1.0 copy-start.6
  33.8 1.0 copy-start.9
  33.9 1.0 copy-start.10
  34.9 0.6 copy-start.11
  50.4 38.9 %all-to-all-start = ((bf16[128,32,256]{0,2,1:T(8,128)(2,1)}), bf16[128,32,256]{0,2,1:T(8,128)(2,1)S(1)}, u32[]{:S(2)}, u32[]{:S(2)}) async-start(bf16[128,32,256]{0,2,1:T(8,128)(2,1)} %bitcast.54), calls=%async_computation | async-start | bytes 4194304 | tf_op jit(solution)/shard_map/all_to_all | solution.py:362
  61.0 2.7 %copy-start.2 = (bf16[1,512,128]{2,1,0:T(8,128)(2,1)S(1)}, bf16[1,512,128]{2,1,0:T(8,128)(2,1)}, u32[]{:S(2)}) copy-start(bf16[1,512,128]{2,1,0:T(8,128)(2,1)} %param.11) | copy-start | bytes 393220
  61.0 3.5 %copy-start.3 = (bf16[1,128,512]{2,1,0:T(8,128)(2,1)S(1)}, bf16[1,128,512]{2,1,0:T(8,128)(2,1)}, u32[]{:S(2)}) copy-start(bf16[1,128,512]{2,1,0:T(8,128)(2,1)} %param.13) | copy-start | bytes 393220
  89.3 1.8 %copy-start = (bf16[128,32,256]{0,2,1:T(8,128)(2,1)}, bf16[128,32,256]{0,2,1:T(8,128)(2,1)S(1)}, u32[]{:S(2)}) copy-start(bf16[128,32,256]{0,2,1:T(8,128)(2,1)S(1)} %all-to-all-done) | copy-start | bytes 6291460

commit v22 on v21

--- a/solution.py
+++ b/solution.py
@@ -265,7 +265,7 @@
     )(nonzero, rows_in, first, middle, last)
 
 
-UNROLL = 64
+UNROLL = 128
 
 
 def pack_kernel(t_ref, cur_ref, o_ref, rows, full):

time: 161 us -> 160 us (level)
  Pallas kernels: 58 us -> 50.4 us
  blocking collectives: 33.5 us -> 39.4 us
    pallas_call x1, Pallas kernels: 25.9 us -> 18.5 us  [network(): pl.pallas_call(network_kernel, grid_spec=pltpu.PrefetchScalarGridSpec(num...]
    all_to_all x1, blocking collectives: 33.5 us -> 39.4 us  [local(): lax.all_to_all(result.reshape(features, experts, width), 'lon', split_axi...]
where the time goes in v22:
time: 160 us; the launch traced here: 159 us
  Pallas kernels  50.4 us (32%)
  blocking collectives  39.4 us (25%)
  starting transfers between devices  28.9 us (18%)
  waiting for transfers between devices  25.1 us (16%)
  local copies, waits for them, and re-layouts  9.56 us (6%)
  matrix products  2.92 us (2%)
  other arithmetic  2.69 us (2%)
    all_to_all x1, blocking collectives, local(): lax.all_to_all(result.reshape(features, experts, width), 'lon', split_axi...  39.4 us
    all_to_all x1, waiting for transfers between devices, local(): lax.all_to_all(part, 'lon', split_axis=1, concat_axis=1, tiled=True)  24.1 us
    pallas_call x1, Pallas kernels, network(): pl.pallas_call(network_kernel, grid_spec=pltpu.PrefetchScalarGridSpec(num...  18.5 us
    pallas_call x2, Pallas kernels, sweep(): pl.pallas_call(sweep_kernel, grid=(nb,), in_specs=[big, edge_row, edge_ro...  12.7 us
    all_to_all x1, starting transfers between devices, local(): lax.all_to_all(part, 'lon', split_axis=1, concat_axis=1, tiled=True)  10.6 us
    pallas_call x1, Pallas kernels, combine(): pl.pallas_call(combine_kernel, grid_spec=pltpu.PrefetchScalarGridSpec(num...  10.3 us
    pallas_call x1, Pallas kernels, pack(): pl.pallas_call(pack_kernel, grid_spec=pltpu.PrefetchScalarGridSpec(num_sc...  8.84 us
    ppermute x2, starting transfers between devices, exchange(): hs = lax.ppermute(bottom, 'lat', lat_forward)  8.79 us
  transfers between devices with their start and end apart: 9, of which 2 were waited for; matrix products, arithmetic and copies ran while one was open for 4% of the time, Pallas kernels for 0%

profile of v22, /device:TPU:1, one launch (start us, length us, event | category | flops | bytes accessed | tf_op | source)
XLA Modules:
  0.0 159.2 jit_solution(8668129512900836963)
XLA Ops:
  0.0 1.4 fusion.11
  1.4 2.6 %fusion.8 = f32[2,4096]{1,0:T(2,128)S(1)} fusion(f32[4096,128]{1,0:T(8,128)} %bitcast.50, s32[2]{0:T(128)S(1)} %iota_multiply_fusion), kind=kOutput, calls=%fused_computation.15 | convolution fusion | flops 12583424 | bytes 2129928 | tf_op jit(solution)/shard_map/dot_general | solution.py:102
  4.3 1.5 collective-permute-start.2
  6.0 1.3 collective-permute-start.3
  7.3 1.3 collective-permute-start
  8.6 4.2 %collective-permute-start.1 = (f32[128,1,128]{2,1,0:T(1,128)S(1)}, f32[128,1,128]{2,1,0:T(1,128)S(1)}, u32[]{:S(2)}, u32[]{:S(2)}) collective-permute-start(f32[128,1,128]{2,1,0:T(1,128)S(1)} %get-tuple-element.13), channel_id=1, source_target_pairs={{0,32},{32,64},{64,96},{1,33},{33,65},{65,97},{2,34},{34,66},{66,9... | collective-permute-start | bytes 196616 | tf_op jit(solution)/shard_map/ppermute | solution.py:91
  12.8 1.1 slice_bitcast_fusion
  15.1 6.7 %shard_map.73 = (f32[128,32,128]{2,1,0:T(8,128)}, f32[128,1,128]{2,1,0:T(1,128)}, f32[128,1,128]{2,1,0:T(1,128)}, f32[2,4096]{1,0:T(2,128)}) custom-call(f32[128,32,128]{2,1,0:T(8,128)} %bitcast.51, f32[128,1,128]{2,1,0:T(1,128)} %copy-done.7, f32[128,1,128]{2,1,0:T(1,128)} %copy-done.8, f32[4,32,32]{2,1,0:T(8,128)} %copy-done.4, f32[4,32,32]{2,1,0:T(8,128)} %copy-done.5, ...), custom_call_target="tpu_custom_call" | custom-call | flops 10485760 | bytes 5767168 | tf_op jit(solution)/shard_map/pallas_call | solution.py:72
  21.9 0.9 slice_reduce_fusion
  23.0 4.1 %collective-permute-start.6 = (f32[4,32,32]{2,1,0:T(8,128)S(1)}, f32[4,32,32]{2,1,0:T(8,128)S(1)}, u32[]{:S(2)}, u32[]{:S(2)}) collective-permute-start(f32[4,32,32]{2,1,0:T(8,128)S(1)} %bitcast.62), channel_id=1, source_target_pairs={{1,0},{2,1},{3,2},{4,3},{5,4},{6,5},{7,6},{8,7},{9,8},{10,9},{11,1... | collective-permute-start | bytes 49160 | tf_op jit(solution)/shard_map/ppermute | solution.py:92
  27.3 1.3 collective-permute-start.4
  28.6 4.6 %collective-permute-start.5 = (f32[128,1,128]{2,1,0:T(1,128)}, f32[128,1,128]{2,1,0:T(1,128)S(1)}, u32[]{:S(2)}, u32[]{:S(2)}) collective-permute-start(f32[128,1,128]{2,1,0:T(1,128)} %get-tuple-element.17), channel_id=1, source_target_pairs={{0,32},{32,64},{64,96},{1,33},{33,65},{65,97},{2,34},{34,66},{66,9... | collective-permute-start | bytes 196616 | tf_op jit(solution)/shard_map/ppermute | solution.py:91
  33.9 1.0 collective-permute-done.5.hs_ref
  35.5 6.0 %shard_map.74.cur_ref = f32[128,32,128]{2,1,0:T(8,128)} custom-call(f32[128,32,128]{2,1,0:T(8,128)} %get-tuple-element.15.q_ref, f32[128,1,128]{2,1,0:T(1,128)} %copy-done.10, f32[128,1,128]{2,1,0:T(1,128)} %copy-done.11, f32[4,32,32]{2,1,0:T(8,128)} %copy-done.6, f32[4,32,32]{2,1,0:T(8,128)} %copy-done.9, f32[32,32,128]{2,1,0:T(8,128)} %get-tuple-element.26.u_ref, ...), custom_call_target="tpu_custom_call" | custom-call | flops 10485760 | bytes 5767168 | tf_op jit(solution)/shard_map/pallas_call | solution.py:72
  41.4 8.8 %shard_map.75 = bf16[8192,128]{1,0:T(8,128)(2,1)} custom-call(s32[4096]{0:T(1024)} %bitcast_add_fusion.t_ref, f32[128,32,128]{2,1,0:T(8,128)} %shard_map.74.cur_ref), custom_call_target="tpu_custom_call" | custom-call | tf_op jit(solution)/shard_map/pallas_call | solution.py:290
  50.3 10.6 %all-to-all-start = ((bf16[128,32,256]{0,2,1:T(8,128)(2,1)}), bf16[128,32,256]{0,2,1:T(8,128)(2,1)S(1)}, u32[]{:S(2)}, u32[]{:S(2)}) async-start(bf16[128,32,256]{0,2,1:T(8,128)(2,1)} %bitcast.54), calls=%async_computation | async-start | bytes 4194304 | tf_op jit(solution)/shard_map/all_to_all | solution.py:362
  60.9 2.7 %copy.23 = bf16[1,3,512,512]{2,3,1,0:T(8,128)(2,1)} copy(bf16[1,3,512,512]{3,2,1,0:T(8,128)(2,1)} %param.12) | data formatting | bytes 3145728 | tf_op args[5]
  63.5 0.8 copy.22
  64.3 0.8 copy.24
  65.1 24.1 %all-to-all-done = bf16[128,32,256]{0,2,1:T(8,128)(2,1)S(1)} async-done(((bf16[128,32,256]{0,2,1:T(8,128)(2,1)}), bf16[128,32,256]{0,2,1:T(8,128)(2,1)S(1)}, u32[]{:S(2)}, u32[]{:S(2)}) %all-to-all-start) | async-done | bytes 2097184 | tf_op jit(solution)/shard_map/all_to_all | solution.py:362
  89.1 1.2 compare_reduce_fusion
  90.9 18.5 %shard_map.76 = bf16[8192,128]{1,0:T(8,128)(2,1)} custom-call(s32[64]{0:T(128)} %convert_element_type.23.nonzero_ref, bf16[8192,128]{1,0:T(8,128)(2,1)} %bitcast.53, bf16[128,512]{1,0:T(8,128)(2,1)} %bitcast.57, bf16[3,512,512]{2,1,0:T(8,128)(2,1)} %bitcast.56, bf16[512,128]{1,0:T(8,128)(2,1)} %bitcast.58), custom_call_target="tpu_custom_call" | custom-call | flops 15032385536 | bytes 6029312 | tf_op jit(solution)/shard_map/pallas_call | solution.py:238
  109.5 39.4 %all_to_all.10 = bf16[128,32,256]{0,2,1:T(8,128)(2,1)} all-to-all(bf16[128,32,256]{0,2,1:T(8,128)(2,1)} %bitcast.55), channel_id=1, replica_groups=mesh['lat'=4,'lon'=32] {'lon'}, dimensions={1} | all-to-all | bytes 4194304 | tf_op jit(solution)/shard_map/all_to_all | solution.py:366
  148.9 10.3 %shard_map.77 = f32[128,32,128]{2,1,0:T(8,128)} custom-call(s32[4096]{0:T(1024)} %bitcast_add_fusion.t_ref, bf16[8192,128]{1,0:T(8,128)(2,1)} %bitcast.52, f32[128,32,128]{2,1,0:T(8,128)} %shard_map.74.cur_ref), custom_call_target="tpu_custom_call" | custom-call | tf_op jit(solution)/shard_map/pallas_call | solution.py:321
  (52 shorter events, 3.9 us)
Async XLA Ops:
  0.0 12.8 %copy-start.1 = (f32[2,32,32,128]{3,2,1,0:T(8,128)S(1)}, f32[2,32,32,128]{3,2,1,0:T(8,128)}, u32[]{:S(2)}) copy-start(f32[2,32,32,128]{3,2,1,0:T(8,128)} %param.8) | copy-start | bytes 3145732
  1.4 12.5 %copy-start.12 = (s32[1,4096,1]{1,2,0:T(1,128)S(1)}, s32[1,4096,1]{1,2,0:T(1,128)}, u32[]{:S(2)}) copy-start(s32[1,4096,1]{1,2,0:T(1,128)} %param.10) | copy-start | bytes 49156
  4.3 10.1 %collective-permute-start.2 = (f32[4,32,32]{2,1,0:T(8,128)S(1)}, f32[4,32,32]{2,1,0:T(8,128)S(1)}, u32[]{:S(2)}, u32[]{:S(2)}) collective-permute-start(f32[4,32,32]{2,1,0:T(8,128)S(1)} %bitcast.60), channel_id=1, source_target_pairs={{1,0},{2,1},{3,2},{4,3},{5,4},{6,5},{7,6},{8,7},{9,8},{10,9},{11,1... | collective-permute-start | bytes 49160 | tf_op jit(solution)/shard_map/ppermute | solution.py:92
  6.0 8.5 %collective-permute-start.3 = (f32[4,32,32]{2,1,0:T(8,128)S(1)}, f32[4,32,32]{2,1,0:T(8,128)S(1)}, u32[]{:S(2)}, u32[]{:S(2)}) collective-permute-start(f32[4,32,32]{2,1,0:T(8,128)S(1)} %bitcast.61), channel_id=1, source_target_pairs={{0,1},{1,2},{2,3},{3,4},{4,5},{5,6},{6,7},{7,8},{8,9},{9,10},{10,1... | collective-permute-start | bytes 49160 | tf_op jit(solution)/shard_map/ppermute | solution.py:93
  7.3 7.2 %collective-permute-start = (f32[128,1,128]{2,1,0:T(1,128)S(1)}, f32[128,1,128]{2,1,0:T(1,128)S(1)}, u32[]{:S(2)}, u32[]{:S(2)}) collective-permute-start(f32[128,1,128]{2,1,0:T(1,128)S(1)} %get-tuple-element.12), channel_id=1, source_target_pairs={{32,0},{64,32},{96,64},{33,1},{65,33},{97,65},{34,2},{66,34},{98,6... | collective-permute-start | bytes 196616 | tf_op jit(solution)/shard_map/ppermute | solution.py:90
  8.6 5.9 %collective-permute-start.1 = (f32[128,1,128]{2,1,0:T(1,128)S(1)}, f32[128,1,128]{2,1,0:T(1,128)S(1)}, u32[]{:S(2)}, u32[]{:S(2)}) collective-permute-start(f32[128,1,128]{2,1,0:T(1,128)S(1)} %get-tuple-element.13), channel_id=1, source_target_pairs={{0,32},{32,64},{64,96},{1,33},{33,65},{65,97},{2,34},{34,66},{66,9... | collective-permute-start | bytes 196616 | tf_op jit(solution)/shard_map/ppermute | solution.py:91
  14.5 0.6 copy-start.4
  14.5 0.6 copy-start.5
  14.5 0.6 copy-start.7
  14.5 0.6 copy-start.8
  23.0 10.8 %collective-permute-start.6 = (f32[4,32,32]{2,1,0:T(8,128)S(1)}, f32[4,32,32]{2,1,0:T(8,128)S(1)}, u32[]{:S(2)}, u32[]{:S(2)}) collective-permute-start(f32[4,32,32]{2,1,0:T(8,128)S(1)} %bitcast.62), channel_id=1, source_target_pairs={{1,0},{2,1},{3,2},{4,3},{5,4},{6,5},{7,6},{8,7},{9,8},{10,9},{11,1... | collective-permute-start | bytes 49160 | tf_op jit(solution)/shard_map/ppermute | solution.py:92
  27.2 6.6 %collective-permute-start.7 = (f32[4,32,32]{2,1,0:T(8,128)S(1)}, f32[4,32,32]{2,1,0:T(8,128)S(1)}, u32[]{:S(2)}, u32[]{:S(2)}) collective-permute-start(f32[4,32,32]{2,1,0:T(8,128)S(1)} %bitcast.63), channel_id=1, source_target_pairs={{0,1},{1,2},{2,3},{3,4},{4,5},{5,6},{6,7},{7,8},{8,9},{9,10},{10,1... | collective-permute-start | bytes 49160 | tf_op jit(solution)/shard_map/ppermute | solution.py:93
  27.3 6.6 %collective-permute-start.4 = (f32[128,1,128]{2,1,0:T(1,128)}, f32[128,1,128]{2,1,0:T(1,128)S(1)}, u32[]{:S(2)}, u32[]{:S(2)}) collective-permute-start(f32[128,1,128]{2,1,0:T(1,128)} %get-tuple-element.16), channel_id=1, source_target_pairs={{32,0},{64,32},{96,64},{33,1},{65,33},{97,65},{34,2},{66,34},{98,6... | collective-permute-start | bytes 196616 | tf_op jit(solution)/shard_map/ppermute | solution.py:90
  28.6 6.2 %collective-permute-start.5 = (f32[128,1,128]{2,1,0:T(1,128)}, f32[128,1,128]{2,1,0:T(1,128)S(1)}, u32[]{:S(2)}, u32[]{:S(2)}) collective-permute-start(f32[128,1,128]{2,1,0:T(1,128)} %get-tuple-element.17), channel_id=1, source_target_pairs={{0,32},{32,64},{64,96},{1,33},{33,65},{65,97},{2,34},{34,66},{66,9... | collective-permute-start | bytes 196616 | tf_op jit(solution)/shard_map/ppermute | solution.py:91
  33.8 1.0 copy-start.6
  33.8 1.0 copy-start.9
  33.9 1.0 copy-start.10
  34.9 0.6 copy-start.11
  50.3 38.9 %all-to-all-start = ((bf16[128,32,256]{0,2,1:T(8,128)(2,1)}), bf16[128,32,256]{0,2,1:T(8,128)(2,1)S(1)}, u32[]{:S(2)}, u32[]{:S(2)}) async-start(bf16[128,32,256]{0,2,1:T(8,128)(2,1)} %bitcast.54), calls=%async_computation | async-start | bytes 4194304 | tf_op jit(solution)/shard_map/all_to_all | solution.py:362
  60.8 2.7 %copy-start.2 = (bf16[1,512,128]{2,1,0:T(8,128)(2,1)S(1)}, bf16[1,512,128]{2,1,0:T(8,128)(2,1)}, u32[]{:S(2)}) copy-start(bf16[1,512,128]{2,1,0:T(8,128)(2,1)} %param.11) | copy-start | bytes 393220
  60.9 3.5 %copy-start.3 = (bf16[1,128,512]{2,1,0:T(8,128)(2,1)S(1)}, bf16[1,128,512]{2,1,0:T(8,128)(2,1)}, u32[]{:S(2)}) copy-start(bf16[1,128,512]{2,1,0:T(8,128)(2,1)} %param.13) | copy-start | bytes 393220
  89.1 1.8 %copy-start = (bf16[128,32,256]{0,2,1:T(8,128)(2,1)}, bf16[128,32,256]{0,2,1:T(8,128)(2,1)S(1)}, u32[]{:S(2)}) copy-start(bf16[128,32,256]{0,2,1:T(8,128)(2,1)S(1)} %all-to-all-done) | copy-start | bytes 6291460
